TPU v7x, 128 devices: a whole 4x4x4 slice. The times are simulated.
128 devices in a mesh: dom: 8 (over y, core), fsdp: 16 (over z, x).
Axes of the slice: x: 4, y: 4, z: 4, core: 2. Of those that a mesh axis runs over, the one named last changes fastest.
Arguments:
- features: bfloat16 [512, 1024, 128], P(('dom', 'fsdp')), may hold values from -24 to 24
- history_first: bfloat16 [1024, 1024, 128], P('dom', 'fsdp'), may hold values from -6 to 6
- history_second: bfloat16 [1024, 1024, 128], P('dom', 'fsdp'), may hold values from -3 to 3
- pull_list: int32 [8, 128, 4], P('dom'), may hold values from 0 to 127
- pull_count: int32 [8, 128], P('dom'), may hold values from 1 to 4, as said below
- tile_src: int32 [512, 6], P(('dom', 'fsdp')), may hold values from 0 to 35
- tile_count: int32 [512], P(('dom', 'fsdp')), may hold values from 1 to 6
- tile_values: bfloat16 [512, 6, 128, 128], P(('dom', 'fsdp')), may hold values from -0.21875 to 0.21875
- w_first: bfloat16 [1024, 1024], P('fsdp'), may hold values from -0.1875 to 0.1875
- w_second: bfloat16 [1024, 1024], P('fsdp'), may hold values from -0.1875 to 0.1875
- bias_first: bfloat16 [1024], P('fsdp'), may hold values from -3 to 3
- out_grad: bfloat16 [512, 1024, 128], P(('dom', 'fsdp')), may hold values from -0.0625 to 0.0625
Outputs:
- hidden_new: bfloat16 [512, 1024, 128], P(('dom', 'fsdp'))
- grad_w1: float32 [1024, 1024], P('fsdp')
- grad_w2: float32 [1024, 1024], P('fsdp')
- grad_b1: float32 [1024], P('fsdp')
Inputs may be any that keep to these rules, and one draw needn't show every extreme that they name: pull_list[o, q, c] numbers a block within partition o. Slot c of list (o, q) is live when c < pull_count[o, q]; every device q has 4 live slots from at least one partition. tile_src below 4 names one of the device's own batch blocks; 4 + s names its pulled slot s.
All inputs are finite; a program needn't handle non-finite values.
Results may differ from a plain program's by a relative error of at most 0.0075.
Values may be sent and summed in bfloat16 or wider, within the bound.
No kernel may reach another device: no remote copies, remote signals or barrier semaphores. Data moves between devices by JAX's collectives and lax.ppermute only.
A program may use at most 192 MiB of HBM per device.

v0:
```python
import jax
import jax.numpy as jnp
from jax import lax
from jax.sharding import PartitionSpec as P


def gelu_tanh(inputs):
    return jax.nn.gelu(inputs, approximate=True)


def pull_rows(table, chosen, is_live):
    taken = jnp.take(table, chosen.reshape(-1), axis=0)
    taken = taken.reshape(chosen.shape + table.shape[1:])
    return jnp.where(is_live[:, :, None, None], taken, jnp.zeros((), table.dtype))


def aggregate(sources, source_ids, tile_live, tile_vals):
    running = jnp.zeros((source_ids.shape[0], sources.shape[1], sources.shape[2]), jnp.float32)
    for tile_slot in range(source_ids.shape[1]):
        blocks = jnp.take(sources, source_ids[:, tile_slot], axis=0)
        product = jnp.einsum(
            "vfj,vji->vfi", blocks, tile_vals[:, tile_slot], preferred_element_type=jnp.float32
        )
        running = running + jnp.where(tile_live[:, tile_slot][:, None, None], product, 0.0)
    return running


def spread_back(back_second, source_ids, tile_live, tile_vals):
    batch_count = back_second.shape[0]
    targets = lax.broadcasted_iota(jnp.int32, (batch_count, batch_count), 1)
    running = jnp.zeros(back_second.shape, jnp.float32)
    for tile_slot in range(source_ids.shape[1]):
        product = jnp.einsum(
            "vai,vji->vaj", back_second, tile_vals[:, tile_slot], preferred_element_type=jnp.float32
        )
        matches = jnp.where(
            (source_ids[:, tile_slot][:, None] == targets) & tile_live[:, tile_slot][:, None],
            1.0,
            0.0,
        ).astype(jnp.float32)
        running = running + jnp.einsum(
            "vu,vaj->uaj", matches, product, precision=lax.Precision.HIGHEST
        )
    return running


def on_device(
    features,
    history_first,
    history_second,
    pull_list,
    pull_count,
    tile_src,
    tile_count,
    tile_values,
    w_first,
    w_second,
    bias_first,
    out_grad,
):
    first_full, second_full, bias_full = (
        lax.all_gather(w_first, "fsdp", axis=0, tiled=True),
        lax.all_gather(w_second, "fsdp", axis=0, tiled=True),
        lax.all_gather(bias_first, "fsdp", axis=0, tiled=True),
    )
    dom_size = lax.axis_size("dom")
    fsdp_size = lax.axis_size("fsdp")
    chosen = pull_list[0]
    requesters = chosen.shape[0]
    slot_cap = chosen.shape[1]
    is_live = lax.broadcasted_iota(jnp.int32, chosen.shape, 1) < pull_count[0][:, None]
    sent_first = pull_rows(history_first, chosen, is_live)
    sent_second = pull_rows(history_second, chosen, is_live)
    block_len = features.shape[2]
    first_cols = history_first.shape[1]
    second_cols = history_second.shape[1]
    arrived_first, arrived_second = (
        lax.all_to_all(
            sent_first.reshape(requesters, slot_cap, 1, first_cols, block_len),
            ("dom", "fsdp"),
            split_axis=0,
            concat_axis=2,
            tiled=True,
        ),
        lax.all_to_all(
            sent_second.reshape(requesters, slot_cap, 1, second_cols, block_len),
            ("dom", "fsdp"),
            split_axis=0,
            concat_axis=2,
            tiled=True,
        ),
    )
    pulled_first = arrived_first.reshape(slot_cap * dom_size, fsdp_size * first_cols, block_len)
    pulled_second = arrived_second.reshape(slot_cap * dom_size, fsdp_size * second_cols, block_len)
    tile_live = lax.broadcasted_iota(jnp.int32, tile_src.shape, 1) < tile_count[:, None]
    agg_first = aggregate(
        jnp.concatenate([features, pulled_first], 0), tile_src, tile_live, tile_values
    ).astype(jnp.bfloat16)
    pre_act = (
        jnp.einsum("fh,vfn->vhn", first_full, agg_first, preferred_element_type=jnp.float32)
        + bias_full.astype(jnp.float32)[None, :, None]
    )
    hidden_new = gelu_tanh(pre_act).astype(jnp.bfloat16)
    agg_second = aggregate(
        jnp.concatenate([hidden_new, pulled_second], 0), tile_src, tile_live, tile_values
    ).astype(jnp.bfloat16)
    back_second = jnp.einsum(
        "ab,vbn->van", second_full, out_grad, preferred_element_type=jnp.float32
    ).astype(jnp.bfloat16)
    back_hidden = spread_back(back_second, tile_src, tile_live, tile_values)
    _, pullback = jax.vjp(gelu_tanh, pre_act)
    back_pre = pullback(back_hidden)[0].astype(jnp.bfloat16)
    first_term = jnp.einsum("vfn,vhn->fh", agg_first, back_pre, preferred_element_type=jnp.float32)
    bias_term = jnp.sum(back_pre.astype(jnp.float32), axis=(0, 2))
    second_term = jnp.einsum(
        "van,vbn->ab", agg_second, out_grad, preferred_element_type=jnp.float32
    )
    first_shard, second_shard, bias_shard = (
        lax.psum_scatter(first_term, "fsdp", scatter_dimension=0, tiled=True),
        lax.psum_scatter(second_term, "fsdp", scatter_dimension=0, tiled=True),
        lax.psum_scatter(bias_term, "fsdp", scatter_dimension=0, tiled=True),
    )
    first_total, second_total, bias_total = lax.psum((first_shard, second_shard, bias_shard), "dom")
    return (hidden_new, first_total, second_total, bias_total)


def solution(mesh):
    return jax.shard_map(
        on_device,
        mesh=mesh,
        in_specs=(
            P(("dom", "fsdp"), None, None),
            P("dom", "fsdp", None),
            P("dom", "fsdp", None),
            P("dom", None, None),
            P("dom", None),
            P(("dom", "fsdp"), None),
            P(("dom", "fsdp")),
            P(("dom", "fsdp"), None, None, None),
            P("fsdp", None),
            P("fsdp", None),
            P("fsdp"),
            P(("dom", "fsdp"), None, None),
        ),
        out_specs=(P(("dom", "fsdp"), None, None), P("fsdp", None), P("fsdp", None), P("fsdp")),
        check_vma=False,
    )
```

profile of v0, /device:TPU:1, one launch (start us, length us, event | category | flops | bytes accessed | tf_op | source)
XLA Modules:
  0.0 652.3 jit_solution(17746432183007675651)
XLA Ops:
  8.8 13.4 %gather_fusion = bf16[512,64,128]{2,1,0:T(8,128)(2,1)} fusion(bf16[128,64,128]{2,1,0:T(8,128)(2,1)S(1)} %copy-done, s32[1024]{0:T(1024)S(1)} %pad_clamp_fusion.6), kind=kCustom, calls=%fused_computation.clone | custom fusion | bytes 16779264 | tf_op jit(solution)/shard_map/jit(_take)/gather | solution.py:12
  22.2 21.2 %gather_fusion.7 = bf16[512,64,128]{2,1,0:T(8,128)(2,1)} fusion(bf16[128,64,128]{2,1,0:T(8,128)(2,1)} %param.18, s32[1024]{0:T(1024)S(1)} %pad_clamp_fusion.6), kind=kCustom, calls=%fused_computation.2.clone | custom fusion | bytes 16779264 | tf_op jit(solution)/shard_map/jit(_take)/gather | solution.py:12
  43.6 7.2 %broadcast_select_fusion = (bf16[512,64,128]{2,1,0:T(8,128)(2,1)S(1)}, bf16[512,64,128]{2,1,0:T(8,128)(2,1)S(1)}) fusion(bf16[512,64,128]{2,1,0:T(8,128)(2,1)} %gather_fusion.7, pred[512]{0:T(512)(128)(4,1)S(1)} %compare_and_fusion.6, bf16[512,64,128]{2,1,0:T(8,128)(2,1)} %gather_fusion), kind=kLoop, calls=%fused_computation.18 | loop fusion | flops 8388608 | bytes 33554944 | tf_op jit(solution)/shard_map/jit(_take)/select_n | solution.py:12
  50.8 6.2 select_bitcast_fusion
  56.9 12.0 %all-to-all-start = ((bf16[128,4,1,64,128]{4,3,1,2,0:T(8,128)(2,1)}), bf16[128,4,1,64,128]{4,3,1,2,0:T(8,128)(2,1)}, u32[]{:S(2)}, u32[]{:S(2)}) async-start(bf16[128,4,1,64,128]{4,3,1,2,0:T(8,128)(2,1)} %get-tuple-element.34), calls=%async_computation | async-start | bytes 16777216 | tf_op jit(solution)/shard_map/all_to_all | solution.py:78
  71.9 118.4 %all-reduce = bf16[1024]{0:T(1024)(128)(2,1)S(1)} all-reduce(bf16[1024]{0:T(1024)(128)(2,1)S(1)} %dynamic-update-slice), channel_id=1, replica_groups=mesh['dom'=8,'fsdp'=16] {'fsdp'}, use_global_device_ids=true, to_apply=%add | all-reduce | flops 1024 | bytes 4096
  190.8 17.9 %all-to-all-start.1 = ((bf16[128,4,1,64,128]{4,3,1,2,0:T(8,128)(2,1)}), bf16[128,4,1,64,128]{4,3,1,2,0:T(8,128)(2,1)}, u32[]{:S(2)}, u32[]{:S(2)}) async-start(bf16[128,4,1,64,128]{4,3,1,2,0:T(8,128)(2,1)} %get-tuple-element.33), calls=%async_computation.2 | async-start | bytes 16777216 | tf_op jit(solution)/shard_map/all_to_all | solution.py:85
  213.2 8.3 %fusion.20 = f32[4,1024,128]{2,0,1:T(4,128)} fusion(f32[4,1024,128]{2,1,0:T(8,128)S(1)} %fusion.99, s32[4]{0:T(128)S(1)} %get-tuple-element.24, pred[4]{0:T(512)(128)(4,1)S(1)} %get-tuple-element.39), kind=kOutput, calls=%fused_computation.46 | convolution fusion | flops 25165872 | bytes 4194324 | tf_op jit(solution)/shard_map/vu,vaj->uaj/dot_general | solution.py:41
  225.9 8.3 %fusion.18 = f32[4,1024,128]{2,0,1:T(4,128)} fusion(f32[4,1024,128]{2,1,0:T(8,128)S(1)} %fusion.95, s32[4]{0:T(128)S(1)} %get-tuple-element.23, pred[4]{0:T(512)(128)(4,1)S(1)} %get-tuple-element.38), kind=kOutput, calls=%fused_computation.44 | convolution fusion | flops 25165872 | bytes 4194324 | tf_op jit(solution)/shard_map/vu,vaj->uaj/dot_general | solution.py:41
  238.6 8.7 %fusion.16 = f32[4,1024,128]{2,0,1:T(4,128)} fusion(f32[4,1024,128]{2,1,0:T(8,128)S(1)} %fusion.91, s32[4]{0:T(128)S(1)} %get-tuple-element.27, pred[4]{0:T(512)(128)(4,1)S(1)} %get-tuple-element.37), kind=kOutput, calls=%fused_computation.42 | convolution fusion | flops 25165872 | bytes 4194324 | tf_op jit(solution)/shard_map/vu,vaj->uaj/dot_general | solution.py:41
  251.7 8.3 %fusion.14 = f32[4,1024,128]{2,0,1:T(4,128)} fusion(f32[4,1024,128]{2,1,0:T(8,128)S(1)} %fusion.87, s32[4]{0:T(128)S(1)} %get-tuple-element.22, pred[4]{0:T(512)(128)(4,1)S(1)} %get-tuple-element.36), kind=kOutput, calls=%fused_computation.40 | convolution fusion | flops 25165872 | bytes 4194324 | tf_op jit(solution)/shard_map/vu,vaj->uaj/dot_general | solution.py:41
  264.4 8.5 %fusion.24 = f32[4,1024,128]{2,0,1:T(4,128)} fusion(f32[4,1024,128]{2,1,0:T(8,128)S(1)} %fusion.107, s32[4]{0:T(128)S(1)} %get-tuple-element.26, pred[4]{0:T(512)(128)(4,1)S(1)} %get-tuple-element.35), kind=kOutput, calls=%fused_computation.50 | convolution fusion | flops 25165872 | bytes 4194324 | tf_op jit(solution)/shard_map/vu,vaj->uaj/dot_general | solution.py:41
  277.3 7.3 %fusion.22 = f32[4,1024,128]{2,0,1:T(4,128)S(1)} fusion(f32[4,1024,128]{2,1,0:T(8,128)S(1)} %fusion.103, s32[4]{0:T(128)S(1)} %get-tuple-element.25, pred[4]{0:T(512)(128)(4,1)S(1)} %get-tuple-element.40), kind=kOutput, calls=%fused_computation.48 | convolution fusion | flops 25165872 | bytes 4194324 | tf_op jit(solution)/shard_map/vu,vaj->uaj/dot_general | solution.py:41
  286.7 9.5 %copy.85 = bf16[128,4,1,64,128]{4,3,0,1,2:T(8,128)(2,1)} copy(bf16[128,4,1,64,128]{4,3,1,2,0:T(8,128)(2,1)} %all-to-all-done) | data formatting | bytes 16777216 | tf_op jit(solution)/shard_map/all_to_all | solution.py:78
  296.2 7.8 %pad_maximum_fusion = bf16[36,1024,128]{2,1,0:T(8,128)(2,1)} fusion(bf16[32,1024,128]{2,1,0:T(8,128)(2,1)} %bitcast.149, bf16[4,1024,128]{2,1,0:T(8,128)(2,1)S(1)} %copy-done.14), kind=kLoop, calls=%fused_computation.14 | loop fusion | flops 4718592 | bytes 18874368 | tf_op jit(solution)/shard_map/concatenate | solution.py:97
  344.2 9.5 %convert_reduce_fusion = (f32[1024]{0:T(1024)S(1)}, bf16[4,1024,128]{1,2,0:T(8,128)(2,1)}, bf16[4,1024,128]{1,2,0:T(8,128)(2,1)S(1)}) fusion(f32[1024]{0:T(1024)S(1)} %convert_element_type.23, f32[4,1024,128]{1,2,0:T(8,128)} %copy.111, f32[4,1024,128]{1,2,0:T(8,128)} %copy.108, f32[4,1024,128]{1,2,0:T(8,128)} %copy.105, f32[4,1024,128]{1,2,0:T(8,128)} %copy.102, ...), kind=kOutput, calls=%fused_computation.52 | convolution fusion | flops 1089469440 | bytes 17833984 | tf_op jit(solution)/shard_map/fh,vfn->vhn/dot_general | solution.py:100
  354.6 9.8 %copy.114 = bf16[128,4,1,64,128]{4,3,0,1,2:T(8,128)(2,1)} copy(bf16[128,4,1,64,128]{4,3,1,2,0:T(8,128)(2,1)} %all-to-all-done.1) | data formatting | bytes 16777216 | tf_op jit(solution)/shard_map/all_to_all | solution.py:85
  364.5 7.8 %pad_maximum_fusion.1 = bf16[36,1024,128]{2,1,0:T(8,128)(2,1)} fusion(bf16[32,1024,128]{2,1,0:T(8,128)(2,1)} %bitcast.150, bf16[4,1024,128]{2,1,0:T(8,128)(2,1)S(1)} %copy.116), kind=kLoop, calls=%fused_computation.15 | loop fusion | flops 4718592 | bytes 18874368 | tf_op jit(solution)/shard_map/concatenate | solution.py:105
  413.5 7.9 %convolution_bitcast_fusion = f32[1024,1024]{1,0:T(8,128)} fusion(bf16[4,1024,128]{2,1,0:T(8,128)(2,1)} %param.27, f32[4,1024,128]{2,1,0:T(8,128)} %fusion.31, f32[4,1024,128]{2,1,0:T(8,128)S(1)} %fusion.33, f32[4,1024,128]{2,1,0:T(8,128)} %fusion.35, f32[4,1024,128]{2,1,0:T(8,128)} %fusion.37, f32[4,1024,128]{2,1,0:T(8,128)} %fusion.39, ...), kind=kOutput, calls=%fused_computation.22 | convolution fusion | flops 1214775296 | bytes 16911872 | tf_op jit(solution)/shard_map/van,vbn->ab/dot_general | solution.py:115
  426.3 73.0 %reduce-scatter.5.cloned.1.call-done = f32[64,1024]{1,0:T(8,128)} async-done(((f32[1024,1024]{1,0:T(8,128)}), f32[64,1024]{1,0:T(8,128)}) %reduce-scatter.5.cloned.1.call-update) | async-done | bytes 262160 | tf_op jit(solution)/shard_map/reduce_scatter | solution.py:120
  499.3 80.6 %reduce-scatter.3.cloned.1.call-done = f32[64,1024]{1,0:T(8,128)} async-done(((f32[1024,1024]{1,0:T(8,128)}), f32[64,1024]{1,0:T(8,128)}) %reduce-scatter.3.cloned.1.call-update) | async-done | bytes 262160 | tf_op jit(solution)/shard_map/reduce_scatter | solution.py:119
  580.5 31.0 %all-reduce.1 = f32[1024]{0:T(1024)S(1)} all-reduce(f32[1024]{0:T(1024)S(1)} %get-tuple-element.30), channel_id=4, replica_groups=mesh['dom'=8,'fsdp'=16] {'fsdp'}, use_global_device_ids=true, to_apply=%region_5.8.clone | all-reduce | flops 1024 | bytes 8192
  611.6 21.8 %psum.23 = f32[64]{0:T(128)} all-reduce(f32[64]{0:T(128)S(1)} %dynamic-slice.2), channel_id=1, replica_groups=mesh['dom'=8,'fsdp'=16] {'dom'}, use_global_device_ids=true, to_apply=%region_6.9 | all-reduce | flops 64 | bytes 512 | tf_op jit(solution)/shard_map/psum | solution.py:123
  633.4 8.6 %all-reduce.5.cloned.1.call-done = (f32[64,1024]{1,0:T(8,128)}, f32[64,1024]{1,0:T(8,128)}) async-done(((f32[64,1024]{1,0:T(8,128)}, f32[64,1024]{1,0:T(8,128)}), (f32[64,1024]{1,0:T(8,128)}, f32[64,1024]{1,0:T(8,128)})) %all-reduce.5.cloned.1.call-update) | async-done | bytes 524304 | tf_op jit(solution)/shard_map/psum | solution.py:123
  (125 shorter events, 123.1 us)
Async XLA Ops:
  7.2 1.6 copy-start
  22.2 21.3 %copy-start.19 = (s32[1,128]{1,0:T(1,128)S(1)}, s32[1,128]{1,0:T(1,128)}, u32[]{:S(2)}) copy-start(s32[1,128]{1,0:T(1,128)} %param.20) | copy-start | bytes 1540
  56.9 13.5 %copy-start.18 = (u32[128]{0:T(128)S(1)}, u32[128]{0:T(128)}, u32[]{:S(2)}) copy-start(u32[128]{0:T(128)} %constant.46) | copy-start | bytes 1540
  56.9 14.7 %copy-start.20 = (bf16[64]{0:T(256)(128)(2,1)S(1)}, bf16[64]{0:T(256)(128)(2,1)}, u32[]{:S(2)}) copy-start(bf16[64]{0:T(256)(128)(2,1)} %param.26) | copy-start | bytes 388
  56.9 133.4 %copy-start.17 = (s32[4,6]{1,0:T(4,128)S(1)}, s32[4,6]{1,0:T(4,128)}, u32[]{:S(2)}) copy-start(s32[4,6]{1,0:T(4,128)} %param.21) | copy-start | bytes 292
  56.9 133.8 %copy-start.21 = (s32[4]{0:T(128)S(1)}, s32[4]{0:T(128)}, u32[]{:S(2)}) copy-start(s32[4]{0:T(128)} %param.22) | copy-start | bytes 52
  56.9 133.9 %all-to-all-start = ((bf16[128,4,1,64,128]{4,3,1,2,0:T(8,128)(2,1)}), bf16[128,4,1,64,128]{4,3,1,2,0:T(8,128)(2,1)}, u32[]{:S(2)}, u32[]{:S(2)}) async-start(bf16[128,4,1,64,128]{4,3,1,2,0:T(8,128)(2,1)} %get-tuple-element.34), calls=%async_computation | async-start | bytes 16777216 | tf_op jit(solution)/shard_map/all_to_all | solution.py:78
  68.9 139.9 %all-gather.5.cloned.1.call-start = ((), (), s32[]{:S(2)}) async-start(), calls=%async_computation.5 | async-start | bytes 2228224 | tf_op jit(solution)/shard_map/all_gather | solution.py:63
  69.6 274.5 %all-gather.3.cloned.1.call-start = ((), (), s32[]{:S(2)}) async-start(), calls=%async_computation.4 | async-start | bytes 2228224 | tf_op jit(solution)/shard_map/all_gather | solution.py:62
  190.8 18.0 %copy-start.16 = (bf16[4,1024,128]{2,1,0:T(8,128)(2,1)S(1)}, bf16[4,1024,128]{2,1,0:T(8,128)(2,1)}, u32[]{:S(2)}) copy-start(bf16[4,1024,128]{2,1,0:T(8,128)(2,1)} %param.27) | copy-start | bytes 3145732
  190.8 163.8 %all-to-all-start.1 = ((bf16[128,4,1,64,128]{4,3,1,2,0:T(8,128)(2,1)}), bf16[128,4,1,64,128]{4,3,1,2,0:T(8,128)(2,1)}, u32[]{:S(2)}, u32[]{:S(2)}) async-start(bf16[128,4,1,64,128]{4,3,1,2,0:T(8,128)(2,1)} %get-tuple-element.33), calls=%async_computation.2 | async-start | bytes 16777216 | tf_op jit(solution)/shard_map/all_to_all | solution.py:85
  208.7 290.6 %reduce-scatter.5.cloned.1.call-start = ((), (), s32[]{:S(2)}) async-start(), calls=%async_computation.7 | async-start | bytes 4456448 | tf_op jit(solution)/shard_map/reduce_scatter | solution.py:120
  286.7 9.5 %copy-start.14 = (bf16[4,1024,128]{2,1,0:T(8,128)(2,1)S(1)}, bf16[4,1024,128]{2,1,0:T(8,128)(2,1)}, u32[]{:S(2)}) copy-start(bf16[4,1024,128]{2,1,0:T(8,128)(2,1)} %param.16) | copy-start | bytes 3145732
  325.4 10.8 %copy-start.2 = (bf16[4,6,128,128]{3,2,1,0:T(8,128)(2,1)S(1)}, bf16[4,6,128,128]{3,2,1,0:T(8,128)(2,1)}, u32[]{:S(2)}) copy-start(bf16[4,6,128,128]{3,2,1,0:T(8,128)(2,1)} %param.23) | copy-start | bytes 2359300
  336.2 1.8 copy-start.13
  354.6 9.9 %copy-start.5 = (bf16[4,1024,128]{2,1,0:T(8,128)(2,1)}, bf16[4,1024,128]{2,1,0:T(8,128)(2,1)S(1)}, u32[]{:S(2)}) copy-start(bf16[4,1024,128]{2,1,0:T(8,128)(2,1)S(1)} %copy.116) | copy-start | bytes 3145732
  404.4 1.8 copy-start.9
  406.2 1.8 copy-start.8
  408.0 1.8 copy-start.7
  409.9 1.9 copy-start.6
  421.4 1.5 copy-start.15
  421.5 158.4 %reduce-scatter.3.cloned.1.call-start = ((), (), s32[]{:S(2)}) async-start(), calls=%async_computation.6 | async-start | bytes 4456448 | tf_op jit(solution)/shard_map/reduce_scatter | solution.py:119
  426.2 219.1 %copy-start.1 = (bf16[128,64,128]{2,1,0:T(8,128)(2,1)S(1)}, bf16[128,64,128]{2,1,0:T(8,128)(2,1)}, u32[]{:S(2)}) copy-start(bf16[128,64,128]{2,1,0:T(8,128)(2,1)} %param.17) | copy-start | bytes 6291460
  426.2 215.7 %all-reduce.5.cloned.1.call-start = ((), (), s32[]{:S(2)}) async-start(), calls=%async_computation.8 | async-start | bytes 1048576 | tf_op jit(solution)/shard_map/psum | solution.py:123
  (5 other events, 6.2 us)
Sparse Core Ops, SparseCore 0:
  71.9 117.9 all-gather.4
  192.0 121.4 all-gather.2
  421.6 77.6 reduce-scatter.4
  502.9 76.9 reduce-scatter.2
  582.1 59.7 all-reduce.4
where the time goes:
time: 664 us; the launch traced here: 652 us
  blocking collectives  171 us (26%)
  waiting for transfers between devices  164 us (25%)
  local copies, waits for them, and re-layouts  146 us (22%)
  matrix products  96.4 us (15%)
  starting transfers between devices  30 us (5%)
  other arithmetic  29.3 us (4%)
  between operations  16 us (2%)
    unnamed x2, blocking collectives  149 us
    reduce_scatter x1, waiting for transfers between devices, on_device(): lax.psum_scatter(first_term, 'fsdp', scatter_dimension=0, tiled=True)  80.6 us
    reduce_scatter x1, waiting for transfers between devices, on_device(): lax.psum_scatter(second_term, 'fsdp', scatter_dimension=0, tiled=True)  73 us
    gather x12, local copies, waits for them, and re-layouts, aggregate(): blocks = jnp.take(sources, source_ids[:, tile_slot], axis=0)  64.3 us
    dot_general x6, matrix products, spread_back(): jnp.einsum('vu,vaj->uaj', matches, product, precision=lax.Precision.HIGHEST)  49.5 us
    gather x2, local copies, waits for them, and re-layouts, pull_rows(): taken = jnp.take(table, chosen.reshape(-1), axis=0)  34.7 us
    psum x1, blocking collectives, on_device(): lax.psum((first_shard, second_shard, bias_shard), 'dom')  21.8 us
    all_to_all x1, starting transfers between devices, on_device(): lax.all_to_all(sent_second.reshape(requesters, slot_cap, 1, second_cols,...  17.9 us
  transfers between devices with their start and end apart: 7, of which 3 were waited for; matrix products, arithmetic and copies ran while one was open for 23% of the time, Pallas kernels for 0%

commit v1 on v0

v1 whole, which is shorter than its diff:
```python
import functools

import jax
import jax.numpy as jnp
from jax import lax
from jax.experimental import pallas as pl
from jax.experimental.pallas import tpu as pltpu
from jax.sharding import PartitionSpec as P


def gelu_tanh(inputs):
    return jax.nn.gelu(inputs, approximate=True)


def _agg_kernel(own_count, last_tile, src_ref, cnt_ref, live_ref, own_ref, pulled_ref, tile_ref, out_ref, acc_ref):
    v = pl.program_id(0)
    t = pl.program_id(1)

    @pl.when(t == 0)
    def _():
        acc_ref[...] = jnp.zeros_like(acc_ref)

    src = src_ref[v, t]
    tile_live = t < cnt_ref[v]
    own_ok = tile_live & (src < own_count)
    pull_ok = tile_live & (src >= own_count) & (live_ref[jnp.maximum(src - own_count, 0)] > 0)

    @pl.when(own_ok)
    def _():
        acc_ref[...] += jnp.dot(own_ref[0], tile_ref[0, 0], preferred_element_type=jnp.float32)

    @pl.when(pull_ok)
    def _():
        block = pulled_ref[0, 0]
        block = block.reshape(block.shape[0] * block.shape[1], block.shape[2])
        acc_ref[...] += jnp.dot(block, tile_ref[0, 0], preferred_element_type=jnp.float32)

    @pl.when(t == last_tile)
    def _():
        out_ref[0] = acc_ref[...].astype(out_ref.dtype)


def aggregate(own, pulled, tile_src, tile_count, slot_live, tile_values):
    nb, feat, blk = own.shape
    cap, dom = pulled.shape[0], pulled.shape[1]
    tiles = tile_src.shape[1]

    def eff(v, t, src_ref, cnt_ref):
        return jnp.minimum(t, cnt_ref[v] - 1)

    def own_map(v, t, src_ref, cnt_ref, live_ref):
        s = src_ref[v, eff(v, t, src_ref, cnt_ref)]
        return (jnp.clip(s, 0, nb - 1), 0, 0)

    def pulled_map(v, t, src_ref, cnt_ref, live_ref):
        s = jnp.clip(src_ref[v, eff(v, t, src_ref, cnt_ref)] - nb, 0, cap * dom - 1)
        return (s // dom, s % dom, 0, 0, 0)

    def tile_map(v, t, src_ref, cnt_ref, live_ref):
        return (v, eff(v, t, src_ref, cnt_ref), 0, 0)

    def out_map(v, t, src_ref, cnt_ref, live_ref):
        return (v, 0, 0)

    grid_spec = pltpu.PrefetchScalarGridSpec(
        num_scalar_prefetch=3,
        grid=(nb, tiles),
        in_specs=[
            pl.BlockSpec((1, feat, blk), own_map),
            pl.BlockSpec((1, 1) + pulled.shape[2:], pulled_map),
            pl.BlockSpec((1, 1, blk, blk), tile_map),
        ],
        out_specs=pl.BlockSpec((1, feat, blk), out_map),
        scratch_shapes=[pltpu.VMEM((feat, blk), jnp.float32)],
    )
    flops = 2 * nb * tiles * feat * blk * blk
    return pl.pallas_call(
        functools.partial(_agg_kernel, nb, tiles - 1),
        grid_spec=grid_spec,
        out_shape=jax.ShapeDtypeStruct(own.shape, jnp.bfloat16),
        compiler_params=pltpu.CompilerParams(dimension_semantics=("arbitrary", "arbitrary")),
        cost_estimate=pl.CostEstimate(
            flops=flops, transcendentals=0, bytes_accessed=nb * tiles * (2 * feat * blk * 2 + blk * blk * 2) + own.size * 2
        ),
    )(tile_src, tile_count, slot_live, own, pulled, tile_values)


def _spread_kernel(own_count, src_ref, cnt_ref, back_ref, tile_ref, out_ref):
    v = pl.program_id(0)
    t = pl.program_id(1)

    @pl.when((v == 0) & (t == 0))
    def _():
        out_ref[...] = jnp.zeros_like(out_ref)

    src = src_ref[v, t]

    @pl.when((t < cnt_ref[v]) & (src < own_count))
    def _():
        term = lax.dot_general(
            back_ref[0], tile_ref[0, 0], (((1,), (1,)), ((), ())), preferred_element_type=jnp.float32
        )
        out_ref[src] = out_ref[src] + term


def spread_back(back_second, tile_src, tile_count, tile_values):
    nb, width, blk = back_second.shape
    tiles = tile_src.shape[1]

    def eff(v, t, cnt_ref):
        return jnp.minimum(t, cnt_ref[v] - 1)

    grid_spec = pltpu.PrefetchScalarGridSpec(
        num_scalar_prefetch=2,
        grid=(nb, tiles),
        in_specs=[
            pl.BlockSpec((1, width, blk), lambda v, t, s, c: (v, 0, 0)),
            pl.BlockSpec((1, 1, blk, blk), lambda v, t, s, c: (v, eff(v, t, c), 0, 0)),
        ],
        out_specs=pl.BlockSpec((nb, width, blk), lambda v, t, s, c: (0, 0, 0)),
    )
    return pl.pallas_call(
        functools.partial(_spread_kernel, nb),
        grid_spec=grid_spec,
        out_shape=jax.ShapeDtypeStruct(back_second.shape, jnp.float32),
        compiler_params=pltpu.CompilerParams(dimension_semantics=("arbitrary", "arbitrary")),
        cost_estimate=pl.CostEstimate(
            flops=2 * nb * tiles * width * blk * blk,
            transcendentals=0,
            bytes_accessed=back_second.size * 2 + nb * tiles * blk * blk * 2 + back_second.size * 4,
        ),
    )(tile_src, tile_count, back_second, tile_values)


def on_device(
    features,
    history_first,
    history_second,
    pull_list,
    pull_count,
    tile_src,
    tile_count,
    tile_values,
    w_first,
    w_second,
    bias_first,
    out_grad,
):
    dom_size = lax.axis_size("dom")
    fsdp_size = lax.axis_size("fsdp")
    me = lax.axis_index("dom") * fsdp_size + lax.axis_index("fsdp")
    rows, hidden = w_first.shape
    bias_cols = jnp.broadcast_to(bias_first[:, None], (rows, 128))
    packed = lax.all_gather(jnp.concatenate([w_first, bias_cols], axis=1), "fsdp", axis=0, tiled=True)
    first_full = packed[:, :hidden]
    bias_full = packed[:, hidden].astype(jnp.float32)
    second_full = lax.all_gather(w_second, "fsdp", axis=0, tiled=True)

    chosen = pull_list[0]
    requesters, slot_cap = chosen.shape
    counts_all = lax.all_gather(pull_count, "dom", axis=0, tiled=True)
    my_counts = lax.dynamic_index_in_dim(counts_all, me, axis=1, keepdims=False)
    slot_live = (lax.broadcasted_iota(jnp.int32, (slot_cap, dom_size), 0) < my_counts[None, :]).astype(jnp.int32)
    slot_live = slot_live.reshape(-1)

    block_len = features.shape[2]
    first_cols = history_first.shape[1]
    second_cols = history_second.shape[1]
    sent_first = jnp.take(history_first, chosen.reshape(-1), axis=0, mode="clip").reshape(requesters, slot_cap, 1, first_cols, block_len)
    sent_second = jnp.take(history_second, chosen.reshape(-1), axis=0, mode="clip").reshape(requesters, slot_cap, 1, second_cols, block_len)
    arrived_first = lax.all_to_all(sent_first, ("dom", "fsdp"), split_axis=0, concat_axis=2, tiled=True)
    arrived_second = lax.all_to_all(sent_second, ("dom", "fsdp"), split_axis=0, concat_axis=2, tiled=True)
    pulled_first = arrived_first.reshape(slot_cap, dom_size, fsdp_size, first_cols, block_len)
    pulled_second = arrived_second.reshape(slot_cap, dom_size, fsdp_size, second_cols, block_len)

    back_second = jnp.einsum(
        "ab,vbn->van", second_full, out_grad, preferred_element_type=jnp.float32
    ).astype(jnp.bfloat16)
    back_hidden = spread_back(back_second, tile_src, tile_count, tile_values)

    agg_first = aggregate(features, pulled_first, tile_src, tile_count, slot_live, tile_values)
    pre_act = (
        jnp.einsum("fh,vfn->vhn", first_full, agg_first, preferred_element_type=jnp.float32)
        + bias_full[None, :, None]
    )
    hidden_new = gelu_tanh(pre_act).astype(jnp.bfloat16)
    _, pullback = jax.vjp(gelu_tanh, pre_act)
    back_pre = pullback(back_hidden)[0].astype(jnp.bfloat16)
    first_term = jnp.einsum("vfn,vhn->fh", agg_first, back_pre, preferred_element_type=jnp.float32)
    bias_term = jnp.sum(back_pre.astype(jnp.float32), axis=(0, 2))

    agg_second = aggregate(hidden_new, pulled_second, tile_src, tile_count, slot_live, tile_values)
    second_term = jnp.einsum(
        "van,vbn->ab", agg_second, out_grad, preferred_element_type=jnp.float32
    )
    first_shard, second_shard, bias_shard = (
        lax.psum_scatter(first_term, "fsdp", scatter_dimension=0, tiled=True),
        lax.psum_scatter(second_term, "fsdp", scatter_dimension=0, tiled=True),
        lax.psum_scatter(bias_term, "fsdp", scatter_dimension=0, tiled=True),
    )
    first_total, second_total, bias_total = lax.psum((first_shard, second_shard, bias_shard), "dom")
    return (hidden_new, first_total, second_total, bias_total)


def solution(mesh):
    return jax.shard_map(
        on_device,
        mesh=mesh,
        in_specs=(
            P(("dom", "fsdp"), None, None),
            P("dom", "fsdp", None),
            P("dom", "fsdp", None),
            P("dom", None, None),
            P("dom", None),
            P(("dom", "fsdp"), None),
            P(("dom", "fsdp")),
            P(("dom", "fsdp"), None, None, None),
            P("fsdp", None),
            P("fsdp", None),
            P("fsdp"),
            P(("dom", "fsdp"), None, None),
        ),
        out_specs=(P(("dom", "fsdp"), None, None), P("fsdp", None), P("fsdp", None), P("fsdp")),
        check_vma=False,
    )
```

time: 664 us -> 575 us (0.87); the launches traced: 652 us -> 572 us
  waiting for transfers between devices: 164 us -> 270 us
  local copies, waits for them, and re-layouts: 146 us -> 53.7 us
  matrix products: 96.4 us -> 17.6 us
  Pallas kernels: 0 us -> 42.1 us
  other arithmetic: 29.3 us -> 1.78 us
  blocking collectives: 171 us -> 147 us
    unnamed x2 -> x1, blocking collectives: 149 us -> 30.9 us
    all_gather x0 -> x1, blocking collectives: none -> 94.1 us  [on_device(): counts_all = lax.all_gather(pull_count, 'dom', axis=0, tiled=True)]
    all_to_all x2, waiting for transfers between devices: 0.01 us -> 88.3 us  [the longest x1 88.3 us: on_device(): lax.all_to_all(sent_first, ('dom', 'fsdp'), split_axis=0, concat_axis=2,...]
    dot_general x23 -> x0, matrix products: 72.9 us -> none  [the longest x6 49.5 us: spread_back(): jnp.einsum('vu,vaj->uaj', matches, product, precision=lax.Precision.HIGHEST)]
    gather x14 -> x2, local copies, waits for them, and re-layouts: 99 us -> 26.9 us  [the longest x1 13.5 us: on_device(): jnp.take(history_second, chosen.reshape(-1), axis=0, mode='clip')]
    pallas_call x0 -> x3, Pallas kernels: none -> 42.1 us  [the longest x2 30.3 us: aggregate(): pl.pallas_call(functools.partial(_agg_kernel, nb, tiles - 1), grid_spec=g...]
    all_gather x2, waiting for transfers between devices: 0.02 us -> 20.9 us  [the longest x1 20.9 us: on_device(): lax.all_gather(jnp.concatenate([w_first, bias_cols], axis=1), 'fsdp', axi...]
    dot_general x6 -> x0, local copies, waits for them, and re-layouts: 16.8 us -> none  [spread_back(): jnp.einsum('vu,vaj->uaj', matches, product, precision=lax.Precision.HIGHEST)]
  transfers between devices with their start and end apart: 7 -> 7, of which waited for: 3 -> 5; matrix products, arithmetic and copies ran while one was open for 23% -> 6% of each run, Pallas kernels for 0% -> 2%
where the time goes in v1:
time: 575 us; the launch traced here: 572 us
  waiting for transfers between devices  270 us (47%)
  blocking collectives  147 us (26%)
  local copies, waits for them, and re-layouts  53.7 us (9%)
  Pallas kernels  42.1 us (7%)
  starting transfers between devices  25.8 us (4%)
  matrix products  17.6 us (3%)
  between operations  14.5 us (3%)
    all_gather x1, blocking collectives, on_device(): counts_all = lax.all_gather(pull_count, 'dom', axis=0, tiled=True)  94.1 us
    all_to_all x1, waiting for transfers between devices, on_device(): lax.all_to_all(sent_first, ('dom', 'fsdp'), split_axis=0, concat_axis=2,...  88.3 us
    reduce_scatter x1, waiting for transfers between devices, on_device(): lax.psum_scatter(first_term, 'fsdp', scatter_dimension=0, tiled=True)  80.5 us
    reduce_scatter x1, waiting for transfers between devices, on_device(): lax.psum_scatter(second_term, 'fsdp', scatter_dimension=0, tiled=True)  71.1 us
    unnamed x1, blocking collectives  30.9 us
    pallas_call x2, Pallas kernels, aggregate(): pl.pallas_call(functools.partial(_agg_kernel, nb, tiles - 1), grid_spec=g...  30.3 us
    psum x1, blocking collectives, on_device(): lax.psum((first_shard, second_shard, bias_shard), 'dom')  21.8 us
    all_gather x1, waiting for transfers between devices, on_device(): lax.all_gather(jnp.concatenate([w_first, bias_cols], axis=1), 'fsdp', axi...  20.9 us
  transfers between devices with their start and end apart: 7, of which 5 were waited for; matrix products, arithmetic and copies ran while one was open for 6% of the time, Pallas kernels for 2%

profile of v1, /device:TPU:1, one launch (start us, length us, event | category | flops | bytes accessed | tf_op | source)
XLA Modules:
  0.0 572.1 jit_solution(1460759282208128152)
XLA Ops:
  8.8 13.4 %gather_fusion = bf16[512,64,128]{2,1,0:T(8,128)(2,1)} fusion(bf16[128,64,128]{2,1,0:T(8,128)(2,1)S(1)} %copy-done, s32[1024]{0:T(1024)S(1)} %pad_clamp_fusion), kind=kCustom, calls=%fused_computation | custom fusion | bytes 16779264 | tf_op jit(solution)/shard_map/jit(_take)/gather | solution.py:169
  22.2 12.0 %all-to-all-start = ((bf16[128,4,1,64,128]{4,3,1,2,0:T(8,128)(2,1)}), bf16[128,4,1,64,128]{4,3,1,2,0:T(8,128)(2,1)}, u32[]{:S(2)}, u32[]{:S(2)}) async-start(bf16[128,4,1,64,128]{4,3,1,2,0:T(8,128)(2,1)} %bitcast.55), calls=%async_computation | async-start | bytes 16777216 | tf_op jit(solution)/shard_map/all_to_all | solution.py:171
  34.9 13.5 %gather_fusion.1 = bf16[512,64,128]{2,1,0:T(8,128)(2,1)} fusion(bf16[128,64,128]{2,1,0:T(8,128)(2,1)S(1)} %copy-done.2, s32[1024]{0:T(1024)S(1)} %pad_clamp_fusion), kind=kCustom, calls=%fused_computation.1 | custom fusion | bytes 16779264 | tf_op jit(solution)/shard_map/jit(_take)/gather | solution.py:170
  48.4 88.3 %all-to-all-done = bf16[128,4,1,64,128]{4,3,1,2,0:T(8,128)(2,1)} async-done(((bf16[128,4,1,64,128]{4,3,1,2,0:T(8,128)(2,1)}), bf16[128,4,1,64,128]{4,3,1,2,0:T(8,128)(2,1)}, u32[]{:S(2)}, u32[]{:S(2)}) %all-to-all-start) | async-done | bytes 8388640 | tf_op jit(solution)/shard_map/all_to_all | solution.py:171
  136.7 13.6 %all-to-all-start.1 = ((bf16[128,4,1,64,128]{4,3,1,2,0:T(8,128)(2,1)}), bf16[128,4,1,64,128]{4,3,1,2,0:T(8,128)(2,1)}, u32[]{:S(2)}, u32[]{:S(2)}) async-start(bf16[128,4,1,64,128]{4,3,1,2,0:T(8,128)(2,1)} %bitcast.54), calls=%async_computation.2 | async-start | bytes 16777216 | tf_op jit(solution)/shard_map/all_to_all | solution.py:172
  151.3 94.1 %all-gather = s32[8,1,128]{2,1,0:T(1,128)S(1)} all-gather(s32[1,1,128]{2,1,0:T(1,128)S(1)} %bitcast.58), channel_id=1, replica_groups=mesh['dom'=8,'fsdp'=16] {'dom'}, dimensions={0}, use_global_device_ids=true | all-gather | bytes 4608 | tf_op jit(solution)/shard_map/all_gather | solution.py:161
  246.3 3.8 fusion.16.back_ref
  250.1 11.8 %shard_map.148 = f32[4,1024,128]{2,1,0:T(8,128)} custom-call(s32[4,6]{1,0:T(4,128)} %src_ref.5, s32[4]{0:T(128)} %cnt_ref.5, bf16[4,1024,128]{2,1,0:T(8,128)(2,1)} %fusion.16.back_ref, bf16[4,6,128,128]{3,2,1,0:T(8,128)(2,1)} %tile_ref.5), custom_call_target="tpu_custom_call" | custom-call | flops 805306368 | bytes 3932160 | tf_op jit(solution)/shard_map/pallas_call | solution.py:122
  262.0 20.9 %all-gather.4.cloned.1.call-done = bf16[1024,1152]{1,0:T(8,128)(2,1)} async-done(((bf16[64,1152]{1,0:T(8,128)(2,1)}), bf16[1024,1152]{1,0:T(8,128)(2,1)}) %all-gather.4.cloned.1.call-update) | async-done | bytes 2359312 | tf_op jit(solution)/shard_map/all_gather | solution.py:154
  284.0 9.4 %copy.30 = bf16[1,4,128,1,64,128]{5,4,2,1,3,0:T(8,128)(2,1)} copy(bf16[1,4,128,1,64,128]{5,4,1,2,3,0:T(8,128)(2,1)} %bitcast.3) | data formatting | bytes 16777216 | tf_op jit(solution)/shard_map/all_to_all | solution.py:171
  293.4 9.4 %copy.35 = bf16[1,4,128,1,64,128]{5,4,2,1,3,0:T(8,128)(2,1)} copy(bf16[1,4,128,1,64,128]{5,4,1,2,3,0:T(8,128)(2,1)} %bitcast.12) | data formatting | bytes 16777216 | tf_op jit(solution)/shard_map/all_to_all | solution.py:172
  302.8 15.2 %shard_map.147 = bf16[4,1024,128]{2,1,0:T(8,128)(2,1)} custom-call(s32[4,6]{1,0:T(4,128)} %src_ref.5, s32[4]{0:T(128)} %cnt_ref.5, s32[32]{0:T(128)} %reshape.43.live_ref, bf16[4,1024,128]{2,1,0:T(8,128)(2,1)} %own_ref.1, bf16[4,8,16,64,128]{4,3,2,1,0:T(8,128)(2,1)} %bitcast.57, bf16[4,6,128,128]{3,2,1,0:T(8,128)(2,1)} %tile_ref.5), custom_call_target="tpu_custom_call" | custom-call | flops 805306368 | bytes 14417920 | tf_op jit(solution)/shard_map/pallas_call | solution.py:77
  318.0 6.1 %convert_reduce_fusion = (f32[1024]{0:T(1024)S(1)}, bf16[4,1024,128]{2,1,0:T(8,128)(2,1)}, bf16[4,1024,128]{2,1,0:T(8,128)(2,1)}) fusion(f32[4,1024,128]{2,1,0:T(8,128)S(1)} %copy-done.3, f32[1024]{0:T(1024)S(1)} %convert_reduce_fusion.1, bf16[4,1024,128]{2,1,0:T(8,128)(2,1)} %shard_map.147, bf16[1024,1152]{1,0:T(8,128)(2,1)} %all-gather.4.cloned.1.call-done), kind=kOutput, calls=%fused_computation.22 | convolution fusion | flops 1086848000 | bytes 7348224 | tf_op jit(solution)/shard_map/fh,vfn->vhn/dot_general | solution.py:183
  324.1 15.1 %shard_map.149 = bf16[4,1024,128]{2,1,0:T(8,128)(2,1)} custom-call(s32[4,6]{1,0:T(4,128)} %src_ref.5, s32[4]{0:T(128)} %cnt_ref.5, s32[32]{0:T(128)} %reshape.43.live_ref, bf16[4,1024,128]{2,1,0:T(8,128)(2,1)} %get-tuple-element.9.own_ref, bf16[4,8,16,64,128]{4,3,2,1,0:T(8,128)(2,1)} %bitcast.56, bf16[4,6,128,128]{3,2,1,0:T(8,128)(2,1)} %tile_ref.5), custom_call_target="tpu_custom_call" | custom-call | flops 805306368 | bytes 14417920 | tf_op jit(solution)/shard_map/pallas_call | solution.py:77
  339.2 4.5 convolution_bitcast_fusion
  343.7 1.1 copy-done.4
  345.2 3.3 convolution_bitcast_fusion.1
  348.5 71.1 %reduce-scatter.5.cloned.1.call-done = f32[64,1024]{1,0:T(8,128)} async-done(((f32[1024,1024]{1,0:T(8,128)}), f32[64,1024]{1,0:T(8,128)}) %reduce-scatter.5.cloned.1.call-update) | async-done | bytes 262160 | tf_op jit(solution)/shard_map/reduce_scatter | solution.py:198
  419.6 80.5 %reduce-scatter.3.cloned.1.call-done = f32[64,1024]{1,0:T(8,128)} async-done(((f32[1024,1024]{1,0:T(8,128)}), f32[64,1024]{1,0:T(8,128)}) %reduce-scatter.3.cloned.1.call-update) | async-done | bytes 262160 | tf_op jit(solution)/shard_map/reduce_scatter | solution.py:197
  501.4 30.9 %all-reduce = f32[1024]{0:T(1024)S(1)} all-reduce(f32[1024]{0:T(1024)S(1)} %get-tuple-element.6), channel_id=4, replica_groups=mesh['dom'=8,'fsdp'=16] {'fsdp'}, use_global_device_ids=true, to_apply=%region_5.6.clone | all-reduce | flops 1024 | bytes 8192
  532.4 21.8 %psum.23 = f32[64]{0:T(128)} all-reduce(f32[64]{0:T(128)S(1)} %dynamic-slice.2), channel_id=1, replica_groups=mesh['dom'=8,'fsdp'=16] {'dom'}, use_global_device_ids=true, to_apply=%region_6.7 | all-reduce | flops 64 | bytes 512 | tf_op jit(solution)/shard_map/psum | solution.py:201
  554.2 7.9 %all-reduce.4.cloned.1.call-done = (f32[64,1024]{1,0:T(8,128)}, f32[64,1024]{1,0:T(8,128)}) async-done(((f32[64,1024]{1,0:T(8,128)}, f32[64,1024]{1,0:T(8,128)}), (f32[64,1024]{1,0:T(8,128)}, f32[64,1024]{1,0:T(8,128)})) %all-reduce.4.cloned.1.call-update) | async-done | bytes 524304 | tf_op jit(solution)/shard_map/psum | solution.py:201
  562.2 1.7 copy.42
  563.9 1.7 copy.43
  (44 shorter events, 6.3 us)
Async XLA Ops:
  7.2 1.6 copy-start
  22.2 12.7 %copy-start.2 = (bf16[128,64,128]{2,1,0:T(8,128)(2,1)S(1)}, bf16[128,64,128]{2,1,0:T(8,128)(2,1)}, u32[]{:S(2)}) copy-start(bf16[128,64,128]{2,1,0:T(8,128)(2,1)} %param.14) | copy-start | bytes 6291460
  22.2 114.5 %all-to-all-start = ((bf16[128,4,1,64,128]{4,3,1,2,0:T(8,128)(2,1)}), bf16[128,4,1,64,128]{4,3,1,2,0:T(8,128)(2,1)}, u32[]{:S(2)}, u32[]{:S(2)}) async-start(bf16[128,4,1,64,128]{4,3,1,2,0:T(8,128)(2,1)} %bitcast.55), calls=%async_computation | async-start | bytes 16777216 | tf_op jit(solution)/shard_map/all_to_all | solution.py:171
  34.2 212.1 %all-gather.6.cloned.1.call-start = ((), (), s32[]{:S(2)}) async-start(), calls=%async_computation.5 | async-start | bytes 2228224 | tf_op jit(solution)/shard_map/all_gather | solution.py:157
  136.7 13.7 %copy-start.6 = (bf16[64]{0:T(256)(128)(2,1)S(1)}, bf16[64]{0:T(256)(128)(2,1)}, u32[]{:S(2)}) copy-start(bf16[64]{0:T(256)(128)(2,1)} %param.22) | copy-start | bytes 388
  136.7 13.8 %copy-start.5 = (bf16[64,1024]{1,0:T(8,128)(2,1)S(1)}, bf16[64,1024]{1,0:T(8,128)(2,1)}, u32[]{:S(2)}) copy-start(bf16[64,1024]{1,0:T(8,128)(2,1)} %param.20) | copy-start | bytes 393220
  136.7 14.5 %copy-start.7 = (s32[1,128]{1,0:T(1,128)S(1)}, s32[1,128]{1,0:T(1,128)}, u32[]{:S(2)}) copy-start(s32[1,128]{1,0:T(1,128)} %param.16) | copy-start | bytes 1540
  136.7 109.6 %copy-start.8 = (bf16[4,1024,128]{2,1,0:T(8,128)(2,1)S(1)}, bf16[4,1024,128]{2,1,0:T(8,128)(2,1)}, u32[]{:S(2)}) copy-start(bf16[4,1024,128]{2,1,0:T(8,128)(2,1)} %param.23) | copy-start | bytes 3145732
  136.7 156.7 %all-to-all-start.1 = ((bf16[128,4,1,64,128]{4,3,1,2,0:T(8,128)(2,1)}), bf16[128,4,1,64,128]{4,3,1,2,0:T(8,128)(2,1)}, u32[]{:S(2)}, u32[]{:S(2)}) async-start(bf16[128,4,1,64,128]{4,3,1,2,0:T(8,128)(2,1)} %bitcast.54), calls=%async_computation.2 | async-start | bytes 16777216 | tf_op jit(solution)/shard_map/all_to_all | solution.py:172
  150.4 132.6 %all-gather.4.cloned.1.call-start = ((), (), s32[]{:S(2)}) async-start(), calls=%async_computation.4 | async-start | bytes 2506752 | tf_op jit(solution)/shard_map/all_gather | solution.py:154
  151.2 268.4 %reduce-scatter.5.cloned.1.call-start = ((), (), s32[]{:S(2)}) async-start(), calls=%async_computation.7 | async-start | bytes 4456448 | tf_op jit(solution)/shard_map/reduce_scatter | solution.py:198
  302.8 15.2 %copy-start.3 = (f32[4,1024,128]{2,1,0:T(8,128)S(1)}, f32[4,1024,128]{2,1,0:T(8,128)}, u32[]{:S(2)}) copy-start(f32[4,1024,128]{2,1,0:T(8,128)} %shard_map.148) | copy-start | bytes 6291460
  343.6 1.2 copy-start.4
  343.6 1.5 copy-start.10
  343.7 156.5 %reduce-scatter.3.cloned.1.call-start = ((), (), s32[]{:S(2)}) async-start(), calls=%async_computation.6 | async-start | bytes 4456448 | tf_op jit(solution)/shard_map/reduce_scatter | solution.py:197
  348.4 217.1 %copy-start.1 = (bf16[128,64,128]{2,1,0:T(8,128)(2,1)S(1)}, bf16[128,64,128]{2,1,0:T(8,128)(2,1)}, u32[]{:S(2)}) copy-start(bf16[128,64,128]{2,1,0:T(8,128)(2,1)} %param.13) | copy-start | bytes 6291460
  348.4 151.8 %copy-start.9 = (u32[128]{0:T(128)S(1)}, u32[128]{0:T(128)}, u32[]{:S(2)}) copy-start(u32[128]{0:T(128)} %constant.41) | copy-start | bytes 1540
  348.5 213.7 %all-reduce.4.cloned.1.call-start = ((), (), s32[]{:S(2)}) async-start(), calls=%async_computation.8 | async-start | bytes 1048576 | tf_op jit(solution)/shard_map/psum | solution.py:201
Sparse Core Ops, SparseCore 0:
  37.2 143.0 all-gather.5
  182.9 99.9 all-gather.3
  343.8 75.7 reduce-scatter.4
  423.2 76.9 reduce-scatter.2
  502.4 59.7 all-reduce.3

commit v2 on v1

--- a/solution.py
+++ b/solution.py
@@ -31,7 +31,7 @@
 
     @pl.when(pull_ok)
     def _():
-        block = pulled_ref[0, 0]
+        block = pulled_ref[0, :, 0]
         block = block.reshape(block.shape[0] * block.shape[1], block.shape[2])
         acc_ref[...] += jnp.dot(block, tile_ref[0, 0], preferred_element_type=jnp.float32)
 
@@ -42,7 +42,7 @@
 
 def aggregate(own, pulled, tile_src, tile_count, slot_live, tile_values):
     nb, feat, blk = own.shape
-    cap, dom = pulled.shape[0], pulled.shape[1]
+    dom, fsdp, cap = pulled.shape[0], pulled.shape[1], pulled.shape[2]
     tiles = tile_src.shape[1]
 
     def eff(v, t, src_ref, cnt_ref):
@@ -54,7 +54,7 @@
 
     def pulled_map(v, t, src_ref, cnt_ref, live_ref):
         s = jnp.clip(src_ref[v, eff(v, t, src_ref, cnt_ref)] - nb, 0, cap * dom - 1)
-        return (s // dom, s % dom, 0, 0, 0)
+        return (s % dom, 0, s // dom, 0, 0)
 
     def tile_map(v, t, src_ref, cnt_ref, live_ref):
         return (v, eff(v, t, src_ref, cnt_ref), 0, 0)
@@ -67,7 +67,7 @@
         grid=(nb, tiles),
         in_specs=[
             pl.BlockSpec((1, feat, blk), own_map),
-            pl.BlockSpec((1, 1) + pulled.shape[2:], pulled_map),
+            pl.BlockSpec((1, fsdp, 1) + pulled.shape[3:], pulled_map),
             pl.BlockSpec((1, 1, blk, blk), tile_map),
         ],
         out_specs=pl.BlockSpec((1, feat, blk), out_map),
@@ -159,6 +159,7 @@
     chosen = pull_list[0]
     requesters, slot_cap = chosen.shape
     counts_all = lax.all_gather(pull_count, "dom", axis=0, tiled=True)
+    counts_all, chosen = lax.optimization_barrier((counts_all, chosen))
     my_counts = lax.dynamic_index_in_dim(counts_all, me, axis=1, keepdims=False)
     slot_live = (lax.broadcasted_iota(jnp.int32, (slot_cap, dom_size), 0) < my_counts[None, :]).astype(jnp.int32)
     slot_live = slot_live.reshape(-1)
@@ -166,18 +167,28 @@
     block_len = features.shape[2]
     first_cols = history_first.shape[1]
     second_cols = history_second.shape[1]
-    sent_first = jnp.take(history_first, chosen.reshape(-1), axis=0, mode="clip").reshape(requesters, slot_cap, 1, first_cols, block_len)
-    sent_second = jnp.take(history_second, chosen.reshape(-1), axis=0, mode="clip").reshape(requesters, slot_cap, 1, second_cols, block_len)
-    arrived_first = lax.all_to_all(sent_first, ("dom", "fsdp"), split_axis=0, concat_axis=2, tiled=True)
-    arrived_second = lax.all_to_all(sent_second, ("dom", "fsdp"), split_axis=0, concat_axis=2, tiled=True)
-    pulled_first = arrived_first.reshape(slot_cap, dom_size, fsdp_size, first_cols, block_len)
-    pulled_second = arrived_second.reshape(slot_cap, dom_size, fsdp_size, second_cols, block_len)
+    sent_first = jnp.take(history_first, chosen.reshape(-1), axis=0, mode="clip").reshape(requesters, slot_cap, first_cols, block_len)
+    sent_second = jnp.take(history_second, chosen.reshape(-1), axis=0, mode="clip").reshape(requesters, slot_cap, second_cols, block_len)
+    arrived_first = lax.all_to_all(sent_first, ("dom", "fsdp"), split_axis=0, concat_axis=0, tiled=True)
+    arrived_second = lax.all_to_all(sent_second, ("dom", "fsdp"), split_axis=0, concat_axis=0, tiled=True)
+    pulled_first = arrived_first.reshape(dom_size, fsdp_size, slot_cap, first_cols, block_len)
+    pulled_second = arrived_second.reshape(dom_size, fsdp_size, slot_cap, second_cols, block_len)
+
+    core = lax.axis_index("dom") % 2
+    pair = [(d, d ^ 1) for d in range(dom_size)]
+    partner_grad = lax.ppermute(out_grad, "dom", pair)
 
     back_second = jnp.einsum(
         "ab,vbn->van", second_full, out_grad, preferred_element_type=jnp.float32
     ).astype(jnp.bfloat16)
     back_hidden = spread_back(back_second, tile_src, tile_count, tile_values)
 
+    def halves(x):
+        split = x.reshape(x.shape[0], fsdp_size, 2, x.shape[1] // (2 * fsdp_size), x.shape[2])
+        mine = lax.dynamic_index_in_dim(split, core, axis=2, keepdims=False)
+        theirs = lax.dynamic_index_in_dim(split, 1 - core, axis=2, keepdims=False)
+        return mine, theirs
+
     agg_first = aggregate(features, pulled_first, tile_src, tile_count, slot_live, tile_values)
     pre_act = (
         jnp.einsum("fh,vfn->vhn", first_full, agg_first, preferred_element_type=jnp.float32)
@@ -186,19 +197,40 @@
     hidden_new = gelu_tanh(pre_act).astype(jnp.bfloat16)
     _, pullback = jax.vjp(gelu_tanh, pre_act)
     back_pre = pullback(back_hidden)[0].astype(jnp.bfloat16)
-    first_term = jnp.einsum("vfn,vhn->fh", agg_first, back_pre, preferred_element_type=jnp.float32)
     bias_term = jnp.sum(back_pre.astype(jnp.float32), axis=(0, 2))
+    first_mine, first_theirs = halves(agg_first)
+    first_got, back_got = lax.ppermute((first_theirs, back_pre), "dom", pair)
+    first_term = jnp.einsum(
+        "vprn,vhn->prh", first_mine, back_pre, preferred_element_type=jnp.float32
+    ) + jnp.einsum("vprn,vhn->prh", first_got, back_got, preferred_element_type=jnp.float32)
 
     agg_second = aggregate(hidden_new, pulled_second, tile_src, tile_count, slot_live, tile_values)
+    second_mine, second_theirs = halves(agg_second)
+    second_got = lax.ppermute(second_theirs, "dom", pair)
     second_term = jnp.einsum(
-        "van,vbn->ab", agg_second, out_grad, preferred_element_type=jnp.float32
-    )
-    first_shard, second_shard, bias_shard = (
-        lax.psum_scatter(first_term, "fsdp", scatter_dimension=0, tiled=True),
-        lax.psum_scatter(second_term, "fsdp", scatter_dimension=0, tiled=True),
-        lax.psum_scatter(bias_term, "fsdp", scatter_dimension=0, tiled=True),
-    )
-    first_total, second_total, bias_total = lax.psum((first_shard, second_shard, bias_shard), "dom")
+        "vprn,vbn->prb", second_mine, out_grad, preferred_element_type=jnp.float32
+    ) + jnp.einsum("vprn,vbn->prb", second_got, partner_grad, preferred_element_type=jnp.float32)
+
+    half_rows = first_term.shape[1]
+    lanes = 128
+    bias_cols = jnp.zeros((fsdp_size, 2 * half_rows, lanes), jnp.float32)
+    bias_cols = bias_cols.at[:, 0, : hidden // fsdp_size].set(bias_term.reshape(fsdp_size, hidden // fsdp_size))
+    packed_terms = jnp.concatenate([jnp.concatenate([first_term, second_term], axis=1), bias_cols], axis=2)
+    packed_terms = packed_terms.reshape(fsdp_size * 2 * half_rows, hidden + lanes)
+    shard = lax.psum_scatter(packed_terms, "fsdp", scatter_dimension=0, tiled=True)
+    zero_half = jnp.zeros((half_rows, hidden), jnp.float32)
+
+    def placed(part):
+        return jnp.where(core == 0, jnp.concatenate([part, zero_half], 0), jnp.concatenate([zero_half, part], 0))
+
+    bias_block = jnp.zeros((8, hidden), jnp.float32).at[0, :lanes].set(shard[0, hidden:])
+    full = jnp.concatenate(
+        [placed(shard[:half_rows, :hidden]), placed(shard[half_rows:, :hidden]), bias_block], axis=0
+    )
+    total = lax.psum(full, "dom")
+    first_total = total[: 2 * half_rows]
+    second_total = total[2 * half_rows : 4 * half_rows]
+    bias_total = total[4 * half_rows, : hidden // fsdp_size]
     return (hidden_new, first_total, second_total, bias_total)
 
 

time: 575 us -> 494 us (0.86)
  blocking collectives: 147 us -> 12.4 us
  waiting for transfers between devices: 270 us -> 339 us
  local copies, waits for them, and re-layouts: 53.7 us -> 37.8 us
    all_gather x1, blocking collectives: 94.1 us -> 12.4 us  [on_device(): counts_all = lax.all_gather(pull_count, 'dom', axis=0, tiled=True)]
    reduce_scatter x2 -> x1, waiting for transfers between devices: 152 us -> 77 us  [on_device(): lax.psum_scatter(packed_terms, 'fsdp', scatter_dimension=0, tiled=True)]
    all_gather x1, waiting for transfers between devices: 20.9 us -> 92.4 us  [on_device(): lax.all_gather(jnp.concatenate([w_first, bias_cols], axis=1), 'fsdp', axi...]
    psum x1, waiting for transfers between devices: 7.94 us -> 59.6 us  [on_device(): total = lax.psum(full, 'dom')]
    unnamed x1 -> x0, blocking collectives: 30.9 us -> none
    psum x1 -> x0, blocking collectives: 21.8 us -> none  [on_device(): lax.psum((first_shard, second_shard, bias_shard), 'dom')]
    all_gather x1, waiting for transfers between devices: 0.01 us -> 20.4 us  [on_device(): second_full = lax.all_gather(w_second, 'fsdp', axis=0, tiled=True)]
    all_to_all x2 -> x0, local copies, waits for them, and re-layouts: 18.8 us -> none  [the longest x1 9.39 us: on_device(): lax.all_to_all(sent_first, ('dom', 'fsdp'), split_axis=0, concat_axis=2,...]
  transfers between devices with their start and end apart: 7 -> 10, of which waited for: 5 -> 5; matrix products, arithmetic and copies ran while one was open for 6% -> 8% of each run, Pallas kernels for 2% -> 9%
where the time goes in v2:
time: 494 us
  waiting for transfers between devices  339 us (69%)
  Pallas kernels  42.5 us (9%)
  local copies, waits for them, and re-layouts  37.8 us (8%)
  starting transfers between devices  23.6 us (5%)
  matrix products  20.1 us (4%)
  between operations  13.9 us (3%)
  blocking collectives  12.4 us (3%)
  other arithmetic  5.23 us (1%)
    all_gather x1, waiting for transfers between devices, on_device(): lax.all_gather(jnp.concatenate([w_first, bias_cols], axis=1), 'fsdp', axi...  92.4 us
    all_to_all x1, waiting for transfers between devices, on_device(): lax.all_to_all(sent_first, ('dom', 'fsdp'), split_axis=0, concat_axis=0,...  88.3 us
    reduce_scatter x1, waiting for transfers between devices, on_device(): lax.psum_scatter(packed_terms, 'fsdp', scatter_dimension=0, tiled=True)  77 us
    psum x1, waiting for transfers between devices, on_device(): total = lax.psum(full, 'dom')  59.6 us
    pallas_call x2, Pallas kernels, aggregate(): pl.pallas_call(functools.partial(_agg_kernel, nb, tiles - 1), grid_spec=g...  30.7 us
    all_gather x1, waiting for transfers between devices, on_device(): second_full = lax.all_gather(w_second, 'fsdp', axis=0, tiled=True)  20.4 us
    all_to_all x1, starting transfers between devices, on_device(): lax.all_to_all(sent_second, ('dom', 'fsdp'), split_axis=0, concat_axis=0,...  13.7 us
    gather x1, local copies, waits for them, and re-layouts, on_device(): jnp.take(history_first, chosen.reshape(-1), axis=0, mode='clip')  13.5 us
  transfers between devices with their start and end apart: 10, of which 5 were waited for; matrix products, arithmetic and copies ran while one was open for 8% of the time, Pallas kernels for 9%

profile of v2, /device:TPU:1, one launch (start us, length us, event | category | flops | bytes accessed | tf_op | source)
XLA Modules:
  0.0 494.1 jit_solution(17906032754084081068)
XLA Ops:
  7.2 12.4 %all-gather = s32[8,1,128]{2,1,0:T(1,128)S(1)} all-gather(s32[1,1,128]{2,1,0:T(1,128)} %bitcast.92), channel_id=1, replica_groups=mesh['dom'=8,'fsdp'=16] {'dom'}, dimensions={0}, use_global_device_ids=true | all-gather | bytes 4608 | tf_op jit(solution)/shard_map/all_gather | solution.py:161
  20.5 13.5 %gather_fusion = bf16[512,64,128]{2,1,0:T(8,128)(2,1)} fusion(bf16[128,64,128]{2,1,0:T(8,128)(2,1)S(1)} %copy-done, s32[1024]{0:T(1024)S(1)} %pad_clamp_fusion), kind=kCustom, calls=%fused_computation | custom fusion | bytes 16779264 | tf_op jit(solution)/shard_map/jit(_take)/gather | solution.py:170
  33.9 8.3 %all-to-all-start = ((bf16[128,4,64,128]{3,2,1,0:T(8,128)(2,1)}), bf16[128,4,64,128]{3,2,1,0:T(8,128)(2,1)}, u32[]{:S(2)}, u32[]{:S(2)}) async-start(bf16[128,4,64,128]{3,2,1,0:T(8,128)(2,1)} %bitcast.85), calls=%async_computation | async-start | bytes 16777216 | tf_op jit(solution)/shard_map/all_to_all | solution.py:172
  43.0 13.4 %gather_fusion.1 = bf16[512,64,128]{2,1,0:T(8,128)(2,1)} fusion(bf16[128,64,128]{2,1,0:T(8,128)(2,1)S(1)} %copy-done.2, s32[1024]{0:T(1024)S(1)} %pad_clamp_fusion), kind=kCustom, calls=%fused_computation.1 | custom fusion | bytes 16779264 | tf_op jit(solution)/shard_map/jit(_take)/gather | solution.py:171
  56.4 88.3 %all-to-all-done = bf16[128,4,64,128]{3,2,1,0:T(8,128)(2,1)} async-done(((bf16[128,4,64,128]{3,2,1,0:T(8,128)(2,1)}), bf16[128,4,64,128]{3,2,1,0:T(8,128)(2,1)}, u32[]{:S(2)}, u32[]{:S(2)}) %all-to-all-start) | async-done | bytes 8388640 | tf_op jit(solution)/shard_map/all_to_all | solution.py:172
  144.8 13.7 %all-to-all-start.1 = ((bf16[128,4,64,128]{3,2,1,0:T(8,128)(2,1)}), bf16[128,4,64,128]{3,2,1,0:T(8,128)(2,1)}, u32[]{:S(2)}, u32[]{:S(2)}) async-start(bf16[128,4,64,128]{3,2,1,0:T(8,128)(2,1)} %bitcast.84), calls=%async_computation.1 | async-start | bytes 16777216 | tf_op jit(solution)/shard_map/all_to_all | solution.py:173
  159.3 1.4 collective-permute-start.3
  161.5 20.4 %all-gather.6.cloned.1.call-done = bf16[1024,1024]{1,0:T(8,128)(2,1)} async-done(((bf16[64,1024]{1,0:T(8,128)(2,1)}), bf16[1024,1024]{1,0:T(8,128)(2,1)}) %all-gather.6.cloned.1.call-update) | async-done | bytes 2097168 | tf_op jit(solution)/shard_map/all_gather | solution.py:157
  182.0 4.1 fusion.16.back_ref
  186.1 11.8 %shard_map.148 = f32[4,1024,128]{2,1,0:T(8,128)} custom-call(s32[4,6]{1,0:T(4,128)} %src_ref.5, s32[4]{0:T(128)} %cnt_ref.5, bf16[4,1024,128]{2,1,0:T(8,128)(2,1)} %fusion.16.back_ref, bf16[4,6,128,128]{3,2,1,0:T(8,128)(2,1)} %tile_ref.5), custom_call_target="tpu_custom_call" | custom-call | flops 805306368 | bytes 3932160 | tf_op jit(solution)/shard_map/pallas_call | solution.py:122
  197.8 92.4 %all-gather.4.cloned.1.call-done = bf16[1024,1152]{1,0:T(8,128)(2,1)} async-done(((bf16[64,1152]{1,0:T(8,128)(2,1)}), bf16[1024,1152]{1,0:T(8,128)(2,1)}) %all-gather.4.cloned.1.call-update) | async-done | bytes 2359312 | tf_op jit(solution)/shard_map/all_gather | solution.py:154
  291.3 15.4 %shard_map.147 = bf16[4,1024,128]{2,1,0:T(8,128)(2,1)} custom-call(s32[4,6]{1,0:T(4,128)} %src_ref.5, s32[4]{0:T(128)} %cnt_ref.5, s32[32]{0:T(128)} %reshape.124.live_ref, bf16[4,1024,128]{2,1,0:T(8,128)(2,1)} %own_ref.1, bf16[8,16,4,64,128]{4,3,2,1,0:T(8,128)(2,1)} %bitcast.4.pulled_ref, bf16[4,6,128,128]{3,2,1,0:T(8,128)(2,1)} %tile_ref.5), custom_call_target="tpu_custom_call" | custom-call | flops 805306368 | bytes 14417920 | tf_op jit(solution)/shard_map/pallas_call | solution.py:77
  306.7 1.5 constant_dynamic-slice_fusion.2
  309.0 5.8 %convert_reduce_fusion = (f32[1024]{0:T(1024)S(1)}, bf16[4,1024,128]{2,1,0:T(8,128)(2,1)}, bf16[4,1024,128]{2,1,0:T(8,128)(2,1)}) fusion(f32[4,1024,128]{2,1,0:T(8,128)S(1)} %copy-done.4, f32[1024]{0:T(1024)S(1)} %convert_reduce_fusion.1, bf16[4,1024,128]{2,1,0:T(8,128)(2,1)S(1)} %copy-done.3, bf16[1024,1152]{1,0:T(8,128)(2,1)} %all-gather.4.cloned.1.call-done), kind=kOutput, calls=%fused_computation.24 | convolution fusion | flops 1086848000 | bytes 7348224 | tf_op jit(solution)/shard_map/fh,vfn->vhn/dot_general | solution.py:194
  314.8 15.4 %shard_map.149 = bf16[4,1024,128]{2,1,0:T(8,128)(2,1)} custom-call(s32[4,6]{1,0:T(4,128)} %src_ref.5, s32[4]{0:T(128)} %cnt_ref.5, s32[32]{0:T(128)} %reshape.124.live_ref, bf16[4,1024,128]{2,1,0:T(8,128)(2,1)} %get-tuple-element.34.own_ref, bf16[8,16,4,64,128]{4,3,2,1,0:T(8,128)(2,1)} %bitcast.19.pulled_ref, bf16[4,6,128,128]{3,2,1,0:T(8,128)(2,1)} %tile_ref.5), custom_call_target="tpu_custom_call" | custom-call | flops 805306368 | bytes 14417920 | tf_op jit(solution)/shard_map/pallas_call | solution.py:77
  330.1 1.3 constant_dynamic-slice_fusion
  332.3 2.0 fusion.23
  334.3 3.3 fusion.20
  337.7 2.8 bitcast_add_fusion
  340.5 2.1 bitcast_add_fusion.1
  342.7 2.5 select_maximum_fusion
  345.3 77.0 %reduce-scatter.2.cloned.1.call-done = f32[64,1152]{1,0:T(8,128)} async-done(((f32[1024,1152]{1,0:T(8,128)}), f32[64,1152]{1,0:T(8,128)}) %reduce-scatter.2.cloned.1.call-update) | async-done | bytes 294928 | tf_op jit(solution)/shard_map/reduce_scatter | solution.py:220
  424.9 59.6 %all-reduce.8.cloned.1.call-done = f32[136,1024]{1,0:T(8,128)} async-done(((f32[136,1024]{1,0:T(8,128)}), f32[136,1024]{1,0:T(8,128)}) %all-reduce.8.cloned.1.call-update) | async-done | bytes 557072 | tf_op jit(solution)/shard_map/psum | solution.py:230
  484.5 1.9 fusion.31
  (47 shorter events, 9.9 us)
Async XLA Ops:
  7.2 13.3 %copy-start = (bf16[128,64,128]{2,1,0:T(8,128)(2,1)S(1)}, bf16[128,64,128]{2,1,0:T(8,128)(2,1)}, u32[]{:S(2)}) copy-start(bf16[128,64,128]{2,1,0:T(8,128)(2,1)} %param.17) | copy-start | bytes 6291460
  33.9 9.0 %copy-start.2 = (bf16[128,64,128]{2,1,0:T(8,128)(2,1)S(1)}, bf16[128,64,128]{2,1,0:T(8,128)(2,1)}, u32[]{:S(2)}) copy-start(bf16[128,64,128]{2,1,0:T(8,128)(2,1)} %param.18) | copy-start | bytes 6291460
  33.9 110.8 %all-to-all-start = ((bf16[128,4,64,128]{3,2,1,0:T(8,128)(2,1)}), bf16[128,4,64,128]{3,2,1,0:T(8,128)(2,1)}, u32[]{:S(2)}, u32[]{:S(2)}) async-start(bf16[128,4,64,128]{3,2,1,0:T(8,128)(2,1)} %bitcast.85), calls=%async_computation | async-start | bytes 16777216 | tf_op jit(solution)/shard_map/all_to_all | solution.py:172
  42.2 139.7 %all-gather.6.cloned.1.call-start = ((), (), s32[]{:S(2)}) async-start(), calls=%async_computation.4 | async-start | bytes 2228224 | tf_op jit(solution)/shard_map/all_gather | solution.py:157
  144.8 13.7 %copy-start.6 = (bf16[64]{0:T(256)(128)(2,1)S(1)}, bf16[64]{0:T(256)(128)(2,1)}, u32[]{:S(2)}) copy-start(bf16[64]{0:T(256)(128)(2,1)} %param.26) | copy-start | bytes 388
  144.8 13.8 %copy-start.5 = (bf16[64,1024]{1,0:T(8,128)(2,1)S(1)}, bf16[64,1024]{1,0:T(8,128)(2,1)}, u32[]{:S(2)}) copy-start(bf16[64,1024]{1,0:T(8,128)(2,1)} %param.24) | copy-start | bytes 393220
  144.8 170.0 %all-to-all-start.1 = ((bf16[128,4,64,128]{3,2,1,0:T(8,128)(2,1)}), bf16[128,4,64,128]{3,2,1,0:T(8,128)(2,1)}, u32[]{:S(2)}, u32[]{:S(2)}) async-start(bf16[128,4,64,128]{3,2,1,0:T(8,128)(2,1)} %bitcast.84), calls=%async_computation.1 | async-start | bytes 16777216 | tf_op jit(solution)/shard_map/all_to_all | solution.py:173
  158.5 131.8 %all-gather.4.cloned.1.call-start = ((), (), s32[]{:S(2)}) async-start(), calls=%async_computation.3 | async-start | bytes 2506752 | tf_op jit(solution)/shard_map/all_gather | solution.py:154
  159.3 263.0 %reduce-scatter.2.cloned.1.call-start = ((), (), s32[]{:S(2)}) async-start(), calls=%async_computation.5 | async-start | bytes 5013504 | tf_op jit(solution)/shard_map/reduce_scatter | solution.py:220
  159.3 178.3 %collective-permute-start.3 = (bf16[4,1024,128]{2,1,0:T(8,128)(2,1)}, bf16[4,1024,128]{2,1,0:T(8,128)(2,1)}, u32[]{:S(2)}, u32[]{:S(2)}) collective-permute-start(bf16[4,1024,128]{2,1,0:T(8,128)(2,1)} %param.27), channel_id=1, source_target_pairs={{0,16},{16,0},{32,48},{48,32},{64,80},{80,64},{96,112},{112,96},{1... | collective-permute-start | bytes 3145736 | tf_op jit(solution)/shard_map/ppermute | solution.py:179
  306.7 1.6 copy-start.3
  306.7 2.2 copy-start.4
  308.2 32.3 %collective-permute-start = (bf16[4,16,32,128]{3,2,0,1:T(8,128)(2,1)S(1)}, bf16[4,16,32,128]{3,2,0,1:T(8,128)(2,1)}, u32[]{:S(2)}, u32[]{:S(2)}) collective-permute-start(bf16[4,16,32,128]{3,2,0,1:T(8,128)(2,1)S(1)} %bitcast.89), channel_id=1, source_target_pairs={{0,16},{16,0},{32,48},{48,32},{64,80},{80,64},{96,112},{112,96},{1... | collective-permute-start | bytes 1572872 | tf_op jit(solution)/shard_map/ppermute | solution.py:202
  314.8 25.8 %collective-permute-start.1 = (bf16[4,1024,128]{2,1,0:T(8,128)(2,1)}, bf16[4,1024,128]{2,1,0:T(8,128)(2,1)}, u32[]{:S(2)}, u32[]{:S(2)}) collective-permute-start(bf16[4,1024,128]{2,1,0:T(8,128)(2,1)} %get-tuple-element.33), channel_id=1, source_target_pairs={{0,16},{16,0},{32,48},{48,32},{64,80},{80,64},{96,112},{112,96},{1... | collective-permute-start | bytes 3145736 | tf_op jit(solution)/shard_map/ppermute | solution.py:202
  332.3 5.4 %collective-permute-start.2 = (bf16[4,16,32,128]{3,2,0,1:T(8,128)(2,1)}, bf16[4,16,32,128]{3,2,0,1:T(8,128)(2,1)}, u32[]{:S(2)}, u32[]{:S(2)}) collective-permute-start(bf16[4,16,32,128]{3,2,0,1:T(8,128)(2,1)} %bitcast.82), channel_id=1, source_target_pairs={{0,16},{16,0},{32,48},{48,32},{64,80},{80,64},{96,112},{112,96},{1... | collective-permute-start | bytes 1572872 | tf_op jit(solution)/shard_map/ppermute | solution.py:209
  345.2 142.3 %copy-start.1 = (bf16[128,64,128]{2,1,0:T(8,128)(2,1)S(1)}, bf16[128,64,128]{2,1,0:T(8,128)(2,1)}, u32[]{:S(2)}) copy-start(bf16[128,64,128]{2,1,0:T(8,128)(2,1)} %param.17) | copy-start | bytes 6291460
  345.2 139.2 %all-reduce.8.cloned.1.call-start = ((), (), s32[]{:S(2)}) async-start(), calls=%async_computation.6 | async-start | bytes 1114112 | tf_op jit(solution)/shard_map/psum | solution.py:230
Sparse Core Ops, SparseCore 0:
  45.2 136.7 all-gather.5
  184.7 105.5 all-gather.3
  345.4 76.8 reduce-scatter.1
  425.0 59.4 all-reduce.7

commit v3 on v2

--- a/solution.py
+++ b/solution.py
@@ -152,8 +152,6 @@
     rows, hidden = w_first.shape
     bias_cols = jnp.broadcast_to(bias_first[:, None], (rows, 128))
     packed = lax.all_gather(jnp.concatenate([w_first, bias_cols], axis=1), "fsdp", axis=0, tiled=True)
-    first_full = packed[:, :hidden]
-    bias_full = packed[:, hidden].astype(jnp.float32)
     second_full = lax.all_gather(w_second, "fsdp", axis=0, tiled=True)
 
     chosen = pull_list[0]
@@ -169,6 +167,9 @@
     second_cols = history_second.shape[1]
     sent_first = jnp.take(history_first, chosen.reshape(-1), axis=0, mode="clip").reshape(requesters, slot_cap, first_cols, block_len)
     sent_second = jnp.take(history_second, chosen.reshape(-1), axis=0, mode="clip").reshape(requesters, slot_cap, second_cols, block_len)
+    packed, second_full, sent_first, sent_second = lax.optimization_barrier((packed, second_full, sent_first, sent_second))
+    first_full = packed[:, :hidden]
+    bias_full = packed[:, hidden].astype(jnp.float32)
     arrived_first = lax.all_to_all(sent_first, ("dom", "fsdp"), split_axis=0, concat_axis=0, tiled=True)
     arrived_second = lax.all_to_all(sent_second, ("dom", "fsdp"), split_axis=0, concat_axis=0, tiled=True)
     pulled_first = arrived_first.reshape(dom_size, fsdp_size, slot_cap, first_cols, block_len)

time: 494 us -> 509 us (1.030)
  blocking collectives: 12.4 us -> 117 us
  waiting for transfers between devices: 339 us -> 256 us
  starting transfers between devices: 23.6 us -> 7.26 us
  local copies, waits for them, and re-layouts: 37.8 us -> 46.2 us
    all_to_all x0 -> x1, blocking collectives: none -> 105 us  [on_device(): lax.all_to_all(sent_first, ('dom', 'fsdp'), split_axis=0, concat_axis=0,...]
    all_to_all x1 -> x0, waiting for transfers between devices: 88.3 us -> none  [on_device(): lax.all_to_all(sent_first, ('dom', 'fsdp'), split_axis=0, concat_axis=0,...]
    all_to_all x1, waiting for transfers between devices: 0.01 us -> 59.3 us  [on_device(): lax.all_to_all(sent_second, ('dom', 'fsdp'), split_axis=0, concat_axis=0,...]
    all_gather x1, waiting for transfers between devices: 92.4 us -> 47.4 us  [on_device(): lax.all_gather(jnp.concatenate([w_first, bias_cols], axis=1), 'fsdp', axi...]
    all_gather x1, waiting for transfers between devices: 20.4 us -> 0.02 us  [on_device(): second_full = lax.all_gather(w_second, 'fsdp', axis=0, tiled=True)]
    reduce_scatter x1, waiting for transfers between devices: 77 us -> 88.6 us  [on_device(): lax.psum_scatter(packed_terms, 'fsdp', scatter_dimension=0, tiled=True)]
    all_to_all x1 -> x0, starting transfers between devices: 8.29 us -> none  [on_device(): lax.all_to_all(sent_first, ('dom', 'fsdp'), split_axis=0, concat_axis=0,...]
    all_to_all x1, starting transfers between devices: 13.7 us -> 5.79 us  [on_device(): lax.all_to_all(sent_second, ('dom', 'fsdp'), split_axis=0, concat_axis=0,...]
  transfers between devices with their start and end apart: 10 -> 9, of which waited for: 5 -> 4; matrix products, arithmetic and copies ran while one was open for 8% -> 12% of each run, Pallas kernels for 9% -> 8%
where the time goes in v3:
time: 509 us; the launch traced here: 506 us
  waiting for transfers between devices  256 us (50%)
  blocking collectives  117 us (23%)
  local copies, waits for them, and re-layouts  46.2 us (9%)
  Pallas kernels  39.4 us (8%)
  matrix products  20.1 us (4%)
  between operations  13.9 us (3%)
  starting transfers between devices  7.26 us (1%)
  other arithmetic  6.15 us (1%)
    all_to_all x1, blocking collectives, on_device(): lax.all_to_all(sent_first, ('dom', 'fsdp'), split_axis=0, concat_axis=0,...  105 us
    reduce_scatter x1, waiting for transfers between devices, on_device(): lax.psum_scatter(packed_terms, 'fsdp', scatter_dimension=0, tiled=True)  88.6 us
    psum x1, waiting for transfers between devices, on_device(): total = lax.psum(full, 'dom')  59.6 us
    all_to_all x1, waiting for transfers between devices, on_device(): lax.all_to_all(sent_second, ('dom', 'fsdp'), split_axis=0, concat_axis=0,...  59.3 us
    all_gather x1, waiting for transfers between devices, on_device(): lax.all_gather(jnp.concatenate([w_first, bias_cols], axis=1), 'fsdp', axi...  47.4 us
    pallas_call x2, Pallas kernels, aggregate(): pl.pallas_call(functools.partial(_agg_kernel, nb, tiles - 1), grid_spec=g...  28.7 us
    gather x1, local copies, waits for them, and re-layouts, on_device(): jnp.take(history_second, chosen.reshape(-1), axis=0, mode='clip')  21.2 us
    gather x1, local copies, waits for them, and re-layouts, on_device(): jnp.take(history_first, chosen.reshape(-1), axis=0, mode='clip')  13.4 us
  transfers between devices with their start and end apart: 9, of which 4 were waited for; matrix products, arithmetic and copies ran while one was open for 12% of the time, Pallas kernels for 8%

profile of v3, /device:TPU:1, one launch (start us, length us, event | category | flops | bytes accessed | tf_op | source)
XLA Modules:
  0.0 506.0 jit_solution(7944501930415986738)
XLA Ops:
  8.7 1.6 pad_maximum_fusion
  10.3 12.2 %all-gather = s32[8,1,128]{2,1,0:T(1,128)S(1)} all-gather(s32[1,1,128]{2,1,0:T(1,128)} %bitcast.93), channel_id=1, replica_groups=mesh['dom'=8,'fsdp'=16] {'dom'}, dimensions={0}, use_global_device_ids=true | all-gather | bytes 4608 | tf_op jit(solution)/shard_map/all_gather | solution.py:159
  23.4 13.4 %gather_fusion = bf16[512,64,128]{2,1,0:T(8,128)(2,1)} fusion(bf16[128,64,128]{2,1,0:T(8,128)(2,1)S(1)} %copy-done, s32[1024]{0:T(1024)S(1)} %pad_clamp_fusion), kind=kCustom, calls=%fused_computation | custom fusion | bytes 16779264 | tf_op jit(solution)/shard_map/jit(_take)/gather | solution.py:168
  36.9 21.2 %gather_fusion.1 = bf16[512,64,128]{2,1,0:T(8,128)(2,1)} fusion(bf16[128,64,128]{2,1,0:T(8,128)(2,1)} %param.18, s32[1024]{0:T(1024)S(1)} %pad_clamp_fusion), kind=kCustom, calls=%fused_computation.1 | custom fusion | bytes 16779264 | tf_op jit(solution)/shard_map/jit(_take)/gather | solution.py:169
  58.1 47.4 %all-gather.4.cloned.1.call-done = bf16[1024,1152]{1,0:T(8,128)(2,1)} async-done(((bf16[64,1152]{1,0:T(8,128)(2,1)}), bf16[1024,1152]{1,0:T(8,128)(2,1)}) %all-gather.4.cloned.1.call-update) | async-done | bytes 2359312 | tf_op jit(solution)/shard_map/all_gather | solution.py:154
  105.5 105.1 %all_to_all.10 = bf16[128,4,64,128]{3,2,1,0:T(8,128)(2,1)} all-to-all(bf16[128,4,64,128]{3,2,1,0:T(8,128)(2,1)} %bitcast.86), channel_id=1, replica_groups=mesh['dom'=8,'fsdp'=16] {'dom','fsdp'}, dimensions={0} | all-to-all | bytes 16777216 | tf_op jit(solution)/shard_map/all_to_all | solution.py:173
  210.6 5.8 %all-to-all-start.1 = ((bf16[128,4,64,128]{3,2,1,0:T(8,128)(2,1)}), bf16[128,4,64,128]{3,2,1,0:T(8,128)(2,1)}, u32[]{:S(2)}, u32[]{:S(2)}) async-start(bf16[128,4,64,128]{3,2,1,0:T(8,128)(2,1)} %bitcast.84), calls=%async_computation.1 | async-start | bytes 16777216 | tf_op jit(solution)/shard_map/all_to_all | solution.py:174
  216.5 1.2 collective-permute-start.3
  218.5 4.1 fusion.18.back_ref
  222.5 10.8 %shard_map.148 = f32[4,1024,128]{2,1,0:T(8,128)} custom-call(s32[4,6]{1,0:T(4,128)} %src_ref.5, s32[4]{0:T(128)} %cnt_ref.5, bf16[4,1024,128]{2,1,0:T(8,128)(2,1)} %fusion.18.back_ref, bf16[4,6,128,128]{3,2,1,0:T(8,128)(2,1)} %tile_ref.5), custom_call_target="tpu_custom_call" | custom-call | flops 805306368 | bytes 3932160 | tf_op jit(solution)/shard_map/pallas_call | solution.py:122
  234.4 14.3 %shard_map.147 = bf16[4,1024,128]{2,1,0:T(8,128)(2,1)} custom-call(s32[4,6]{1,0:T(4,128)} %src_ref.5, s32[4]{0:T(128)} %cnt_ref.5, s32[32]{0:T(128)} %reshape.124.live_ref, bf16[4,1024,128]{2,1,0:T(8,128)(2,1)} %own_ref.1, bf16[8,16,4,64,128]{4,3,2,1,0:T(8,128)(2,1)} %bitcast.85, bf16[4,6,128,128]{3,2,1,0:T(8,128)(2,1)} %tile_ref.5), custom_call_target="tpu_custom_call" | custom-call | flops 805306368 | bytes 14417920 | tf_op jit(solution)/shard_map/pallas_call | solution.py:77
  248.8 1.5 constant_dynamic-slice_fusion.2
  251.0 5.8 %convert_reduce_fusion = (f32[1024]{0:T(1024)S(1)}, bf16[4,1024,128]{2,1,0:T(8,128)(2,1)}, bf16[4,1024,128]{2,1,0:T(8,128)(2,1)}) fusion(f32[4,1024,128]{2,1,0:T(8,128)S(1)} %copy-done.3, f32[1024]{0:T(1024)S(1)} %convert_reduce_fusion.1, bf16[4,1024,128]{2,1,0:T(8,128)(2,1)S(1)} %copy-done.2, bf16[1024,1152]{1,0:T(8,128)(2,1)} %all-gather.4.cloned.1.call-done), kind=kOutput, calls=%fused_computation.24 | convolution fusion | flops 1086848000 | bytes 7348224 | tf_op jit(solution)/shard_map/fh,vfn->vhn/dot_general | solution.py:195
  256.8 59.3 %all-to-all-done.1 = bf16[128,4,64,128]{3,2,1,0:T(8,128)(2,1)} async-done(((bf16[128,4,64,128]{3,2,1,0:T(8,128)(2,1)}), bf16[128,4,64,128]{3,2,1,0:T(8,128)(2,1)}, u32[]{:S(2)}, u32[]{:S(2)}) %all-to-all-start.1) | async-done | bytes 8388640 | tf_op jit(solution)/shard_map/all_to_all | solution.py:174
  316.1 14.3 %shard_map.149 = bf16[4,1024,128]{2,1,0:T(8,128)(2,1)} custom-call(s32[4,6]{1,0:T(4,128)} %src_ref.5, s32[4]{0:T(128)} %cnt_ref.5, s32[32]{0:T(128)} %reshape.124.live_ref, bf16[4,1024,128]{2,1,0:T(8,128)(2,1)} %get-tuple-element.42.own_ref, bf16[8,16,4,64,128]{4,3,2,1,0:T(8,128)(2,1)} %bitcast.19.pulled_ref, bf16[4,6,128,128]{3,2,1,0:T(8,128)(2,1)} %tile_ref.5), custom_call_target="tpu_custom_call" | custom-call | flops 805306368 | bytes 14417920 | tf_op jit(solution)/shard_map/pallas_call | solution.py:77
  330.5 1.3 constant_dynamic-slice_fusion
  332.7 2.0 fusion.25
  334.6 3.3 fusion.22
  338.0 2.8 bitcast_add_fusion
  340.9 2.1 bitcast_add_fusion.1
  343.0 2.6 select_maximum_fusion
  345.6 88.6 %reduce-scatter.2.cloned.1.call-done = f32[64,1152]{1,0:T(8,128)} async-done(((f32[1024,1152]{1,0:T(8,128)}), f32[64,1152]{1,0:T(8,128)}) %reduce-scatter.2.cloned.1.call-update) | async-done | bytes 294928 | tf_op jit(solution)/shard_map/reduce_scatter | solution.py:221
  436.8 59.6 %all-reduce.8.cloned.1.call-done = f32[136,1024]{1,0:T(8,128)} async-done(((f32[136,1024]{1,0:T(8,128)}), f32[136,1024]{1,0:T(8,128)}) %all-reduce.8.cloned.1.call-update) | async-done | bytes 557072 | tf_op jit(solution)/shard_map/psum | solution.py:231
  496.4 1.9 fusion.33
  (40 shorter events, 9.9 us)
Async XLA Ops:
  7.2 16.3 %copy-start = (bf16[128,64,128]{2,1,0:T(8,128)(2,1)S(1)}, bf16[128,64,128]{2,1,0:T(8,128)(2,1)}, u32[]{:S(2)}) copy-start(bf16[128,64,128]{2,1,0:T(8,128)(2,1)} %param.17) | copy-start | bytes 6291460
  7.2 51.0 %all-gather.6.cloned.1.call-start = ((), (), s32[]{:S(2)}) async-start(), calls=%async_computation.4 | async-start | bytes 2228224 | tf_op jit(solution)/shard_map/all_gather | solution.py:155
  7.9 97.6 %all-gather.4.cloned.1.call-start = ((), (), s32[]{:S(2)}) async-start(), calls=%async_computation.3 | async-start | bytes 2506752 | tf_op jit(solution)/shard_map/all_gather | solution.py:154
  210.6 105.5 %all-to-all-start.1 = ((bf16[128,4,64,128]{3,2,1,0:T(8,128)(2,1)}), bf16[128,4,64,128]{3,2,1,0:T(8,128)(2,1)}, u32[]{:S(2)}, u32[]{:S(2)}) async-start(bf16[128,4,64,128]{3,2,1,0:T(8,128)(2,1)} %bitcast.84), calls=%async_computation.1 | async-start | bytes 16777216 | tf_op jit(solution)/shard_map/all_to_all | solution.py:174
  216.4 217.8 %reduce-scatter.2.cloned.1.call-start = ((), (), s32[]{:S(2)}) async-start(), calls=%async_computation.5 | async-start | bytes 5013504 | tf_op jit(solution)/shard_map/reduce_scatter | solution.py:221
  216.5 121.5 %collective-permute-start.3 = (bf16[4,1024,128]{2,1,0:T(8,128)(2,1)}, bf16[4,1024,128]{2,1,0:T(8,128)(2,1)}, u32[]{:S(2)}, u32[]{:S(2)}) collective-permute-start(bf16[4,1024,128]{2,1,0:T(8,128)(2,1)} %param.27), channel_id=1, source_target_pairs={{0,16},{16,0},{32,48},{48,32},{64,80},{80,64},{96,112},{112,96},{1... | collective-permute-start | bytes 3145736 | tf_op jit(solution)/shard_map/ppermute | solution.py:180
  248.8 1.6 copy-start.2
  248.8 2.2 copy-start.3
  250.3 90.6 %collective-permute-start = (bf16[4,16,32,128]{3,2,0,1:T(8,128)(2,1)S(1)}, bf16[4,16,32,128]{3,2,0,1:T(8,128)(2,1)}, u32[]{:S(2)}, u32[]{:S(2)}) collective-permute-start(bf16[4,16,32,128]{3,2,0,1:T(8,128)(2,1)S(1)} %bitcast.90), channel_id=1, source_target_pairs={{0,16},{16,0},{32,48},{48,32},{64,80},{80,64},{96,112},{112,96},{1... | collective-permute-start | bytes 1572872 | tf_op jit(solution)/shard_map/ppermute | solution.py:203
  256.8 84.0 %collective-permute-start.1 = (bf16[4,1024,128]{2,1,0:T(8,128)(2,1)}, bf16[4,1024,128]{2,1,0:T(8,128)(2,1)}, u32[]{:S(2)}, u32[]{:S(2)}) collective-permute-start(bf16[4,1024,128]{2,1,0:T(8,128)(2,1)} %get-tuple-element.41), channel_id=1, source_target_pairs={{0,16},{16,0},{32,48},{48,32},{64,80},{80,64},{96,112},{112,96},{1... | collective-permute-start | bytes 3145736 | tf_op jit(solution)/shard_map/ppermute | solution.py:203
  332.7 5.4 %collective-permute-start.2 = (bf16[4,16,32,128]{3,2,0,1:T(8,128)(2,1)}, bf16[4,16,32,128]{3,2,0,1:T(8,128)(2,1)}, u32[]{:S(2)}, u32[]{:S(2)}) collective-permute-start(bf16[4,16,32,128]{3,2,0,1:T(8,128)(2,1)} %bitcast.82), channel_id=1, source_target_pairs={{0,16},{16,0},{32,48},{48,32},{64,80},{80,64},{96,112},{112,96},{1... | collective-permute-start | bytes 1572872 | tf_op jit(solution)/shard_map/ppermute | solution.py:210
  345.6 153.9 %copy-start.1 = (bf16[128,64,128]{2,1,0:T(8,128)(2,1)S(1)}, bf16[128,64,128]{2,1,0:T(8,128)(2,1)}, u32[]{:S(2)}) copy-start(bf16[128,64,128]{2,1,0:T(8,128)(2,1)} %param.17) | copy-start | bytes 6291460
  345.6 150.8 %all-reduce.8.cloned.1.call-start = ((), (), s32[]{:S(2)}) async-start(), calls=%async_computation.6 | async-start | bytes 1114112 | tf_op jit(solution)/shard_map/psum | solution.py:231
Sparse Core Ops, SparseCore 0:
  10.2 47.4 all-gather.5
  60.3 45.1 all-gather.3
  345.7 88.5 reduce-scatter.1
  437.0 59.4 all-reduce.7

commit v4 on v2

--- a/solution.py
+++ b/solution.py
@@ -130,6 +130,12 @@
             bytes_accessed=back_second.size * 2 + nb * tiles * blk * blk * 2 + back_second.size * 4,
         ),
     )(tile_src, tile_count, back_second, tile_values)
+
+
+def gather_rows(x, axis):
+    n = lax.axis_size(axis)
+    spread = lax.all_to_all(jnp.broadcast_to(x[None], (n,) + x.shape), axis, split_axis=0, concat_axis=0, tiled=True)
+    return spread.reshape((n * x.shape[0],) + x.shape[1:])
 
 
 def on_device(
@@ -151,10 +157,10 @@
     me = lax.axis_index("dom") * fsdp_size + lax.axis_index("fsdp")
     rows, hidden = w_first.shape
     bias_cols = jnp.broadcast_to(bias_first[:, None], (rows, 128))
-    packed = lax.all_gather(jnp.concatenate([w_first, bias_cols], axis=1), "fsdp", axis=0, tiled=True)
+    packed = gather_rows(jnp.concatenate([w_first, bias_cols], axis=1), "fsdp")
     first_full = packed[:, :hidden]
     bias_full = packed[:, hidden].astype(jnp.float32)
-    second_full = lax.all_gather(w_second, "fsdp", axis=0, tiled=True)
+    second_full = gather_rows(w_second, "fsdp")
 
     chosen = pull_list[0]
     requesters, slot_cap = chosen.shape
@@ -217,20 +223,17 @@
     bias_cols = bias_cols.at[:, 0, : hidden // fsdp_size].set(bias_term.reshape(fsdp_size, hidden // fsdp_size))
     packed_terms = jnp.concatenate([jnp.concatenate([first_term, second_term], axis=1), bias_cols], axis=2)
     packed_terms = packed_terms.reshape(fsdp_size * 2 * half_rows, hidden + lanes)
-    shard = lax.psum_scatter(packed_terms, "fsdp", scatter_dimension=0, tiled=True)
-    zero_half = jnp.zeros((half_rows, hidden), jnp.float32)
-
-    def placed(part):
-        return jnp.where(core == 0, jnp.concatenate([part, zero_half], 0), jnp.concatenate([zero_half, part], 0))
-
-    bias_block = jnp.zeros((8, hidden), jnp.float32).at[0, :lanes].set(shard[0, hidden:])
-    full = jnp.concatenate(
-        [placed(shard[:half_rows, :hidden]), placed(shard[half_rows:, :hidden]), bias_block], axis=0
-    )
-    total = lax.psum(full, "dom")
-    first_total = total[: 2 * half_rows]
-    second_total = total[2 * half_rows : 4 * half_rows]
-    bias_total = total[4 * half_rows, : hidden // fsdp_size]
+    arrived_terms = lax.all_to_all(
+        packed_terms.reshape(fsdp_size, 2 * half_rows, hidden + lanes), "fsdp", split_axis=0, concat_axis=0, tiled=True
+    )
+    shard = jnp.sum(arrived_terms, axis=0)
+    everyone = lax.all_to_all(
+        jnp.broadcast_to(shard[None], (dom_size,) + shard.shape), "dom", split_axis=0, concat_axis=0, tiled=True
+    )
+    by_core = jnp.sum(everyone.reshape(dom_size // 2, 2, 2 * half_rows, hidden + lanes), axis=0)
+    first_total = by_core[:, :half_rows, :hidden].reshape(2 * half_rows, hidden)
+    second_total = by_core[:, half_rows:, :hidden].reshape(2 * half_rows, hidden)
+    bias_total = jnp.sum(by_core[:, 0, hidden : hidden + hidden // fsdp_size], axis=0)
     return (hidden_new, first_total, second_total, bias_total)
 
 

time: 494 us -> 449 us (0.909)
  waiting for transfers between devices: 339 us -> 177 us
  blocking collectives: 12.4 us -> 115 us
  starting transfers between devices: 23.6 us -> 50.7 us
  between operations: 13.9 us -> 0.84 us
    all_gather x2 -> x0, waiting for transfers between devices: 113 us -> none  [the longest x1 92.4 us: on_device(): lax.all_gather(jnp.concatenate([w_first, bias_cols], axis=1), 'fsdp', axi...]
    all_to_all x0 -> x2, blocking collectives: none -> 102 us  [the longest x1 67.8 us: on_device(): lax.all_to_all(packed_terms.reshape(fsdp_size, 2 * half_rows, hidden + la...]
    reduce_scatter x1 -> x0, waiting for transfers between devices: 77 us -> none  [on_device(): lax.psum_scatter(packed_terms, 'fsdp', scatter_dimension=0, tiled=True)]
    psum x1 -> x0, waiting for transfers between devices: 59.6 us -> none  [on_device(): total = lax.psum(full, 'dom')]
    all_to_all x1, waiting for transfers between devices: 0.01 us -> 56.2 us  [on_device(): lax.all_to_all(sent_second, ('dom', 'fsdp'), split_axis=0, concat_axis=0,...]
    all_to_all x0 -> x2, waiting for transfers between devices: none -> 34.8 us  [gather_rows(): lax.all_to_all(jnp.broadcast_to(x[None], (n,) + x.shape), axis, split_axi...]
    all_to_all x0 -> x2, starting transfers between devices: none -> 13.2 us  [gather_rows(): lax.all_to_all(jnp.broadcast_to(x[None], (n,) + x.shape), axis, split_axi...]
    all_to_all x1, starting transfers between devices: 13.7 us -> 19 us  [on_device(): lax.all_to_all(sent_second, ('dom', 'fsdp'), split_axis=0, concat_axis=0,...]
  transfers between devices with their start and end apart: 10 -> 8, of which waited for: 5 -> 4; matrix products, arithmetic and copies ran while one was open for 8% -> 11% of each run, Pallas kernels for 9% -> 9%
where the time goes in v4:
time: 449 us; the launch traced here: 446 us
  waiting for transfers between devices  177 us (39%)
  blocking collectives  115 us (26%)
  starting transfers between devices  50.7 us (11%)
  Pallas kernels  38.6 us (9%)
  local copies, waits for them, and re-layouts  37.3 us (8%)
  matrix products  20.1 us (4%)
  other arithmetic  6.53 us (1%)
    all_to_all x1, waiting for transfers between devices, on_device(): lax.all_to_all(sent_first, ('dom', 'fsdp'), split_axis=0, concat_axis=0,...  86.3 us
    all_to_all x1, blocking collectives, on_device(): lax.all_to_all(packed_terms.reshape(fsdp_size, 2 * half_rows, hidden + la...  67.8 us
    all_to_all x1, waiting for transfers between devices, on_device(): lax.all_to_all(sent_second, ('dom', 'fsdp'), split_axis=0, concat_axis=0,...  56.2 us
    all_to_all x2, waiting for transfers between devices, gather_rows(): lax.all_to_all(jnp.broadcast_to(x[None], (n,) + x.shape), axis, split_axi...  34.8 us
    all_to_all x1, blocking collectives, on_device(): lax.all_to_all(jnp.broadcast_to(shard[None], (dom_size,) + shard.shape),...  34.5 us
    pallas_call x2, Pallas kernels, aggregate(): pl.pallas_call(functools.partial(_agg_kernel, nb, tiles - 1), grid_spec=g...  27.7 us
    all_to_all x1, starting transfers between devices, on_device(): lax.all_to_all(sent_second, ('dom', 'fsdp'), split_axis=0, concat_axis=0,...  19 us
    gather x1, local copies, waits for them, and re-layouts, on_device(): jnp.take(history_first, chosen.reshape(-1), axis=0, mode='clip')  13.5 us
  transfers between devices with their start and end apart: 8, of which 4 were waited for; matrix products, arithmetic and copies ran while one was open for 11% of the time, Pallas kernels for 9%

profile of v4, /device:TPU:1, one launch (start us, length us, event | category | flops | bytes accessed | tf_op | source)
XLA Modules:
  0.0 446.4 jit_solution(4844610671126461041)
XLA Ops:
  0.6 2.7 broadcast_in_dim.16
  3.3 8.6 %all-to-all-start.2 = ((bf16[16,64,1024]{2,1,0:T(8,128)(2,1)}), bf16[16,64,1024]{2,1,0:T(8,128)(2,1)}, u32[]{:S(2)}, u32[]{:S(2)}) async-start(bf16[16,64,1024]{2,1,0:T(8,128)(2,1)} %broadcast_in_dim.16), calls=%async_computation.2 | async-start | bytes 4194304 | tf_op jit(solution)/shard_map/all_to_all | solution.py:137
  12.0 30.4 %all-to-all-done.2 = bf16[16,64,1024]{2,1,0:T(8,128)(2,1)} async-done(((bf16[16,64,1024]{2,1,0:T(8,128)(2,1)}), bf16[16,64,1024]{2,1,0:T(8,128)(2,1)}, u32[]{:S(2)}, u32[]{:S(2)}) %all-to-all-start.2) | async-done | bytes 2097184 | tf_op jit(solution)/shard_map/all_to_all | solution.py:137
  44.3 4.6 %all-to-all-start.1 = ((bf16[16,64,1152]{2,1,0:T(8,128)(2,1)}), bf16[16,64,1152]{2,1,0:T(8,128)(2,1)}, u32[]{:S(2)}, u32[]{:S(2)}) async-start(bf16[16,64,1152]{2,1,0:T(8,128)(2,1)} %broadcast_in_dim.14), calls=%async_computation.1 | async-start | bytes 4718592 | tf_op jit(solution)/shard_map/all_to_all | solution.py:137
  48.9 12.7 %all-gather = s32[8,1,128]{2,1,0:T(1,128)S(1)} all-gather(s32[1,1,128]{2,1,0:T(1,128)S(1)} %bitcast.92), channel_id=1, replica_groups=mesh['dom'=8,'fsdp'=16] {'dom'}, dimensions={0}, use_global_device_ids=true | all-gather | bytes 4608 | tf_op jit(solution)/shard_map/all_gather | solution.py:167
  61.8 13.5 %gather_fusion = bf16[512,64,128]{2,1,0:T(8,128)(2,1)} fusion(bf16[128,64,128]{2,1,0:T(8,128)(2,1)S(1)} %copy-done, s32[1024]{0:T(1024)S(1)} %pad_clamp_fusion), kind=kCustom, calls=%fused_computation | custom fusion | bytes 16779264 | tf_op jit(solution)/shard_map/jit(_take)/gather | solution.py:176
  75.3 4.4 all-to-all-done.1
  79.7 9.6 %all-to-all-start = ((bf16[128,4,64,128]{3,2,1,0:T(8,128)(2,1)}), bf16[128,4,64,128]{3,2,1,0:T(8,128)(2,1)}, u32[]{:S(2)}, u32[]{:S(2)}) async-start(bf16[128,4,64,128]{3,2,1,0:T(8,128)(2,1)} %bitcast.83), calls=%async_computation | async-start | bytes 16777216 | tf_op jit(solution)/shard_map/all_to_all | solution.py:178
  89.3 13.4 %gather_fusion.1 = bf16[512,64,128]{2,1,0:T(8,128)(2,1)} fusion(bf16[128,64,128]{2,1,0:T(8,128)(2,1)S(1)} %copy-done.2, s32[1024]{0:T(1024)S(1)} %pad_clamp_fusion), kind=kCustom, calls=%fused_computation.1 | custom fusion | bytes 16779264 | tf_op jit(solution)/shard_map/jit(_take)/gather | solution.py:177
  102.8 86.3 %all-to-all-done = bf16[128,4,64,128]{3,2,1,0:T(8,128)(2,1)} async-done(((bf16[128,4,64,128]{3,2,1,0:T(8,128)(2,1)}), bf16[128,4,64,128]{3,2,1,0:T(8,128)(2,1)}, u32[]{:S(2)}, u32[]{:S(2)}) %all-to-all-start) | async-done | bytes 8388640 | tf_op jit(solution)/shard_map/all_to_all | solution.py:178
  189.0 19.0 %all-to-all-start.3 = ((bf16[128,4,64,128]{3,2,1,0:T(8,128)(2,1)}), bf16[128,4,64,128]{3,2,1,0:T(8,128)(2,1)}, u32[]{:S(2)}, u32[]{:S(2)}) async-start(bf16[128,4,64,128]{3,2,1,0:T(8,128)(2,1)} %bitcast.82), calls=%async_computation.3 | async-start | bytes 16777216 | tf_op jit(solution)/shard_map/all_to_all | solution.py:179
  210.2 4.1 fusion.11.back_ref
  214.3 10.9 %shard_map.148 = f32[4,1024,128]{2,1,0:T(8,128)} custom-call(s32[4,6]{1,0:T(4,128)} %src_ref.5, s32[4]{0:T(128)} %cnt_ref.5, bf16[4,1024,128]{2,1,0:T(8,128)(2,1)} %fusion.11.back_ref, bf16[4,6,128,128]{3,2,1,0:T(8,128)(2,1)} %tile_ref.5), custom_call_target="tpu_custom_call" | custom-call | flops 805306368 | bytes 3932160 | tf_op jit(solution)/shard_map/pallas_call | solution.py:122
  226.3 13.9 %shard_map.147 = bf16[4,1024,128]{2,1,0:T(8,128)(2,1)} custom-call(s32[4,6]{1,0:T(4,128)} %src_ref.5, s32[4]{0:T(128)} %cnt_ref.5, s32[32]{0:T(128)} %reshape.116.live_ref, bf16[4,1024,128]{2,1,0:T(8,128)(2,1)} %own_ref.1, bf16[8,16,4,64,128]{4,3,2,1,0:T(8,128)(2,1)} %bitcast.4.pulled_ref, bf16[4,6,128,128]{3,2,1,0:T(8,128)(2,1)} %tile_ref.5), custom_call_target="tpu_custom_call" | custom-call | flops 805306368 | bytes 14417920 | tf_op jit(solution)/shard_map/pallas_call | solution.py:77
  241.6 3.4 collective-permute-start
  245.1 5.8 %convert_reduce_fusion = (f32[1024]{0:T(1024)S(1)}, bf16[4,1024,128]{2,1,0:T(8,128)(2,1)}, bf16[4,1024,128]{2,1,0:T(8,128)(2,1)}) fusion(f32[4,1024,128]{2,1,0:T(8,128)S(1)} %copy-done.4, f32[1024]{0:T(1024)S(1)} %convert_reduce_fusion.1, bf16[4,1024,128]{2,1,0:T(8,128)(2,1)S(1)} %copy-done.3, bf16[1024,1152]{1,0:T(8,128)(2,1)} %bitcast.5), kind=kOutput, calls=%fused_computation.22 | convolution fusion | flops 1086848000 | bytes 7348224 | tf_op jit(solution)/shard_map/fh,vfn->vhn/dot_general | solution.py:200
  251.5 56.2 %all-to-all-done.3 = bf16[128,4,64,128]{3,2,1,0:T(8,128)(2,1)} async-done(((bf16[128,4,64,128]{3,2,1,0:T(8,128)(2,1)}), bf16[128,4,64,128]{3,2,1,0:T(8,128)(2,1)}, u32[]{:S(2)}, u32[]{:S(2)}) %all-to-all-start.3) | async-done | bytes 8388640 | tf_op jit(solution)/shard_map/all_to_all | solution.py:179
  307.8 13.9 %shard_map.149 = bf16[4,1024,128]{2,1,0:T(8,128)(2,1)} custom-call(s32[4,6]{1,0:T(4,128)} %src_ref.5, s32[4]{0:T(128)} %cnt_ref.5, s32[32]{0:T(128)} %reshape.116.live_ref, bf16[4,1024,128]{2,1,0:T(8,128)(2,1)} %get-tuple-element.22.own_ref, bf16[8,16,4,64,128]{4,3,2,1,0:T(8,128)(2,1)} %bitcast.21.pulled_ref, bf16[4,6,128,128]{3,2,1,0:T(8,128)(2,1)} %tile_ref.5), custom_call_target="tpu_custom_call" | custom-call | flops 805306368 | bytes 14417920 | tf_op jit(solution)/shard_map/pallas_call | solution.py:77
  323.8 3.5 collective-permute-start.2
  329.2 3.3 fusion.13
  332.6 2.8 bitcast_add_fusion
  338.1 67.8 %all_to_all.30 = f32[16,64,1152]{2,1,0:T(8,128)} all-to-all(f32[16,64,1152]{2,1,0:T(8,128)S(1)} %select_maximum_fusion), channel_id=1, replica_groups=mesh['dom'=8,'fsdp'=16] {'fsdp'}, dimensions={0} | all-to-all | bytes 9437184 | tf_op jit(solution)/shard_map/all_to_all | solution.py:226
  405.9 2.6 reduce_sum.37
  408.6 34.5 %all_to_all.31 = f32[8,64,1152]{2,1,0:T(8,128)} all-to-all(f32[8,64,1152]{2,1,0:T(8,128)S(1)} %broadcast_in_dim.17), channel_id=1, replica_groups=mesh['dom'=8,'fsdp'=16] {'dom'}, dimensions={0} | all-to-all | bytes 4718592 | tf_op jit(solution)/shard_map/all_to_all | solution.py:230
  (46 shorter events, 17.7 us)
Async XLA Ops:
  0.6 61.2 %copy-start = (bf16[128,64,128]{2,1,0:T(8,128)(2,1)S(1)}, bf16[128,64,128]{2,1,0:T(8,128)(2,1)}, u32[]{:S(2)}) copy-start(bf16[128,64,128]{2,1,0:T(8,128)(2,1)} %param.15) | copy-start | bytes 6291460
  3.3 8.6 %copy-start.7 = (bf16[64]{0:T(256)(128)(2,1)S(1)}, bf16[64]{0:T(256)(128)(2,1)}, u32[]{:S(2)}) copy-start(bf16[64]{0:T(256)(128)(2,1)} %param.24) | copy-start | bytes 388
  3.3 8.7 %copy-start.5 = (bf16[64,1024]{1,0:T(8,128)(2,1)S(1)}, bf16[64,1024]{1,0:T(8,128)(2,1)}, u32[]{:S(2)}) copy-start(bf16[64,1024]{1,0:T(8,128)(2,1)} %param.22) | copy-start | bytes 393220
  3.3 39.2 %all-to-all-start.2 = ((bf16[16,64,1024]{2,1,0:T(8,128)(2,1)}), bf16[16,64,1024]{2,1,0:T(8,128)(2,1)}, u32[]{:S(2)}, u32[]{:S(2)}) async-start(bf16[16,64,1024]{2,1,0:T(8,128)(2,1)} %broadcast_in_dim.16), calls=%async_computation.2 | async-start | bytes 4194304 | tf_op jit(solution)/shard_map/all_to_all | solution.py:137
  44.3 4.6 %copy-start.8 = (s32[1,128]{1,0:T(1,128)S(1)}, s32[1,128]{1,0:T(1,128)}, u32[]{:S(2)}) copy-start(s32[1,128]{1,0:T(1,128)} %param.18) | copy-start | bytes 1540
  44.3 17.3 %copy-start.6 = (s32[1,128,4]{1,2,0:T(4,128)S(1)}, s32[1,128,4]{1,2,0:T(4,128)}, u32[]{:S(2)}) copy-start(s32[1,128,4]{1,2,0:T(4,128)} %param.17) | copy-start | bytes 6148
  44.3 35.4 %all-to-all-start.1 = ((bf16[16,64,1152]{2,1,0:T(8,128)(2,1)}), bf16[16,64,1152]{2,1,0:T(8,128)(2,1)}, u32[]{:S(2)}, u32[]{:S(2)}) async-start(bf16[16,64,1152]{2,1,0:T(8,128)(2,1)} %broadcast_in_dim.14), calls=%async_computation.1 | async-start | bytes 4718592 | tf_op jit(solution)/shard_map/all_to_all | solution.py:137
  79.7 9.6 %copy-start.2 = (bf16[128,64,128]{2,1,0:T(8,128)(2,1)S(1)}, bf16[128,64,128]{2,1,0:T(8,128)(2,1)}, u32[]{:S(2)}) copy-start(bf16[128,64,128]{2,1,0:T(8,128)(2,1)} %param.16) | copy-start | bytes 6291460
  79.7 109.3 %all-to-all-start = ((bf16[128,4,64,128]{3,2,1,0:T(8,128)(2,1)}), bf16[128,4,64,128]{3,2,1,0:T(8,128)(2,1)}, u32[]{:S(2)}, u32[]{:S(2)}) async-start(bf16[128,4,64,128]{3,2,1,0:T(8,128)(2,1)} %bitcast.83), calls=%async_computation | async-start | bytes 16777216 | tf_op jit(solution)/shard_map/all_to_all | solution.py:178
  189.0 118.8 %all-to-all-start.3 = ((bf16[128,4,64,128]{3,2,1,0:T(8,128)(2,1)}), bf16[128,4,64,128]{3,2,1,0:T(8,128)(2,1)}, u32[]{:S(2)}, u32[]{:S(2)}) async-start(bf16[128,4,64,128]{3,2,1,0:T(8,128)(2,1)} %bitcast.82), calls=%async_computation.3 | async-start | bytes 16777216 | tf_op jit(solution)/shard_map/all_to_all | solution.py:179
  208.0 124.6 %collective-permute-start.3 = (bf16[4,1024,128]{2,1,0:T(8,128)(2,1)}, bf16[4,1024,128]{2,1,0:T(8,128)(2,1)}, u32[]{:S(2)}, u32[]{:S(2)}) collective-permute-start(bf16[4,1024,128]{2,1,0:T(8,128)(2,1)} %param.25), channel_id=1, source_target_pairs={{0,16},{16,0},{32,48},{48,32},{64,80},{80,64},{96,112},{112,96},{1... | collective-permute-start | bytes 3145736 | tf_op jit(solution)/shard_map/ppermute | solution.py:185
  240.1 4.9 %copy-start.3 = (bf16[4,1024,128]{2,1,0:T(8,128)(2,1)S(1)}, bf16[4,1024,128]{2,1,0:T(8,128)(2,1)}, u32[]{:S(2)}) copy-start(bf16[4,1024,128]{2,1,0:T(8,128)(2,1)} %shard_map.147) | copy-start | bytes 3145732
  240.1 4.9 %copy-start.4 = (f32[4,1024,128]{2,1,0:T(8,128)S(1)}, f32[4,1024,128]{2,1,0:T(8,128)}, u32[]{:S(2)}) copy-start(f32[4,1024,128]{2,1,0:T(8,128)} %shard_map.148) | copy-start | bytes 6291460
  241.6 93.8 %collective-permute-start = (bf16[4,16,32,128]{3,2,0,1:T(8,128)(2,1)S(1)}, bf16[4,16,32,128]{3,2,0,1:T(8,128)(2,1)}, u32[]{:S(2)}, u32[]{:S(2)}) collective-permute-start(bf16[4,16,32,128]{3,2,0,1:T(8,128)(2,1)S(1)} %bitcast.87), channel_id=1, source_target_pairs={{0,16},{16,0},{32,48},{48,32},{64,80},{80,64},{96,112},{112,96},{1... | collective-permute-start | bytes 1572872 | tf_op jit(solution)/shard_map/ppermute | solution.py:208
  250.9 84.6 %collective-permute-start.1 = (bf16[4,1024,128]{2,1,0:T(8,128)(2,1)}, bf16[4,1024,128]{2,1,0:T(8,128)(2,1)}, u32[]{:S(2)}, u32[]{:S(2)}) collective-permute-start(bf16[4,1024,128]{2,1,0:T(8,128)(2,1)} %get-tuple-element.21), channel_id=1, source_target_pairs={{0,16},{16,0},{32,48},{48,32},{64,80},{80,64},{96,112},{112,96},{1... | collective-permute-start | bytes 3145736 | tf_op jit(solution)/shard_map/ppermute | solution.py:208
  323.8 8.8 %collective-permute-start.2 = (bf16[4,16,32,128]{3,2,0,1:T(8,128)(2,1)}, bf16[4,16,32,128]{3,2,0,1:T(8,128)(2,1)}, u32[]{:S(2)}, u32[]{:S(2)}) collective-permute-start(bf16[4,16,32,128]{3,2,0,1:T(8,128)(2,1)} %bitcast.80), channel_id=1, source_target_pairs={{0,16},{16,0},{32,48},{48,32},{64,80},{80,64},{96,112},{112,96},{1... | collective-permute-start | bytes 1572872 | tf_op jit(solution)/shard_map/ppermute | solution.py:215
  408.6 37.8 %copy-start.1 = (bf16[128,64,128]{2,1,0:T(8,128)(2,1)S(1)}, bf16[128,64,128]{2,1,0:T(8,128)(2,1)}, u32[]{:S(2)}) copy-start(bf16[128,64,128]{2,1,0:T(8,128)(2,1)} %param.15) | copy-start | bytes 6291460

commit v5 on v4

--- a/solution.py
+++ b/solution.py
@@ -210,30 +210,30 @@
         "vprn,vhn->prh", first_mine, back_pre, preferred_element_type=jnp.float32
     ) + jnp.einsum("vprn,vhn->prh", first_got, back_got, preferred_element_type=jnp.float32)
 
+    half_rows = first_term.shape[1]
+    lanes = 128
+    bias_cols = jnp.zeros((fsdp_size, half_rows, lanes), jnp.float32)
+    bias_cols = bias_cols.at[:, 0, : hidden // fsdp_size].set(bias_term.reshape(fsdp_size, hidden // fsdp_size))
+    first_packed = jnp.concatenate([first_term, bias_cols], axis=2)
+    first_shard = jnp.sum(lax.all_to_all(first_packed, "fsdp", split_axis=0, concat_axis=0, tiled=True), axis=0)
+
     agg_second = aggregate(hidden_new, pulled_second, tile_src, tile_count, slot_live, tile_values)
     second_mine, second_theirs = halves(agg_second)
     second_got = lax.ppermute(second_theirs, "dom", pair)
     second_term = jnp.einsum(
         "vprn,vbn->prb", second_mine, out_grad, preferred_element_type=jnp.float32
     ) + jnp.einsum("vprn,vbn->prb", second_got, partner_grad, preferred_element_type=jnp.float32)
-
-    half_rows = first_term.shape[1]
-    lanes = 128
-    bias_cols = jnp.zeros((fsdp_size, 2 * half_rows, lanes), jnp.float32)
-    bias_cols = bias_cols.at[:, 0, : hidden // fsdp_size].set(bias_term.reshape(fsdp_size, hidden // fsdp_size))
-    packed_terms = jnp.concatenate([jnp.concatenate([first_term, second_term], axis=1), bias_cols], axis=2)
-    packed_terms = packed_terms.reshape(fsdp_size * 2 * half_rows, hidden + lanes)
-    arrived_terms = lax.all_to_all(
-        packed_terms.reshape(fsdp_size, 2 * half_rows, hidden + lanes), "fsdp", split_axis=0, concat_axis=0, tiled=True
-    )
-    shard = jnp.sum(arrived_terms, axis=0)
-    everyone = lax.all_to_all(
-        jnp.broadcast_to(shard[None], (dom_size,) + shard.shape), "dom", split_axis=0, concat_axis=0, tiled=True
-    )
-    by_core = jnp.sum(everyone.reshape(dom_size // 2, 2, 2 * half_rows, hidden + lanes), axis=0)
-    first_total = by_core[:, :half_rows, :hidden].reshape(2 * half_rows, hidden)
-    second_total = by_core[:, half_rows:, :hidden].reshape(2 * half_rows, hidden)
-    bias_total = jnp.sum(by_core[:, 0, hidden : hidden + hidden // fsdp_size], axis=0)
+    second_shard = jnp.sum(lax.all_to_all(second_term, "fsdp", split_axis=0, concat_axis=0, tiled=True), axis=0)
+
+    shard = jnp.concatenate([first_shard, jnp.pad(second_shard, ((0, 0), (0, lanes)))], axis=0)
+    for flip in (2, 4):
+        shard = shard + lax.ppermute(shard, "dom", [(d, d ^ flip) for d in range(dom_size)])
+    other = lax.ppermute(shard, "dom", pair)
+    low = jnp.where(core == 0, shard, other)
+    high = jnp.where(core == 0, other, shard)
+    first_total = jnp.concatenate([low[:half_rows, :hidden], high[:half_rows, :hidden]], axis=0)
+    second_total = jnp.concatenate([low[half_rows:, :hidden], high[half_rows:, :hidden]], axis=0)
+    bias_total = (shard + other)[0, hidden : hidden + hidden // fsdp_size]
     return (hidden_new, first_total, second_total, bias_total)
 
 

time: 449 us -> 440 us (0.980)
  blocking collectives: 115 us -> 12.7 us
  waiting for transfers between devices: 177 us -> 255 us
  starting transfers between devices: 50.7 us -> 70.2 us
    all_to_all x2 -> x0, blocking collectives: 102 us -> none  [the longest x1 67.8 us: on_device(): lax.all_to_all(packed_terms.reshape(fsdp_size, 2 * half_rows, hidden + la...]
    all_to_all x0 -> x2, waiting for transfers between devices: none -> 58.7 us  [the longest x1 33.3 us: on_device(): lax.all_to_all(first_packed, 'fsdp', split_axis=0, concat_axis=0, tiled=T...]
    all_to_all x0 -> x2, starting transfers between devices: none -> 16.1 us  [the longest x1 11.6 us: on_device(): lax.all_to_all(second_term, 'fsdp', split_axis=0, concat_axis=0, tiled=True)]
    ppermute x0 -> x3, waiting for transfers between devices: none -> 11.6 us  [the longest x2 10.4 us: on_device(): lax.ppermute(shard, 'dom', [(d, d ^ flip) for d in range(dom_size)])]
    ppermute x0 -> x3, starting transfers between devices: none -> 8.1 us  [the longest x2 4.67 us: on_device(): lax.ppermute(shard, 'dom', [(d, d ^ flip) for d in range(dom_size)])]
    all_to_all x1, waiting for transfers between devices: 56.2 us -> 62.2 us  [on_device(): lax.all_to_all(sent_second, ('dom', 'fsdp'), split_axis=0, concat_axis=0,...]
  transfers between devices with their start and end apart: 8 -> 13, of which waited for: 4 -> 10; matrix products, arithmetic and copies ran while one was open for 11% -> 11% of each run, Pallas kernels for 9% -> 9%
where the time goes in v5:
time: 440 us; the launch traced here: 436 us
  waiting for transfers between devices  255 us (58%)
  starting transfers between devices  70.2 us (16%)
  Pallas kernels  38.1 us (9%)
  local copies, waits for them, and re-layouts  34.9 us (8%)
  matrix products  18 us (4%)
  blocking collectives  12.7 us (3%)
  other arithmetic  6.78 us (2%)
    all_to_all x1, waiting for transfers between devices, on_device(): lax.all_to_all(sent_first, ('dom', 'fsdp'), split_axis=0, concat_axis=0,...  86.3 us
    all_to_all x1, waiting for transfers between devices, on_device(): lax.all_to_all(sent_second, ('dom', 'fsdp'), split_axis=0, concat_axis=0,...  62.2 us
    all_to_all x2, waiting for transfers between devices, gather_rows(): lax.all_to_all(jnp.broadcast_to(x[None], (n,) + x.shape), axis, split_axi...  34.8 us
    all_to_all x1, waiting for transfers between devices, on_device(): lax.all_to_all(first_packed, 'fsdp', split_axis=0, concat_axis=0, tiled=T...  33.3 us
    pallas_call x2, Pallas kernels, aggregate(): pl.pallas_call(functools.partial(_agg_kernel, nb, tiles - 1), grid_spec=g...  27.8 us
    all_to_all x1, waiting for transfers between devices, on_device(): lax.all_to_all(second_term, 'fsdp', split_axis=0, concat_axis=0, tiled=True)  25.4 us
    all_to_all x1, starting transfers between devices, on_device(): lax.all_to_all(sent_second, ('dom', 'fsdp'), split_axis=0, concat_axis=0,...  19 us
    gather x1, local copies, waits for them, and re-layouts, on_device(): jnp.take(history_first, chosen.reshape(-1), axis=0, mode='clip')  13.5 us
  transfers between devices with their start and end apart: 13, of which 10 were waited for; matrix products, arithmetic and copies ran while one was open for 11% of the time, Pallas kernels for 9%

profile of v5, /device:TPU:1, one launch (start us, length us, event | category | flops | bytes accessed | tf_op | source)
XLA Modules:
  0.0 436.1 jit_solution(12409130054251600104)
XLA Ops:
  3.3 8.6 %all-to-all-start.2 = ((bf16[16,64,1024]{2,1,0:T(8,128)(2,1)}), bf16[16,64,1024]{2,1,0:T(8,128)(2,1)}, u32[]{:S(2)}, u32[]{:S(2)}) async-start(bf16[16,64,1024]{2,1,0:T(8,128)(2,1)} %broadcast_in_dim.13), calls=%async_computation.2 | async-start | bytes 4194304 | tf_op jit(solution)/shard_map/all_to_all | solution.py:137
  12.0 30.4 %all-to-all-done.2 = bf16[16,64,1024]{2,1,0:T(8,128)(2,1)} async-done(((bf16[16,64,1024]{2,1,0:T(8,128)(2,1)}), bf16[16,64,1024]{2,1,0:T(8,128)(2,1)}, u32[]{:S(2)}, u32[]{:S(2)}) %all-to-all-start.2) | async-done | bytes 2097184 | tf_op jit(solution)/shard_map/all_to_all | solution.py:137
  44.3 4.6 %all-to-all-start.1 = ((bf16[16,64,1152]{2,1,0:T(8,128)(2,1)}), bf16[16,64,1152]{2,1,0:T(8,128)(2,1)}, u32[]{:S(2)}, u32[]{:S(2)}) async-start(bf16[16,64,1152]{2,1,0:T(8,128)(2,1)} %broadcast_in_dim.12), calls=%async_computation.1 | async-start | bytes 4718592 | tf_op jit(solution)/shard_map/all_to_all | solution.py:137
  48.9 12.7 %all-gather = s32[8,1,128]{2,1,0:T(1,128)S(1)} all-gather(s32[1,1,128]{2,1,0:T(1,128)S(1)} %bitcast.89), channel_id=1, replica_groups=mesh['dom'=8,'fsdp'=16] {'dom'}, dimensions={0}, use_global_device_ids=true | all-gather | bytes 4608 | tf_op jit(solution)/shard_map/all_gather | solution.py:167
  61.8 13.5 %gather_fusion = bf16[512,64,128]{2,1,0:T(8,128)(2,1)} fusion(bf16[128,64,128]{2,1,0:T(8,128)(2,1)S(1)} %copy-done, s32[1024]{0:T(1024)S(1)} %pad_clamp_fusion), kind=kCustom, calls=%fused_computation | custom fusion | bytes 16779264 | tf_op jit(solution)/shard_map/jit(_take)/gather | solution.py:176
  75.3 4.4 %all-to-all-done.1 = bf16[16,64,1152]{2,1,0:T(8,128)(2,1)} async-done(((bf16[16,64,1152]{2,1,0:T(8,128)(2,1)}), bf16[16,64,1152]{2,1,0:T(8,128)(2,1)}, u32[]{:S(2)}, u32[]{:S(2)}) %all-to-all-start.1) | async-done | bytes 2359328 | tf_op jit(solution)/shard_map/all_to_all | solution.py:137
  79.7 9.6 %all-to-all-start = ((bf16[128,4,64,128]{3,2,1,0:T(8,128)(2,1)}), bf16[128,4,64,128]{3,2,1,0:T(8,128)(2,1)}, u32[]{:S(2)}, u32[]{:S(2)}) async-start(bf16[128,4,64,128]{3,2,1,0:T(8,128)(2,1)} %bitcast.82), calls=%async_computation | async-start | bytes 16777216 | tf_op jit(solution)/shard_map/all_to_all | solution.py:178
  89.3 13.4 %gather_fusion.1 = bf16[512,64,128]{2,1,0:T(8,128)(2,1)} fusion(bf16[128,64,128]{2,1,0:T(8,128)(2,1)S(1)} %copy-done.2, s32[1024]{0:T(1024)S(1)} %pad_clamp_fusion), kind=kCustom, calls=%fused_computation.1 | custom fusion | bytes 16779264 | tf_op jit(solution)/shard_map/jit(_take)/gather | solution.py:177
  102.7 86.3 %all-to-all-done = bf16[128,4,64,128]{3,2,1,0:T(8,128)(2,1)} async-done(((bf16[128,4,64,128]{3,2,1,0:T(8,128)(2,1)}), bf16[128,4,64,128]{3,2,1,0:T(8,128)(2,1)}, u32[]{:S(2)}, u32[]{:S(2)}) %all-to-all-start) | async-done | bytes 8388640 | tf_op jit(solution)/shard_map/all_to_all | solution.py:178
  189.0 19.0 %all-to-all-start.4 = ((bf16[128,4,64,128]{3,2,1,0:T(8,128)(2,1)}), bf16[128,4,64,128]{3,2,1,0:T(8,128)(2,1)}, u32[]{:S(2)}, u32[]{:S(2)}) async-start(bf16[128,4,64,128]{3,2,1,0:T(8,128)(2,1)} %bitcast.81), calls=%async_computation.4 | async-start | bytes 16777216 | tf_op jit(solution)/shard_map/all_to_all | solution.py:179
  210.2 3.8 fusion.11.back_ref
  214.0 10.3 %shard_map.148 = f32[4,1024,128]{2,1,0:T(8,128)} custom-call(s32[4,6]{1,0:T(4,128)} %src_ref.5, s32[4]{0:T(128)} %cnt_ref.5, bf16[4,1024,128]{2,1,0:T(8,128)(2,1)} %fusion.11.back_ref, bf16[4,6,128,128]{3,2,1,0:T(8,128)(2,1)} %tile_ref.5), custom_call_target="tpu_custom_call" | custom-call | flops 805306368 | bytes 3932160 | tf_op jit(solution)/shard_map/pallas_call | solution.py:122
  225.5 14.0 %shard_map.147 = bf16[4,1024,128]{2,1,0:T(8,128)(2,1)} custom-call(s32[4,6]{1,0:T(4,128)} %src_ref.5, s32[4]{0:T(128)} %cnt_ref.5, s32[32]{0:T(128)} %reshape.103.live_ref, bf16[4,1024,128]{2,1,0:T(8,128)(2,1)} %own_ref.1, bf16[8,16,4,64,128]{4,3,2,1,0:T(8,128)(2,1)} %bitcast.4.pulled_ref, bf16[4,6,128,128]{3,2,1,0:T(8,128)(2,1)} %tile_ref.5), custom_call_target="tpu_custom_call" | custom-call | flops 805306368 | bytes 14417920 | tf_op jit(solution)/shard_map/pallas_call | solution.py:77
  239.4 6.1 %convert_reduce_fusion = (f32[1024]{0:T(1024)S(1)}, bf16[4,1024,128]{2,1,0:T(8,128)(2,1)}, bf16[4,1024,128]{2,1,0:T(8,128)(2,1)}) fusion(f32[4,1024,128]{2,1,0:T(8,128)S(1)} %copy-done.4, f32[1024]{0:T(1024)S(1)} %convert_reduce_fusion.1, bf16[4,1024,128]{2,1,0:T(8,128)(2,1)} %shard_map.147, bf16[1024,1152]{1,0:T(8,128)(2,1)} %bitcast.5), kind=kOutput, calls=%fused_computation.22 | convolution fusion | flops 1086848000 | bytes 7348224 | tf_op jit(solution)/shard_map/fh,vfn->vhn/dot_general | solution.py:200
  245.5 62.2 %all-to-all-done.4 = bf16[128,4,64,128]{3,2,1,0:T(8,128)(2,1)} async-done(((bf16[128,4,64,128]{3,2,1,0:T(8,128)(2,1)}), bf16[128,4,64,128]{3,2,1,0:T(8,128)(2,1)}, u32[]{:S(2)}, u32[]{:S(2)}) %all-to-all-start.4) | async-done | bytes 8388640 | tf_op jit(solution)/shard_map/all_to_all | solution.py:179
  307.7 13.9 %shard_map.149 = bf16[4,1024,128]{2,1,0:T(8,128)(2,1)} custom-call(s32[4,6]{1,0:T(4,128)} %src_ref.5, s32[4]{0:T(128)} %cnt_ref.5, s32[32]{0:T(128)} %reshape.103.live_ref, bf16[4,1024,128]{2,1,0:T(8,128)(2,1)} %get-tuple-element.22.own_ref, bf16[8,16,4,64,128]{4,3,2,1,0:T(8,128)(2,1)} %bitcast.21.pulled_ref, bf16[4,6,128,128]{3,2,1,0:T(8,128)(2,1)} %tile_ref.5), custom_call_target="tpu_custom_call" | custom-call | flops 805306368 | bytes 14417920 | tf_op jit(solution)/shard_map/pallas_call | solution.py:77
  326.7 3.3 bitcast_add_fusion
  330.0 11.6 %all-to-all-start.5 = ((f32[16,32,1024]{2,1,0:T(8,128)}), f32[16,32,1024]{2,1,0:T(8,128)S(1)}, u32[]{:S(2)}, u32[]{:S(2)}) async-start(f32[16,32,1024]{2,1,0:T(8,128)} %bitcast_add_fusion), calls=%async_computation.5 | async-start | bytes 4194304 | tf_op jit(solution)/shard_map/all_to_all | solution.py:226
  349.1 25.4 %all-to-all-done.5 = f32[16,32,1024]{2,1,0:T(8,128)S(1)} async-done(((f32[16,32,1024]{2,1,0:T(8,128)}), f32[16,32,1024]{2,1,0:T(8,128)S(1)}, u32[]{:S(2)}, u32[]{:S(2)}) %all-to-all-start.5) | async-done | bytes 2097184 | tf_op jit(solution)/shard_map/all_to_all | solution.py:226
  374.5 4.4 %all-to-all-start.3 = ((f32[16,32,1152]{2,1,0:T(8,128)}), f32[16,32,1152]{2,1,0:T(8,128)}, u32[]{:S(2)}, u32[]{:S(2)}) async-start(f32[16,32,1152]{2,1,0:T(8,128)} %select_maximum_fusion), calls=%async_computation.3 | async-start | bytes 4718592 | tf_op jit(solution)/shard_map/all_to_all | solution.py:218
  379.1 33.3 %all-to-all-done.3 = f32[16,32,1152]{2,1,0:T(8,128)} async-done(((f32[16,32,1152]{2,1,0:T(8,128)}), f32[16,32,1152]{2,1,0:T(8,128)}, u32[]{:S(2)}, u32[]{:S(2)}) %all-to-all-start.3) | async-done | bytes 2359328 | tf_op jit(solution)/shard_map/all_to_all | solution.py:218
  416.2 4.9 %collective-permute-done.4 = f32[64,1152]{1,0:T(8,128)S(1)} collective-permute-done((f32[64,1152]{1,0:T(8,128)S(1)}, f32[64,1152]{1,0:T(8,128)S(1)}, u32[]{:S(2)}, u32[]{:S(2)}) %collective-permute-start.4) | collective-permute-done | bytes 294944 | tf_op jit(solution)/shard_map/ppermute | solution.py:230
  423.8 5.5 %collective-permute-done.5 = f32[64,1152]{1,0:T(8,128)S(1)} collective-permute-done((f32[64,1152]{1,0:T(8,128)S(1)}, f32[64,1152]{1,0:T(8,128)S(1)}, u32[]{:S(2)}, u32[]{:S(2)}) %collective-permute-start.5) | collective-permute-done | bytes 294944 | tf_op jit(solution)/shard_map/ppermute | solution.py:230
  429.4 3.4 collective-permute-start.6
  (61 shorter events, 30.5 us)
Async XLA Ops:
  0.6 61.1 %copy-start = (bf16[128,64,128]{2,1,0:T(8,128)(2,1)S(1)}, bf16[128,64,128]{2,1,0:T(8,128)(2,1)}, u32[]{:S(2)}) copy-start(bf16[128,64,128]{2,1,0:T(8,128)(2,1)} %param.15) | copy-start | bytes 6291460
  3.3 8.6 %copy-start.8 = (bf16[64]{0:T(256)(128)(2,1)S(1)}, bf16[64]{0:T(256)(128)(2,1)}, u32[]{:S(2)}) copy-start(bf16[64]{0:T(256)(128)(2,1)} %param.24) | copy-start | bytes 388
  3.3 8.7 %copy-start.6 = (bf16[64,1024]{1,0:T(8,128)(2,1)S(1)}, bf16[64,1024]{1,0:T(8,128)(2,1)}, u32[]{:S(2)}) copy-start(bf16[64,1024]{1,0:T(8,128)(2,1)} %param.22) | copy-start | bytes 393220
  3.3 39.2 %all-to-all-start.2 = ((bf16[16,64,1024]{2,1,0:T(8,128)(2,1)}), bf16[16,64,1024]{2,1,0:T(8,128)(2,1)}, u32[]{:S(2)}, u32[]{:S(2)}) async-start(bf16[16,64,1024]{2,1,0:T(8,128)(2,1)} %broadcast_in_dim.13), calls=%async_computation.2 | async-start | bytes 4194304 | tf_op jit(solution)/shard_map/all_to_all | solution.py:137
  44.3 4.6 %copy-start.9 = (s32[1,128]{1,0:T(1,128)S(1)}, s32[1,128]{1,0:T(1,128)}, u32[]{:S(2)}) copy-start(s32[1,128]{1,0:T(1,128)} %param.18) | copy-start | bytes 1540
  44.3 17.3 %copy-start.7 = (s32[1,128,4]{1,2,0:T(4,128)S(1)}, s32[1,128,4]{1,2,0:T(4,128)}, u32[]{:S(2)}) copy-start(s32[1,128,4]{1,2,0:T(4,128)} %param.17) | copy-start | bytes 6148
  44.3 35.4 %all-to-all-start.1 = ((bf16[16,64,1152]{2,1,0:T(8,128)(2,1)}), bf16[16,64,1152]{2,1,0:T(8,128)(2,1)}, u32[]{:S(2)}, u32[]{:S(2)}) async-start(bf16[16,64,1152]{2,1,0:T(8,128)(2,1)} %broadcast_in_dim.12), calls=%async_computation.1 | async-start | bytes 4718592 | tf_op jit(solution)/shard_map/all_to_all | solution.py:137
  79.7 9.6 %copy-start.2 = (bf16[128,64,128]{2,1,0:T(8,128)(2,1)S(1)}, bf16[128,64,128]{2,1,0:T(8,128)(2,1)}, u32[]{:S(2)}) copy-start(bf16[128,64,128]{2,1,0:T(8,128)(2,1)} %param.16) | copy-start | bytes 6291460
  79.7 109.3 %all-to-all-start = ((bf16[128,4,64,128]{3,2,1,0:T(8,128)(2,1)}), bf16[128,4,64,128]{3,2,1,0:T(8,128)(2,1)}, u32[]{:S(2)}, u32[]{:S(2)}) async-start(bf16[128,4,64,128]{3,2,1,0:T(8,128)(2,1)} %bitcast.82), calls=%async_computation | async-start | bytes 16777216 | tf_op jit(solution)/shard_map/all_to_all | solution.py:178
  189.0 19.0 %copy-start.5 = (bf16[4,1024,128]{2,1,0:T(8,128)(2,1)S(1)}, bf16[4,1024,128]{2,1,0:T(8,128)(2,1)}, u32[]{:S(2)}) copy-start(bf16[4,1024,128]{2,1,0:T(8,128)(2,1)} %param.25) | copy-start | bytes 3145732
  189.0 118.8 %all-to-all-start.4 = ((bf16[128,4,64,128]{3,2,1,0:T(8,128)(2,1)}), bf16[128,4,64,128]{3,2,1,0:T(8,128)(2,1)}, u32[]{:S(2)}, u32[]{:S(2)}) async-start(bf16[128,4,64,128]{3,2,1,0:T(8,128)(2,1)} %bitcast.81), calls=%async_computation.4 | async-start | bytes 16777216 | tf_op jit(solution)/shard_map/all_to_all | solution.py:179
  208.0 117.8 %collective-permute-start.3 = (bf16[4,1024,128]{2,1,0:T(8,128)(2,1)S(1)}, bf16[4,1024,128]{2,1,0:T(8,128)(2,1)}, u32[]{:S(2)}, u32[]{:S(2)}) collective-permute-start(bf16[4,1024,128]{2,1,0:T(8,128)(2,1)S(1)} %copy-done.5), channel_id=1, source_target_pairs={{0,16},{16,0},{32,48},{48,32},{64,80},{80,64},{96,112},{112,96},{1... | collective-permute-start | bytes 3145736 | tf_op jit(solution)/shard_map/ppermute | solution.py:185
  225.4 14.0 %copy-start.4 = (f32[4,1024,128]{2,1,0:T(8,128)S(1)}, f32[4,1024,128]{2,1,0:T(8,128)}, u32[]{:S(2)}) copy-start(f32[4,1024,128]{2,1,0:T(8,128)} %shard_map.148) | copy-start | bytes 6291460
  323.0 3.7 collective-permute-start.2
  330.0 12.2 %copy-start.3 = (bf16[4,1024,128]{2,1,0:T(8,128)(2,1)S(1)}, bf16[4,1024,128]{2,1,0:T(8,128)(2,1)}, u32[]{:S(2)}) copy-start(bf16[4,1024,128]{2,1,0:T(8,128)(2,1)} %shard_map.147) | copy-start | bytes 3145732
  330.0 44.5 %all-to-all-start.5 = ((f32[16,32,1024]{2,1,0:T(8,128)}), f32[16,32,1024]{2,1,0:T(8,128)S(1)}, u32[]{:S(2)}, u32[]{:S(2)}) async-start(f32[16,32,1024]{2,1,0:T(8,128)} %bitcast_add_fusion), calls=%async_computation.5 | async-start | bytes 4194304 | tf_op jit(solution)/shard_map/all_to_all | solution.py:226
  341.6 3.9 collective-permute-start.1
  343.1 2.4 collective-permute-start
  374.5 37.9 %all-to-all-start.3 = ((f32[16,32,1152]{2,1,0:T(8,128)}), f32[16,32,1152]{2,1,0:T(8,128)}, u32[]{:S(2)}, u32[]{:S(2)}) async-start(f32[16,32,1152]{2,1,0:T(8,128)} %select_maximum_fusion), calls=%async_computation.3 | async-start | bytes 4718592 | tf_op jit(solution)/shard_map/all_to_all | solution.py:218
  414.3 6.8 %collective-permute-start.4 = (f32[64,1152]{1,0:T(8,128)S(1)}, f32[64,1152]{1,0:T(8,128)S(1)}, u32[]{:S(2)}, u32[]{:S(2)}) collective-permute-start(f32[64,1152]{1,0:T(8,128)S(1)} %select_maximum_fusion.1), channel_id=1, source_target_pairs={{0,32},{16,48},{32,0},{48,16},{64,96},{80,112},{96,64},{112,80},{1... | collective-permute-start | bytes 884744 | tf_op jit(solution)/shard_map/ppermute | solution.py:230
  421.0 15.1 %copy-start.1 = (bf16[128,64,128]{2,1,0:T(8,128)(2,1)S(1)}, bf16[128,64,128]{2,1,0:T(8,128)(2,1)}, u32[]{:S(2)}) copy-start(bf16[128,64,128]{2,1,0:T(8,128)(2,1)} %param.15) | copy-start | bytes 6291460
  421.1 8.3 %collective-permute-start.5 = (f32[64,1152]{1,0:T(8,128)S(1)}, f32[64,1152]{1,0:T(8,128)S(1)}, u32[]{:S(2)}, u32[]{:S(2)}) collective-permute-start(f32[64,1152]{1,0:T(8,128)S(1)} %fusion.24), channel_id=1, source_target_pairs={{0,64},{16,80},{32,96},{48,112},{64,0},{80,16},{96,32},{112,48},{1... | collective-permute-start | bytes 884744 | tf_op jit(solution)/shard_map/ppermute | solution.py:230
  429.4 4.6 %collective-permute-start.6 = (f32[64,1152]{1,0:T(8,128)S(1)}, f32[64,1152]{1,0:T(8,128)S(1)}, u32[]{:S(2)}, u32[]{:S(2)}) collective-permute-start(f32[64,1152]{1,0:T(8,128)S(1)} %add.75), channel_id=1, source_target_pairs={{0,16},{16,0},{32,48},{48,32},{64,80},{80,64},{96,112},{112,96},{1... | collective-permute-start | bytes 884744 | tf_op jit(solution)/shard_map/ppermute | solution.py:231

commit v6 on v5

--- a/solution.py
+++ b/solution.py
@@ -212,20 +212,18 @@
 
     half_rows = first_term.shape[1]
     lanes = 128
-    bias_cols = jnp.zeros((fsdp_size, half_rows, lanes), jnp.float32)
-    bias_cols = bias_cols.at[:, 0, : hidden // fsdp_size].set(bias_term.reshape(fsdp_size, hidden // fsdp_size))
-    first_packed = jnp.concatenate([first_term, bias_cols], axis=2)
-    first_shard = jnp.sum(lax.all_to_all(first_packed, "fsdp", split_axis=0, concat_axis=0, tiled=True), axis=0)
-
     agg_second = aggregate(hidden_new, pulled_second, tile_src, tile_count, slot_live, tile_values)
     second_mine, second_theirs = halves(agg_second)
     second_got = lax.ppermute(second_theirs, "dom", pair)
     second_term = jnp.einsum(
         "vprn,vbn->prb", second_mine, out_grad, preferred_element_type=jnp.float32
     ) + jnp.einsum("vprn,vbn->prb", second_got, partner_grad, preferred_element_type=jnp.float32)
-    second_shard = jnp.sum(lax.all_to_all(second_term, "fsdp", split_axis=0, concat_axis=0, tiled=True), axis=0)
-
-    shard = jnp.concatenate([first_shard, jnp.pad(second_shard, ((0, 0), (0, lanes)))], axis=0)
+
+    bias_cols = jnp.zeros((fsdp_size, 2 * half_rows, lanes), jnp.float32)
+    bias_cols = bias_cols.at[:, 0, : hidden // fsdp_size].set(bias_term.reshape(fsdp_size, hidden // fsdp_size))
+    packed_terms = jnp.concatenate([jnp.concatenate([first_term, second_term], axis=1), bias_cols], axis=2)
+    arrived_terms = lax.all_to_all(packed_terms.astype(jnp.bfloat16), "fsdp", split_axis=0, concat_axis=0, tiled=True)
+    shard = jnp.sum(arrived_terms.astype(jnp.float32), axis=0)
     for flip in (2, 4):
         shard = shard + lax.ppermute(shard, "dom", [(d, d ^ flip) for d in range(dom_size)])
     other = lax.ppermute(shard, "dom", pair)

time: 440 us -> 405 us (0.920)
  waiting for transfers between devices: 255 us -> 194 us
  blocking collectives: 12.7 us -> 55.4 us
  starting transfers between devices: 70.2 us -> 53.3 us
    all_to_all x2 -> x0, waiting for transfers between devices: 58.7 us -> none  [the longest x1 33.3 us: on_device(): lax.all_to_all(first_packed, 'fsdp', split_axis=0, concat_axis=0, tiled=T...]
    all_to_all x0 -> x1, blocking collectives: none -> 42.8 us  [on_device(): lax.all_to_all(packed_terms.astype(jnp.bfloat16), 'fsdp', split_axis=0, c...]
    all_to_all x2 -> x0, starting transfers between devices: 16.1 us -> none  [the longest x1 11.6 us: on_device(): lax.all_to_all(second_term, 'fsdp', split_axis=0, concat_axis=0, tiled=True)]
  transfers between devices with their start and end apart: 13 -> 11, of which waited for: 10 -> 7; matrix products, arithmetic and copies ran while one was open for 11% -> 12% of each run, Pallas kernels for 9% -> 10%
where the time goes in v6:
time: 405 us; the launch traced here: 402 us
  waiting for transfers between devices  194 us (48%)
  blocking collectives  55.4 us (14%)
  starting transfers between devices  53.3 us (13%)
  Pallas kernels  39.6 us (10%)
  local copies, waits for them, and re-layouts  36.4 us (9%)
  matrix products  15.6 us (4%)
  other arithmetic  6.13 us (2%)
    all_to_all x1, waiting for transfers between devices, on_device(): lax.all_to_all(sent_first, ('dom', 'fsdp'), split_axis=0, concat_axis=0,...  86.3 us
    all_to_all x1, waiting for transfers between devices, on_device(): lax.all_to_all(sent_second, ('dom', 'fsdp'), split_axis=0, concat_axis=0,...  60.1 us
    all_to_all x1, blocking collectives, on_device(): lax.all_to_all(packed_terms.astype(jnp.bfloat16), 'fsdp', split_axis=0, c...  42.8 us
    all_to_all x2, waiting for transfers between devices, gather_rows(): lax.all_to_all(jnp.broadcast_to(x[None], (n,) + x.shape), axis, split_axi...  34.8 us
    pallas_call x2, Pallas kernels, aggregate(): pl.pallas_call(functools.partial(_agg_kernel, nb, tiles - 1), grid_spec=g...  29.2 us
    all_to_all x1, starting transfers between devices, on_device(): lax.all_to_all(sent_second, ('dom', 'fsdp'), split_axis=0, concat_axis=0,...  19 us
    gather x1, local copies, waits for them, and re-layouts, on_device(): jnp.take(history_first, chosen.reshape(-1), axis=0, mode='clip')  13.5 us
    gather x1, local copies, waits for them, and re-layouts, on_device(): jnp.take(history_second, chosen.reshape(-1), axis=0, mode='clip')  13.4 us
  transfers between devices with their start and end apart: 11, of which 7 were waited for; matrix products, arithmetic and copies ran while one was open for 12% of the time, Pallas kernels for 10%

profile of v6, /device:TPU:1, one launch (start us, length us, event | category | flops | bytes accessed | tf_op | source)
XLA Modules:
  0.0 401.6 jit_solution(13448261852904640901)
XLA Ops:
  0.6 2.7 broadcast_in_dim.13
  3.3 8.6 %all-to-all-start.2 = ((bf16[16,64,1024]{2,1,0:T(8,128)(2,1)}), bf16[16,64,1024]{2,1,0:T(8,128)(2,1)}, u32[]{:S(2)}, u32[]{:S(2)}) async-start(bf16[16,64,1024]{2,1,0:T(8,128)(2,1)} %broadcast_in_dim.13), calls=%async_computation.2 | async-start | bytes 4194304 | tf_op jit(solution)/shard_map/all_to_all | solution.py:137
  12.0 30.4 %all-to-all-done.2 = bf16[16,64,1024]{2,1,0:T(8,128)(2,1)} async-done(((bf16[16,64,1024]{2,1,0:T(8,128)(2,1)}), bf16[16,64,1024]{2,1,0:T(8,128)(2,1)}, u32[]{:S(2)}, u32[]{:S(2)}) %all-to-all-start.2) | async-done | bytes 2097184 | tf_op jit(solution)/shard_map/all_to_all | solution.py:137
  44.3 4.6 %all-to-all-start.1 = ((bf16[16,64,1152]{2,1,0:T(8,128)(2,1)}), bf16[16,64,1152]{2,1,0:T(8,128)(2,1)}, u32[]{:S(2)}, u32[]{:S(2)}) async-start(bf16[16,64,1152]{2,1,0:T(8,128)(2,1)} %broadcast_in_dim.12), calls=%async_computation.1 | async-start | bytes 4718592 | tf_op jit(solution)/shard_map/all_to_all | solution.py:137
  48.9 12.7 %all-gather = s32[8,1,128]{2,1,0:T(1,128)S(1)} all-gather(s32[1,1,128]{2,1,0:T(1,128)S(1)} %bitcast.93), channel_id=1, replica_groups=mesh['dom'=8,'fsdp'=16] {'dom'}, dimensions={0}, use_global_device_ids=true | all-gather | bytes 4608 | tf_op jit(solution)/shard_map/all_gather | solution.py:167
  61.8 13.5 %gather_fusion = bf16[512,64,128]{2,1,0:T(8,128)(2,1)} fusion(bf16[128,64,128]{2,1,0:T(8,128)(2,1)S(1)} %copy-done, s32[1024]{0:T(1024)S(1)} %pad_clamp_fusion), kind=kCustom, calls=%fused_computation | custom fusion | bytes 16779264 | tf_op jit(solution)/shard_map/jit(_take)/gather | solution.py:176
  75.3 4.4 %all-to-all-done.1 = bf16[16,64,1152]{2,1,0:T(8,128)(2,1)} async-done(((bf16[16,64,1152]{2,1,0:T(8,128)(2,1)}), bf16[16,64,1152]{2,1,0:T(8,128)(2,1)}, u32[]{:S(2)}, u32[]{:S(2)}) %all-to-all-start.1) | async-done | bytes 2359328 | tf_op jit(solution)/shard_map/all_to_all | solution.py:137
  79.7 9.6 %all-to-all-start = ((bf16[128,4,64,128]{3,2,1,0:T(8,128)(2,1)}), bf16[128,4,64,128]{3,2,1,0:T(8,128)(2,1)}, u32[]{:S(2)}, u32[]{:S(2)}) async-start(bf16[128,4,64,128]{3,2,1,0:T(8,128)(2,1)} %bitcast.86), calls=%async_computation | async-start | bytes 16777216 | tf_op jit(solution)/shard_map/all_to_all | solution.py:178
  89.3 13.4 %gather_fusion.1 = bf16[512,64,128]{2,1,0:T(8,128)(2,1)} fusion(bf16[128,64,128]{2,1,0:T(8,128)(2,1)S(1)} %copy-done.2, s32[1024]{0:T(1024)S(1)} %pad_clamp_fusion), kind=kCustom, calls=%fused_computation.1 | custom fusion | bytes 16779264 | tf_op jit(solution)/shard_map/jit(_take)/gather | solution.py:177
  102.7 86.3 %all-to-all-done = bf16[128,4,64,128]{3,2,1,0:T(8,128)(2,1)} async-done(((bf16[128,4,64,128]{3,2,1,0:T(8,128)(2,1)}), bf16[128,4,64,128]{3,2,1,0:T(8,128)(2,1)}, u32[]{:S(2)}, u32[]{:S(2)}) %all-to-all-start) | async-done | bytes 8388640 | tf_op jit(solution)/shard_map/all_to_all | solution.py:178
  189.0 19.0 %all-to-all-start.3 = ((bf16[128,4,64,128]{3,2,1,0:T(8,128)(2,1)}), bf16[128,4,64,128]{3,2,1,0:T(8,128)(2,1)}, u32[]{:S(2)}, u32[]{:S(2)}) async-start(bf16[128,4,64,128]{3,2,1,0:T(8,128)(2,1)} %bitcast.85), calls=%async_computation.3 | async-start | bytes 16777216 | tf_op jit(solution)/shard_map/all_to_all | solution.py:179
  210.2 4.1 %fusion.15.back_ref = bf16[4,1024,128]{2,1,0:T(8,128)(2,1)} fusion(bf16[1024,1024,1]{1,0,2:T(8,128)(2,1)} %bitcast.11, bf16[4,1024,128]{2,1,0:T(8,128)(2,1)} %param.25), kind=kOutput, calls=%fused_computation.27 | convolution fusion | flops 1074266112 | bytes 4194304 | tf_op jit(solution)/shard_map/ab,vbn->van/dot_general | solution.py:187
  214.3 10.4 %shard_map.148 = f32[4,1024,128]{2,1,0:T(8,128)} custom-call(s32[4,6]{1,0:T(4,128)} %src_ref.5, s32[4]{0:T(128)} %cnt_ref.5, bf16[4,1024,128]{2,1,0:T(8,128)(2,1)} %fusion.15.back_ref, bf16[4,6,128,128]{3,2,1,0:T(8,128)(2,1)} %tile_ref.5), custom_call_target="tpu_custom_call" | custom-call | flops 805306368 | bytes 3932160 | tf_op jit(solution)/shard_map/pallas_call | solution.py:122
  225.8 14.5 %shard_map.147 = bf16[4,1024,128]{2,1,0:T(8,128)(2,1)} custom-call(s32[4,6]{1,0:T(4,128)} %src_ref.5, s32[4]{0:T(128)} %cnt_ref.5, s32[32]{0:T(128)} %reshape.104.live_ref, bf16[4,1024,128]{2,1,0:T(8,128)(2,1)} %own_ref.1, bf16[8,16,4,64,128]{4,3,2,1,0:T(8,128)(2,1)} %bitcast.4.pulled_ref, bf16[4,6,128,128]{3,2,1,0:T(8,128)(2,1)} %tile_ref.5), custom_call_target="tpu_custom_call" | custom-call | flops 805306368 | bytes 14417920 | tf_op jit(solution)/shard_map/pallas_call | solution.py:77
  240.4 4.8 %fusion.14 = (bf16[4,1024,128]{2,1,0:T(8,128)(2,1)}, f32[4,128,1024]{1,2,0:T(8,128)S(1)}) fusion(f32[1024]{0:T(1024)S(1)} %convert_reduce_fusion.1, bf16[4,1024,128]{2,1,0:T(8,128)(2,1)} %shard_map.147, bf16[1024,1152]{1,0:T(8,128)(2,1)} %bitcast.5), kind=kOutput, calls=%fused_computation.25 | convolution fusion | flops 1078984704 | bytes 6295552 | tf_op jit(solution)/shard_map/fh,vfn->vhn/dot_general | solution.py:200
  247.7 60.1 %all-to-all-done.3 = bf16[128,4,64,128]{3,2,1,0:T(8,128)(2,1)} async-done(((bf16[128,4,64,128]{3,2,1,0:T(8,128)(2,1)}), bf16[128,4,64,128]{3,2,1,0:T(8,128)(2,1)}, u32[]{:S(2)}, u32[]{:S(2)}) %all-to-all-start.3) | async-done | bytes 8388640 | tf_op jit(solution)/shard_map/all_to_all | solution.py:179
  307.7 14.7 %shard_map.149 = bf16[4,1024,128]{2,1,0:T(8,128)(2,1)} custom-call(s32[4,6]{1,0:T(4,128)} %src_ref.5, s32[4]{0:T(128)} %cnt_ref.5, s32[32]{0:T(128)} %reshape.104.live_ref, bf16[4,1024,128]{2,1,0:T(8,128)(2,1)} %get-tuple-element.32.own_ref, bf16[8,16,4,64,128]{4,3,2,1,0:T(8,128)(2,1)} %bitcast.21.pulled_ref, bf16[4,6,128,128]{3,2,1,0:T(8,128)(2,1)} %tile_ref.5), custom_call_target="tpu_custom_call" | custom-call | flops 805306368 | bytes 14417920 | tf_op jit(solution)/shard_map/pallas_call | solution.py:77
  322.4 2.6 constant_dynamic-slice_fusion
  334.1 42.8 %all_to_all.25 = bf16[16,64,1152]{2,1,0:T(8,128)(2,1)S(1)} all-to-all(bf16[16,64,1152]{2,1,0:T(8,128)(2,1)S(1)} %fusion.1), channel_id=1, replica_groups=mesh['dom'=8,'fsdp'=16] {'fsdp'}, dimensions={0} | all-to-all | bytes 4718592 | tf_op jit(solution)/shard_map/all_to_all | solution.py:225
  377.1 3.3 collective-permute-start.4
  380.5 5.9 %collective-permute-done.4 = f32[64,1152]{1,0:T(8,128)S(1)} collective-permute-done((f32[64,1152]{1,0:T(8,128)S(1)}, f32[64,1152]{1,0:T(8,128)S(1)}, u32[]{:S(2)}, u32[]{:S(2)}) %collective-permute-start.4) | collective-permute-done | bytes 294944 | tf_op jit(solution)/shard_map/ppermute | solution.py:228
  386.4 3.4 collective-permute-start.5
  389.8 6.0 %collective-permute-done.5 = f32[64,1152]{1,0:T(8,128)S(1)} collective-permute-done((f32[64,1152]{1,0:T(8,128)S(1)}, f32[64,1152]{1,0:T(8,128)S(1)}, u32[]{:S(2)}, u32[]{:S(2)}) %collective-permute-start.5) | collective-permute-done | bytes 294944 | tf_op jit(solution)/shard_map/ppermute | solution.py:228
  395.8 2.5 collective-permute-start.6
  (57 shorter events, 20.4 us)
Async XLA Ops:
  0.6 61.1 %copy-start = (bf16[128,64,128]{2,1,0:T(8,128)(2,1)S(1)}, bf16[128,64,128]{2,1,0:T(8,128)(2,1)}, u32[]{:S(2)}) copy-start(bf16[128,64,128]{2,1,0:T(8,128)(2,1)} %param.15) | copy-start | bytes 6291460
  3.3 8.6 %copy-start.8 = (bf16[64]{0:T(256)(128)(2,1)S(1)}, bf16[64]{0:T(256)(128)(2,1)}, u32[]{:S(2)}) copy-start(bf16[64]{0:T(256)(128)(2,1)} %param.24) | copy-start | bytes 388
  3.3 8.7 %copy-start.6 = (bf16[64,1024]{1,0:T(8,128)(2,1)S(1)}, bf16[64,1024]{1,0:T(8,128)(2,1)}, u32[]{:S(2)}) copy-start(bf16[64,1024]{1,0:T(8,128)(2,1)} %param.22) | copy-start | bytes 393220
  3.3 39.2 %all-to-all-start.2 = ((bf16[16,64,1024]{2,1,0:T(8,128)(2,1)}), bf16[16,64,1024]{2,1,0:T(8,128)(2,1)}, u32[]{:S(2)}, u32[]{:S(2)}) async-start(bf16[16,64,1024]{2,1,0:T(8,128)(2,1)} %broadcast_in_dim.13), calls=%async_computation.2 | async-start | bytes 4194304 | tf_op jit(solution)/shard_map/all_to_all | solution.py:137
  44.3 4.6 %copy-start.9 = (s32[1,128]{1,0:T(1,128)S(1)}, s32[1,128]{1,0:T(1,128)}, u32[]{:S(2)}) copy-start(s32[1,128]{1,0:T(1,128)} %param.18) | copy-start | bytes 1540
  44.3 17.3 %copy-start.7 = (s32[1,128,4]{1,2,0:T(4,128)S(1)}, s32[1,128,4]{1,2,0:T(4,128)}, u32[]{:S(2)}) copy-start(s32[1,128,4]{1,2,0:T(4,128)} %param.17) | copy-start | bytes 6148
  44.3 35.4 %all-to-all-start.1 = ((bf16[16,64,1152]{2,1,0:T(8,128)(2,1)}), bf16[16,64,1152]{2,1,0:T(8,128)(2,1)}, u32[]{:S(2)}, u32[]{:S(2)}) async-start(bf16[16,64,1152]{2,1,0:T(8,128)(2,1)} %broadcast_in_dim.12), calls=%async_computation.1 | async-start | bytes 4718592 | tf_op jit(solution)/shard_map/all_to_all | solution.py:137
  79.7 9.6 %copy-start.2 = (bf16[128,64,128]{2,1,0:T(8,128)(2,1)S(1)}, bf16[128,64,128]{2,1,0:T(8,128)(2,1)}, u32[]{:S(2)}) copy-start(bf16[128,64,128]{2,1,0:T(8,128)(2,1)} %param.16) | copy-start | bytes 6291460
  79.7 109.3 %all-to-all-start = ((bf16[128,4,64,128]{3,2,1,0:T(8,128)(2,1)}), bf16[128,4,64,128]{3,2,1,0:T(8,128)(2,1)}, u32[]{:S(2)}, u32[]{:S(2)}) async-start(bf16[128,4,64,128]{3,2,1,0:T(8,128)(2,1)} %bitcast.86), calls=%async_computation | async-start | bytes 16777216 | tf_op jit(solution)/shard_map/all_to_all | solution.py:178
  189.0 118.8 %all-to-all-start.3 = ((bf16[128,4,64,128]{3,2,1,0:T(8,128)(2,1)}), bf16[128,4,64,128]{3,2,1,0:T(8,128)(2,1)}, u32[]{:S(2)}, u32[]{:S(2)}) async-start(bf16[128,4,64,128]{3,2,1,0:T(8,128)(2,1)} %bitcast.85), calls=%async_computation.3 | async-start | bytes 16777216 | tf_op jit(solution)/shard_map/all_to_all | solution.py:179
  208.0 121.8 %collective-permute-start.3 = (bf16[4,1024,128]{2,1,0:T(8,128)(2,1)}, bf16[4,1024,128]{2,1,0:T(8,128)(2,1)}, u32[]{:S(2)}, u32[]{:S(2)}) collective-permute-start(bf16[4,1024,128]{2,1,0:T(8,128)(2,1)} %param.25), channel_id=1, source_target_pairs={{0,16},{16,0},{32,48},{48,32},{64,80},{80,64},{96,112},{112,96},{1... | collective-permute-start | bytes 3145736 | tf_op jit(solution)/shard_map/ppermute | solution.py:185
  240.4 4.8 %copy-start.3 = (f32[4,1024,128]{2,1,0:T(8,128)S(1)}, f32[4,1024,128]{2,1,0:T(8,128)}, u32[]{:S(2)}) copy-start(f32[4,1024,128]{2,1,0:T(8,128)} %shard_map.148) | copy-start | bytes 6291460
  247.6 84.2 %collective-permute-start.1 = (bf16[4,1024,128]{2,1,0:T(8,128)(2,1)S(1)}, bf16[4,1024,128]{2,1,0:T(8,128)(2,1)}, u32[]{:S(2)}, u32[]{:S(2)}) collective-permute-start(bf16[4,1024,128]{2,1,0:T(8,128)(2,1)S(1)} %get-tuple-element.21), channel_id=1, source_target_pairs={{0,16},{16,0},{32,48},{48,32},{64,80},{80,64},{96,112},{112,96},{1... | collective-permute-start | bytes 3145736 | tf_op jit(solution)/shard_map/ppermute | solution.py:208
  307.7 14.7 %copy-start.4 = (bf16[4,1024,128]{2,1,0:T(8,128)(2,1)S(1)}, bf16[4,1024,128]{2,1,0:T(8,128)(2,1)}, u32[]{:S(2)}) copy-start(bf16[4,1024,128]{2,1,0:T(8,128)(2,1)} %shard_map.147) | copy-start | bytes 3145732
  326.2 3.6 collective-permute-start.2
  326.9 2.1 copy-start.5
  326.9 4.9 %collective-permute-start = (bf16[4,16,32,128]{3,2,0,1:T(8,128)(2,1)S(1)}, bf16[4,16,32,128]{3,2,0,1:T(8,128)(2,1)S(1)}, u32[]{:S(2)}, u32[]{:S(2)}) collective-permute-start(bf16[4,16,32,128]{3,2,0,1:T(8,128)(2,1)S(1)} %bitcast.89), channel_id=1, source_target_pairs={{0,16},{16,0},{32,48},{48,32},{64,80},{80,64},{96,112},{112,96},{1... | collective-permute-start | bytes 1572872 | tf_op jit(solution)/shard_map/ppermute | solution.py:208
  377.1 9.2 %collective-permute-start.4 = (f32[64,1152]{1,0:T(8,128)S(1)}, f32[64,1152]{1,0:T(8,128)S(1)}, u32[]{:S(2)}, u32[]{:S(2)}) collective-permute-start(f32[64,1152]{1,0:T(8,128)S(1)} %convert_reduce_fusion), channel_id=1, source_target_pairs={{0,32},{16,48},{32,0},{48,16},{64,96},{80,112},{96,64},{112,80},{1... | collective-permute-start | bytes 884744 | tf_op jit(solution)/shard_map/ppermute | solution.py:228
  386.3 15.2 %copy-start.1 = (bf16[128,64,128]{2,1,0:T(8,128)(2,1)S(1)}, bf16[128,64,128]{2,1,0:T(8,128)(2,1)}, u32[]{:S(2)}) copy-start(bf16[128,64,128]{2,1,0:T(8,128)(2,1)} %param.15) | copy-start | bytes 6291460
  386.4 9.4 %collective-permute-start.5 = (f32[64,1152]{1,0:T(8,128)S(1)}, f32[64,1152]{1,0:T(8,128)S(1)}, u32[]{:S(2)}, u32[]{:S(2)}) collective-permute-start(f32[64,1152]{1,0:T(8,128)S(1)} %add.72), channel_id=1, source_target_pairs={{0,64},{16,80},{32,96},{48,112},{64,0},{80,16},{96,32},{112,48},{1... | collective-permute-start | bytes 884744 | tf_op jit(solution)/shard_map/ppermute | solution.py:228
  395.8 3.7 collective-permute-start.6

commit v7 on v6

--- a/solution.py
+++ b/solution.py
@@ -31,7 +31,7 @@
 
     @pl.when(pull_ok)
     def _():
-        block = pulled_ref[0, :, 0]
+        block = pulled_ref[0]
         block = block.reshape(block.shape[0] * block.shape[1], block.shape[2])
         acc_ref[...] += jnp.dot(block, tile_ref[0, 0], preferred_element_type=jnp.float32)
 
@@ -40,9 +40,10 @@
         out_ref[0] = acc_ref[...].astype(out_ref.dtype)
 
 
-def aggregate(own, pulled, tile_src, tile_count, slot_live, tile_values):
+def aggregate(own, pulled, cap, tile_src, tile_count, slot_live, tile_values):
     nb, feat, blk = own.shape
-    dom, fsdp, cap = pulled.shape[0], pulled.shape[1], pulled.shape[2]
+    dom, fsdp = pulled.shape[0], pulled.shape[1]
+    cols = feat // fsdp
     tiles = tile_src.shape[1]
 
     def eff(v, t, src_ref, cnt_ref):
@@ -54,7 +55,7 @@
 
     def pulled_map(v, t, src_ref, cnt_ref, live_ref):
         s = jnp.clip(src_ref[v, eff(v, t, src_ref, cnt_ref)] - nb, 0, cap * dom - 1)
-        return (s % dom, 0, s // dom, 0, 0)
+        return (s % dom, 0, s // dom, 0)
 
     def tile_map(v, t, src_ref, cnt_ref, live_ref):
         return (v, eff(v, t, src_ref, cnt_ref), 0, 0)
@@ -67,7 +68,7 @@
         grid=(nb, tiles),
         in_specs=[
             pl.BlockSpec((1, feat, blk), own_map),
-            pl.BlockSpec((1, fsdp, 1) + pulled.shape[3:], pulled_map),
+            pl.BlockSpec((1, fsdp, cols, blk), pulled_map),
             pl.BlockSpec((1, 1, blk, blk), tile_map),
         ],
         out_specs=pl.BlockSpec((1, feat, blk), out_map),
@@ -130,12 +131,6 @@
             bytes_accessed=back_second.size * 2 + nb * tiles * blk * blk * 2 + back_second.size * 4,
         ),
     )(tile_src, tile_count, back_second, tile_values)
-
-
-def gather_rows(x, axis):
-    n = lax.axis_size(axis)
-    spread = lax.all_to_all(jnp.broadcast_to(x[None], (n,) + x.shape), axis, split_axis=0, concat_axis=0, tiled=True)
-    return spread.reshape((n * x.shape[0],) + x.shape[1:])
 
 
 def on_device(
@@ -154,31 +149,53 @@
 ):
     dom_size = lax.axis_size("dom")
     fsdp_size = lax.axis_size("fsdp")
-    me = lax.axis_index("dom") * fsdp_size + lax.axis_index("fsdp")
+    dom_idx = lax.axis_index("dom")
+    me = dom_idx * fsdp_size + lax.axis_index("fsdp")
     rows, hidden = w_first.shape
-    bias_cols = jnp.broadcast_to(bias_first[:, None], (rows, 128))
-    packed = gather_rows(jnp.concatenate([w_first, bias_cols], axis=1), "fsdp")
-    first_full = packed[:, :hidden]
-    bias_full = packed[:, hidden].astype(jnp.float32)
-    second_full = gather_rows(w_second, "fsdp")
-
     chosen = pull_list[0]
     requesters, slot_cap = chosen.shape
-    counts_all = lax.all_gather(pull_count, "dom", axis=0, tiled=True)
-    counts_all, chosen = lax.optimization_barrier((counts_all, chosen))
-    my_counts = lax.dynamic_index_in_dim(counts_all, me, axis=1, keepdims=False)
-    slot_live = (lax.broadcasted_iota(jnp.int32, (slot_cap, dom_size), 0) < my_counts[None, :]).astype(jnp.int32)
-    slot_live = slot_live.reshape(-1)
-
     block_len = features.shape[2]
     first_cols = history_first.shape[1]
     second_cols = history_second.shape[1]
-    sent_first = jnp.take(history_first, chosen.reshape(-1), axis=0, mode="clip").reshape(requesters, slot_cap, first_cols, block_len)
+    piece = rows // dom_size
+    piece_rows = piece * hidden // block_len
+
+    def weight_piece(w):
+        part = lax.dynamic_slice_in_dim(w, dom_idx * piece, piece, axis=0).reshape(1, piece_rows, block_len)
+        return jnp.broadcast_to(part, (requesters, piece_rows, block_len))
+
+    misc = jnp.zeros((requesters, 8, block_len), jnp.bfloat16)
+    misc = misc.at[:, 0, :piece].set(lax.dynamic_slice_in_dim(bias_first, dom_idx * piece, piece)[None, :])
+    misc = misc.at[:, 0, piece].set(pull_count[0].astype(jnp.bfloat16))
+    taken_first = jnp.take(history_first, chosen.reshape(-1), axis=0, mode="clip")
+    sent_first = jnp.concatenate(
+        [
+            taken_first.reshape(requesters, slot_cap * first_cols, block_len),
+            weight_piece(w_first),
+            weight_piece(w_second),
+            misc,
+        ],
+        axis=1,
+    )
     sent_second = jnp.take(history_second, chosen.reshape(-1), axis=0, mode="clip").reshape(requesters, slot_cap, second_cols, block_len)
     arrived_first = lax.all_to_all(sent_first, ("dom", "fsdp"), split_axis=0, concat_axis=0, tiled=True)
     arrived_second = lax.all_to_all(sent_second, ("dom", "fsdp"), split_axis=0, concat_axis=0, tiled=True)
-    pulled_first = arrived_first.reshape(dom_size, fsdp_size, slot_cap, first_cols, block_len)
-    pulled_second = arrived_second.reshape(dom_size, fsdp_size, slot_cap, second_cols, block_len)
+    by_source = arrived_first.reshape(dom_size, fsdp_size, arrived_first.shape[1], block_len)
+    pulled_first = by_source
+    pulled_second = arrived_second.reshape(dom_size, fsdp_size, slot_cap * second_cols, block_len)
+
+    def weight_from(offset):
+        got = by_source[:, :, offset : offset + piece_rows].reshape(dom_size, fsdp_size, piece, hidden)
+        return jnp.transpose(got, (1, 0, 2, 3)).reshape(fsdp_size * dom_size * piece, hidden)
+
+    hist_rows = slot_cap * first_cols
+    first_full = weight_from(hist_rows)
+    second_full = weight_from(hist_rows + piece_rows)
+    misc_rows = by_source[:, :, hist_rows + 2 * piece_rows]
+    bias_full = jnp.transpose(misc_rows[:, :, :piece], (1, 0, 2)).reshape(-1).astype(jnp.float32)
+    my_counts = misc_rows[:, 0, piece].astype(jnp.int32)
+    slot_live = (lax.broadcasted_iota(jnp.int32, (slot_cap, dom_size), 0) < my_counts[None, :]).astype(jnp.int32)
+    slot_live = slot_live.reshape(-1)
 
     core = lax.axis_index("dom") % 2
     pair = [(d, d ^ 1) for d in range(dom_size)]
@@ -195,7 +212,7 @@
         theirs = lax.dynamic_index_in_dim(split, 1 - core, axis=2, keepdims=False)
         return mine, theirs
 
-    agg_first = aggregate(features, pulled_first, tile_src, tile_count, slot_live, tile_values)
+    agg_first = aggregate(features, pulled_first, slot_cap, tile_src, tile_count, slot_live, tile_values)
     pre_act = (
         jnp.einsum("fh,vfn->vhn", first_full, agg_first, preferred_element_type=jnp.float32)
         + bias_full[None, :, None]
@@ -212,7 +229,7 @@
 
     half_rows = first_term.shape[1]
     lanes = 128
-    agg_second = aggregate(hidden_new, pulled_second, tile_src, tile_count, slot_live, tile_values)
+    agg_second = aggregate(hidden_new, pulled_second, slot_cap, tile_src, tile_count, slot_live, tile_values)
     second_mine, second_theirs = halves(agg_second)
     second_got = lax.ppermute(second_theirs, "dom", pair)
     second_term = jnp.einsum(

time: 405 us -> 447 us (1.10)
  local copies, waits for them, and re-layouts: 36.4 us -> 65 us
  waiting for transfers between devices: 194 us -> 220 us
  other arithmetic: 6.13 us -> 19.8 us
  blocking collectives: 55.4 us -> 42.9 us
  starting transfers between devices: 53.3 us -> 43.7 us
    all_to_all x1, waiting for transfers between devices: 86.3 us -> 159 us  [on_device(): lax.all_to_all(sent_first, ('dom', 'fsdp'), split_axis=0, concat_axis=0,...]
    all_to_all x2 -> x0, waiting for transfers between devices: 34.8 us -> none  [gather_rows(): lax.all_to_all(jnp.broadcast_to(x[None], (n,) + x.shape), axis, split_axi...]
    all_to_all x2 -> x0, starting transfers between devices: 13.2 us -> none  [gather_rows(): lax.all_to_all(jnp.broadcast_to(x[None], (n,) + x.shape), axis, split_axi...]
    all_to_all x1, waiting for transfers between devices: 60.1 us -> 47.3 us  [on_device(): lax.all_to_all(sent_second, ('dom', 'fsdp'), split_axis=0, concat_axis=0,...]
    all_gather x1 -> x0, blocking collectives: 12.7 us -> none  [on_device(): counts_all = lax.all_gather(pull_count, 'dom', axis=0, tiled=True)]
    scatter x0 -> x3, local copies, waits for them, and re-layouts: none -> 12.3 us  [the longest x1 12.3 us: on_device(): misc = misc.at[:, 0, piece].set(pull_count[0].astype(jnp.bfloat16))]
    concatenate x1, other arithmetic: 0.01 us -> 11.1 us  [on_device(): jnp.concatenate([taken_first.reshape(requesters, slot_cap * first_cols, b...]
    slice x0 -> x2, local copies, waits for them, and re-layouts: none -> 6.58 us  [the longest x1 5.59 us: weight_from(): by_source[:, :, offset:offset + piece_rows]]
  transfers between devices with their start and end apart: 11 -> 9, of which waited for: 7 -> 5; matrix products, arithmetic and copies ran while one was open for 12% -> 11% of each run, Pallas kernels for 10% -> 8%
where the time goes in v7:
time: 447 us; the launch traced here: 445 us
  waiting for transfers between devices  220 us (49%)
  local copies, waits for them, and re-layouts  65 us (15%)
  starting transfers between devices  43.7 us (10%)
  blocking collectives  42.9 us (10%)
  Pallas kernels  36.7 us (8%)
  other arithmetic  19.8 us (4%)
  matrix products  16.5 us (4%)
    all_to_all x1, waiting for transfers between devices, on_device(): lax.all_to_all(sent_first, ('dom', 'fsdp'), split_axis=0, concat_axis=0,...  159 us
    all_to_all x1, waiting for transfers between devices, on_device(): lax.all_to_all(sent_second, ('dom', 'fsdp'), split_axis=0, concat_axis=0,...  47.3 us
    all_to_all x1, blocking collectives, on_device(): lax.all_to_all(packed_terms.astype(jnp.bfloat16), 'fsdp', split_axis=0, c...  42.9 us
    pallas_call x2, Pallas kernels, aggregate(): pl.pallas_call(functools.partial(_agg_kernel, nb, tiles - 1), grid_spec=g...  27.3 us
    all_to_all x1, starting transfers between devices, on_device(): lax.all_to_all(sent_second, ('dom', 'fsdp'), split_axis=0, concat_axis=0,...  16.9 us
    gather x1, local copies, waits for them, and re-layouts, on_device(): jnp.take(history_second, chosen.reshape(-1), axis=0, mode='clip')  13.5 us
    gather x1, local copies, waits for them, and re-layouts, on_device(): jnp.take(history_first, chosen.reshape(-1), axis=0, mode='clip')  13.5 us
    scatter x1, local copies, waits for them, and re-layouts, on_device(): misc = misc.at[:, 0, piece].set(pull_count[0].astype(jnp.bfloat16))  12.3 us
  transfers between devices with their start and end apart: 9, of which 5 were waited for; matrix products, arithmetic and copies ran while one was open for 11% of the time, Pallas kernels for 8%

profile of v7, /device:TPU:1, one launch (start us, length us, event | category | flops | bytes accessed | tf_op | source)
XLA Modules:
  0.0 445.1 jit_solution(360030223727256627)
XLA Ops:
  9.1 12.3 %scatter.22 = bf16[128,8,128]{2,1,0:T(8,128)(2,1)S(1)} dynamic-update-slice(bf16[128,8,128]{2,1,0:T(8,128)(2,1)S(1)} %scatter.20, bf16[128,1,1]{2,1,0:T(2,128)(2,1)S(1)} %copy.26, s32[]{:T(128)} %constant.116.clone.1, s32[]{:T(128)} %bitcast.2, s32[]{:T(128)} %bitcast.3) | dynamic-update-slice | bytes 516 | tf_op jit(solution)/shard_map/scatter | solution.py:169
  21.4 13.5 %gather_fusion = bf16[512,64,128]{2,1,0:T(8,128)(2,1)} fusion(bf16[128,64,128]{2,1,0:T(8,128)(2,1)S(1)} %copy-done, s32[1024]{0:T(1024)S(1)} %pad_clamp_fusion), kind=kCustom, calls=%fused_computation | custom fusion | bytes 16779264 | tf_op jit(solution)/shard_map/jit(_take)/gather | solution.py:170
  35.9 11.1 %pad_maximum_fusion = bf16[128,392,128]{2,1,0:T(8,128)(2,1)} fusion(bf16[128,8,128]{2,1,0:T(8,128)(2,1)S(1)} %scatter.22, bf16[128,64,128]{2,1,0:T(8,128)(2,1)S(1)} %broadcast_in_dim.31, bf16[128,64,128]{2,1,0:T(8,128)(2,1)S(1)} %broadcast_in_dim.15, bf16[128,256,128]{2,1,0:T(8,128)(2,1)} %bitcast.98), kind=kLoop, calls=%fused_computation.2 | loop fusion | flops 51380224 | bytes 25690112 | tf_op jit(solution)/shard_map/concatenate | solution.py:171
  47.1 11.9 %all-to-all-start = ((bf16[128,392,128]{2,1,0:T(8,128)(2,1)}), bf16[128,392,128]{2,1,0:T(8,128)(2,1)}, u32[]{:S(2)}, u32[]{:S(2)}) async-start(bf16[128,392,128]{2,1,0:T(8,128)(2,1)} %pad_maximum_fusion), calls=%async_computation | async-start | bytes 25690112 | tf_op jit(solution)/shard_map/all_to_all | solution.py:181
  59.0 13.5 %gather_fusion.1 = bf16[512,64,128]{2,1,0:T(8,128)(2,1)} fusion(bf16[128,64,128]{2,1,0:T(8,128)(2,1)S(1)} %copy-done.2, s32[1024]{0:T(1024)S(1)} %pad_clamp_fusion), kind=kCustom, calls=%fused_computation.1 | custom fusion | bytes 16779264 | tf_op jit(solution)/shard_map/jit(_take)/gather | solution.py:180
  72.5 159.2 %all-to-all-done = bf16[128,392,128]{2,1,0:T(8,128)(2,1)} async-done(((bf16[128,392,128]{2,1,0:T(8,128)(2,1)}), bf16[128,392,128]{2,1,0:T(8,128)(2,1)}, u32[]{:S(2)}, u32[]{:S(2)}) %all-to-all-start) | async-done | bytes 12845088 | tf_op jit(solution)/shard_map/all_to_all | solution.py:181
  231.7 16.9 %all-to-all-start.1 = ((bf16[128,4,64,128]{3,2,1,0:T(8,128)(2,1)}), bf16[128,4,64,128]{3,2,1,0:T(8,128)(2,1)}, u32[]{:S(2)}, u32[]{:S(2)}) async-start(bf16[128,4,64,128]{3,2,1,0:T(8,128)(2,1)} %bitcast.99), calls=%async_computation.1 | async-start | bytes 16777216 | tf_op jit(solution)/shard_map/all_to_all | solution.py:182
  251.9 5.6 %fusion.31 = (bf16[8,16,64,128]{3,2,1,0:T(8,128)(2,1)}, bf16[8,16,64,128]{3,2,1,0:T(8,128)(2,1)}) fusion(bf16[8,16,392,128]{3,2,1,0:T(8,128)(2,1)} %bitcast.6.pulled_ref), kind=kLoop, calls=%fused_computation.65 | loop fusion | bytes 8388608 | tf_op jit(solution)/shard_map/slice | solution.py:188
  257.5 2.8 reshape.203
  261.9 2.8 reshape.206
  264.9 3.5 fusion.14.back_ref
  268.4 9.4 %shard_map.148 = f32[4,1024,128]{2,1,0:T(8,128)} custom-call(s32[4,6]{1,0:T(4,128)} %src_ref.5, s32[4]{0:T(128)} %cnt_ref.5, bf16[4,1024,128]{2,1,0:T(8,128)(2,1)} %fusion.14.back_ref, bf16[4,6,128,128]{3,2,1,0:T(8,128)(2,1)} %tile_ref.5), custom_call_target="tpu_custom_call" | custom-call | flops 805306368 | bytes 3932160 | tf_op jit(solution)/shard_map/pallas_call | solution.py:123
  277.8 13.6 %shard_map.147 = bf16[4,1024,128]{2,1,0:T(8,128)(2,1)} custom-call(s32[4,6]{1,0:T(4,128)} %src_ref.5, s32[4]{0:T(128)} %cnt_ref.5, s32[32]{0:T(128)} %reshape.213.live_ref, bf16[4,1024,128]{2,1,0:T(8,128)(2,1)} %own_ref.1, bf16[8,16,392,128]{3,2,1,0:T(8,128)(2,1)} %bitcast.6.pulled_ref, bf16[4,6,128,128]{3,2,1,0:T(8,128)(2,1)} %tile_ref.5), custom_call_target="tpu_custom_call" | custom-call | flops 805306368 | bytes 14417920 | tf_op jit(solution)/shard_map/pallas_call | solution.py:78
  291.4 4.8 %fusion.13 = (bf16[4,1024,128]{2,1,0:T(8,128)(2,1)}, f32[4,128,1024]{1,2,0:T(8,128)S(1)}) fusion(f32[1024]{0:T(1024)S(1)} %reshape.214, bf16[4,1024,128]{2,1,0:T(8,128)(2,1)} %shard_map.147, bf16[1024,1024,1]{1,0,2:T(8,128)(2,1)} %bitcast.104), kind=kOutput, calls=%fused_computation.24 | convolution fusion | flops 1078984704 | bytes 6295552 | tf_op jit(solution)/shard_map/fh,vfn->vhn/dot_general | solution.py:217
  296.3 2.4 fusion.29
  301.0 47.3 %all-to-all-done.1 = bf16[128,4,64,128]{3,2,1,0:T(8,128)(2,1)} async-done(((bf16[128,4,64,128]{3,2,1,0:T(8,128)(2,1)}), bf16[128,4,64,128]{3,2,1,0:T(8,128)(2,1)}, u32[]{:S(2)}, u32[]{:S(2)}) %all-to-all-start.1) | async-done | bytes 8388640 | tf_op jit(solution)/shard_map/all_to_all | solution.py:182
  348.3 13.7 %shard_map.149 = bf16[4,1024,128]{2,1,0:T(8,128)(2,1)} custom-call(s32[4,6]{1,0:T(4,128)} %src_ref.5, s32[4]{0:T(128)} %cnt_ref.5, s32[32]{0:T(128)} %reshape.213.live_ref, bf16[4,1024,128]{2,1,0:T(8,128)(2,1)} %get-tuple-element.56.own_ref, bf16[8,16,256,128]{3,2,1,0:T(8,128)(2,1)} %bitcast.26.pulled_ref, bf16[4,6,128,128]{3,2,1,0:T(8,128)(2,1)} %tile_ref.5), custom_call_target="tpu_custom_call" | custom-call | flops 805306368 | bytes 14417920 | tf_op jit(solution)/shard_map/pallas_call | solution.py:78
  369.1 2.1 fusion.9
  373.6 42.9 %all_to_all.15 = bf16[16,64,1152]{2,1,0:T(8,128)(2,1)S(1)} all-to-all(bf16[16,64,1152]{2,1,0:T(8,128)(2,1)S(1)} %fusion.1), channel_id=1, replica_groups=mesh['dom'=8,'fsdp'=16] {'fsdp'}, dimensions={0} | all-to-all | bytes 4718592 | tf_op jit(solution)/shard_map/all_to_all | solution.py:242
  416.9 3.4 collective-permute-start.4
  420.3 5.9 %collective-permute-done.4 = f32[64,1152]{1,0:T(8,128)S(1)} collective-permute-done((f32[64,1152]{1,0:T(8,128)S(1)}, f32[64,1152]{1,0:T(8,128)S(1)}, u32[]{:S(2)}, u32[]{:S(2)}) %collective-permute-start.4) | collective-permute-done | bytes 294944 | tf_op jit(solution)/shard_map/ppermute | solution.py:245
  426.2 7.3 %collective-permute-start.5 = (f32[64,1152]{1,0:T(8,128)S(1)}, f32[64,1152]{1,0:T(8,128)S(1)}, u32[]{:S(2)}, u32[]{:S(2)}) collective-permute-start(f32[64,1152]{1,0:T(8,128)S(1)} %add.75), channel_id=1, source_target_pairs={{0,64},{16,80},{32,96},{48,112},{64,0},{80,16},{96,32},{112,48},{1... | collective-permute-start | bytes 884744 | tf_op jit(solution)/shard_map/ppermute | solution.py:245
  433.5 5.8 %collective-permute-done.5 = f32[64,1152]{1,0:T(8,128)S(1)} collective-permute-done((f32[64,1152]{1,0:T(8,128)S(1)}, f32[64,1152]{1,0:T(8,128)S(1)}, u32[]{:S(2)}, u32[]{:S(2)}) %collective-permute-start.5) | collective-permute-done | bytes 294944 | tf_op jit(solution)/shard_map/ppermute | solution.py:245
  439.4 2.5 collective-permute-start.6
  (64 shorter events, 29.9 us)
Async XLA Ops:
  0.6 20.8 %copy-start = (bf16[128,64,128]{2,1,0:T(8,128)(2,1)S(1)}, bf16[128,64,128]{2,1,0:T(8,128)(2,1)}, u32[]{:S(2)}) copy-start(bf16[128,64,128]{2,1,0:T(8,128)(2,1)} %param.19) | copy-start | bytes 6291460
  47.1 11.9 %copy-start.2 = (bf16[128,64,128]{2,1,0:T(8,128)(2,1)S(1)}, bf16[128,64,128]{2,1,0:T(8,128)(2,1)}, u32[]{:S(2)}) copy-start(bf16[128,64,128]{2,1,0:T(8,128)(2,1)} %param.20) | copy-start | bytes 6291460
  47.1 184.6 %all-to-all-start = ((bf16[128,392,128]{2,1,0:T(8,128)(2,1)}), bf16[128,392,128]{2,1,0:T(8,128)(2,1)}, u32[]{:S(2)}, u32[]{:S(2)}) async-start(bf16[128,392,128]{2,1,0:T(8,128)(2,1)} %pad_maximum_fusion), calls=%async_computation | async-start | bytes 25690112 | tf_op jit(solution)/shard_map/all_to_all | solution.py:181
  231.7 116.7 %all-to-all-start.1 = ((bf16[128,4,64,128]{3,2,1,0:T(8,128)(2,1)}), bf16[128,4,64,128]{3,2,1,0:T(8,128)(2,1)}, u32[]{:S(2)}, u32[]{:S(2)}) async-start(bf16[128,4,64,128]{3,2,1,0:T(8,128)(2,1)} %bitcast.99), calls=%async_computation.1 | async-start | bytes 16777216 | tf_op jit(solution)/shard_map/all_to_all | solution.py:182
  248.6 120.4 %collective-permute-start.3 = (bf16[4,1024,128]{2,1,0:T(8,128)(2,1)}, bf16[4,1024,128]{2,1,0:T(8,128)(2,1)}, u32[]{:S(2)}, u32[]{:S(2)}) collective-permute-start(bf16[4,1024,128]{2,1,0:T(8,128)(2,1)} %param.29), channel_id=1, source_target_pairs={{0,16},{16,0},{32,48},{48,32},{64,80},{80,64},{96,112},{112,96},{1... | collective-permute-start | bytes 3145736 | tf_op jit(solution)/shard_map/ppermute | solution.py:202
  291.4 4.8 %copy-start.3 = (f32[4,1024,128]{2,1,0:T(8,128)S(1)}, f32[4,1024,128]{2,1,0:T(8,128)}, u32[]{:S(2)}) copy-start(f32[4,1024,128]{2,1,0:T(8,128)} %shard_map.148) | copy-start | bytes 6291460
  296.3 2.5 copy-start.4
  298.7 72.6 %collective-permute-start.1 = (bf16[4,1024,128]{2,1,0:T(8,128)(2,1)S(1)}, bf16[4,1024,128]{2,1,0:T(8,128)(2,1)}, u32[]{:S(2)}, u32[]{:S(2)}) collective-permute-start(bf16[4,1024,128]{2,1,0:T(8,128)(2,1)S(1)} %get-tuple-element.41), channel_id=1, source_target_pairs={{0,16},{16,0},{32,48},{48,32},{64,80},{80,64},{96,112},{112,96},{1... | collective-permute-start | bytes 3145736 | tf_op jit(solution)/shard_map/ppermute | solution.py:225
  300.5 70.7 %collective-permute-start = (bf16[4,16,32,128]{3,2,0,1:T(8,128)(2,1)}, bf16[4,16,32,128]{3,2,0,1:T(8,128)(2,1)}, u32[]{:S(2)}, u32[]{:S(2)}) collective-permute-start(bf16[4,16,32,128]{3,2,0,1:T(8,128)(2,1)} %bitcast.96), channel_id=1, source_target_pairs={{0,16},{16,0},{32,48},{48,32},{64,80},{80,64},{96,112},{112,96},{1... | collective-permute-start | bytes 1572872 | tf_op jit(solution)/shard_map/ppermute | solution.py:225
  365.1 4.0 collective-permute-start.2
  416.9 9.3 %collective-permute-start.4 = (f32[64,1152]{1,0:T(8,128)S(1)}, f32[64,1152]{1,0:T(8,128)S(1)}, u32[]{:S(2)}, u32[]{:S(2)}) collective-permute-start(f32[64,1152]{1,0:T(8,128)S(1)} %convert_reduce_fusion), channel_id=1, source_target_pairs={{0,32},{16,48},{32,0},{48,16},{64,96},{80,112},{96,64},{112,80},{1... | collective-permute-start | bytes 884744 | tf_op jit(solution)/shard_map/ppermute | solution.py:245
  426.2 18.9 %copy-start.1 = (bf16[128,64,128]{2,1,0:T(8,128)(2,1)S(1)}, bf16[128,64,128]{2,1,0:T(8,128)(2,1)}, u32[]{:S(2)}) copy-start(bf16[128,64,128]{2,1,0:T(8,128)(2,1)} %param.19) | copy-start | bytes 6291460
  426.2 13.1 %collective-permute-start.5 = (f32[64,1152]{1,0:T(8,128)S(1)}, f32[64,1152]{1,0:T(8,128)S(1)}, u32[]{:S(2)}, u32[]{:S(2)}) collective-permute-start(f32[64,1152]{1,0:T(8,128)S(1)} %add.75), channel_id=1, source_target_pairs={{0,64},{16,80},{32,96},{48,112},{64,0},{80,16},{96,32},{112,48},{1... | collective-permute-start | bytes 884744 | tf_op jit(solution)/shard_map/ppermute | solution.py:245
  439.4 3.7 collective-permute-start.6

commit v8 on v6

--- a/solution.py
+++ b/solution.py
@@ -157,10 +157,10 @@
     me = lax.axis_index("dom") * fsdp_size + lax.axis_index("fsdp")
     rows, hidden = w_first.shape
     bias_cols = jnp.broadcast_to(bias_first[:, None], (rows, 128))
-    packed = gather_rows(jnp.concatenate([w_first, bias_cols], axis=1), "fsdp")
+    packed = gather_rows(jnp.concatenate([w_first, w_second, bias_cols], axis=1), "fsdp")
     first_full = packed[:, :hidden]
-    bias_full = packed[:, hidden].astype(jnp.float32)
-    second_full = gather_rows(w_second, "fsdp")
+    second_full = packed[:, hidden : 2 * hidden]
+    bias_full = packed[:, 2 * hidden].astype(jnp.float32)
 
     chosen = pull_list[0]
     requesters, slot_cap = chosen.shape

time: 405 us -> 402 us (level)
  waiting for transfers between devices: 194 us -> 207 us
  Pallas kernels: 39.6 us -> 27.1 us
  starting transfers between devices: 53.3 us -> 47.6 us
    pallas_call x2, Pallas kernels: 29.2 us -> 20.2 us  [aggregate(): pl.pallas_call(functools.partial(_agg_kernel, nb, tiles - 1), grid_spec=g...]
    all_to_all x1, waiting for transfers between devices: 60.1 us -> 68 us  [on_device(): lax.all_to_all(sent_second, ('dom', 'fsdp'), split_axis=0, concat_axis=0,...]
    all_to_all x2 -> x1, waiting for transfers between devices: 34.8 us -> 40.9 us  [gather_rows(): lax.all_to_all(jnp.broadcast_to(x[None], (n,) + x.shape), axis, split_axi...]
    all_to_all x1, blocking collectives: 42.8 us -> 47.8 us  [on_device(): lax.all_to_all(packed_terms.astype(jnp.bfloat16), 'fsdp', split_axis=0, c...]
    all_to_all x2 -> x1, starting transfers between devices: 13.2 us -> 8.6 us  [gather_rows(): lax.all_to_all(jnp.broadcast_to(x[None], (n,) + x.shape), axis, split_axi...]
  transfers between devices with their start and end apart: 11 -> 10, of which waited for: 7 -> 6; matrix products, arithmetic and copies ran while one was open for 12% -> 12% of each run, Pallas kernels for 10% -> 7%
where the time goes in v8:
time: 402 us; the launch traced here: 400 us
  waiting for transfers between devices  207 us (51%)
  blocking collectives  59.3 us (15%)
  starting transfers between devices  47.6 us (12%)
  local copies, waits for them, and re-layouts  35.3 us (9%)
  Pallas kernels  27.1 us (7%)
  matrix products  15.6 us (4%)
  other arithmetic  7.11 us (2%)
    all_to_all x1, waiting for transfers between devices, on_device(): lax.all_to_all(sent_first, ('dom', 'fsdp'), split_axis=0, concat_axis=0,...  86.3 us
    all_to_all x1, waiting for transfers between devices, on_device(): lax.all_to_all(sent_second, ('dom', 'fsdp'), split_axis=0, concat_axis=0,...  68 us
    all_to_all x1, blocking collectives, on_device(): lax.all_to_all(packed_terms.astype(jnp.bfloat16), 'fsdp', split_axis=0, c...  47.8 us
    all_to_all x1, waiting for transfers between devices, gather_rows(): lax.all_to_all(jnp.broadcast_to(x[None], (n,) + x.shape), axis, split_axi...  40.9 us
    pallas_call x2, Pallas kernels, aggregate(): pl.pallas_call(functools.partial(_agg_kernel, nb, tiles - 1), grid_spec=g...  20.2 us
    all_to_all x1, starting transfers between devices, on_device(): lax.all_to_all(sent_second, ('dom', 'fsdp'), split_axis=0, concat_axis=0,...  19 us
    gather x1, local copies, waits for them, and re-layouts, on_device(): jnp.take(history_first, chosen.reshape(-1), axis=0, mode='clip')  13.5 us
    gather x1, local copies, waits for them, and re-layouts, on_device(): jnp.take(history_second, chosen.reshape(-1), axis=0, mode='clip')  13.4 us
  transfers between devices with their start and end apart: 10, of which 6 were waited for; matrix products, arithmetic and copies ran while one was open for 12% of the time, Pallas kernels for 7%

profile of v8, /device:TPU:1, one launch (start us, length us, event | category | flops | bytes accessed | tf_op | source)
XLA Modules:
  0.0 400.1 jit_solution(8990538456521060856)
XLA Ops:
  2.5 2.6 broadcast_in_dim.10
  5.2 8.6 %all-to-all-start.1 = ((bf16[16,64,2176]{2,1,0:T(8,128)(2,1)}), bf16[16,64,2176]{2,1,0:T(8,128)(2,1)}, u32[]{:S(2)}, u32[]{:S(2)}) async-start(bf16[16,64,2176]{2,1,0:T(8,128)(2,1)} %broadcast_in_dim.10), calls=%async_computation.1 | async-start | bytes 8912896 | tf_op jit(solution)/shard_map/all_to_all | solution.py:137
  13.8 11.5 %all-gather = s32[8,1,128]{2,1,0:T(1,128)S(1)} all-gather(s32[1,1,128]{2,1,0:T(1,128)S(1)} %bitcast.96), channel_id=1, replica_groups=mesh['dom'=8,'fsdp'=16] {'dom'}, dimensions={0}, use_global_device_ids=true | all-gather | bytes 4608 | tf_op jit(solution)/shard_map/all_gather | solution.py:167
  25.5 13.5 %gather_fusion = bf16[512,64,128]{2,1,0:T(8,128)(2,1)} fusion(bf16[128,64,128]{2,1,0:T(8,128)(2,1)S(1)} %copy-done, s32[1024]{0:T(1024)S(1)} %pad_clamp_fusion), kind=kCustom, calls=%fused_computation | custom fusion | bytes 16779264 | tf_op jit(solution)/shard_map/jit(_take)/gather | solution.py:176
  39.0 40.9 %all-to-all-done.1 = bf16[16,64,2176]{2,1,0:T(8,128)(2,1)} async-done(((bf16[16,64,2176]{2,1,0:T(8,128)(2,1)}), bf16[16,64,2176]{2,1,0:T(8,128)(2,1)}, u32[]{:S(2)}, u32[]{:S(2)}) %all-to-all-start.1) | async-done | bytes 4456480 | tf_op jit(solution)/shard_map/all_to_all | solution.py:137
  79.9 9.3 %all-to-all-start = ((bf16[128,4,64,128]{3,2,1,0:T(8,128)(2,1)}), bf16[128,4,64,128]{3,2,1,0:T(8,128)(2,1)}, u32[]{:S(2)}, u32[]{:S(2)}) async-start(bf16[128,4,64,128]{3,2,1,0:T(8,128)(2,1)} %bitcast.89), calls=%async_computation | async-start | bytes 16777216 | tf_op jit(solution)/shard_map/all_to_all | solution.py:178
  89.2 13.4 %gather_fusion.1 = bf16[512,64,128]{2,1,0:T(8,128)(2,1)} fusion(bf16[128,64,128]{2,1,0:T(8,128)(2,1)S(1)} %copy-done.2, s32[1024]{0:T(1024)S(1)} %pad_clamp_fusion), kind=kCustom, calls=%fused_computation.1 | custom fusion | bytes 16779264 | tf_op jit(solution)/shard_map/jit(_take)/gather | solution.py:177
  102.6 86.3 %all-to-all-done = bf16[128,4,64,128]{3,2,1,0:T(8,128)(2,1)} async-done(((bf16[128,4,64,128]{3,2,1,0:T(8,128)(2,1)}), bf16[128,4,64,128]{3,2,1,0:T(8,128)(2,1)}, u32[]{:S(2)}, u32[]{:S(2)}) %all-to-all-start) | async-done | bytes 8388640 | tf_op jit(solution)/shard_map/all_to_all | solution.py:178
  188.9 19.0 %all-to-all-start.2 = ((bf16[128,4,64,128]{3,2,1,0:T(8,128)(2,1)}), bf16[128,4,64,128]{3,2,1,0:T(8,128)(2,1)}, u32[]{:S(2)}, u32[]{:S(2)}) async-start(bf16[128,4,64,128]{3,2,1,0:T(8,128)(2,1)} %bitcast.88), calls=%async_computation.2 | async-start | bytes 16777216 | tf_op jit(solution)/shard_map/all_to_all | solution.py:179
  210.2 4.1 %fusion.17.back_ref = bf16[4,1024,128]{2,1,0:T(8,128)(2,1)} fusion(bf16[4,1024,128]{2,1,0:T(8,128)(2,1)} %param.25, bf16[1024,2176]{1,0:T(8,128)(2,1)} %bitcast.5), kind=kOutput, calls=%fused_computation.29 | convolution fusion | flops 1074266112 | bytes 4194304 | tf_op jit(solution)/shard_map/ab,vbn->van/dot_general | solution.py:187
  214.2 7.0 %shard_map.148 = f32[4,1024,128]{2,1,0:T(8,128)} custom-call(s32[4,6]{1,0:T(4,128)} %src_ref.5, s32[4]{0:T(128)} %cnt_ref.5, bf16[4,1024,128]{2,1,0:T(8,128)(2,1)} %fusion.17.back_ref, bf16[4,6,128,128]{3,2,1,0:T(8,128)(2,1)} %tile_ref.5), custom_call_target="tpu_custom_call" | custom-call | flops 805306368 | bytes 3932160 | tf_op jit(solution)/shard_map/pallas_call | solution.py:122
  222.3 10.0 %shard_map.147 = bf16[4,1024,128]{2,1,0:T(8,128)(2,1)} custom-call(s32[4,6]{1,0:T(4,128)} %src_ref.5, s32[4]{0:T(128)} %cnt_ref.5, s32[32]{0:T(128)} %reshape.99.live_ref, bf16[4,1024,128]{2,1,0:T(8,128)(2,1)} %own_ref.1, bf16[8,16,4,64,128]{4,3,2,1,0:T(8,128)(2,1)} %bitcast.4.pulled_ref, bf16[4,6,128,128]{3,2,1,0:T(8,128)(2,1)} %tile_ref.5), custom_call_target="tpu_custom_call" | custom-call | flops 805306368 | bytes 14417920 | tf_op jit(solution)/shard_map/pallas_call | solution.py:77
  232.3 4.8 %fusion.15 = (bf16[4,1024,128]{2,1,0:T(8,128)(2,1)}, f32[4,128,1024]{1,2,0:T(8,128)S(1)}) fusion(f32[1024]{0:T(1024)S(1)} %convert_reduce_fusion.1, bf16[4,1024,128]{2,1,0:T(8,128)(2,1)} %shard_map.147, bf16[1024,2176]{1,0:T(8,128)(2,1)} %bitcast.5), kind=kOutput, calls=%fused_computation.27 | convolution fusion | flops 1078984704 | bytes 6295552 | tf_op jit(solution)/shard_map/fh,vfn->vhn/dot_general | solution.py:200
  237.2 2.4 fusion.30
  239.6 68.0 %all-to-all-done.2 = bf16[128,4,64,128]{3,2,1,0:T(8,128)(2,1)} async-done(((bf16[128,4,64,128]{3,2,1,0:T(8,128)(2,1)}), bf16[128,4,64,128]{3,2,1,0:T(8,128)(2,1)}, u32[]{:S(2)}, u32[]{:S(2)}) %all-to-all-start.2) | async-done | bytes 8388640 | tf_op jit(solution)/shard_map/all_to_all | solution.py:179
  307.7 10.2 %shard_map.149 = bf16[4,1024,128]{2,1,0:T(8,128)(2,1)} custom-call(s32[4,6]{1,0:T(4,128)} %src_ref.5, s32[4]{0:T(128)} %cnt_ref.5, s32[32]{0:T(128)} %reshape.99.live_ref, bf16[4,1024,128]{2,1,0:T(8,128)(2,1)} %get-tuple-element.32.own_ref, bf16[8,16,4,64,128]{4,3,2,1,0:T(8,128)(2,1)} %bitcast.20.pulled_ref, bf16[4,6,128,128]{3,2,1,0:T(8,128)(2,1)} %tile_ref.5), custom_call_target="tpu_custom_call" | custom-call | flops 805306368 | bytes 14417920 | tf_op jit(solution)/shard_map/pallas_call | solution.py:77
  317.8 2.6 constant_dynamic-slice_fusion
  323.4 2.0 fusion.19
  328.2 2.0 fusion.12
  330.5 47.8 %all_to_all.20 = bf16[16,64,1152]{2,1,0:T(8,128)(2,1)S(1)} all-to-all(bf16[16,64,1152]{2,1,0:T(8,128)(2,1)S(1)} %fusion.1), channel_id=1, replica_groups=mesh['dom'=8,'fsdp'=16] {'fsdp'}, dimensions={0} | all-to-all | bytes 4718592 | tf_op jit(solution)/shard_map/all_to_all | solution.py:225
  379.8 5.9 %collective-permute-done.4 = f32[64,1152]{1,0:T(8,128)S(1)} collective-permute-done((f32[64,1152]{1,0:T(8,128)S(1)}, f32[64,1152]{1,0:T(8,128)S(1)}, u32[]{:S(2)}, u32[]{:S(2)}) %collective-permute-start.4) | collective-permute-done | bytes 294944 | tf_op jit(solution)/shard_map/ppermute | solution.py:228
  385.8 2.8 collective-permute-start.5
  388.5 4.9 %collective-permute-done.5 = f32[64,1152]{1,0:T(8,128)S(1)} collective-permute-done((f32[64,1152]{1,0:T(8,128)S(1)}, f32[64,1152]{1,0:T(8,128)S(1)}, u32[]{:S(2)}, u32[]{:S(2)}) %collective-permute-start.5) | collective-permute-done | bytes 294944 | tf_op jit(solution)/shard_map/ppermute | solution.py:228
  393.5 3.4 collective-permute-start.6
  (50 shorter events, 16.3 us)
Async XLA Ops:
  0.6 24.9 %copy-start = (bf16[128,64,128]{2,1,0:T(8,128)(2,1)S(1)}, bf16[128,64,128]{2,1,0:T(8,128)(2,1)}, u32[]{:S(2)}) copy-start(bf16[128,64,128]{2,1,0:T(8,128)(2,1)} %param.15) | copy-start | bytes 6291460
  5.2 8.6 %copy-start.7 = (s32[1,128]{1,0:T(1,128)S(1)}, s32[1,128]{1,0:T(1,128)}, u32[]{:S(2)}) copy-start(s32[1,128]{1,0:T(1,128)} %param.18) | copy-start | bytes 1540
  5.2 20.1 %copy-start.6 = (s32[1,128,4]{1,2,0:T(4,128)S(1)}, s32[1,128,4]{1,2,0:T(4,128)}, u32[]{:S(2)}) copy-start(s32[1,128,4]{1,2,0:T(4,128)} %param.17) | copy-start | bytes 6148
  5.2 74.7 %all-to-all-start.1 = ((bf16[16,64,2176]{2,1,0:T(8,128)(2,1)}), bf16[16,64,2176]{2,1,0:T(8,128)(2,1)}, u32[]{:S(2)}, u32[]{:S(2)}) async-start(bf16[16,64,2176]{2,1,0:T(8,128)(2,1)} %broadcast_in_dim.10), calls=%async_computation.1 | async-start | bytes 8912896 | tf_op jit(solution)/shard_map/all_to_all | solution.py:137
  79.9 9.3 %copy-start.2 = (bf16[128,64,128]{2,1,0:T(8,128)(2,1)S(1)}, bf16[128,64,128]{2,1,0:T(8,128)(2,1)}, u32[]{:S(2)}) copy-start(bf16[128,64,128]{2,1,0:T(8,128)(2,1)} %param.16) | copy-start | bytes 6291460
  79.9 109.1 %all-to-all-start = ((bf16[128,4,64,128]{3,2,1,0:T(8,128)(2,1)}), bf16[128,4,64,128]{3,2,1,0:T(8,128)(2,1)}, u32[]{:S(2)}, u32[]{:S(2)}) async-start(bf16[128,4,64,128]{3,2,1,0:T(8,128)(2,1)} %bitcast.89), calls=%async_computation | async-start | bytes 16777216 | tf_op jit(solution)/shard_map/all_to_all | solution.py:178
  188.9 118.8 %all-to-all-start.2 = ((bf16[128,4,64,128]{3,2,1,0:T(8,128)(2,1)}), bf16[128,4,64,128]{3,2,1,0:T(8,128)(2,1)}, u32[]{:S(2)}, u32[]{:S(2)}) async-start(bf16[128,4,64,128]{3,2,1,0:T(8,128)(2,1)} %bitcast.88), calls=%async_computation.2 | async-start | bytes 16777216 | tf_op jit(solution)/shard_map/all_to_all | solution.py:179
  208.0 118.3 %collective-permute-start.3 = (bf16[4,1024,128]{2,1,0:T(8,128)(2,1)}, bf16[4,1024,128]{2,1,0:T(8,128)(2,1)}, u32[]{:S(2)}, u32[]{:S(2)}) collective-permute-start(bf16[4,1024,128]{2,1,0:T(8,128)(2,1)} %param.25), channel_id=1, source_target_pairs={{0,16},{16,0},{32,48},{48,32},{64,80},{80,64},{96,112},{112,96},{1... | collective-permute-start | bytes 3145736 | tf_op jit(solution)/shard_map/ppermute | solution.py:185
  232.3 4.8 %copy-start.3 = (f32[4,1024,128]{2,1,0:T(8,128)S(1)}, f32[4,1024,128]{2,1,0:T(8,128)}, u32[]{:S(2)}) copy-start(f32[4,1024,128]{2,1,0:T(8,128)} %shard_map.148) | copy-start | bytes 6291460
  239.5 88.7 %collective-permute-start.1 = (bf16[4,1024,128]{2,1,0:T(8,128)(2,1)S(1)}, bf16[4,1024,128]{2,1,0:T(8,128)(2,1)}, u32[]{:S(2)}, u32[]{:S(2)}) collective-permute-start(bf16[4,1024,128]{2,1,0:T(8,128)(2,1)S(1)} %get-tuple-element.21), channel_id=1, source_target_pairs={{0,16},{16,0},{32,48},{48,32},{64,80},{80,64},{96,112},{112,96},{1... | collective-permute-start | bytes 3145736 | tf_op jit(solution)/shard_map/ppermute | solution.py:208
  307.7 10.2 %copy-start.4 = (bf16[4,1024,128]{2,1,0:T(8,128)(2,1)S(1)}, bf16[4,1024,128]{2,1,0:T(8,128)(2,1)}, u32[]{:S(2)}) copy-start(bf16[4,1024,128]{2,1,0:T(8,128)(2,1)} %shard_map.147) | copy-start | bytes 3145732
  321.6 4.6 %collective-permute-start.2 = (bf16[4,16,32,128]{3,2,0,1:T(8,128)(2,1)S(1)}, bf16[4,16,32,128]{3,2,0,1:T(8,128)(2,1)S(1)}, u32[]{:S(2)}, u32[]{:S(2)}) collective-permute-start(bf16[4,16,32,128]{3,2,0,1:T(8,128)(2,1)S(1)} %bitcast.93), channel_id=1, source_target_pairs={{0,16},{16,0},{32,48},{48,32},{64,80},{80,64},{96,112},{112,96},{1... | collective-permute-start | bytes 1572872 | tf_op jit(solution)/shard_map/ppermute | solution.py:217
  323.3 2.1 copy-start.5
  323.3 4.9 %collective-permute-start = (bf16[4,16,32,128]{3,2,0,1:T(8,128)(2,1)S(1)}, bf16[4,16,32,128]{3,2,0,1:T(8,128)(2,1)S(1)}, u32[]{:S(2)}, u32[]{:S(2)}) collective-permute-start(bf16[4,16,32,128]{3,2,0,1:T(8,128)(2,1)S(1)} %bitcast.92), channel_id=1, source_target_pairs={{0,16},{16,0},{32,48},{48,32},{64,80},{80,64},{96,112},{112,96},{1... | collective-permute-start | bytes 1572872 | tf_op jit(solution)/shard_map/ppermute | solution.py:208
  378.6 7.1 %collective-permute-start.4 = (f32[64,1152]{1,0:T(8,128)S(1)}, f32[64,1152]{1,0:T(8,128)S(1)}, u32[]{:S(2)}, u32[]{:S(2)}) collective-permute-start(f32[64,1152]{1,0:T(8,128)S(1)} %convert_reduce_fusion), channel_id=1, source_target_pairs={{0,32},{16,48},{32,0},{48,16},{64,96},{80,112},{96,64},{112,80},{1... | collective-permute-start | bytes 884744 | tf_op jit(solution)/shard_map/ppermute | solution.py:228
  385.7 14.4 %copy-start.1 = (bf16[128,64,128]{2,1,0:T(8,128)(2,1)S(1)}, bf16[128,64,128]{2,1,0:T(8,128)(2,1)}, u32[]{:S(2)}) copy-start(bf16[128,64,128]{2,1,0:T(8,128)(2,1)} %param.15) | copy-start | bytes 6291460
  385.8 7.7 %collective-permute-start.5 = (f32[64,1152]{1,0:T(8,128)S(1)}, f32[64,1152]{1,0:T(8,128)S(1)}, u32[]{:S(2)}, u32[]{:S(2)}) collective-permute-start(f32[64,1152]{1,0:T(8,128)S(1)} %add.72), channel_id=1, source_target_pairs={{0,64},{16,80},{32,96},{48,112},{64,0},{80,16},{96,32},{112,48},{1... | collective-permute-start | bytes 884744 | tf_op jit(solution)/shard_map/ppermute | solution.py:228
  393.5 4.6 %collective-permute-start.6 = (f32[64,1152]{1,0:T(8,128)S(1)}, f32[64,1152]{1,0:T(8,128)S(1)}, u32[]{:S(2)}, u32[]{:S(2)}) collective-permute-start(f32[64,1152]{1,0:T(8,128)S(1)} %add.73), channel_id=1, source_target_pairs={{0,16},{16,0},{32,48},{48,32},{64,80},{80,64},{96,112},{112,96},{1... | collective-permute-start | bytes 884744 | tf_op jit(solution)/shard_map/ppermute | solution.py:229

commit v9 on v8

--- a/solution.py
+++ b/solution.py
@@ -157,7 +157,7 @@
     me = lax.axis_index("dom") * fsdp_size + lax.axis_index("fsdp")
     rows, hidden = w_first.shape
     bias_cols = jnp.broadcast_to(bias_first[:, None], (rows, 128))
-    packed = gather_rows(jnp.concatenate([w_first, w_second, bias_cols], axis=1), "fsdp")
+    packed = lax.all_gather(jnp.concatenate([w_first, w_second, bias_cols], axis=1), "fsdp", axis=0, tiled=True)
     first_full = packed[:, :hidden]
     second_full = packed[:, hidden : 2 * hidden]
     bias_full = packed[:, 2 * hidden].astype(jnp.float32)

time: 402 us -> 374 us (0.930)
  waiting for transfers between devices: 207 us -> 176 us
  starting transfers between devices: 47.6 us -> 32.8 us
  between operations: 0.87 us -> 14.3 us
  Pallas kernels: 27.1 us -> 35.6 us
    all_gather x0 -> x1, waiting for transfers between devices: none -> 63.9 us  [on_device(): lax.all_gather(jnp.concatenate([w_first, w_second, bias_cols], axis=1), '...]
    all_to_all x1, waiting for transfers between devices: 68 us -> 9.89 us  [on_device(): lax.all_to_all(sent_second, ('dom', 'fsdp'), split_axis=0, concat_axis=0,...]
    all_to_all x1 -> x0, waiting for transfers between devices: 40.9 us -> none  [gather_rows(): lax.all_to_all(jnp.broadcast_to(x[None], (n,) + x.shape), axis, split_axi...]
    all_to_all x1 -> x0, starting transfers between devices: 8.6 us -> none  [gather_rows(): lax.all_to_all(jnp.broadcast_to(x[None], (n,) + x.shape), axis, split_axi...]
    pallas_call x2, Pallas kernels: 20.2 us -> 25.7 us  [aggregate(): pl.pallas_call(functools.partial(_agg_kernel, nb, tiles - 1), grid_spec=g...]
    all_to_all x1, starting transfers between devices: 19 us -> 14 us  [on_device(): lax.all_to_all(sent_second, ('dom', 'fsdp'), split_axis=0, concat_axis=0,...]
  transfers between devices with their start and end apart: 10 -> 10, of which waited for: 6 -> 7; matrix products, arithmetic and copies ran while one was open for 12% -> 9% of each run, Pallas kernels for 7% -> 10%
where the time goes in v9:
time: 374 us; the launch traced here: 372 us
  waiting for transfers between devices  176 us (47%)
  blocking collectives  59.1 us (16%)
  Pallas kernels  35.6 us (10%)
  local copies, waits for them, and re-layouts  33.1 us (9%)
  starting transfers between devices  32.8 us (9%)
  between operations  14.3 us (4%)
  matrix products  14.1 us (4%)
  other arithmetic  6.87 us (2%)
    all_to_all x1, waiting for transfers between devices, on_device(): lax.all_to_all(sent_first, ('dom', 'fsdp'), split_axis=0, concat_axis=0,...  89 us
    all_gather x1, waiting for transfers between devices, on_device(): lax.all_gather(jnp.concatenate([w_first, w_second, bias_cols], axis=1), '...  63.9 us
    all_to_all x1, blocking collectives, on_device(): lax.all_to_all(packed_terms.astype(jnp.bfloat16), 'fsdp', split_axis=0, c...  46.8 us
    pallas_call x2, Pallas kernels, aggregate(): pl.pallas_call(functools.partial(_agg_kernel, nb, tiles - 1), grid_spec=g...  25.7 us
    all_to_all x1, starting transfers between devices, on_device(): lax.all_to_all(sent_second, ('dom', 'fsdp'), split_axis=0, concat_axis=0,...  14 us
    gather x1, local copies, waits for them, and re-layouts, on_device(): jnp.take(history_first, chosen.reshape(-1), axis=0, mode='clip')  13.5 us
    gather x1, local copies, waits for them, and re-layouts, on_device(): jnp.take(history_second, chosen.reshape(-1), axis=0, mode='clip')  13.4 us
    all_gather x1, blocking collectives, on_device(): counts_all = lax.all_gather(pull_count, 'dom', axis=0, tiled=True)  12.4 us
  transfers between devices with their start and end apart: 10, of which 7 were waited for; matrix products, arithmetic and copies ran while one was open for 9% of the time, Pallas kernels for 10%

profile of v9, /device:TPU:1, one launch (start us, length us, event | category | flops | bytes accessed | tf_op | source)
XLA Modules:
  0.0 372.0 jit_solution(568381809674332231)
XLA Ops:
  7.2 12.4 %all-gather = s32[8,1,128]{2,1,0:T(1,128)S(1)} all-gather(s32[1,1,128]{2,1,0:T(1,128)} %bitcast.93), channel_id=1, replica_groups=mesh['dom'=8,'fsdp'=16] {'dom'}, dimensions={0}, use_global_device_ids=true | all-gather | bytes 4608 | tf_op jit(solution)/shard_map/all_gather | solution.py:167
  20.5 13.5 %gather_fusion = bf16[512,64,128]{2,1,0:T(8,128)(2,1)} fusion(bf16[128,64,128]{2,1,0:T(8,128)(2,1)S(1)} %copy-done, s32[1024]{0:T(1024)S(1)} %pad_clamp_fusion), kind=kCustom, calls=%fused_computation | custom fusion | bytes 16779264 | tf_op jit(solution)/shard_map/jit(_take)/gather | solution.py:176
  33.9 8.3 %all-to-all-start = ((bf16[128,4,64,128]{3,2,1,0:T(8,128)(2,1)}), bf16[128,4,64,128]{3,2,1,0:T(8,128)(2,1)}, u32[]{:S(2)}, u32[]{:S(2)}) async-start(bf16[128,4,64,128]{3,2,1,0:T(8,128)(2,1)} %bitcast.88), calls=%async_computation | async-start | bytes 16777216 | tf_op jit(solution)/shard_map/all_to_all | solution.py:178
  43.2 13.4 %gather_fusion.1 = bf16[512,64,128]{2,1,0:T(8,128)(2,1)} fusion(bf16[128,64,128]{2,1,0:T(8,128)(2,1)S(1)} %copy-done.2, s32[1024]{0:T(1024)S(1)} %pad_clamp_fusion), kind=kCustom, calls=%fused_computation.1 | custom fusion | bytes 16779264 | tf_op jit(solution)/shard_map/jit(_take)/gather | solution.py:177
  56.6 89.0 %all-to-all-done = bf16[128,4,64,128]{3,2,1,0:T(8,128)(2,1)} async-done(((bf16[128,4,64,128]{3,2,1,0:T(8,128)(2,1)}), bf16[128,4,64,128]{3,2,1,0:T(8,128)(2,1)}, u32[]{:S(2)}, u32[]{:S(2)}) %all-to-all-start) | async-done | bytes 8388640 | tf_op jit(solution)/shard_map/all_to_all | solution.py:178
  145.6 14.0 %all-to-all-start.1 = ((bf16[128,4,64,128]{3,2,1,0:T(8,128)(2,1)}), bf16[128,4,64,128]{3,2,1,0:T(8,128)(2,1)}, u32[]{:S(2)}, u32[]{:S(2)}) async-start(bf16[128,4,64,128]{3,2,1,0:T(8,128)(2,1)} %bitcast.87), calls=%async_computation.1 | async-start | bytes 16777216 | tf_op jit(solution)/shard_map/all_to_all | solution.py:179
  161.7 12.9 %shard_map.147 = bf16[4,1024,128]{2,1,0:T(8,128)(2,1)} custom-call(s32[4,6]{1,0:T(4,128)} %src_ref.5, s32[4]{0:T(128)} %cnt_ref.5, s32[32]{0:T(128)} %reshape.94.live_ref, bf16[4,1024,128]{2,1,0:T(8,128)(2,1)} %own_ref.1, bf16[8,16,4,64,128]{4,3,2,1,0:T(8,128)(2,1)} %bitcast.4.pulled_ref, bf16[4,6,128,128]{3,2,1,0:T(8,128)(2,1)} %tile_ref.5), custom_call_target="tpu_custom_call" | custom-call | flops 805306368 | bytes 14417920 | tf_op jit(solution)/shard_map/pallas_call | solution.py:77
  174.5 1.3 constant_dynamic-slice_fusion.2
  176.7 63.9 %all-gather.3.cloned.1.call-done = bf16[1024,2176]{1,0:T(8,128)(2,1)} async-done(((bf16[64,2176]{1,0:T(8,128)(2,1)}), bf16[1024,2176]{1,0:T(8,128)(2,1)}) %all-gather.3.cloned.1.call-update) | async-done | bytes 4456464 | tf_op jit(solution)/shard_map/all_gather | solution.py:160
  240.6 3.8 %fusion.17.back_ref = bf16[4,1024,128]{2,1,0:T(8,128)(2,1)} fusion(bf16[4,1024,128]{2,1,0:T(8,128)(2,1)S(1)} %copy-done.5, bf16[1024,2176]{1,0:T(8,128)(2,1)} %all-gather.3.cloned.1.call-done), kind=kOutput, calls=%fused_computation.29 | convolution fusion | flops 1074266112 | bytes 4194304 | tf_op jit(solution)/shard_map/ab,vbn->van/dot_general | solution.py:187
  244.4 9.9 %shard_map.148 = f32[4,1024,128]{2,1,0:T(8,128)} custom-call(s32[4,6]{1,0:T(4,128)} %src_ref.5, s32[4]{0:T(128)} %cnt_ref.5, bf16[4,1024,128]{2,1,0:T(8,128)(2,1)} %fusion.17.back_ref, bf16[4,6,128,128]{3,2,1,0:T(8,128)(2,1)} %tile_ref.5), custom_call_target="tpu_custom_call" | custom-call | flops 805306368 | bytes 3932160 | tf_op jit(solution)/shard_map/pallas_call | solution.py:122
  255.4 4.5 %fusion.15 = (bf16[4,1024,128]{2,1,0:T(8,128)(2,1)}, f32[4,128,1024]{1,2,0:T(8,128)S(1)}) fusion(f32[1024]{0:T(1024)S(1)} %convert_reduce_fusion.1, bf16[4,1024,128]{2,1,0:T(8,128)(2,1)S(1)} %copy-done.4, bf16[1024,2176]{1,0:T(8,128)(2,1)} %all-gather.3.cloned.1.call-done), kind=kOutput, calls=%fused_computation.27 | convolution fusion | flops 1078984704 | bytes 6295552 | tf_op jit(solution)/shard_map/fh,vfn->vhn/dot_general | solution.py:200
  260.0 2.4 fusion.30
  262.5 9.9 %all-to-all-done.1 = bf16[128,4,64,128]{3,2,1,0:T(8,128)(2,1)} async-done(((bf16[128,4,64,128]{3,2,1,0:T(8,128)(2,1)}), bf16[128,4,64,128]{3,2,1,0:T(8,128)(2,1)}, u32[]{:S(2)}, u32[]{:S(2)}) %all-to-all-start.1) | async-done | bytes 8388640 | tf_op jit(solution)/shard_map/all_to_all | solution.py:179
  272.3 12.9 %shard_map.149 = bf16[4,1024,128]{2,1,0:T(8,128)(2,1)} custom-call(s32[4,6]{1,0:T(4,128)} %src_ref.5, s32[4]{0:T(128)} %cnt_ref.5, s32[32]{0:T(128)} %reshape.94.live_ref, bf16[4,1024,128]{2,1,0:T(8,128)(2,1)} %get-tuple-element.32.own_ref, bf16[8,16,4,64,128]{4,3,2,1,0:T(8,128)(2,1)} %bitcast.19.pulled_ref, bf16[4,6,128,128]{3,2,1,0:T(8,128)(2,1)} %tile_ref.5), custom_call_target="tpu_custom_call" | custom-call | flops 805306368 | bytes 14417920 | tf_op jit(solution)/shard_map/pallas_call | solution.py:77
  285.2 1.3 constant_dynamic-slice_fusion
  289.7 2.1 fusion.11
  291.8 2.1 fusion.12
  294.2 46.8 %all_to_all.15 = bf16[16,64,1152]{2,1,0:T(8,128)(2,1)S(1)} all-to-all(bf16[16,64,1152]{2,1,0:T(8,128)(2,1)S(1)} %fusion.1), channel_id=1, replica_groups=mesh['dom'=8,'fsdp'=16] {'fsdp'}, dimensions={0} | all-to-all | bytes 4718592 | tf_op jit(solution)/shard_map/all_to_all | solution.py:225
  341.4 3.6 collective-permute-start.4
  345.0 5.8 %collective-permute-done.4 = f32[64,1152]{1,0:T(8,128)S(1)} collective-permute-done((f32[64,1152]{1,0:T(8,128)S(1)}, f32[64,1152]{1,0:T(8,128)S(1)}, u32[]{:S(2)}, u32[]{:S(2)}) %collective-permute-start.4) | collective-permute-done | bytes 294944 | tf_op jit(solution)/shard_map/ppermute | solution.py:228
  350.8 2.4 collective-permute-start.5
  353.1 5.5 %collective-permute-done.5 = f32[64,1152]{1,0:T(8,128)S(1)} collective-permute-done((f32[64,1152]{1,0:T(8,128)S(1)}, f32[64,1152]{1,0:T(8,128)S(1)}, u32[]{:S(2)}, u32[]{:S(2)}) %collective-permute-start.5) | collective-permute-done | bytes 294944 | tf_op jit(solution)/shard_map/ppermute | solution.py:228
  358.7 3.2 collective-permute-start.6
  (52 shorter events, 12.8 us)
Async XLA Ops:
  7.2 13.3 %copy-start = (bf16[128,64,128]{2,1,0:T(8,128)(2,1)S(1)}, bf16[128,64,128]{2,1,0:T(8,128)(2,1)}, u32[]{:S(2)}) copy-start(bf16[128,64,128]{2,1,0:T(8,128)(2,1)} %param.15) | copy-start | bytes 6291460
  33.9 8.4 %copy-start.8 = (bf16[64]{0:T(256)(128)(2,1)S(1)}, bf16[64]{0:T(256)(128)(2,1)}, u32[]{:S(2)}) copy-start(bf16[64]{0:T(256)(128)(2,1)} %param.24) | copy-start | bytes 388
  33.9 8.4 %copy-start.6 = (bf16[64,1024]{1,0:T(8,128)(2,1)S(1)}, bf16[64,1024]{1,0:T(8,128)(2,1)}, u32[]{:S(2)}) copy-start(bf16[64,1024]{1,0:T(8,128)(2,1)} %param.23) | copy-start | bytes 393220
  33.9 8.4 %copy-start.7 = (bf16[64,1024]{1,0:T(8,128)(2,1)S(1)}, bf16[64,1024]{1,0:T(8,128)(2,1)}, u32[]{:S(2)}) copy-start(bf16[64,1024]{1,0:T(8,128)(2,1)} %param.22) | copy-start | bytes 393220
  33.9 9.2 %copy-start.2 = (bf16[128,64,128]{2,1,0:T(8,128)(2,1)S(1)}, bf16[128,64,128]{2,1,0:T(8,128)(2,1)}, u32[]{:S(2)}) copy-start(bf16[128,64,128]{2,1,0:T(8,128)(2,1)} %param.16) | copy-start | bytes 6291460
  33.9 111.7 %all-to-all-start = ((bf16[128,4,64,128]{3,2,1,0:T(8,128)(2,1)}), bf16[128,4,64,128]{3,2,1,0:T(8,128)(2,1)}, u32[]{:S(2)}, u32[]{:S(2)}) async-start(bf16[128,4,64,128]{3,2,1,0:T(8,128)(2,1)} %bitcast.88), calls=%async_computation | async-start | bytes 16777216 | tf_op jit(solution)/shard_map/all_to_all | solution.py:178
  42.2 198.4 %all-gather.3.cloned.1.call-start = ((), (), s32[]{:S(2)}) async-start(), calls=%async_computation.3 | async-start | bytes 4734976 | tf_op jit(solution)/shard_map/all_gather | solution.py:160
  145.6 14.0 %copy-start.5 = (bf16[4,1024,128]{2,1,0:T(8,128)(2,1)S(1)}, bf16[4,1024,128]{2,1,0:T(8,128)(2,1)}, u32[]{:S(2)}) copy-start(bf16[4,1024,128]{2,1,0:T(8,128)(2,1)} %param.25) | copy-start | bytes 3145732
  145.6 126.7 %all-to-all-start.1 = ((bf16[128,4,64,128]{3,2,1,0:T(8,128)(2,1)}), bf16[128,4,64,128]{3,2,1,0:T(8,128)(2,1)}, u32[]{:S(2)}, u32[]{:S(2)}) async-start(bf16[128,4,64,128]{3,2,1,0:T(8,128)(2,1)} %bitcast.87), calls=%async_computation.1 | async-start | bytes 16777216 | tf_op jit(solution)/shard_map/all_to_all | solution.py:179
  159.6 129.3 %collective-permute-start.3 = (bf16[4,1024,128]{2,1,0:T(8,128)(2,1)S(1)}, bf16[4,1024,128]{2,1,0:T(8,128)(2,1)}, u32[]{:S(2)}, u32[]{:S(2)}) collective-permute-start(bf16[4,1024,128]{2,1,0:T(8,128)(2,1)S(1)} %copy-done.5), channel_id=1, source_target_pairs={{0,16},{16,0},{32,48},{48,32},{64,80},{80,64},{96,112},{112,96},{1... | collective-permute-start | bytes 3145736 | tf_op jit(solution)/shard_map/ppermute | solution.py:185
  176.7 115.1 %collective-permute-start = (bf16[4,16,32,128]{3,2,0,1:T(8,128)(2,1)}, bf16[4,16,32,128]{3,2,0,1:T(8,128)(2,1)}, u32[]{:S(2)}, u32[]{:S(2)}) collective-permute-start(bf16[4,16,32,128]{3,2,0,1:T(8,128)(2,1)} %bitcast.86), channel_id=1, source_target_pairs={{0,16},{16,0},{32,48},{48,32},{64,80},{80,64},{96,112},{112,96},{1... | collective-permute-start | bytes 1572872 | tf_op jit(solution)/shard_map/ppermute | solution.py:208
  244.4 11.0 %copy-start.4 = (bf16[4,1024,128]{2,1,0:T(8,128)(2,1)S(1)}, bf16[4,1024,128]{2,1,0:T(8,128)(2,1)}, u32[]{:S(2)}) copy-start(bf16[4,1024,128]{2,1,0:T(8,128)(2,1)} %shard_map.147) | copy-start | bytes 3145732
  255.4 4.5 %copy-start.3 = (f32[4,1024,128]{2,1,0:T(8,128)S(1)}, f32[4,1024,128]{2,1,0:T(8,128)}, u32[]{:S(2)}) copy-start(f32[4,1024,128]{2,1,0:T(8,128)} %shard_map.148) | copy-start | bytes 6291460
  262.4 29.5 %collective-permute-start.1 = (bf16[4,1024,128]{2,1,0:T(8,128)(2,1)S(1)}, bf16[4,1024,128]{2,1,0:T(8,128)(2,1)}, u32[]{:S(2)}, u32[]{:S(2)}) collective-permute-start(bf16[4,1024,128]{2,1,0:T(8,128)(2,1)S(1)} %get-tuple-element.21), channel_id=1, source_target_pairs={{0,16},{16,0},{32,48},{48,32},{64,80},{80,64},{96,112},{112,96},{1... | collective-permute-start | bytes 3145736 | tf_op jit(solution)/shard_map/ppermute | solution.py:208
  287.4 2.3 collective-permute-start.2
  341.4 9.4 %collective-permute-start.4 = (f32[64,1152]{1,0:T(8,128)S(1)}, f32[64,1152]{1,0:T(8,128)S(1)}, u32[]{:S(2)}, u32[]{:S(2)}) collective-permute-start(f32[64,1152]{1,0:T(8,128)S(1)} %convert_reduce_fusion), channel_id=1, source_target_pairs={{0,32},{16,48},{32,0},{48,16},{64,96},{80,112},{96,64},{112,80},{1... | collective-permute-start | bytes 884744 | tf_op jit(solution)/shard_map/ppermute | solution.py:228
  350.7 14.4 %copy-start.1 = (bf16[128,64,128]{2,1,0:T(8,128)(2,1)S(1)}, bf16[128,64,128]{2,1,0:T(8,128)(2,1)}, u32[]{:S(2)}) copy-start(bf16[128,64,128]{2,1,0:T(8,128)(2,1)} %param.15) | copy-start | bytes 6291460
  350.8 7.9 %collective-permute-start.5 = (f32[64,1152]{1,0:T(8,128)S(1)}, f32[64,1152]{1,0:T(8,128)S(1)}, u32[]{:S(2)}, u32[]{:S(2)}) collective-permute-start(f32[64,1152]{1,0:T(8,128)S(1)} %add.72), channel_id=1, source_target_pairs={{0,64},{16,80},{32,96},{48,112},{64,0},{80,16},{96,32},{112,48},{1... | collective-permute-start | bytes 884744 | tf_op jit(solution)/shard_map/ppermute | solution.py:228
  358.7 4.4 %collective-permute-start.6 = (f32[64,1152]{1,0:T(8,128)S(1)}, f32[64,1152]{1,0:T(8,128)S(1)}, u32[]{:S(2)}, u32[]{:S(2)}) collective-permute-start(f32[64,1152]{1,0:T(8,128)S(1)} %add.73), channel_id=1, source_target_pairs={{0,16},{16,0},{32,48},{48,32},{64,80},{80,64},{96,112},{112,96},{1... | collective-permute-start | bytes 884744 | tf_op jit(solution)/shard_map/ppermute | solution.py:229
Sparse Core Ops, SparseCore 0:
  45.2 195.3 all-gather.2

commit v10 on v9

--- a/solution.py
+++ b/solution.py
@@ -156,11 +156,15 @@
     fsdp_size = lax.axis_size("fsdp")
     me = lax.axis_index("dom") * fsdp_size + lax.axis_index("fsdp")
     rows, hidden = w_first.shape
+    core = lax.axis_index("dom") % 2
+    pair = [(d, d ^ 1) for d in range(dom_size)]
     bias_cols = jnp.broadcast_to(bias_first[:, None], (rows, 128))
-    packed = lax.all_gather(jnp.concatenate([w_first, w_second, bias_cols], axis=1), "fsdp", axis=0, tiled=True)
-    first_full = packed[:, :hidden]
-    second_full = packed[:, hidden : 2 * hidden]
-    bias_full = packed[:, 2 * hidden].astype(jnp.float32)
+    own_weight = jnp.where(core == 0, w_first, w_second)
+    mine = lax.all_gather(jnp.concatenate([own_weight, bias_cols], axis=1), "fsdp", axis=0, tiled=True)
+    theirs = lax.ppermute(mine[:, :hidden], "dom", pair)
+    first_full = jnp.where(core == 0, mine[:, :hidden], theirs)
+    second_full = jnp.where(core == 0, theirs, mine[:, :hidden])
+    bias_full = mine[:, hidden].astype(jnp.float32)
 
     chosen = pull_list[0]
     requesters, slot_cap = chosen.shape
@@ -180,8 +184,6 @@
     pulled_first = arrived_first.reshape(dom_size, fsdp_size, slot_cap, first_cols, block_len)
     pulled_second = arrived_second.reshape(dom_size, fsdp_size, slot_cap, second_cols, block_len)
 
-    core = lax.axis_index("dom") % 2
-    pair = [(d, d ^ 1) for d in range(dom_size)]
     partner_grad = lax.ppermute(out_grad, "dom", pair)
 
     back_second = jnp.einsum(

time: 374 us -> 377 us (level)
  blocking collectives: 59.1 us -> 64.9 us
    all_to_all x1, waiting for transfers between devices: 9.89 us -> 0.01 us  [on_device(): lax.all_to_all(sent_second, ('dom', 'fsdp'), split_axis=0, concat_axis=0,...]
    all_gather x1, waiting for transfers between devices: 63.9 us -> 72.9 us  [on_device(): lax.all_gather(jnp.concatenate([own_weight, bias_cols], axis=1), 'fsdp',...]
    all_to_all x1, blocking collectives: 46.8 us -> 52.6 us  [on_device(): lax.all_to_all(packed_terms.astype(jnp.bfloat16), 'fsdp', split_axis=0, c...]
    ppermute x1, starting transfers between devices: 0.01 us -> 4.24 us  [on_device(): second_got = lax.ppermute(second_theirs, 'dom', pair)]
  transfers between devices with their start and end apart: 10 -> 11, of which waited for: 7 -> 6; matrix products, arithmetic and copies ran while one was open for 9% -> 9% of each run, Pallas kernels for 10% -> 9%
where the time goes in v10:
time: 377 us; the launch traced here: 376 us
  waiting for transfers between devices  176 us (47%)
  blocking collectives  64.9 us (17%)
  starting transfers between devices  35.7 us (9%)
  Pallas kernels  33.3 us (9%)
  local copies, waits for them, and re-layouts  32.2 us (9%)
  between operations  14.3 us (4%)
  matrix products  13.5 us (4%)
  other arithmetic  6.84 us (2%)
    all_to_all x1, waiting for transfers between devices, on_device(): lax.all_to_all(sent_first, ('dom', 'fsdp'), split_axis=0, concat_axis=0,...  88.2 us
    all_gather x1, waiting for transfers between devices, on_device(): lax.all_gather(jnp.concatenate([own_weight, bias_cols], axis=1), 'fsdp',...  72.9 us
    all_to_all x1, blocking collectives, on_device(): lax.all_to_all(packed_terms.astype(jnp.bfloat16), 'fsdp', split_axis=0, c...  52.6 us
    pallas_call x2, Pallas kernels, aggregate(): pl.pallas_call(functools.partial(_agg_kernel, nb, tiles - 1), grid_spec=g...  24.7 us
    gather x1, local copies, waits for them, and re-layouts, on_device(): jnp.take(history_first, chosen.reshape(-1), axis=0, mode='clip')  13.5 us
    gather x1, local copies, waits for them, and re-layouts, on_device(): jnp.take(history_second, chosen.reshape(-1), axis=0, mode='clip')  13.4 us
    all_gather x1, blocking collectives, on_device(): counts_all = lax.all_gather(pull_count, 'dom', axis=0, tiled=True)  12.4 us
    all_to_all x1, starting transfers between devices, on_device(): lax.all_to_all(sent_second, ('dom', 'fsdp'), split_axis=0, concat_axis=0,...  12.3 us
  transfers between devices with their start and end apart: 11, of which 6 were waited for; matrix products, arithmetic and copies ran while one was open for 9% of the time, Pallas kernels for 9%

profile of v10, /device:TPU:1, one launch (start us, length us, event | category | flops | bytes accessed | tf_op | source)
XLA Modules:
  0.0 376.3 jit_solution(10011340600531760617)
XLA Ops:
  7.2 12.4 %all-gather = s32[8,1,128]{2,1,0:T(1,128)S(1)} all-gather(s32[1,1,128]{2,1,0:T(1,128)} %bitcast.95), channel_id=1, replica_groups=mesh['dom'=8,'fsdp'=16] {'dom'}, dimensions={0}, use_global_device_ids=true | all-gather | bytes 4608 | tf_op jit(solution)/shard_map/all_gather | solution.py:171
  20.5 13.5 %gather_fusion = bf16[512,64,128]{2,1,0:T(8,128)(2,1)} fusion(bf16[128,64,128]{2,1,0:T(8,128)(2,1)S(1)} %copy-done, s32[1024]{0:T(1024)S(1)} %pad_clamp_fusion), kind=kCustom, calls=%fused_computation | custom fusion | bytes 16779264 | tf_op jit(solution)/shard_map/jit(_take)/gather | solution.py:180
  34.0 8.3 %all-to-all-start = ((bf16[128,4,64,128]{3,2,1,0:T(8,128)(2,1)}), bf16[128,4,64,128]{3,2,1,0:T(8,128)(2,1)}, u32[]{:S(2)}, u32[]{:S(2)}) async-start(bf16[128,4,64,128]{3,2,1,0:T(8,128)(2,1)} %bitcast.88), calls=%async_computation | async-start | bytes 16777216 | tf_op jit(solution)/shard_map/all_to_all | solution.py:182
  43.2 13.4 %gather_fusion.1 = bf16[512,64,128]{2,1,0:T(8,128)(2,1)} fusion(bf16[128,64,128]{2,1,0:T(8,128)(2,1)S(1)} %copy-done.2, s32[1024]{0:T(1024)S(1)} %pad_clamp_fusion), kind=kCustom, calls=%fused_computation.1 | custom fusion | bytes 16779264 | tf_op jit(solution)/shard_map/jit(_take)/gather | solution.py:181
  56.6 88.2 %all-to-all-done = bf16[128,4,64,128]{3,2,1,0:T(8,128)(2,1)} async-done(((bf16[128,4,64,128]{3,2,1,0:T(8,128)(2,1)}), bf16[128,4,64,128]{3,2,1,0:T(8,128)(2,1)}, u32[]{:S(2)}, u32[]{:S(2)}) %all-to-all-start) | async-done | bytes 8388640 | tf_op jit(solution)/shard_map/all_to_all | solution.py:182
  144.8 12.3 %all-to-all-start.1 = ((bf16[128,4,64,128]{3,2,1,0:T(8,128)(2,1)}), bf16[128,4,64,128]{3,2,1,0:T(8,128)(2,1)}, u32[]{:S(2)}, u32[]{:S(2)}) async-start(bf16[128,4,64,128]{3,2,1,0:T(8,128)(2,1)} %bitcast.87), calls=%async_computation.1 | async-start | bytes 16777216 | tf_op jit(solution)/shard_map/all_to_all | solution.py:183
  157.2 72.9 %all-gather.3.cloned.1.call-done = bf16[1024,1152]{1,0:T(8,128)(2,1)} async-done(((bf16[64,1152]{1,0:T(8,128)(2,1)}), bf16[1024,1152]{1,0:T(8,128)(2,1)}) %all-gather.3.cloned.1.call-update) | async-done | bytes 2359312 | tf_op jit(solution)/shard_map/all_gather | solution.py:163
  230.1 1.8 slice.57
  234.9 1.7 collective-permute-done
  236.7 3.8 %fusion.25.back_ref = bf16[4,1024,128]{2,1,0:T(8,128)(2,1)} fusion(bf16[4,1024,128]{2,1,0:T(8,128)(2,1)S(1)} %copy-done.5, bf16[1024,1024]{1,0:T(8,128)(2,1)} %collective-permute-done, pred[]{:T(512)S(6)} %eq.4, bf16[1024,1152]{1,0:T(8,128)(2,1)} %all-gather.3.cloned.1.call-done), kind=kOutput, calls=%fused_computation.33 | convolution fusion | flops 1075314688 | bytes 6291457 | tf_op jit(solution)/shard_map/ab,vbn->van/dot_general | solution.py:189
  240.5 8.6 %shard_map.148 = f32[4,1024,128]{2,1,0:T(8,128)} custom-call(s32[4,6]{1,0:T(4,128)} %src_ref.5, s32[4]{0:T(128)} %cnt_ref.5, bf16[4,1024,128]{2,1,0:T(8,128)(2,1)} %fusion.25.back_ref, bf16[4,6,128,128]{3,2,1,0:T(8,128)(2,1)} %tile_ref.5), custom_call_target="tpu_custom_call" | custom-call | flops 805306368 | bytes 3932160 | tf_op jit(solution)/shard_map/pallas_call | solution.py:122
  249.1 12.3 %shard_map.147 = bf16[4,1024,128]{2,1,0:T(8,128)(2,1)} custom-call(s32[4,6]{1,0:T(4,128)} %src_ref.5, s32[4]{0:T(128)} %cnt_ref.5, s32[32]{0:T(128)} %reshape.94.live_ref, bf16[4,1024,128]{2,1,0:T(8,128)(2,1)} %own_ref.1, bf16[8,16,4,64,128]{4,3,2,1,0:T(8,128)(2,1)} %bitcast.4.pulled_ref, bf16[4,6,128,128]{3,2,1,0:T(8,128)(2,1)} %tile_ref.5), custom_call_target="tpu_custom_call" | custom-call | flops 805306368 | bytes 14417920 | tf_op jit(solution)/shard_map/pallas_call | solution.py:77
  261.4 5.5 %fusion.15 = (bf16[4,1024,128]{2,1,0:T(8,128)(2,1)}, f32[4,128,1024]{1,2,0:T(8,128)S(1)}) fusion(f32[1024]{0:T(1024)S(1)} %convert_reduce_fusion.1, bf16[4,1024,128]{2,1,0:T(8,128)(2,1)} %shard_map.147, bf16[1024,1024]{1,0:T(8,128)(2,1)} %collective-permute-done, pred[]{:T(512)S(6)} %eq.4, bf16[1024,1152]{1,0:T(8,128)(2,1)} %all-gather.3.cloned.1.call-done), kind=kOutput, calls=%fused_computation.25 | convolution fusion | flops 1080033280 | bytes 8392705 | tf_op jit(solution)/shard_map/fh,vfn->vhn/dot_general | solution.py:202
  266.9 2.4 fusion.42
  269.4 12.3 %shard_map.149 = bf16[4,1024,128]{2,1,0:T(8,128)(2,1)} custom-call(s32[4,6]{1,0:T(4,128)} %src_ref.5, s32[4]{0:T(128)} %cnt_ref.5, s32[32]{0:T(128)} %reshape.94.live_ref, bf16[4,1024,128]{2,1,0:T(8,128)(2,1)} %get-tuple-element.32.own_ref, bf16[8,16,4,64,128]{4,3,2,1,0:T(8,128)(2,1)} %bitcast.19.pulled_ref, bf16[4,6,128,128]{3,2,1,0:T(8,128)(2,1)} %tile_ref.5), custom_call_target="tpu_custom_call" | custom-call | flops 805306368 | bytes 14417920 | tf_op jit(solution)/shard_map/pallas_call | solution.py:77
  281.7 1.4 constant_dynamic-slice_fusion
  283.2 4.2 %collective-permute-start.3 = (bf16[4,16,32,128]{3,2,0,1:T(8,128)(2,1)S(1)}, bf16[4,16,32,128]{3,2,0,1:T(8,128)(2,1)S(1)}, u32[]{:S(2)}, u32[]{:S(2)}) collective-permute-start(bf16[4,16,32,128]{3,2,0,1:T(8,128)(2,1)S(1)} %bitcast.91), channel_id=1, source_target_pairs={{0,16},{16,0},{32,48},{48,32},{64,80},{80,64},{96,112},{112,96},{1... | collective-permute-start | bytes 1572872 | tf_op jit(solution)/shard_map/ppermute | solution.py:219
  289.7 2.0 fusion.9
  292.7 52.6 %all_to_all.15 = bf16[16,64,1152]{2,1,0:T(8,128)(2,1)S(1)} all-to-all(bf16[16,64,1152]{2,1,0:T(8,128)(2,1)S(1)} %fusion.1), channel_id=1, replica_groups=mesh['dom'=8,'fsdp'=16] {'fsdp'}, dimensions={0} | all-to-all | bytes 4718592 | tf_op jit(solution)/shard_map/all_to_all | solution.py:227
  345.7 7.0 %collective-permute-done.5 = f32[64,1152]{1,0:T(8,128)S(1)} collective-permute-done((f32[64,1152]{1,0:T(8,128)S(1)}, f32[64,1152]{1,0:T(8,128)S(1)}, u32[]{:S(2)}, u32[]{:S(2)}) %collective-permute-start.5) | collective-permute-done | bytes 294944 | tf_op jit(solution)/shard_map/ppermute | solution.py:230
  352.7 5.4 %collective-permute-start.6 = (f32[64,1152]{1,0:T(8,128)S(1)}, f32[64,1152]{1,0:T(8,128)S(1)}, u32[]{:S(2)}, u32[]{:S(2)}) collective-permute-start(f32[64,1152]{1,0:T(8,128)S(1)} %add.72), channel_id=1, source_target_pairs={{0,64},{16,80},{32,96},{48,112},{64,0},{80,16},{96,32},{112,48},{1... | collective-permute-start | bytes 884744 | tf_op jit(solution)/shard_map/ppermute | solution.py:230
  358.1 4.6 %collective-permute-done.6 = f32[64,1152]{1,0:T(8,128)S(1)} collective-permute-done((f32[64,1152]{1,0:T(8,128)S(1)}, f32[64,1152]{1,0:T(8,128)S(1)}, u32[]{:S(2)}, u32[]{:S(2)}) %collective-permute-start.6) | collective-permute-done | bytes 294944 | tf_op jit(solution)/shard_map/ppermute | solution.py:230
  362.7 3.5 collective-permute-start.7
  366.2 1.2 collective-permute-done.7
  (56 shorter events, 10.7 us)
Async XLA Ops:
  7.2 13.3 %copy-start = (bf16[128,64,128]{2,1,0:T(8,128)(2,1)S(1)}, bf16[128,64,128]{2,1,0:T(8,128)(2,1)}, u32[]{:S(2)}) copy-start(bf16[128,64,128]{2,1,0:T(8,128)(2,1)} %param.15) | copy-start | bytes 6291460
  33.9 8.4 %copy-start.6 = (bf16[64,1024]{1,0:T(8,128)(2,1)S(1)}, bf16[64,1024]{1,0:T(8,128)(2,1)}, u32[]{:S(2)}) copy-start(bf16[64,1024]{1,0:T(8,128)(2,1)} %param.22) | copy-start | bytes 393220
  33.9 8.4 %copy-start.7 = (bf16[64,1024]{1,0:T(8,128)(2,1)S(1)}, bf16[64,1024]{1,0:T(8,128)(2,1)}, u32[]{:S(2)}) copy-start(bf16[64,1024]{1,0:T(8,128)(2,1)} %param.23) | copy-start | bytes 393220
  33.9 8.4 %copy-start.8 = (bf16[64]{0:T(256)(128)(2,1)S(1)}, bf16[64]{0:T(256)(128)(2,1)}, u32[]{:S(2)}) copy-start(bf16[64]{0:T(256)(128)(2,1)} %param.24) | copy-start | bytes 388
  33.9 9.2 %copy-start.2 = (bf16[128,64,128]{2,1,0:T(8,128)(2,1)S(1)}, bf16[128,64,128]{2,1,0:T(8,128)(2,1)}, u32[]{:S(2)}) copy-start(bf16[128,64,128]{2,1,0:T(8,128)(2,1)} %param.16) | copy-start | bytes 6291460
  34.0 110.9 %all-to-all-start = ((bf16[128,4,64,128]{3,2,1,0:T(8,128)(2,1)}), bf16[128,4,64,128]{3,2,1,0:T(8,128)(2,1)}, u32[]{:S(2)}, u32[]{:S(2)}) async-start(bf16[128,4,64,128]{3,2,1,0:T(8,128)(2,1)} %bitcast.88), calls=%async_computation | async-start | bytes 16777216 | tf_op jit(solution)/shard_map/all_to_all | solution.py:182
  42.3 187.8 %all-gather.3.cloned.1.call-start = ((), (), s32[]{:S(2)}) async-start(), calls=%async_computation.3 | async-start | bytes 2506752 | tf_op jit(solution)/shard_map/all_gather | solution.py:163
  144.8 124.5 %all-to-all-start.1 = ((bf16[128,4,64,128]{3,2,1,0:T(8,128)(2,1)}), bf16[128,4,64,128]{3,2,1,0:T(8,128)(2,1)}, u32[]{:S(2)}, u32[]{:S(2)}) async-start(bf16[128,4,64,128]{3,2,1,0:T(8,128)(2,1)} %bitcast.87), calls=%async_computation.1 | async-start | bytes 16777216 | tf_op jit(solution)/shard_map/all_to_all | solution.py:183
  157.2 75.6 %copy-start.5 = (bf16[4,1024,128]{2,1,0:T(8,128)(2,1)S(1)}, bf16[4,1024,128]{2,1,0:T(8,128)(2,1)}, u32[]{:S(2)}) copy-start(bf16[4,1024,128]{2,1,0:T(8,128)(2,1)} %param.25) | copy-start | bytes 3145732
  231.8 4.8 %collective-permute-start = (bf16[1024,1024]{1,0:T(8,128)(2,1)S(1)}, bf16[1024,1024]{1,0:T(8,128)(2,1)}, u32[]{:S(2)}, u32[]{:S(2)}) collective-permute-start(bf16[1024,1024]{1,0:T(8,128)(2,1)S(1)} %slice.57), channel_id=1, source_target_pairs={{0,16},{16,0},{32,48},{48,32},{64,80},{80,64},{96,112},{112,96},{1... | collective-permute-start | bytes 6291464 | tf_op jit(solution)/shard_map/ppermute | solution.py:164
  232.8 56.9 %collective-permute-start.4 = (bf16[4,1024,128]{2,1,0:T(8,128)(2,1)S(1)}, bf16[4,1024,128]{2,1,0:T(8,128)(2,1)}, u32[]{:S(2)}, u32[]{:S(2)}) collective-permute-start(bf16[4,1024,128]{2,1,0:T(8,128)(2,1)S(1)} %copy-done.5), channel_id=1, source_target_pairs={{0,16},{16,0},{32,48},{48,32},{64,80},{80,64},{96,112},{112,96},{1... | collective-permute-start | bytes 3145736 | tf_op jit(solution)/shard_map/ppermute | solution.py:187
  261.4 5.5 %copy-start.3 = (f32[4,1024,128]{2,1,0:T(8,128)S(1)}, f32[4,1024,128]{2,1,0:T(8,128)}, u32[]{:S(2)}) copy-start(f32[4,1024,128]{2,1,0:T(8,128)} %shard_map.148) | copy-start | bytes 6291460
  281.7 5.8 %copy-start.4 = (bf16[4,1024,128]{2,1,0:T(8,128)(2,1)S(1)}, bf16[4,1024,128]{2,1,0:T(8,128)(2,1)}, u32[]{:S(2)}) copy-start(bf16[4,1024,128]{2,1,0:T(8,128)(2,1)} %shard_map.147) | copy-start | bytes 3145732
  283.2 6.5 %collective-permute-start.3 = (bf16[4,16,32,128]{3,2,0,1:T(8,128)(2,1)S(1)}, bf16[4,16,32,128]{3,2,0,1:T(8,128)(2,1)S(1)}, u32[]{:S(2)}, u32[]{:S(2)}) collective-permute-start(bf16[4,16,32,128]{3,2,0,1:T(8,128)(2,1)S(1)} %bitcast.91), channel_id=1, source_target_pairs={{0,16},{16,0},{32,48},{48,32},{64,80},{80,64},{96,112},{112,96},{1... | collective-permute-start | bytes 1572872 | tf_op jit(solution)/shard_map/ppermute | solution.py:219
  287.4 4.3 %collective-permute-start.2 = (bf16[4,1024,128]{2,1,0:T(8,128)(2,1)S(1)}, bf16[4,1024,128]{2,1,0:T(8,128)(2,1)S(1)}, u32[]{:S(2)}, u32[]{:S(2)}) collective-permute-start(bf16[4,1024,128]{2,1,0:T(8,128)(2,1)S(1)} %get-tuple-element.21), channel_id=1, source_target_pairs={{0,16},{16,0},{32,48},{48,32},{64,80},{80,64},{96,112},{112,96},{1... | collective-permute-start | bytes 3145736 | tf_op jit(solution)/shard_map/ppermute | solution.py:210
  287.7 4.0 %collective-permute-start.1 = (bf16[4,16,32,128]{3,2,0,1:T(8,128)(2,1)S(1)}, bf16[4,16,32,128]{3,2,0,1:T(8,128)(2,1)S(1)}, u32[]{:S(2)}, u32[]{:S(2)}) collective-permute-start(bf16[4,16,32,128]{3,2,0,1:T(8,128)(2,1)S(1)} %bitcast.92), channel_id=1, source_target_pairs={{0,16},{16,0},{32,48},{48,32},{64,80},{80,64},{96,112},{112,96},{1... | collective-permute-start | bytes 1572872 | tf_op jit(solution)/shard_map/ppermute | solution.py:210
  345.6 7.1 %collective-permute-start.5 = (f32[64,1152]{1,0:T(8,128)S(1)}, f32[64,1152]{1,0:T(8,128)S(1)}, u32[]{:S(2)}, u32[]{:S(2)}) collective-permute-start(f32[64,1152]{1,0:T(8,128)S(1)} %convert_reduce_fusion), channel_id=1, source_target_pairs={{0,32},{16,48},{32,0},{48,16},{64,96},{80,112},{96,64},{112,80},{1... | collective-permute-start | bytes 884744 | tf_op jit(solution)/shard_map/ppermute | solution.py:230
  352.7 16.8 %copy-start.1 = (bf16[128,64,128]{2,1,0:T(8,128)(2,1)S(1)}, bf16[128,64,128]{2,1,0:T(8,128)(2,1)}, u32[]{:S(2)}) copy-start(bf16[128,64,128]{2,1,0:T(8,128)(2,1)} %param.15) | copy-start | bytes 6291460
  352.7 10.0 %collective-permute-start.6 = (f32[64,1152]{1,0:T(8,128)S(1)}, f32[64,1152]{1,0:T(8,128)S(1)}, u32[]{:S(2)}, u32[]{:S(2)}) collective-permute-start(f32[64,1152]{1,0:T(8,128)S(1)} %add.72), channel_id=1, source_target_pairs={{0,64},{16,80},{32,96},{48,112},{64,0},{80,16},{96,32},{112,48},{1... | collective-permute-start | bytes 884744 | tf_op jit(solution)/shard_map/ppermute | solution.py:230
  362.7 4.7 %collective-permute-start.7 = (f32[64,1152]{1,0:T(8,128)S(1)}, f32[64,1152]{1,0:T(8,128)S(1)}, u32[]{:S(2)}, u32[]{:S(2)}) collective-permute-start(f32[64,1152]{1,0:T(8,128)S(1)} %add.73), channel_id=1, source_target_pairs={{0,16},{16,0},{32,48},{48,32},{64,80},{80,64},{96,112},{112,96},{1... | collective-permute-start | bytes 884744 | tf_op jit(solution)/shard_map/ppermute | solution.py:231
Sparse Core Ops, SparseCore 0:
  45.8 184.2 all-gather.2

commit v11 on v9

--- a/solution.py
+++ b/solution.py
@@ -164,8 +164,13 @@
 
     chosen = pull_list[0]
     requesters, slot_cap = chosen.shape
-    counts_all = lax.all_gather(pull_count, "dom", axis=0, tiled=True)
-    counts_all, chosen = lax.optimization_barrier((counts_all, chosen))
+    counts_all = pull_count
+    for flip in (1, 2, 4):
+        other = lax.ppermute(counts_all, "dom", [(d, d ^ flip) for d in range(dom_size)])
+        low_half = (lax.axis_index("dom") & flip) == 0
+        counts_all = jnp.where(
+            low_half, jnp.concatenate([counts_all, other], 0), jnp.concatenate([other, counts_all], 0)
+        )
     my_counts = lax.dynamic_index_in_dim(counts_all, me, axis=1, keepdims=False)
     slot_live = (lax.broadcasted_iota(jnp.int32, (slot_cap, dom_size), 0) < my_counts[None, :]).astype(jnp.int32)
     slot_live = slot_live.reshape(-1)

time: 374 us -> 391 us (1.045)
  starting transfers between devices: 32.8 us -> 55.1 us
  waiting for transfers between devices: 176 us -> 164 us
  blocking collectives: 59.1 us -> 65 us
    all_gather x1, waiting for transfers between devices: 63.9 us -> 0.01 us  [on_device(): lax.all_gather(jnp.concatenate([w_first, w_second, bias_cols], axis=1), '...]
    ppermute x0 -> x3, waiting for transfers between devices: none -> 58.7 us  [on_device(): lax.ppermute(counts_all, 'dom', [(d, d ^ flip) for d in range(dom_size)])]
    ppermute x0 -> x3, starting transfers between devices: none -> 23 us  [on_device(): lax.ppermute(counts_all, 'dom', [(d, d ^ flip) for d in range(dom_size)])]
    all_to_all x1, blocking collectives: 46.8 us -> 65 us  [on_device(): lax.all_to_all(packed_terms.astype(jnp.bfloat16), 'fsdp', split_axis=0, c...]
    all_gather x1 -> x0, blocking collectives: 12.4 us -> none  [on_device(): counts_all = lax.all_gather(pull_count, 'dom', axis=0, tiled=True)]
    all_to_all x1, waiting for transfers between devices: 9.89 us -> 0.01 us  [on_device(): lax.all_to_all(sent_second, ('dom', 'fsdp'), split_axis=0, concat_axis=0,...]
    ppermute x2, starting transfers between devices: 5.98 us -> 0.17 us  [on_device(): lax.ppermute(shard, 'dom', [(d, d ^ flip) for d in range(dom_size)])]
  transfers between devices with their start and end apart: 10 -> 13, of which waited for: 7 -> 8; matrix products, arithmetic and copies ran while one was open for 9% -> 9% of each run, Pallas kernels for 10% -> 9%
where the time goes in v11:
time: 391 us; the launch traced here: 389 us
  waiting for transfers between devices  164 us (42%)
  blocking collectives  65 us (17%)
  starting transfers between devices  55.1 us (14%)
  Pallas kernels  35.9 us (9%)
  local copies, waits for them, and re-layouts  33.8 us (9%)
  between operations  14.3 us (4%)
  matrix products  14.1 us (4%)
  other arithmetic  6.88 us (2%)
    all_to_all x1, waiting for transfers between devices, on_device(): lax.all_to_all(sent_first, ('dom', 'fsdp'), split_axis=0, concat_axis=0,...  89 us
    all_to_all x1, blocking collectives, on_device(): lax.all_to_all(packed_terms.astype(jnp.bfloat16), 'fsdp', split_axis=0, c...  65 us
    ppermute x3, waiting for transfers between devices, on_device(): lax.ppermute(counts_all, 'dom', [(d, d ^ flip) for d in range(dom_size)])  58.7 us
    pallas_call x2, Pallas kernels, aggregate(): pl.pallas_call(functools.partial(_agg_kernel, nb, tiles - 1), grid_spec=g...  26.3 us
    ppermute x3, starting transfers between devices, on_device(): lax.ppermute(counts_all, 'dom', [(d, d ^ flip) for d in range(dom_size)])  23 us
    all_to_all x1, starting transfers between devices, on_device(): lax.all_to_all(sent_second, ('dom', 'fsdp'), split_axis=0, concat_axis=0,...  14 us
    ppermute x2, waiting for transfers between devices, on_device(): lax.ppermute(shard, 'dom', [(d, d ^ flip) for d in range(dom_size)])  14 us
    gather x1, local copies, waits for them, and re-layouts, on_device(): jnp.take(history_first, chosen.reshape(-1), axis=0, mode='clip')  13.5 us
  transfers between devices with their start and end apart: 13, of which 8 were waited for; matrix products, arithmetic and copies ran while one was open for 9% of the time, Pallas kernels for 9%

profile of v11, /device:TPU:1, one launch (start us, length us, event | category | flops | bytes accessed | tf_op | source)
XLA Modules:
  0.0 388.7 jit_solution(646630587402878552)
XLA Ops:
  8.8 13.5 %gather_fusion = bf16[512,64,128]{2,1,0:T(8,128)(2,1)} fusion(bf16[128,64,128]{2,1,0:T(8,128)(2,1)S(1)} %copy-done, s32[1024]{0:T(1024)S(1)} %pad_clamp_fusion), kind=kCustom, calls=%fused_computation | custom fusion | bytes 16779264 | tf_op jit(solution)/shard_map/jit(_take)/gather | solution.py:181
  22.3 12.0 %all-to-all-start = ((bf16[128,4,64,128]{3,2,1,0:T(8,128)(2,1)}), bf16[128,4,64,128]{3,2,1,0:T(8,128)(2,1)}, u32[]{:S(2)}, u32[]{:S(2)}) async-start(bf16[128,4,64,128]{3,2,1,0:T(8,128)(2,1)} %bitcast.85), calls=%async_computation | async-start | bytes 16777216 | tf_op jit(solution)/shard_map/all_to_all | solution.py:183
  35.2 13.4 %gather_fusion.1 = bf16[512,64,128]{2,1,0:T(8,128)(2,1)} fusion(bf16[128,64,128]{2,1,0:T(8,128)(2,1)S(1)} %copy-done.2, s32[1024]{0:T(1024)S(1)} %pad_clamp_fusion), kind=kCustom, calls=%fused_computation.1 | custom fusion | bytes 16779264 | tf_op jit(solution)/shard_map/jit(_take)/gather | solution.py:182
  48.6 89.0 %all-to-all-done = bf16[128,4,64,128]{3,2,1,0:T(8,128)(2,1)} async-done(((bf16[128,4,64,128]{3,2,1,0:T(8,128)(2,1)}), bf16[128,4,64,128]{3,2,1,0:T(8,128)(2,1)}, u32[]{:S(2)}, u32[]{:S(2)}) %all-to-all-start) | async-done | bytes 8388640 | tf_op jit(solution)/shard_map/all_to_all | solution.py:183
  137.6 14.0 %all-to-all-start.1 = ((bf16[128,4,64,128]{3,2,1,0:T(8,128)(2,1)}), bf16[128,4,64,128]{3,2,1,0:T(8,128)(2,1)}, u32[]{:S(2)}, u32[]{:S(2)}) async-start(bf16[128,4,64,128]{3,2,1,0:T(8,128)(2,1)} %bitcast.84), calls=%async_computation.1 | async-start | bytes 16777216 | tf_op jit(solution)/shard_map/all_to_all | solution.py:184
  151.7 1.2 collective-permute-start
  154.3 57.5 %collective-permute-done.1 = s32[2,128]{1,0:T(2,128)S(1)} collective-permute-done((s32[2,128]{1,0:T(2,128)S(1)}, s32[2,128]{1,0:T(2,128)S(1)}, u32[]{:S(2)}, u32[]{:S(2)}) %collective-permute-start.1) | collective-permute-done | bytes 1056 | tf_op jit(solution)/shard_map/ppermute | solution.py:169
  211.9 21.2 %collective-permute-start.2 = (s32[4,128]{1,0:T(4,128)S(1)}, s32[4,128]{1,0:T(4,128)S(1)}, u32[]{:S(2)}, u32[]{:S(2)}) collective-permute-start(s32[4,128]{1,0:T(4,128)S(1)} %add_select_fusion.1), channel_id=1, source_target_pairs={{0,64},{16,80},{32,96},{48,112},{64,0},{80,16},{96,32},{112,48},{1... | collective-permute-start | bytes 6152 | tf_op jit(solution)/shard_map/ppermute | solution.py:169
  235.2 13.1 %shard_map.147 = bf16[4,1024,128]{2,1,0:T(8,128)(2,1)} custom-call(s32[4,6]{1,0:T(4,128)} %src_ref.5, s32[4]{0:T(128)} %cnt_ref.5, s32[32]{0:T(128)} %reshape.92.live_ref, bf16[4,1024,128]{2,1,0:T(8,128)(2,1)} %own_ref.1, bf16[8,16,4,64,128]{4,3,2,1,0:T(8,128)(2,1)} %bitcast.1.pulled_ref, bf16[4,6,128,128]{3,2,1,0:T(8,128)(2,1)} %tile_ref.5), custom_call_target="tpu_custom_call" | custom-call | flops 805306368 | bytes 14417920 | tf_op jit(solution)/shard_map/pallas_call | solution.py:77
  248.3 1.3 constant_dynamic-slice_fusion.2
  251.2 3.8 fusion.17.back_ref
  255.0 9.7 %shard_map.148 = f32[4,1024,128]{2,1,0:T(8,128)} custom-call(s32[4,6]{1,0:T(4,128)} %src_ref.5, s32[4]{0:T(128)} %cnt_ref.5, bf16[4,1024,128]{2,1,0:T(8,128)(2,1)} %fusion.17.back_ref, bf16[4,6,128,128]{3,2,1,0:T(8,128)(2,1)} %tile_ref.5), custom_call_target="tpu_custom_call" | custom-call | flops 805306368 | bytes 3932160 | tf_op jit(solution)/shard_map/pallas_call | solution.py:122
  264.7 1.1 convert_reduce_fusion.1
  265.8 4.5 %fusion.15 = (bf16[4,1024,128]{2,1,0:T(8,128)(2,1)}, f32[4,128,1024]{1,2,0:T(8,128)S(1)}) fusion(f32[1024]{0:T(1024)S(1)} %convert_reduce_fusion.1, bf16[4,1024,128]{2,1,0:T(8,128)(2,1)S(1)} %copy-done.4, bf16[1024,2176]{1,0:T(8,128)(2,1)} %all-gather.2.cloned.1.call-done), kind=kOutput, calls=%fused_computation.27 | convolution fusion | flops 1078984704 | bytes 6295552 | tf_op jit(solution)/shard_map/fh,vfn->vhn/dot_general | solution.py:205
  270.3 2.4 fusion.30
  272.8 13.1 %shard_map.149 = bf16[4,1024,128]{2,1,0:T(8,128)(2,1)} custom-call(s32[4,6]{1,0:T(4,128)} %src_ref.5, s32[4]{0:T(128)} %cnt_ref.5, s32[32]{0:T(128)} %reshape.92.live_ref, bf16[4,1024,128]{2,1,0:T(8,128)(2,1)} %get-tuple-element.28.own_ref, bf16[8,16,4,64,128]{4,3,2,1,0:T(8,128)(2,1)} %bitcast.16.pulled_ref, bf16[4,6,128,128]{3,2,1,0:T(8,128)(2,1)} %tile_ref.5), custom_call_target="tpu_custom_call" | custom-call | flops 805306368 | bytes 14417920 | tf_op jit(solution)/shard_map/pallas_call | solution.py:77
  285.9 1.3 constant_dynamic-slice_fusion
  290.4 2.1 fusion.11
  292.5 2.1 fusion.12
  294.9 65.0 %all_to_all.15 = bf16[16,64,1152]{2,1,0:T(8,128)(2,1)S(1)} all-to-all(bf16[16,64,1152]{2,1,0:T(8,128)(2,1)S(1)} %fusion.1), channel_id=1, replica_groups=mesh['dom'=8,'fsdp'=16] {'fsdp'}, dimensions={0} | all-to-all | bytes 4718592 | tf_op jit(solution)/shard_map/all_to_all | solution.py:230
  360.3 6.9 %collective-permute-done.7 = f32[64,1152]{1,0:T(8,128)S(1)} collective-permute-done((f32[64,1152]{1,0:T(8,128)S(1)}, f32[64,1152]{1,0:T(8,128)S(1)}, u32[]{:S(2)}, u32[]{:S(2)}) %collective-permute-start.7) | collective-permute-done | bytes 294944 | tf_op jit(solution)/shard_map/ppermute | solution.py:233
  367.4 7.1 %collective-permute-done.8 = f32[64,1152]{1,0:T(8,128)S(1)} collective-permute-done((f32[64,1152]{1,0:T(8,128)S(1)}, f32[64,1152]{1,0:T(8,128)S(1)}, u32[]{:S(2)}, u32[]{:S(2)}) %collective-permute-start.8) | collective-permute-done | bytes 294944 | tf_op jit(solution)/shard_map/ppermute | solution.py:233
  374.5 4.1 %collective-permute-start.9 = (f32[64,1152]{1,0:T(8,128)S(1)}, f32[64,1152]{1,0:T(8,128)S(1)}, u32[]{:S(2)}, u32[]{:S(2)}) collective-permute-start(f32[64,1152]{1,0:T(8,128)S(1)} %add.73), channel_id=1, source_target_pairs={{0,16},{16,0},{32,48},{48,32},{64,80},{80,64},{96,112},{112,96},{1... | collective-permute-start | bytes 884744 | tf_op jit(solution)/shard_map/ppermute | solution.py:234
  378.5 1.2 collective-permute-done.9
  (62 shorter events, 13.7 us)
Async XLA Ops:
  7.2 1.6 copy-start
  22.3 12.0 %copy-start.8 = (bf16[64]{0:T(256)(128)(2,1)S(1)}, bf16[64]{0:T(256)(128)(2,1)}, u32[]{:S(2)}) copy-start(bf16[64]{0:T(256)(128)(2,1)} %param.24) | copy-start | bytes 388
  22.3 12.1 %copy-start.6 = (bf16[64,1024]{1,0:T(8,128)(2,1)S(1)}, bf16[64,1024]{1,0:T(8,128)(2,1)}, u32[]{:S(2)}) copy-start(bf16[64,1024]{1,0:T(8,128)(2,1)} %param.23) | copy-start | bytes 393220
  22.3 12.1 %copy-start.7 = (bf16[64,1024]{1,0:T(8,128)(2,1)S(1)}, bf16[64,1024]{1,0:T(8,128)(2,1)}, u32[]{:S(2)}) copy-start(bf16[64,1024]{1,0:T(8,128)(2,1)} %param.22) | copy-start | bytes 393220
  22.3 12.9 %copy-start.2 = (bf16[128,64,128]{2,1,0:T(8,128)(2,1)S(1)}, bf16[128,64,128]{2,1,0:T(8,128)(2,1)}, u32[]{:S(2)}) copy-start(bf16[128,64,128]{2,1,0:T(8,128)(2,1)} %param.16) | copy-start | bytes 6291460
  22.3 115.3 %all-to-all-start = ((bf16[128,4,64,128]{3,2,1,0:T(8,128)(2,1)}), bf16[128,4,64,128]{3,2,1,0:T(8,128)(2,1)}, u32[]{:S(2)}, u32[]{:S(2)}) async-start(bf16[128,4,64,128]{3,2,1,0:T(8,128)(2,1)} %bitcast.85), calls=%async_computation | async-start | bytes 16777216 | tf_op jit(solution)/shard_map/all_to_all | solution.py:183
  34.3 216.9 %all-gather.2.cloned.1.call-start = ((), (), s32[]{:S(2)}) async-start(), calls=%async_computation.3 | async-start | bytes 4734976 | tf_op jit(solution)/shard_map/all_gather | solution.py:160
  137.6 14.0 %copy-start.9 = (s32[1,128]{1,0:T(1,128)S(1)}, s32[1,128]{1,0:T(1,128)}, u32[]{:S(2)}) copy-start(s32[1,128]{1,0:T(1,128)} %param.18) | copy-start | bytes 1540
  137.6 95.4 %copy-start.5 = (bf16[4,1024,128]{2,1,0:T(8,128)(2,1)S(1)}, bf16[4,1024,128]{2,1,0:T(8,128)(2,1)}, u32[]{:S(2)}) copy-start(bf16[4,1024,128]{2,1,0:T(8,128)(2,1)} %param.25) | copy-start | bytes 3145732
  137.6 135.2 %all-to-all-start.1 = ((bf16[128,4,64,128]{3,2,1,0:T(8,128)(2,1)}), bf16[128,4,64,128]{3,2,1,0:T(8,128)(2,1)}, u32[]{:S(2)}, u32[]{:S(2)}) async-start(bf16[128,4,64,128]{3,2,1,0:T(8,128)(2,1)} %bitcast.84), calls=%async_computation.1 | async-start | bytes 16777216 | tf_op jit(solution)/shard_map/all_to_all | solution.py:184
  151.7 2.0 collective-permute-start
  153.7 58.1 %collective-permute-start.1 = (s32[2,128]{1,0:T(2,128)S(1)}, s32[2,128]{1,0:T(2,128)S(1)}, u32[]{:S(2)}, u32[]{:S(2)}) collective-permute-start(s32[2,128]{1,0:T(2,128)S(1)} %add_select_fusion.2), channel_id=1, source_target_pairs={{0,32},{16,48},{32,0},{48,16},{64,96},{80,112},{96,64},{112,80},{1... | collective-permute-start | bytes 3080 | tf_op jit(solution)/shard_map/ppermute | solution.py:169
  211.9 22.5 %collective-permute-start.2 = (s32[4,128]{1,0:T(4,128)S(1)}, s32[4,128]{1,0:T(4,128)S(1)}, u32[]{:S(2)}, u32[]{:S(2)}) collective-permute-start(s32[4,128]{1,0:T(4,128)S(1)} %add_select_fusion.1), channel_id=1, source_target_pairs={{0,64},{16,80},{32,96},{48,112},{64,0},{80,16},{96,32},{112,48},{1... | collective-permute-start | bytes 6152 | tf_op jit(solution)/shard_map/ppermute | solution.py:169
  233.0 56.7 %collective-permute-start.6 = (bf16[4,1024,128]{2,1,0:T(8,128)(2,1)S(1)}, bf16[4,1024,128]{2,1,0:T(8,128)(2,1)}, u32[]{:S(2)}, u32[]{:S(2)}) collective-permute-start(bf16[4,1024,128]{2,1,0:T(8,128)(2,1)S(1)} %copy-done.5), channel_id=1, source_target_pairs={{0,16},{16,0},{32,48},{48,32},{64,80},{80,64},{96,112},{112,96},{1... | collective-permute-start | bytes 3145736 | tf_op jit(solution)/shard_map/ppermute | solution.py:190
  250.5 42.1 %collective-permute-start.3 = (bf16[4,16,32,128]{3,2,0,1:T(8,128)(2,1)}, bf16[4,16,32,128]{3,2,0,1:T(8,128)(2,1)}, u32[]{:S(2)}, u32[]{:S(2)}) collective-permute-start(bf16[4,16,32,128]{3,2,0,1:T(8,128)(2,1)} %bitcast.83), channel_id=1, source_target_pairs={{0,16},{16,0},{32,48},{48,32},{64,80},{80,64},{96,112},{112,96},{1... | collective-permute-start | bytes 1572872 | tf_op jit(solution)/shard_map/ppermute | solution.py:213
  255.0 10.8 %copy-start.4 = (bf16[4,1024,128]{2,1,0:T(8,128)(2,1)S(1)}, bf16[4,1024,128]{2,1,0:T(8,128)(2,1)}, u32[]{:S(2)}) copy-start(bf16[4,1024,128]{2,1,0:T(8,128)(2,1)} %shard_map.147) | copy-start | bytes 3145732
  265.8 4.5 %copy-start.3 = (f32[4,1024,128]{2,1,0:T(8,128)S(1)}, f32[4,1024,128]{2,1,0:T(8,128)}, u32[]{:S(2)}) copy-start(f32[4,1024,128]{2,1,0:T(8,128)} %shard_map.148) | copy-start | bytes 6291460
  272.7 19.8 %collective-permute-start.4 = (bf16[4,1024,128]{2,1,0:T(8,128)(2,1)S(1)}, bf16[4,1024,128]{2,1,0:T(8,128)(2,1)}, u32[]{:S(2)}, u32[]{:S(2)}) collective-permute-start(bf16[4,1024,128]{2,1,0:T(8,128)(2,1)S(1)} %get-tuple-element.17), channel_id=1, source_target_pairs={{0,16},{16,0},{32,48},{48,32},{64,80},{80,64},{96,112},{112,96},{1... | collective-permute-start | bytes 3145736 | tf_op jit(solution)/shard_map/ppermute | solution.py:213
  288.1 2.3 collective-permute-start.5
  360.2 7.0 %collective-permute-start.7 = (f32[64,1152]{1,0:T(8,128)S(1)}, f32[64,1152]{1,0:T(8,128)S(1)}, u32[]{:S(2)}, u32[]{:S(2)}) collective-permute-start(f32[64,1152]{1,0:T(8,128)S(1)} %convert_reduce_fusion), channel_id=1, source_target_pairs={{0,32},{16,48},{32,0},{48,16},{64,96},{80,112},{96,64},{112,80},{1... | collective-permute-start | bytes 884744 | tf_op jit(solution)/shard_map/ppermute | solution.py:233
  367.2 14.6 %copy-start.1 = (bf16[128,64,128]{2,1,0:T(8,128)(2,1)S(1)}, bf16[128,64,128]{2,1,0:T(8,128)(2,1)}, u32[]{:S(2)}) copy-start(bf16[128,64,128]{2,1,0:T(8,128)(2,1)} %param.15) | copy-start | bytes 6291460
  367.3 7.2 %collective-permute-start.8 = (f32[64,1152]{1,0:T(8,128)S(1)}, f32[64,1152]{1,0:T(8,128)S(1)}, u32[]{:S(2)}, u32[]{:S(2)}) collective-permute-start(f32[64,1152]{1,0:T(8,128)S(1)} %add.72), channel_id=1, source_target_pairs={{0,64},{16,80},{32,96},{48,112},{64,0},{80,16},{96,32},{112,48},{1... | collective-permute-start | bytes 884744 | tf_op jit(solution)/shard_map/ppermute | solution.py:233
  374.5 5.3 %collective-permute-start.9 = (f32[64,1152]{1,0:T(8,128)S(1)}, f32[64,1152]{1,0:T(8,128)S(1)}, u32[]{:S(2)}, u32[]{:S(2)}) collective-permute-start(f32[64,1152]{1,0:T(8,128)S(1)} %add.73), channel_id=1, source_target_pairs={{0,16},{16,0},{32,48},{48,32},{64,80},{80,64},{96,112},{112,96},{1... | collective-permute-start | bytes 884744 | tf_op jit(solution)/shard_map/ppermute | solution.py:234
Sparse Core Ops, SparseCore 0:
  37.2 195.0 all-gather.1

commit v12 on v11

--- a/solution.py
+++ b/solution.py
@@ -171,6 +171,7 @@
         counts_all = jnp.where(
             low_half, jnp.concatenate([counts_all, other], 0), jnp.concatenate([other, counts_all], 0)
         )
+    counts_all, chosen = lax.optimization_barrier((counts_all, chosen))
     my_counts = lax.dynamic_index_in_dim(counts_all, me, axis=1, keepdims=False)
     slot_live = (lax.broadcasted_iota(jnp.int32, (slot_cap, dom_size), 0) < my_counts[None, :]).astype(jnp.int32)
     slot_live = slot_live.reshape(-1)

time: 391 us -> 377 us (0.964)
  blocking collectives: 65 us -> 48.9 us
  waiting for transfers between devices: 164 us -> 172 us
    all_gather x1, waiting for transfers between devices: 0.01 us -> 61.1 us  [on_device(): lax.all_gather(jnp.concatenate([w_first, w_second, bias_cols], axis=1), '...]
    ppermute x3, waiting for transfers between devices: 58.7 us -> 2.97 us  [on_device(): lax.ppermute(counts_all, 'dom', [(d, d ^ flip) for d in range(dom_size)])]
    ppermute x3, starting transfers between devices: 23 us -> 5.88 us  [on_device(): lax.ppermute(counts_all, 'dom', [(d, d ^ flip) for d in range(dom_size)])]
    all_to_all x1, blocking collectives: 65 us -> 48.9 us  [on_device(): lax.all_to_all(packed_terms.astype(jnp.bfloat16), 'fsdp', split_axis=0, c...]
    all_to_all x1, waiting for transfers between devices: 0.01 us -> 7.34 us  [on_device(): lax.all_to_all(sent_second, ('dom', 'fsdp'), split_axis=0, concat_axis=0,...]
    ppermute x2, starting transfers between devices: 0.8 us -> 7.14 us  [on_device(): first_got, back_got = lax.ppermute((first_theirs, back_pre), 'dom', pair)]
    ppermute x2, starting transfers between devices: 0.17 us -> 6.34 us  [on_device(): lax.ppermute(shard, 'dom', [(d, d ^ flip) for d in range(dom_size)])]
  transfers between devices with their start and end apart: 13 -> 13, of which waited for: 8 -> 10; matrix products, arithmetic and copies ran while one was open for 9% -> 9% of each run, Pallas kernels for 9% -> 9%
where the time goes in v12:
time: 377 us; the launch traced here: 376 us
  waiting for transfers between devices  172 us (46%)
  starting transfers between devices  52.3 us (14%)
  blocking collectives  48.9 us (13%)
  Pallas kernels  33.3 us (9%)
  local copies, waits for them, and re-layouts  33.1 us (9%)
  between operations  14.3 us (4%)
  matrix products  14.1 us (4%)
  other arithmetic  7.61 us (2%)
    all_to_all x1, waiting for transfers between devices, on_device(): lax.all_to_all(sent_first, ('dom', 'fsdp'), split_axis=0, concat_axis=0,...  89 us
    all_gather x1, waiting for transfers between devices, on_device(): lax.all_gather(jnp.concatenate([w_first, w_second, bias_cols], axis=1), '...  61.1 us
    all_to_all x1, blocking collectives, on_device(): lax.all_to_all(packed_terms.astype(jnp.bfloat16), 'fsdp', split_axis=0, c...  48.9 us
    pallas_call x2, Pallas kernels, aggregate(): pl.pallas_call(functools.partial(_agg_kernel, nb, tiles - 1), grid_spec=g...  24.6 us
    all_to_all x1, starting transfers between devices, on_device(): lax.all_to_all(sent_second, ('dom', 'fsdp'), split_axis=0, concat_axis=0,...  14 us
    gather x1, local copies, waits for them, and re-layouts, on_device(): jnp.take(history_first, chosen.reshape(-1), axis=0, mode='clip')  13.5 us
    gather x1, local copies, waits for them, and re-layouts, on_device(): jnp.take(history_second, chosen.reshape(-1), axis=0, mode='clip')  13.4 us
    all_to_all x1, starting transfers between devices, on_device(): lax.all_to_all(sent_first, ('dom', 'fsdp'), split_axis=0, concat_axis=0,...  13.1 us
  transfers between devices with their start and end apart: 13, of which 10 were waited for; matrix products, arithmetic and copies ran while one was open for 9% of the time, Pallas kernels for 9%

profile of v12, /device:TPU:1, one launch (start us, length us, event | category | flops | bytes accessed | tf_op | source)
XLA Modules:
  0.0 375.7 jit_solution(14428084477555338846)
XLA Ops:
  7.2 1.5 collective-permute-start
  12.8 3.0 collective-permute-start.2
  17.7 13.5 %gather_fusion = bf16[512,64,128]{2,1,0:T(8,128)(2,1)} fusion(bf16[128,64,128]{2,1,0:T(8,128)(2,1)S(1)} %copy-done, s32[1024]{0:T(1024)S(1)} %pad_clamp_fusion), kind=kCustom, calls=%fused_computation | custom fusion | bytes 16779264 | tf_op jit(solution)/shard_map/jit(_take)/gather | solution.py:182
  31.2 13.1 %all-to-all-start = ((bf16[128,4,64,128]{3,2,1,0:T(8,128)(2,1)}), bf16[128,4,64,128]{3,2,1,0:T(8,128)(2,1)}, u32[]{:S(2)}, u32[]{:S(2)}) async-start(bf16[128,4,64,128]{3,2,1,0:T(8,128)(2,1)} %bitcast.86), calls=%async_computation | async-start | bytes 16777216 | tf_op jit(solution)/shard_map/all_to_all | solution.py:184
  45.2 13.4 %gather_fusion.1 = bf16[512,64,128]{2,1,0:T(8,128)(2,1)} fusion(bf16[128,64,128]{2,1,0:T(8,128)(2,1)S(1)} %copy-done.2, s32[1024]{0:T(1024)S(1)} %pad_clamp_fusion), kind=kCustom, calls=%fused_computation.1 | custom fusion | bytes 16779264 | tf_op jit(solution)/shard_map/jit(_take)/gather | solution.py:183
  58.7 89.0 %all-to-all-done = bf16[128,4,64,128]{3,2,1,0:T(8,128)(2,1)} async-done(((bf16[128,4,64,128]{3,2,1,0:T(8,128)(2,1)}), bf16[128,4,64,128]{3,2,1,0:T(8,128)(2,1)}, u32[]{:S(2)}, u32[]{:S(2)}) %all-to-all-start) | async-done | bytes 8388640 | tf_op jit(solution)/shard_map/all_to_all | solution.py:184
  147.7 14.0 %all-to-all-start.1 = ((bf16[128,4,64,128]{3,2,1,0:T(8,128)(2,1)}), bf16[128,4,64,128]{3,2,1,0:T(8,128)(2,1)}, u32[]{:S(2)}, u32[]{:S(2)}) async-start(bf16[128,4,64,128]{3,2,1,0:T(8,128)(2,1)} %bitcast.85), calls=%async_computation.1 | async-start | bytes 16777216 | tf_op jit(solution)/shard_map/all_to_all | solution.py:185
  163.9 12.3 %shard_map.147 = bf16[4,1024,128]{2,1,0:T(8,128)(2,1)} custom-call(s32[4,6]{1,0:T(4,128)} %src_ref.5, s32[4]{0:T(128)} %cnt_ref.5, s32[32]{0:T(128)} %reshape.94.live_ref, bf16[4,1024,128]{2,1,0:T(8,128)(2,1)} %own_ref.1, bf16[8,16,4,64,128]{4,3,2,1,0:T(8,128)(2,1)} %bitcast.2.pulled_ref, bf16[4,6,128,128]{3,2,1,0:T(8,128)(2,1)} %tile_ref.5), custom_call_target="tpu_custom_call" | custom-call | flops 805306368 | bytes 14417920 | tf_op jit(solution)/shard_map/pallas_call | solution.py:77
  178.4 3.2 collective-permute-start.3
  181.6 61.1 %all-gather.2.cloned.1.call-done = bf16[1024,2176]{1,0:T(8,128)(2,1)} async-done(((bf16[64,2176]{1,0:T(8,128)(2,1)}), bf16[1024,2176]{1,0:T(8,128)(2,1)}) %all-gather.2.cloned.1.call-update) | async-done | bytes 4456464 | tf_op jit(solution)/shard_map/all_gather | solution.py:160
  242.7 3.8 %fusion.17.back_ref = bf16[4,1024,128]{2,1,0:T(8,128)(2,1)} fusion(bf16[4,1024,128]{2,1,0:T(8,128)(2,1)S(1)} %copy-done.5, bf16[1024,2176]{1,0:T(8,128)(2,1)} %all-gather.2.cloned.1.call-done), kind=kOutput, calls=%fused_computation.29 | convolution fusion | flops 1074266112 | bytes 4194304 | tf_op jit(solution)/shard_map/ab,vbn->van/dot_general | solution.py:193
  246.5 8.6 %shard_map.148 = f32[4,1024,128]{2,1,0:T(8,128)} custom-call(s32[4,6]{1,0:T(4,128)} %src_ref.5, s32[4]{0:T(128)} %cnt_ref.5, bf16[4,1024,128]{2,1,0:T(8,128)(2,1)} %fusion.17.back_ref, bf16[4,6,128,128]{3,2,1,0:T(8,128)(2,1)} %tile_ref.5), custom_call_target="tpu_custom_call" | custom-call | flops 805306368 | bytes 3932160 | tf_op jit(solution)/shard_map/pallas_call | solution.py:122
  256.3 4.5 %fusion.15 = (bf16[4,1024,128]{2,1,0:T(8,128)(2,1)}, f32[4,128,1024]{1,2,0:T(8,128)S(1)}) fusion(f32[1024]{0:T(1024)S(1)} %convert_reduce_fusion.1, bf16[4,1024,128]{2,1,0:T(8,128)(2,1)S(1)} %copy-done.4, bf16[1024,2176]{1,0:T(8,128)(2,1)} %all-gather.2.cloned.1.call-done), kind=kOutput, calls=%fused_computation.27 | convolution fusion | flops 1078984704 | bytes 6295552 | tf_op jit(solution)/shard_map/fh,vfn->vhn/dot_general | solution.py:206
  260.8 2.4 fusion.30
  263.2 3.9 %collective-permute-start.4 = (bf16[4,1024,128]{2,1,0:T(8,128)(2,1)S(1)}, bf16[4,1024,128]{2,1,0:T(8,128)(2,1)}, u32[]{:S(2)}, u32[]{:S(2)}) collective-permute-start(bf16[4,1024,128]{2,1,0:T(8,128)(2,1)S(1)} %get-tuple-element.21), channel_id=1, source_target_pairs={{0,16},{16,0},{32,48},{48,32},{64,80},{80,64},{96,112},{112,96},{1... | collective-permute-start | bytes 3145736 | tf_op jit(solution)/shard_map/ppermute | solution.py:214
  267.1 7.3 %all-to-all-done.1 = bf16[128,4,64,128]{3,2,1,0:T(8,128)(2,1)} async-done(((bf16[128,4,64,128]{3,2,1,0:T(8,128)(2,1)}), bf16[128,4,64,128]{3,2,1,0:T(8,128)(2,1)}, u32[]{:S(2)}, u32[]{:S(2)}) %all-to-all-start.1) | async-done | bytes 8388640 | tf_op jit(solution)/shard_map/all_to_all | solution.py:185
  274.4 12.3 %shard_map.149 = bf16[4,1024,128]{2,1,0:T(8,128)(2,1)} custom-call(s32[4,6]{1,0:T(4,128)} %src_ref.5, s32[4]{0:T(128)} %cnt_ref.5, s32[32]{0:T(128)} %reshape.94.live_ref, bf16[4,1024,128]{2,1,0:T(8,128)(2,1)} %get-tuple-element.32.own_ref, bf16[8,16,4,64,128]{4,3,2,1,0:T(8,128)(2,1)} %bitcast.17.pulled_ref, bf16[4,6,128,128]{3,2,1,0:T(8,128)(2,1)} %tile_ref.5), custom_call_target="tpu_custom_call" | custom-call | flops 805306368 | bytes 14417920 | tf_op jit(solution)/shard_map/pallas_call | solution.py:77
  291.6 2.1 fusion.11
  293.8 2.1 fusion.12
  296.2 48.9 %all_to_all.15 = bf16[16,64,1152]{2,1,0:T(8,128)(2,1)S(1)} all-to-all(bf16[16,64,1152]{2,1,0:T(8,128)(2,1)S(1)} %fusion.1), channel_id=1, replica_groups=mesh['dom'=8,'fsdp'=16] {'fsdp'}, dimensions={0} | all-to-all | bytes 4718592 | tf_op jit(solution)/shard_map/all_to_all | solution.py:231
  346.8 5.7 %collective-permute-done.7 = f32[64,1152]{1,0:T(8,128)S(1)} collective-permute-done((f32[64,1152]{1,0:T(8,128)S(1)}, f32[64,1152]{1,0:T(8,128)S(1)}, u32[]{:S(2)}, u32[]{:S(2)}) %collective-permute-start.7) | collective-permute-done | bytes 294944 | tf_op jit(solution)/shard_map/ppermute | solution.py:234
  352.5 5.0 %collective-permute-start.8 = (f32[64,1152]{1,0:T(8,128)S(1)}, f32[64,1152]{1,0:T(8,128)S(1)}, u32[]{:S(2)}, u32[]{:S(2)}) collective-permute-start(f32[64,1152]{1,0:T(8,128)S(1)} %add.72), channel_id=1, source_target_pairs={{0,64},{16,80},{32,96},{48,112},{64,0},{80,16},{96,32},{112,48},{1... | collective-permute-start | bytes 884744 | tf_op jit(solution)/shard_map/ppermute | solution.py:234
  357.5 4.5 %collective-permute-done.8 = f32[64,1152]{1,0:T(8,128)S(1)} collective-permute-done((f32[64,1152]{1,0:T(8,128)S(1)}, f32[64,1152]{1,0:T(8,128)S(1)}, u32[]{:S(2)}, u32[]{:S(2)}) %collective-permute-start.8) | collective-permute-done | bytes 294944 | tf_op jit(solution)/shard_map/ppermute | solution.py:234
  362.0 3.6 collective-permute-start.9
  (60 shorter events, 22.4 us)
Async XLA Ops:
  7.2 10.5 %copy-start = (bf16[128,64,128]{2,1,0:T(8,128)(2,1)S(1)}, bf16[128,64,128]{2,1,0:T(8,128)(2,1)}, u32[]{:S(2)}) copy-start(bf16[128,64,128]{2,1,0:T(8,128)(2,1)} %param.15) | copy-start | bytes 6291460
  7.2 2.5 collective-permute-start
  10.4 2.4 collective-permute-start.1
  12.8 4.0 %collective-permute-start.2 = (s32[4,128]{1,0:T(4,128)S(1)}, s32[4,128]{1,0:T(4,128)S(1)}, u32[]{:S(2)}, u32[]{:S(2)}) collective-permute-start(s32[4,128]{1,0:T(4,128)S(1)} %add_select_fusion.1), channel_id=1, source_target_pairs={{0,64},{16,80},{32,96},{48,112},{64,0},{80,16},{96,32},{112,48},{1... | collective-permute-start | bytes 6152 | tf_op jit(solution)/shard_map/ppermute | solution.py:169
  31.2 13.2 %copy-start.8 = (bf16[64]{0:T(256)(128)(2,1)S(1)}, bf16[64]{0:T(256)(128)(2,1)}, u32[]{:S(2)}) copy-start(bf16[64]{0:T(256)(128)(2,1)} %param.24) | copy-start | bytes 388
  31.2 13.3 %copy-start.6 = (bf16[64,1024]{1,0:T(8,128)(2,1)S(1)}, bf16[64,1024]{1,0:T(8,128)(2,1)}, u32[]{:S(2)}) copy-start(bf16[64,1024]{1,0:T(8,128)(2,1)} %param.23) | copy-start | bytes 393220
  31.2 13.3 %copy-start.7 = (bf16[64,1024]{1,0:T(8,128)(2,1)S(1)}, bf16[64,1024]{1,0:T(8,128)(2,1)}, u32[]{:S(2)}) copy-start(bf16[64,1024]{1,0:T(8,128)(2,1)} %param.22) | copy-start | bytes 393220
  31.2 14.0 %copy-start.2 = (bf16[128,64,128]{2,1,0:T(8,128)(2,1)S(1)}, bf16[128,64,128]{2,1,0:T(8,128)(2,1)}, u32[]{:S(2)}) copy-start(bf16[128,64,128]{2,1,0:T(8,128)(2,1)} %param.16) | copy-start | bytes 6291460
  31.2 116.5 %all-to-all-start = ((bf16[128,4,64,128]{3,2,1,0:T(8,128)(2,1)}), bf16[128,4,64,128]{3,2,1,0:T(8,128)(2,1)}, u32[]{:S(2)}, u32[]{:S(2)}) async-start(bf16[128,4,64,128]{3,2,1,0:T(8,128)(2,1)} %bitcast.86), calls=%async_computation | async-start | bytes 16777216 | tf_op jit(solution)/shard_map/all_to_all | solution.py:184
  44.3 198.4 %all-gather.2.cloned.1.call-start = ((), (), s32[]{:S(2)}) async-start(), calls=%async_computation.3 | async-start | bytes 4734976 | tf_op jit(solution)/shard_map/all_gather | solution.py:160
  147.7 14.0 %copy-start.5 = (bf16[4,1024,128]{2,1,0:T(8,128)(2,1)S(1)}, bf16[4,1024,128]{2,1,0:T(8,128)(2,1)}, u32[]{:S(2)}) copy-start(bf16[4,1024,128]{2,1,0:T(8,128)(2,1)} %param.25) | copy-start | bytes 3145732
  147.7 126.8 %all-to-all-start.1 = ((bf16[128,4,64,128]{3,2,1,0:T(8,128)(2,1)}), bf16[128,4,64,128]{3,2,1,0:T(8,128)(2,1)}, u32[]{:S(2)}, u32[]{:S(2)}) async-start(bf16[128,4,64,128]{3,2,1,0:T(8,128)(2,1)} %bitcast.85), calls=%async_computation.1 | async-start | bytes 16777216 | tf_op jit(solution)/shard_map/all_to_all | solution.py:185
  161.7 129.6 %collective-permute-start.6 = (bf16[4,1024,128]{2,1,0:T(8,128)(2,1)S(1)}, bf16[4,1024,128]{2,1,0:T(8,128)(2,1)}, u32[]{:S(2)}, u32[]{:S(2)}) collective-permute-start(bf16[4,1024,128]{2,1,0:T(8,128)(2,1)S(1)} %copy-done.5), channel_id=1, source_target_pairs={{0,16},{16,0},{32,48},{48,32},{64,80},{80,64},{96,112},{112,96},{1... | collective-permute-start | bytes 3145736 | tf_op jit(solution)/shard_map/ppermute | solution.py:191
  178.4 115.4 %collective-permute-start.3 = (bf16[4,16,32,128]{3,2,0,1:T(8,128)(2,1)}, bf16[4,16,32,128]{3,2,0,1:T(8,128)(2,1)}, u32[]{:S(2)}, u32[]{:S(2)}) collective-permute-start(bf16[4,16,32,128]{3,2,0,1:T(8,128)(2,1)} %bitcast.84), channel_id=1, source_target_pairs={{0,16},{16,0},{32,48},{48,32},{64,80},{80,64},{96,112},{112,96},{1... | collective-permute-start | bytes 1572872 | tf_op jit(solution)/shard_map/ppermute | solution.py:214
  246.5 9.7 %copy-start.4 = (bf16[4,1024,128]{2,1,0:T(8,128)(2,1)S(1)}, bf16[4,1024,128]{2,1,0:T(8,128)(2,1)}, u32[]{:S(2)}) copy-start(bf16[4,1024,128]{2,1,0:T(8,128)(2,1)} %shard_map.147) | copy-start | bytes 3145732
  256.3 4.5 %copy-start.3 = (f32[4,1024,128]{2,1,0:T(8,128)S(1)}, f32[4,1024,128]{2,1,0:T(8,128)}, u32[]{:S(2)}) copy-start(f32[4,1024,128]{2,1,0:T(8,128)} %shard_map.148) | copy-start | bytes 6291460
  263.2 30.6 %collective-permute-start.4 = (bf16[4,1024,128]{2,1,0:T(8,128)(2,1)S(1)}, bf16[4,1024,128]{2,1,0:T(8,128)(2,1)}, u32[]{:S(2)}, u32[]{:S(2)}) collective-permute-start(bf16[4,1024,128]{2,1,0:T(8,128)(2,1)S(1)} %get-tuple-element.21), channel_id=1, source_target_pairs={{0,16},{16,0},{32,48},{48,32},{64,80},{80,64},{96,112},{112,96},{1... | collective-permute-start | bytes 3145736 | tf_op jit(solution)/shard_map/ppermute | solution.py:214
  288.9 2.7 collective-permute-start.5
  345.4 7.0 %collective-permute-start.7 = (f32[64,1152]{1,0:T(8,128)S(1)}, f32[64,1152]{1,0:T(8,128)S(1)}, u32[]{:S(2)}, u32[]{:S(2)}) collective-permute-start(f32[64,1152]{1,0:T(8,128)S(1)} %convert_reduce_fusion), channel_id=1, source_target_pairs={{0,32},{16,48},{32,0},{48,16},{64,96},{80,112},{96,64},{112,80},{1... | collective-permute-start | bytes 884744 | tf_op jit(solution)/shard_map/ppermute | solution.py:234
  352.5 16.4 %copy-start.1 = (bf16[128,64,128]{2,1,0:T(8,128)(2,1)S(1)}, bf16[128,64,128]{2,1,0:T(8,128)(2,1)}, u32[]{:S(2)}) copy-start(bf16[128,64,128]{2,1,0:T(8,128)(2,1)} %param.15) | copy-start | bytes 6291460
  352.5 9.5 %collective-permute-start.8 = (f32[64,1152]{1,0:T(8,128)S(1)}, f32[64,1152]{1,0:T(8,128)S(1)}, u32[]{:S(2)}, u32[]{:S(2)}) collective-permute-start(f32[64,1152]{1,0:T(8,128)S(1)} %add.72), channel_id=1, source_target_pairs={{0,64},{16,80},{32,96},{48,112},{64,0},{80,16},{96,32},{112,48},{1... | collective-permute-start | bytes 884744 | tf_op jit(solution)/shard_map/ppermute | solution.py:234
  362.0 4.8 %collective-permute-start.9 = (f32[64,1152]{1,0:T(8,128)S(1)}, f32[64,1152]{1,0:T(8,128)S(1)}, u32[]{:S(2)}, u32[]{:S(2)}) collective-permute-start(f32[64,1152]{1,0:T(8,128)S(1)} %add.73), channel_id=1, source_target_pairs={{0,16},{16,0},{32,48},{48,32},{64,80},{80,64},{96,112},{112,96},{1... | collective-permute-start | bytes 884744 | tf_op jit(solution)/shard_map/ppermute | solution.py:235
Sparse Core Ops, SparseCore 0:
  47.3 195.3 all-gather.1

commit v13 on v9

--- a/solution.py
+++ b/solution.py
@@ -219,19 +219,30 @@
         "vprn,vbn->prb", second_mine, out_grad, preferred_element_type=jnp.float32
     ) + jnp.einsum("vprn,vbn->prb", second_got, partner_grad, preferred_element_type=jnp.float32)
 
-    bias_cols = jnp.zeros((fsdp_size, 2 * half_rows, lanes), jnp.float32)
-    bias_cols = bias_cols.at[:, 0, : hidden // fsdp_size].set(bias_term.reshape(fsdp_size, hidden // fsdp_size))
-    packed_terms = jnp.concatenate([jnp.concatenate([first_term, second_term], axis=1), bias_cols], axis=2)
-    arrived_terms = lax.all_to_all(packed_terms.astype(jnp.bfloat16), "fsdp", split_axis=0, concat_axis=0, tiled=True)
-    shard = jnp.sum(arrived_terms.astype(jnp.float32), axis=0)
-    for flip in (2, 4):
-        shard = shard + lax.ppermute(shard, "dom", [(d, d ^ flip) for d in range(dom_size)])
-    other = lax.ppermute(shard, "dom", pair)
-    low = jnp.where(core == 0, shard, other)
-    high = jnp.where(core == 0, other, shard)
-    first_total = jnp.concatenate([low[:half_rows, :hidden], high[:half_rows, :hidden]], axis=0)
-    second_total = jnp.concatenate([low[half_rows:, :hidden], high[half_rows:, :hidden]], axis=0)
-    bias_total = (shard + other)[0, hidden : hidden + hidden // fsdp_size]
+    sub = half_rows // dom_size
+    bias_share = hidden // fsdp_size // dom_size
+
+    def by_destination(term):
+        split = term.reshape(fsdp_size, dom_size, sub, hidden)
+        return jnp.transpose(split, (1, 0, 2, 3)).reshape(dom_size * fsdp_size, sub, hidden)
+
+    bias_part = jnp.transpose(bias_term.reshape(fsdp_size, dom_size, bias_share), (1, 0, 2))
+    bias_part = jnp.pad(bias_part.reshape(dom_size * fsdp_size, 1, bias_share), ((0, 0), (0, 2 * sub - 1), (0, lanes - bias_share)))
+    packed_terms = jnp.concatenate(
+        [jnp.concatenate([by_destination(first_term), by_destination(second_term)], axis=1), bias_part], axis=2
+    )
+    arrived_terms = lax.all_to_all(packed_terms.astype(jnp.bfloat16), ("dom", "fsdp"), split_axis=0, concat_axis=0, tiled=True)
+    arrived_terms = arrived_terms.astype(jnp.float32).reshape(dom_size // 2, 2, fsdp_size, 2 * sub, hidden + lanes)
+    reduced = jnp.sum(arrived_terms, axis=(0, 2))
+    pieces = reduced[None]
+    for flip in (1, 2, 4):
+        other = lax.ppermute(pieces, "dom", [(d, d ^ flip) for d in range(dom_size)])
+        low_half = (lax.axis_index("dom") & flip) == 0
+        pieces = jnp.where(low_half, jnp.concatenate([pieces, other], 0), jnp.concatenate([other, pieces], 0))
+    ordered = jnp.transpose(pieces, (1, 0, 2, 3))
+    first_total = ordered[:, :, :sub, :hidden].reshape(2 * half_rows, hidden)
+    second_total = ordered[:, :, sub:, :hidden].reshape(2 * half_rows, hidden)
+    bias_total = jnp.sum(pieces[:, :, 0, hidden : hidden + bias_share], axis=1).reshape(-1)
     return (hidden_new, first_total, second_total, bias_total)
 
 

time: 374 us -> 389 us (1.040)
  local copies, waits for them, and re-layouts: 33.1 us -> 42.8 us
  starting transfers between devices: 32.8 us -> 39.1 us
    all_to_all x1, waiting for transfers between devices: 9.89 us -> 0.01 us  [on_device(): lax.all_to_all(sent_second, ('dom', 'fsdp'), split_axis=0, concat_axis=0,...]
    all_gather x1, waiting for transfers between devices: 63.9 us -> 72.6 us  [on_device(): lax.all_gather(jnp.concatenate([w_first, w_second, bias_cols], axis=1), '...]
    ppermute x2, starting transfers between devices: 0.09 us -> 7.63 us  [on_device(): first_got, back_got = lax.ppermute((first_theirs, back_pre), 'dom', pair)]
    reshape x0 -> x9, local copies, waits for them, and re-layouts: none -> 7.33 us  [the longest x4 5.05 us: by_destination(): split = term.reshape(fsdp_size, dom_size, sub, hidden)]
    ppermute x3, starting transfers between devices: 9.18 us -> 2.97 us  [on_device(): lax.ppermute(pieces, 'dom', [(d, d ^ flip) for d in range(dom_size)])]
  transfers between devices with their start and end apart: 10 -> 10, of which waited for: 7 -> 5; matrix products, arithmetic and copies ran while one was open for 9% -> 11% of each run, Pallas kernels for 10% -> 9%
where the time goes in v13:
time: 389 us; the launch traced here: 387 us
  waiting for transfers between devices  175 us (45%)
  blocking collectives  58.5 us (15%)
  local copies, waits for them, and re-layouts  42.8 us (11%)
  starting transfers between devices  39.1 us (10%)
  Pallas kernels  33.6 us (9%)
  matrix products  17.8 us (5%)
  between operations  14.3 us (4%)
  other arithmetic  6.19 us (2%)
    all_to_all x1, waiting for transfers between devices, on_device(): lax.all_to_all(sent_first, ('dom', 'fsdp'), split_axis=0, concat_axis=0,...  89 us
    all_gather x1, waiting for transfers between devices, on_device(): lax.all_gather(jnp.concatenate([w_first, w_second, bias_cols], axis=1), '...  72.6 us
    all_to_all x1, blocking collectives, on_device(): lax.all_to_all(packed_terms.astype(jnp.bfloat16), ('dom', 'fsdp'), split_...  46.2 us
    pallas_call x2, Pallas kernels, aggregate(): pl.pallas_call(functools.partial(_agg_kernel, nb, tiles - 1), grid_spec=g...  24.5 us
    all_to_all x1, starting transfers between devices, on_device(): lax.all_to_all(sent_second, ('dom', 'fsdp'), split_axis=0, concat_axis=0,...  15.4 us
    gather x1, local copies, waits for them, and re-layouts, on_device(): jnp.take(history_first, chosen.reshape(-1), axis=0, mode='clip')  13.5 us
    gather x1, local copies, waits for them, and re-layouts, on_device(): jnp.take(history_second, chosen.reshape(-1), axis=0, mode='clip')  13.4 us
    ppermute x3, waiting for transfers between devices, on_device(): lax.ppermute(pieces, 'dom', [(d, d ^ flip) for d in range(dom_size)])  13.3 us
  transfers between devices with their start and end apart: 10, of which 5 were waited for; matrix products, arithmetic and copies ran while one was open for 11% of the time, Pallas kernels for 9%

profile of v13, /device:TPU:1, one launch (start us, length us, event | category | flops | bytes accessed | tf_op | source)
XLA Modules:
  0.0 387.1 jit_solution(154713265353371759)
XLA Ops:
  7.2 12.4 %all-gather = s32[8,1,128]{2,1,0:T(1,128)S(1)} all-gather(s32[1,1,128]{2,1,0:T(1,128)} %bitcast.113), channel_id=1, replica_groups=mesh['dom'=8,'fsdp'=16] {'dom'}, dimensions={0}, use_global_device_ids=true | all-gather | bytes 4608 | tf_op jit(solution)/shard_map/all_gather | solution.py:167
  20.5 13.5 %gather_fusion = bf16[512,64,128]{2,1,0:T(8,128)(2,1)} fusion(bf16[128,64,128]{2,1,0:T(8,128)(2,1)S(1)} %copy-done, s32[1024]{0:T(1024)S(1)} %pad_clamp_fusion), kind=kCustom, calls=%fused_computation | custom fusion | bytes 16779264 | tf_op jit(solution)/shard_map/jit(_take)/gather | solution.py:176
  33.9 8.3 %all-to-all-start = ((bf16[128,4,64,128]{3,2,1,0:T(8,128)(2,1)}), bf16[128,4,64,128]{3,2,1,0:T(8,128)(2,1)}, u32[]{:S(2)}, u32[]{:S(2)}) async-start(bf16[128,4,64,128]{3,2,1,0:T(8,128)(2,1)} %bitcast.100), calls=%async_computation | async-start | bytes 16777216 | tf_op jit(solution)/shard_map/all_to_all | solution.py:178
  43.2 13.4 %gather_fusion.1 = bf16[512,64,128]{2,1,0:T(8,128)(2,1)} fusion(bf16[128,64,128]{2,1,0:T(8,128)(2,1)S(1)} %copy-done.2, s32[1024]{0:T(1024)S(1)} %pad_clamp_fusion), kind=kCustom, calls=%fused_computation.1 | custom fusion | bytes 16779264 | tf_op jit(solution)/shard_map/jit(_take)/gather | solution.py:177
  56.6 89.0 %all-to-all-done = bf16[128,4,64,128]{3,2,1,0:T(8,128)(2,1)} async-done(((bf16[128,4,64,128]{3,2,1,0:T(8,128)(2,1)}), bf16[128,4,64,128]{3,2,1,0:T(8,128)(2,1)}, u32[]{:S(2)}, u32[]{:S(2)}) %all-to-all-start) | async-done | bytes 8388640 | tf_op jit(solution)/shard_map/all_to_all | solution.py:178
  145.6 15.4 %all-to-all-start.1 = ((bf16[128,4,64,128]{3,2,1,0:T(8,128)(2,1)}), bf16[128,4,64,128]{3,2,1,0:T(8,128)(2,1)}, u32[]{:S(2)}, u32[]{:S(2)}) async-start(bf16[128,4,64,128]{3,2,1,0:T(8,128)(2,1)} %bitcast.99), calls=%async_computation.1 | async-start | bytes 16777216 | tf_op jit(solution)/shard_map/all_to_all | solution.py:179
  162.9 12.2 %shard_map.147 = bf16[4,1024,128]{2,1,0:T(8,128)(2,1)} custom-call(s32[4,6]{1,0:T(4,128)} %src_ref.5, s32[4]{0:T(128)} %cnt_ref.5, s32[32]{0:T(128)} %reshape.101.live_ref, bf16[4,1024,128]{2,1,0:T(8,128)(2,1)} %own_ref.1, bf16[8,16,4,64,128]{4,3,2,1,0:T(8,128)(2,1)} %bitcast.4.pulled_ref, bf16[4,6,128,128]{3,2,1,0:T(8,128)(2,1)} %tile_ref.5), custom_call_target="tpu_custom_call" | custom-call | flops 805306368 | bytes 14417920 | tf_op jit(solution)/shard_map/pallas_call | solution.py:77
  175.2 2.1 constant_dynamic-slice_fusion.2
  178.1 3.6 collective-permute-start
  181.7 72.6 %all-gather.3.cloned.1.call-done = bf16[1024,2176]{1,0:T(8,128)(2,1)} async-done(((bf16[64,2176]{1,0:T(8,128)(2,1)}), bf16[1024,2176]{1,0:T(8,128)(2,1)}) %all-gather.3.cloned.1.call-update) | async-done | bytes 4456464 | tf_op jit(solution)/shard_map/all_gather | solution.py:160
  254.3 4.1 %fusion.17.back_ref = bf16[4,1024,128]{2,1,0:T(8,128)(2,1)} fusion(bf16[4,1024,128]{2,1,0:T(8,128)(2,1)} %param.23, bf16[1024,2176]{1,0:T(8,128)(2,1)} %all-gather.3.cloned.1.call-done), kind=kOutput, calls=%fused_computation.29 | convolution fusion | flops 1074266112 | bytes 4194304 | tf_op jit(solution)/shard_map/ab,vbn->van/dot_general | solution.py:187
  258.4 9.1 %shard_map.148 = f32[4,1024,128]{2,1,0:T(8,128)} custom-call(s32[4,6]{1,0:T(4,128)} %src_ref.5, s32[4]{0:T(128)} %cnt_ref.5, bf16[4,1024,128]{2,1,0:T(8,128)(2,1)} %fusion.17.back_ref, bf16[4,6,128,128]{3,2,1,0:T(8,128)(2,1)} %tile_ref.5), custom_call_target="tpu_custom_call" | custom-call | flops 805306368 | bytes 3932160 | tf_op jit(solution)/shard_map/pallas_call | solution.py:122
  268.6 4.5 %fusion.15 = (bf16[4,1024,128]{2,1,0:T(8,128)(2,1)}, f32[4,128,1024]{1,2,0:T(8,128)S(1)}) fusion(f32[1024]{0:T(1024)S(1)} %convert_reduce_fusion.1, bf16[4,1024,128]{2,1,0:T(8,128)(2,1)S(1)} %copy-done.4, bf16[1024,2176]{1,0:T(8,128)(2,1)} %all-gather.3.cloned.1.call-done), kind=kOutput, calls=%fused_computation.27 | convolution fusion | flops 1078984704 | bytes 6295552 | tf_op jit(solution)/shard_map/fh,vfn->vhn/dot_general | solution.py:200
  273.1 3.3 fusion.29
  276.4 4.0 %collective-permute-start.1 = (bf16[4,1024,128]{2,1,0:T(8,128)(2,1)}, bf16[4,1024,128]{2,1,0:T(8,128)(2,1)}, u32[]{:S(2)}, u32[]{:S(2)}) collective-permute-start(bf16[4,1024,128]{2,1,0:T(8,128)(2,1)} %get-tuple-element.9), channel_id=1, source_target_pairs={{0,16},{16,0},{32,48},{48,32},{64,80},{80,64},{96,112},{112,96},{1... | collective-permute-start | bytes 3145736 | tf_op jit(solution)/shard_map/ppermute | solution.py:208
  280.4 12.3 %shard_map.149 = bf16[4,1024,128]{2,1,0:T(8,128)(2,1)} custom-call(s32[4,6]{1,0:T(4,128)} %src_ref.5, s32[4]{0:T(128)} %cnt_ref.5, s32[32]{0:T(128)} %reshape.101.live_ref, bf16[4,1024,128]{2,1,0:T(8,128)(2,1)} %get-tuple-element.16.own_ref, bf16[8,16,4,64,128]{4,3,2,1,0:T(8,128)(2,1)} %bitcast.21.pulled_ref, bf16[4,6,128,128]{3,2,1,0:T(8,128)(2,1)} %tile_ref.5), custom_call_target="tpu_custom_call" | custom-call | flops 805306368 | bytes 14417920 | tf_op jit(solution)/shard_map/pallas_call | solution.py:77
  294.9 3.6 collective-permute-start.2
  298.6 2.0 fusion.22
  300.6 2.0 fusion.19
  302.6 2.1 fusion.11
  307.8 3.1 fusion.12
  314.5 46.2 %all_to_all.15 = bf16[128,8,1152]{2,1,0:T(8,128)(2,1)S(1)} all-to-all(bf16[128,8,1152]{2,1,0:T(8,128)(2,1)S(1)} %copy.57), channel_id=1, replica_groups=mesh['dom'=8,'fsdp'=16] {'dom','fsdp'}, dimensions={0} | all-to-all | bytes 4718592 | tf_op jit(solution)/shard_map/all_to_all | solution.py:234
  363.7 4.7 %collective-permute-done.5 = f32[2,2,8,1152]{3,1,2,0:T(2,128)S(1)} collective-permute-done((f32[2,2,8,1152]{3,1,2,0:T(2,128)S(1)}, f32[2,2,8,1152]{3,1,2,0:T(2,128)S(1)}, u32[]{:S(2)}, u32[]{:S(2)}) %collective-permute-start.5) | collective-permute-done | bytes 147488 | tf_op jit(solution)/shard_map/ppermute | solution.py:239
  369.9 7.6 %collective-permute-done.6 = f32[4,2,8,1152]{3,1,2,0:T(2,128)S(1)} collective-permute-done((f32[4,2,8,1152]{3,1,2,0:T(2,128)S(1)}, f32[4,2,8,1152]{3,1,2,0:T(2,128)S(1)}, u32[]{:S(2)}, u32[]{:S(2)}) %collective-permute-start.6) | collective-permute-done | bytes 294944 | tf_op jit(solution)/shard_map/ppermute | solution.py:239
  (62 shorter events, 21.9 us)
Async XLA Ops:
  7.2 13.3 %copy-start = (bf16[128,64,128]{2,1,0:T(8,128)(2,1)S(1)}, bf16[128,64,128]{2,1,0:T(8,128)(2,1)}, u32[]{:S(2)}) copy-start(bf16[128,64,128]{2,1,0:T(8,128)(2,1)} %param.13) | copy-start | bytes 6291460
  33.9 8.4 %copy-start.8 = (bf16[64]{0:T(256)(128)(2,1)S(1)}, bf16[64]{0:T(256)(128)(2,1)}, u32[]{:S(2)}) copy-start(bf16[64]{0:T(256)(128)(2,1)} %param.22) | copy-start | bytes 388
  33.9 8.5 %copy-start.6 = (bf16[64,1024]{1,0:T(8,128)(2,1)S(1)}, bf16[64,1024]{1,0:T(8,128)(2,1)}, u32[]{:S(2)}) copy-start(bf16[64,1024]{1,0:T(8,128)(2,1)} %param.21) | copy-start | bytes 393220
  33.9 8.5 %copy-start.7 = (bf16[64,1024]{1,0:T(8,128)(2,1)S(1)}, bf16[64,1024]{1,0:T(8,128)(2,1)}, u32[]{:S(2)}) copy-start(bf16[64,1024]{1,0:T(8,128)(2,1)} %param.20) | copy-start | bytes 393220
  33.9 9.2 %copy-start.2 = (bf16[128,64,128]{2,1,0:T(8,128)(2,1)S(1)}, bf16[128,64,128]{2,1,0:T(8,128)(2,1)}, u32[]{:S(2)}) copy-start(bf16[128,64,128]{2,1,0:T(8,128)(2,1)} %param.14) | copy-start | bytes 6291460
  33.9 111.6 %all-to-all-start = ((bf16[128,4,64,128]{3,2,1,0:T(8,128)(2,1)}), bf16[128,4,64,128]{3,2,1,0:T(8,128)(2,1)}, u32[]{:S(2)}, u32[]{:S(2)}) async-start(bf16[128,4,64,128]{3,2,1,0:T(8,128)(2,1)} %bitcast.100), calls=%async_computation | async-start | bytes 16777216 | tf_op jit(solution)/shard_map/all_to_all | solution.py:178
  42.2 212.1 %all-gather.3.cloned.1.call-start = ((), (), s32[]{:S(2)}) async-start(), calls=%async_computation.3 | async-start | bytes 4734976 | tf_op jit(solution)/shard_map/all_gather | solution.py:160
  145.6 134.9 %all-to-all-start.1 = ((bf16[128,4,64,128]{3,2,1,0:T(8,128)(2,1)}), bf16[128,4,64,128]{3,2,1,0:T(8,128)(2,1)}, u32[]{:S(2)}, u32[]{:S(2)}) async-start(bf16[128,4,64,128]{3,2,1,0:T(8,128)(2,1)} %bitcast.99), calls=%async_computation.1 | async-start | bytes 16777216 | tf_op jit(solution)/shard_map/all_to_all | solution.py:179
  160.9 141.6 %collective-permute-start.3 = (bf16[4,1024,128]{2,1,0:T(8,128)(2,1)}, bf16[4,1024,128]{2,1,0:T(8,128)(2,1)}, u32[]{:S(2)}, u32[]{:S(2)}) collective-permute-start(bf16[4,1024,128]{2,1,0:T(8,128)(2,1)} %param.23), channel_id=1, source_target_pairs={{0,16},{16,0},{32,48},{48,32},{64,80},{80,64},{96,112},{112,96},{1... | collective-permute-start | bytes 3145736 | tf_op jit(solution)/shard_map/ppermute | solution.py:185
  178.1 129.6 %collective-permute-start = (bf16[4,16,32,128]{3,2,0,1:T(8,128)(2,1)}, bf16[4,16,32,128]{3,2,0,1:T(8,128)(2,1)}, u32[]{:S(2)}, u32[]{:S(2)}) collective-permute-start(bf16[4,16,32,128]{3,2,0,1:T(8,128)(2,1)} %bitcast.97), channel_id=1, source_target_pairs={{0,16},{16,0},{32,48},{48,32},{64,80},{80,64},{96,112},{112,96},{1... | collective-permute-start | bytes 1572872 | tf_op jit(solution)/shard_map/ppermute | solution.py:208
  258.4 10.2 %copy-start.4 = (bf16[4,1024,128]{2,1,0:T(8,128)(2,1)S(1)}, bf16[4,1024,128]{2,1,0:T(8,128)(2,1)}, u32[]{:S(2)}) copy-start(bf16[4,1024,128]{2,1,0:T(8,128)(2,1)} %shard_map.147) | copy-start | bytes 3145732
  268.6 4.5 %copy-start.3 = (f32[4,1024,128]{2,1,0:T(8,128)S(1)}, f32[4,1024,128]{2,1,0:T(8,128)}, u32[]{:S(2)}) copy-start(f32[4,1024,128]{2,1,0:T(8,128)} %shard_map.148) | copy-start | bytes 6291460
  276.4 31.3 %collective-permute-start.1 = (bf16[4,1024,128]{2,1,0:T(8,128)(2,1)}, bf16[4,1024,128]{2,1,0:T(8,128)(2,1)}, u32[]{:S(2)}, u32[]{:S(2)}) collective-permute-start(bf16[4,1024,128]{2,1,0:T(8,128)(2,1)} %get-tuple-element.9), channel_id=1, source_target_pairs={{0,16},{16,0},{32,48},{48,32},{64,80},{80,64},{96,112},{112,96},{1... | collective-permute-start | bytes 3145736 | tf_op jit(solution)/shard_map/ppermute | solution.py:208
  292.7 5.9 %copy-start.5 = (bf16[4,16,1,32,128]{4,3,2,1,0:T(8,128)(2,1)S(1)}, bf16[4,16,1,32,128]{4,3,2,1,0:T(8,128)(2,1)}, u32[]{:S(2)}) copy-start(bf16[4,16,1,32,128]{4,3,2,1,0:T(8,128)(2,1)} %get-tuple-element.11) | copy-start | bytes 1572868
  294.9 7.6 %collective-permute-start.2 = (bf16[4,16,32,128]{3,2,0,1:T(8,128)(2,1)}, bf16[4,16,32,128]{3,2,0,1:T(8,128)(2,1)}, u32[]{:S(2)}, u32[]{:S(2)}) collective-permute-start(bf16[4,16,32,128]{3,2,0,1:T(8,128)(2,1)} %bitcast.96), channel_id=1, source_target_pairs={{0,16},{16,0},{32,48},{48,32},{64,80},{80,64},{96,112},{112,96},{1... | collective-permute-start | bytes 1572872 | tf_op jit(solution)/shard_map/ppermute | solution.py:217
  361.1 2.2 collective-permute-start.4
  363.3 5.2 %collective-permute-start.5 = (f32[2,2,8,1152]{3,1,2,0:T(2,128)S(1)}, f32[2,2,8,1152]{3,1,2,0:T(2,128)S(1)}, u32[]{:S(2)}, u32[]{:S(2)}) collective-permute-start(f32[2,2,8,1152]{3,1,2,0:T(2,128)S(1)} %maximum_select_fusion.2), channel_id=1, source_target_pairs={{0,32},{16,48},{32,0},{48,16},{64,96},{80,112},{96,64},{112,80},{1... | collective-permute-start | bytes 442376 | tf_op jit(solution)/shard_map/ppermute | solution.py:239
  368.6 8.9 %collective-permute-start.6 = (f32[4,2,8,1152]{3,1,2,0:T(2,128)S(1)}, f32[4,2,8,1152]{3,1,2,0:T(2,128)S(1)}, u32[]{:S(2)}, u32[]{:S(2)}) collective-permute-start(f32[4,2,8,1152]{3,1,2,0:T(2,128)S(1)} %maximum_select_fusion.1), channel_id=1, source_target_pairs={{0,64},{16,80},{32,96},{48,112},{64,0},{80,16},{96,32},{112,48},{1... | collective-permute-start | bytes 884744 | tf_op jit(solution)/shard_map/ppermute | solution.py:239
  369.9 10.4 %copy-start.1 = (bf16[128,64,128]{2,1,0:T(8,128)(2,1)S(1)}, bf16[128,64,128]{2,1,0:T(8,128)(2,1)}, u32[]{:S(2)}) copy-start(bf16[128,64,128]{2,1,0:T(8,128)(2,1)} %param.13) | copy-start | bytes 6291460
Sparse Core Ops, SparseCore 0:
  45.2 209.0 all-gather.2

commit v14 on v9

--- a/solution.py
+++ b/solution.py
@@ -48,12 +48,21 @@
     def eff(v, t, src_ref, cnt_ref):
         return jnp.minimum(t, cnt_ref[v] - 1)
 
+    def latest(v, t, src_ref, cnt_ref, own_kind):
+        te = eff(v, t, src_ref, cnt_ref)
+        pick = jnp.int32(0)
+        for slot in range(tiles):
+            s = src_ref[v, slot]
+            kind_ok = (s < nb) if own_kind else (s >= nb)
+            pick = jnp.where((slot <= te) & kind_ok, s, pick)
+        return pick
+
     def own_map(v, t, src_ref, cnt_ref, live_ref):
-        s = src_ref[v, eff(v, t, src_ref, cnt_ref)]
+        s = latest(v, t, src_ref, cnt_ref, True)
         return (jnp.clip(s, 0, nb - 1), 0, 0)
 
     def pulled_map(v, t, src_ref, cnt_ref, live_ref):
-        s = jnp.clip(src_ref[v, eff(v, t, src_ref, cnt_ref)] - nb, 0, cap * dom - 1)
+        s = jnp.clip(latest(v, t, src_ref, cnt_ref, False) - nb, 0, cap * dom - 1)
         return (s % dom, 0, s // dom, 0, 0)
 
     def tile_map(v, t, src_ref, cnt_ref, live_ref):

time: 374 us -> 376 us (level)
  blocking collectives: 59.1 us -> 64.3 us
    all_to_all x1, blocking collectives: 46.8 us -> 52 us  [on_device(): lax.all_to_all(packed_terms.astype(jnp.bfloat16), 'fsdp', split_axis=0, c...]
    ppermute x2, starting transfers between devices: 5.98 us -> 0.83 us  [on_device(): lax.ppermute(shard, 'dom', [(d, d ^ flip) for d in range(dom_size)])]
    ppermute x2, starting transfers between devices: 0.09 us -> 5.19 us  [on_device(): first_got, back_got = lax.ppermute((first_theirs, back_pre), 'dom', pair)]
where the time goes in v14:
time: 376 us
  waiting for transfers between devices  173 us (46%)
  blocking collectives  64.3 us (17%)
  Pallas kernels  36.8 us (10%)
  local copies, waits for them, and re-layouts  33.1 us (9%)
  starting transfers between devices  33.1 us (9%)
  between operations  14.3 us (4%)
  matrix products  14.1 us (4%)
  other arithmetic  6.87 us (2%)
    all_to_all x1, waiting for transfers between devices, on_device(): lax.all_to_all(sent_first, ('dom', 'fsdp'), split_axis=0, concat_axis=0,...  89 us
    all_gather x1, waiting for transfers between devices, on_device(): lax.all_gather(jnp.concatenate([w_first, w_second, bias_cols], axis=1), '...  60.8 us
    all_to_all x1, blocking collectives, on_device(): lax.all_to_all(packed_terms.astype(jnp.bfloat16), 'fsdp', split_axis=0, c...  52 us
    pallas_call x2, Pallas kernels, aggregate(): pl.pallas_call(functools.partial(_agg_kernel, nb, tiles - 1), grid_spec=g...  27 us
    all_to_all x1, starting transfers between devices, on_device(): lax.all_to_all(sent_second, ('dom', 'fsdp'), split_axis=0, concat_axis=0,...  14 us
    ppermute x2, waiting for transfers between devices, on_device(): lax.ppermute(shard, 'dom', [(d, d ^ flip) for d in range(dom_size)])  13.9 us
    gather x1, local copies, waits for them, and re-layouts, on_device(): jnp.take(history_first, chosen.reshape(-1), axis=0, mode='clip')  13.5 us
    gather x1, local copies, waits for them, and re-layouts, on_device(): jnp.take(history_second, chosen.reshape(-1), axis=0, mode='clip')  13.4 us
  transfers between devices with their start and end apart: 10, of which 7 were waited for; matrix products, arithmetic and copies ran while one was open for 9% of the time, Pallas kernels for 10%

profile of v14, /device:TPU:1, one launch (start us, length us, event | category | flops | bytes accessed | tf_op | source)
XLA Modules:
  0.0 375.6 jit_solution(17615789826612611882)
XLA Ops:
  7.2 12.4 %all-gather = s32[8,1,128]{2,1,0:T(1,128)S(1)} all-gather(s32[1,1,128]{2,1,0:T(1,128)} %bitcast.93), channel_id=1, replica_groups=mesh['dom'=8,'fsdp'=16] {'dom'}, dimensions={0}, use_global_device_ids=true | all-gather | bytes 4608 | tf_op jit(solution)/shard_map/all_gather | solution.py:176
  20.5 13.5 %gather_fusion = bf16[512,64,128]{2,1,0:T(8,128)(2,1)} fusion(bf16[128,64,128]{2,1,0:T(8,128)(2,1)S(1)} %copy-done, s32[1024]{0:T(1024)S(1)} %pad_clamp_fusion), kind=kCustom, calls=%fused_computation | custom fusion | bytes 16779264 | tf_op jit(solution)/shard_map/jit(_take)/gather | solution.py:185
  33.9 8.3 %all-to-all-start = ((bf16[128,4,64,128]{3,2,1,0:T(8,128)(2,1)}), bf16[128,4,64,128]{3,2,1,0:T(8,128)(2,1)}, u32[]{:S(2)}, u32[]{:S(2)}) async-start(bf16[128,4,64,128]{3,2,1,0:T(8,128)(2,1)} %bitcast.88), calls=%async_computation | async-start | bytes 16777216 | tf_op jit(solution)/shard_map/all_to_all | solution.py:187
  43.2 13.4 %gather_fusion.1 = bf16[512,64,128]{2,1,0:T(8,128)(2,1)} fusion(bf16[128,64,128]{2,1,0:T(8,128)(2,1)S(1)} %copy-done.2, s32[1024]{0:T(1024)S(1)} %pad_clamp_fusion), kind=kCustom, calls=%fused_computation.1 | custom fusion | bytes 16779264 | tf_op jit(solution)/shard_map/jit(_take)/gather | solution.py:186
  56.6 89.0 %all-to-all-done = bf16[128,4,64,128]{3,2,1,0:T(8,128)(2,1)} async-done(((bf16[128,4,64,128]{3,2,1,0:T(8,128)(2,1)}), bf16[128,4,64,128]{3,2,1,0:T(8,128)(2,1)}, u32[]{:S(2)}, u32[]{:S(2)}) %all-to-all-start) | async-done | bytes 8388640 | tf_op jit(solution)/shard_map/all_to_all | solution.py:187
  145.6 14.0 %all-to-all-start.1 = ((bf16[128,4,64,128]{3,2,1,0:T(8,128)(2,1)}), bf16[128,4,64,128]{3,2,1,0:T(8,128)(2,1)}, u32[]{:S(2)}, u32[]{:S(2)}) async-start(bf16[128,4,64,128]{3,2,1,0:T(8,128)(2,1)} %bitcast.87), calls=%async_computation.1 | async-start | bytes 16777216 | tf_op jit(solution)/shard_map/all_to_all | solution.py:188
  161.7 13.5 %shard_map.147 = bf16[4,1024,128]{2,1,0:T(8,128)(2,1)} custom-call(s32[4,6]{1,0:T(4,128)} %src_ref.5, s32[4]{0:T(128)} %cnt_ref.5, s32[32]{0:T(128)} %reshape.94.live_ref, bf16[4,1024,128]{2,1,0:T(8,128)(2,1)} %own_ref.1, bf16[8,16,4,64,128]{4,3,2,1,0:T(8,128)(2,1)} %bitcast.4.pulled_ref, bf16[4,6,128,128]{3,2,1,0:T(8,128)(2,1)} %tile_ref.5), custom_call_target="tpu_custom_call" | custom-call | flops 805306368 | bytes 14417920 | tf_op jit(solution)/shard_map/pallas_call | solution.py:86
  175.2 1.3 constant_dynamic-slice_fusion.2
  177.3 2.6 collective-permute-start
  179.9 60.8 %all-gather.3.cloned.1.call-done = bf16[1024,2176]{1,0:T(8,128)(2,1)} async-done(((bf16[64,2176]{1,0:T(8,128)(2,1)}), bf16[1024,2176]{1,0:T(8,128)(2,1)}) %all-gather.3.cloned.1.call-update) | async-done | bytes 4456464 | tf_op jit(solution)/shard_map/all_gather | solution.py:169
  240.6 3.8 %fusion.17.back_ref = bf16[4,1024,128]{2,1,0:T(8,128)(2,1)} fusion(bf16[4,1024,128]{2,1,0:T(8,128)(2,1)S(1)} %copy-done.5, bf16[1024,2176]{1,0:T(8,128)(2,1)} %all-gather.3.cloned.1.call-done), kind=kOutput, calls=%fused_computation.29 | convolution fusion | flops 1074266112 | bytes 4194304 | tf_op jit(solution)/shard_map/ab,vbn->van/dot_general | solution.py:196
  244.5 9.9 %shard_map.148 = f32[4,1024,128]{2,1,0:T(8,128)} custom-call(s32[4,6]{1,0:T(4,128)} %src_ref.5, s32[4]{0:T(128)} %cnt_ref.5, bf16[4,1024,128]{2,1,0:T(8,128)(2,1)} %fusion.17.back_ref, bf16[4,6,128,128]{3,2,1,0:T(8,128)(2,1)} %tile_ref.5), custom_call_target="tpu_custom_call" | custom-call | flops 805306368 | bytes 3932160 | tf_op jit(solution)/shard_map/pallas_call | solution.py:131
  255.4 4.5 %fusion.15 = (bf16[4,1024,128]{2,1,0:T(8,128)(2,1)}, f32[4,128,1024]{1,2,0:T(8,128)S(1)}) fusion(f32[1024]{0:T(1024)S(1)} %convert_reduce_fusion.1, bf16[4,1024,128]{2,1,0:T(8,128)(2,1)S(1)} %copy-done.4, bf16[1024,2176]{1,0:T(8,128)(2,1)} %all-gather.3.cloned.1.call-done), kind=kOutput, calls=%fused_computation.27 | convolution fusion | flops 1078984704 | bytes 6295552 | tf_op jit(solution)/shard_map/fh,vfn->vhn/dot_general | solution.py:209
  259.9 2.4 fusion.30
  262.3 2.6 collective-permute-start.1
  265.0 7.4 %all-to-all-done.1 = bf16[128,4,64,128]{3,2,1,0:T(8,128)(2,1)} async-done(((bf16[128,4,64,128]{3,2,1,0:T(8,128)(2,1)}), bf16[128,4,64,128]{3,2,1,0:T(8,128)(2,1)}, u32[]{:S(2)}, u32[]{:S(2)}) %all-to-all-start.1) | async-done | bytes 8388640 | tf_op jit(solution)/shard_map/all_to_all | solution.py:188
  272.4 13.5 %shard_map.149 = bf16[4,1024,128]{2,1,0:T(8,128)(2,1)} custom-call(s32[4,6]{1,0:T(4,128)} %src_ref.5, s32[4]{0:T(128)} %cnt_ref.5, s32[32]{0:T(128)} %reshape.94.live_ref, bf16[4,1024,128]{2,1,0:T(8,128)(2,1)} %get-tuple-element.32.own_ref, bf16[8,16,4,64,128]{4,3,2,1,0:T(8,128)(2,1)} %bitcast.19.pulled_ref, bf16[4,6,128,128]{3,2,1,0:T(8,128)(2,1)} %tile_ref.5), custom_call_target="tpu_custom_call" | custom-call | flops 805306368 | bytes 14417920 | tf_op jit(solution)/shard_map/pallas_call | solution.py:86
  285.9 1.3 constant_dynamic-slice_fusion
  290.3 2.1 fusion.11
  292.5 2.1 fusion.12
  294.9 52.0 %all_to_all.15 = bf16[16,64,1152]{2,1,0:T(8,128)(2,1)S(1)} all-to-all(bf16[16,64,1152]{2,1,0:T(8,128)(2,1)S(1)} %fusion.1), channel_id=1, replica_groups=mesh['dom'=8,'fsdp'=16] {'fsdp'}, dimensions={0} | all-to-all | bytes 4718592 | tf_op jit(solution)/shard_map/all_to_all | solution.py:234
  347.3 7.0 %collective-permute-done.4 = f32[64,1152]{1,0:T(8,128)S(1)} collective-permute-done((f32[64,1152]{1,0:T(8,128)S(1)}, f32[64,1152]{1,0:T(8,128)S(1)}, u32[]{:S(2)}, u32[]{:S(2)}) %collective-permute-start.4) | collective-permute-done | bytes 294944 | tf_op jit(solution)/shard_map/ppermute | solution.py:237
  355.1 6.9 %collective-permute-done.5 = f32[64,1152]{1,0:T(8,128)S(1)} collective-permute-done((f32[64,1152]{1,0:T(8,128)S(1)}, f32[64,1152]{1,0:T(8,128)S(1)}, u32[]{:S(2)}, u32[]{:S(2)}) %collective-permute-start.5) | collective-permute-done | bytes 294944 | tf_op jit(solution)/shard_map/ppermute | solution.py:237
  362.0 3.4 collective-permute-start.6
  (52 shorter events, 13.6 us)
Async XLA Ops:
  7.2 13.3 %copy-start = (bf16[128,64,128]{2,1,0:T(8,128)(2,1)S(1)}, bf16[128,64,128]{2,1,0:T(8,128)(2,1)}, u32[]{:S(2)}) copy-start(bf16[128,64,128]{2,1,0:T(8,128)(2,1)} %param.15) | copy-start | bytes 6291460
  33.9 8.4 %copy-start.8 = (bf16[64]{0:T(256)(128)(2,1)S(1)}, bf16[64]{0:T(256)(128)(2,1)}, u32[]{:S(2)}) copy-start(bf16[64]{0:T(256)(128)(2,1)} %param.24) | copy-start | bytes 388
  33.9 8.5 %copy-start.6 = (bf16[64,1024]{1,0:T(8,128)(2,1)S(1)}, bf16[64,1024]{1,0:T(8,128)(2,1)}, u32[]{:S(2)}) copy-start(bf16[64,1024]{1,0:T(8,128)(2,1)} %param.23) | copy-start | bytes 393220
  33.9 8.5 %copy-start.7 = (bf16[64,1024]{1,0:T(8,128)(2,1)S(1)}, bf16[64,1024]{1,0:T(8,128)(2,1)}, u32[]{:S(2)}) copy-start(bf16[64,1024]{1,0:T(8,128)(2,1)} %param.22) | copy-start | bytes 393220
  33.9 9.2 %copy-start.2 = (bf16[128,64,128]{2,1,0:T(8,128)(2,1)S(1)}, bf16[128,64,128]{2,1,0:T(8,128)(2,1)}, u32[]{:S(2)}) copy-start(bf16[128,64,128]{2,1,0:T(8,128)(2,1)} %param.16) | copy-start | bytes 6291460
  33.9 111.7 %all-to-all-start = ((bf16[128,4,64,128]{3,2,1,0:T(8,128)(2,1)}), bf16[128,4,64,128]{3,2,1,0:T(8,128)(2,1)}, u32[]{:S(2)}, u32[]{:S(2)}) async-start(bf16[128,4,64,128]{3,2,1,0:T(8,128)(2,1)} %bitcast.88), calls=%async_computation | async-start | bytes 16777216 | tf_op jit(solution)/shard_map/all_to_all | solution.py:187
  42.3 198.4 %all-gather.3.cloned.1.call-start = ((), (), s32[]{:S(2)}) async-start(), calls=%async_computation.3 | async-start | bytes 4734976 | tf_op jit(solution)/shard_map/all_gather | solution.py:169
  145.6 14.0 %copy-start.5 = (bf16[4,1024,128]{2,1,0:T(8,128)(2,1)S(1)}, bf16[4,1024,128]{2,1,0:T(8,128)(2,1)}, u32[]{:S(2)}) copy-start(bf16[4,1024,128]{2,1,0:T(8,128)(2,1)} %param.25) | copy-start | bytes 3145732
  145.6 126.8 %all-to-all-start.1 = ((bf16[128,4,64,128]{3,2,1,0:T(8,128)(2,1)}), bf16[128,4,64,128]{3,2,1,0:T(8,128)(2,1)}, u32[]{:S(2)}, u32[]{:S(2)}) async-start(bf16[128,4,64,128]{3,2,1,0:T(8,128)(2,1)} %bitcast.87), calls=%async_computation.1 | async-start | bytes 16777216 | tf_op jit(solution)/shard_map/all_to_all | solution.py:188
  159.6 130.1 %collective-permute-start.3 = (bf16[4,1024,128]{2,1,0:T(8,128)(2,1)S(1)}, bf16[4,1024,128]{2,1,0:T(8,128)(2,1)}, u32[]{:S(2)}, u32[]{:S(2)}) collective-permute-start(bf16[4,1024,128]{2,1,0:T(8,128)(2,1)S(1)} %copy-done.5), channel_id=1, source_target_pairs={{0,16},{16,0},{32,48},{48,32},{64,80},{80,64},{96,112},{112,96},{1... | collective-permute-start | bytes 3145736 | tf_op jit(solution)/shard_map/ppermute | solution.py:194
  177.3 115.1 %collective-permute-start = (bf16[4,16,32,128]{3,2,0,1:T(8,128)(2,1)}, bf16[4,16,32,128]{3,2,0,1:T(8,128)(2,1)}, u32[]{:S(2)}, u32[]{:S(2)}) collective-permute-start(bf16[4,16,32,128]{3,2,0,1:T(8,128)(2,1)} %bitcast.86), channel_id=1, source_target_pairs={{0,16},{16,0},{32,48},{48,32},{64,80},{80,64},{96,112},{112,96},{1... | collective-permute-start | bytes 1572872 | tf_op jit(solution)/shard_map/ppermute | solution.py:217
  244.5 11.0 %copy-start.4 = (bf16[4,1024,128]{2,1,0:T(8,128)(2,1)S(1)}, bf16[4,1024,128]{2,1,0:T(8,128)(2,1)}, u32[]{:S(2)}) copy-start(bf16[4,1024,128]{2,1,0:T(8,128)(2,1)} %shard_map.147) | copy-start | bytes 3145732
  255.4 4.5 %copy-start.3 = (f32[4,1024,128]{2,1,0:T(8,128)S(1)}, f32[4,1024,128]{2,1,0:T(8,128)}, u32[]{:S(2)}) copy-start(f32[4,1024,128]{2,1,0:T(8,128)} %shard_map.148) | copy-start | bytes 6291460
  262.3 30.1 %collective-permute-start.1 = (bf16[4,1024,128]{2,1,0:T(8,128)(2,1)S(1)}, bf16[4,1024,128]{2,1,0:T(8,128)(2,1)}, u32[]{:S(2)}, u32[]{:S(2)}) collective-permute-start(bf16[4,1024,128]{2,1,0:T(8,128)(2,1)S(1)} %get-tuple-element.21), channel_id=1, source_target_pairs={{0,16},{16,0},{32,48},{48,32},{64,80},{80,64},{96,112},{112,96},{1... | collective-permute-start | bytes 3145736 | tf_op jit(solution)/shard_map/ppermute | solution.py:217
  288.0 2.3 collective-permute-start.2
  347.2 7.1 %collective-permute-start.4 = (f32[64,1152]{1,0:T(8,128)S(1)}, f32[64,1152]{1,0:T(8,128)S(1)}, u32[]{:S(2)}, u32[]{:S(2)}) collective-permute-start(f32[64,1152]{1,0:T(8,128)S(1)} %convert_reduce_fusion), channel_id=1, source_target_pairs={{0,32},{16,48},{32,0},{48,16},{64,96},{80,112},{96,64},{112,80},{1... | collective-permute-start | bytes 884744 | tf_op jit(solution)/shard_map/ppermute | solution.py:237
  354.3 14.4 %copy-start.1 = (bf16[128,64,128]{2,1,0:T(8,128)(2,1)S(1)}, bf16[128,64,128]{2,1,0:T(8,128)(2,1)}, u32[]{:S(2)}) copy-start(bf16[128,64,128]{2,1,0:T(8,128)(2,1)} %param.15) | copy-start | bytes 6291460
  354.3 7.7 %collective-permute-start.5 = (f32[64,1152]{1,0:T(8,128)S(1)}, f32[64,1152]{1,0:T(8,128)S(1)}, u32[]{:S(2)}, u32[]{:S(2)}) collective-permute-start(f32[64,1152]{1,0:T(8,128)S(1)} %add.72), channel_id=1, source_target_pairs={{0,64},{16,80},{32,96},{48,112},{64,0},{80,16},{96,32},{112,48},{1... | collective-permute-start | bytes 884744 | tf_op jit(solution)/shard_map/ppermute | solution.py:237
  362.0 4.6 %collective-permute-start.6 = (f32[64,1152]{1,0:T(8,128)S(1)}, f32[64,1152]{1,0:T(8,128)S(1)}, u32[]{:S(2)}, u32[]{:S(2)}) collective-permute-start(f32[64,1152]{1,0:T(8,128)S(1)} %add.73), channel_id=1, source_target_pairs={{0,16},{16,0},{32,48},{48,32},{64,80},{80,64},{96,112},{112,96},{1... | collective-permute-start | bytes 884744 | tf_op jit(solution)/shard_map/ppermute | solution.py:238
Sparse Core Ops, SparseCore 0:
  45.2 195.3 all-gather.2

commit v15 on v9

--- a/solution.py
+++ b/solution.py
@@ -12,30 +12,32 @@
     return jax.nn.gelu(inputs, approximate=True)
 
 
-def _agg_kernel(own_count, last_tile, src_ref, cnt_ref, live_ref, own_ref, pulled_ref, tile_ref, out_ref, acc_ref):
+def _agg_kernel(own_count, last_step, src_ref, cnt_ref, live_ref, own_a, own_b, pulled_a, pulled_b, tile_ref, out_ref, acc_ref):
     v = pl.program_id(0)
-    t = pl.program_id(1)
-
-    @pl.when(t == 0)
+    k = pl.program_id(1)
+
+    @pl.when(k == 0)
     def _():
         acc_ref[...] = jnp.zeros_like(acc_ref)
 
-    src = src_ref[v, t]
-    tile_live = t < cnt_ref[v]
-    own_ok = tile_live & (src < own_count)
-    pull_ok = tile_live & (src >= own_count) & (live_ref[jnp.maximum(src - own_count, 0)] > 0)
-
-    @pl.when(own_ok)
-    def _():
-        acc_ref[...] += jnp.dot(own_ref[0], tile_ref[0, 0], preferred_element_type=jnp.float32)
-
-    @pl.when(pull_ok)
-    def _():
-        block = pulled_ref[0, :, 0]
-        block = block.reshape(block.shape[0] * block.shape[1], block.shape[2])
-        acc_ref[...] += jnp.dot(block, tile_ref[0, 0], preferred_element_type=jnp.float32)
-
-    @pl.when(t == last_tile)
+    for j, own_ref, pulled_ref in ((0, own_a, pulled_a), (1, own_b, pulled_b)):
+        t = 2 * k + j
+        src = src_ref[v, t]
+        tile_live = t < cnt_ref[v]
+        own_ok = tile_live & (src < own_count)
+        pull_ok = tile_live & (src >= own_count) & (live_ref[jnp.maximum(src - own_count, 0)] > 0)
+
+        @pl.when(own_ok)
+        def _():
+            acc_ref[...] += jnp.dot(own_ref[0], tile_ref[0, j], preferred_element_type=jnp.float32)
+
+        @pl.when(pull_ok)
+        def _():
+            block = pulled_ref[0, :, 0]
+            block = block.reshape(block.shape[0] * block.shape[1], block.shape[2])
+            acc_ref[...] += jnp.dot(block, tile_ref[0, j], preferred_element_type=jnp.float32)
+
+    @pl.when(k == last_step)
     def _():
         out_ref[0] = acc_ref[...].astype(out_ref.dtype)
 
@@ -44,45 +46,48 @@
     nb, feat, blk = own.shape
     dom, fsdp, cap = pulled.shape[0], pulled.shape[1], pulled.shape[2]
     tiles = tile_src.shape[1]
-
-    def eff(v, t, src_ref, cnt_ref):
+    steps = tiles // 2
+
+    def eff(v, t, cnt_ref):
         return jnp.minimum(t, cnt_ref[v] - 1)
 
-    def own_map(v, t, src_ref, cnt_ref, live_ref):
-        s = src_ref[v, eff(v, t, src_ref, cnt_ref)]
-        return (jnp.clip(s, 0, nb - 1), 0, 0)
-
-    def pulled_map(v, t, src_ref, cnt_ref, live_ref):
-        s = jnp.clip(src_ref[v, eff(v, t, src_ref, cnt_ref)] - nb, 0, cap * dom - 1)
-        return (s % dom, 0, s // dom, 0, 0)
-
-    def tile_map(v, t, src_ref, cnt_ref, live_ref):
-        return (v, eff(v, t, src_ref, cnt_ref), 0, 0)
-
-    def out_map(v, t, src_ref, cnt_ref, live_ref):
-        return (v, 0, 0)
+    def own_map(j):
+        def index(v, k, src_ref, cnt_ref, live_ref):
+            s = src_ref[v, eff(v, 2 * k + j, cnt_ref)]
+            return (jnp.clip(s, 0, nb - 1), 0, 0)
+
+        return index
+
+    def pulled_map(j):
+        def index(v, k, src_ref, cnt_ref, live_ref):
+            s = jnp.clip(src_ref[v, eff(v, 2 * k + j, cnt_ref)] - nb, 0, cap * dom - 1)
+            return (s % dom, 0, s // dom, 0, 0)
+
+        return index
 
     grid_spec = pltpu.PrefetchScalarGridSpec(
         num_scalar_prefetch=3,
-        grid=(nb, tiles),
+        grid=(nb, steps),
         in_specs=[
-            pl.BlockSpec((1, feat, blk), own_map),
-            pl.BlockSpec((1, fsdp, 1) + pulled.shape[3:], pulled_map),
-            pl.BlockSpec((1, 1, blk, blk), tile_map),
+            pl.BlockSpec((1, feat, blk), own_map(0)),
+            pl.BlockSpec((1, feat, blk), own_map(1)),
+            pl.BlockSpec((1, fsdp, 1) + pulled.shape[3:], pulled_map(0)),
+            pl.BlockSpec((1, fsdp, 1) + pulled.shape[3:], pulled_map(1)),
+            pl.BlockSpec((1, 2, blk, blk), lambda v, k, s, c, l: (v, k, 0, 0)),
         ],
-        out_specs=pl.BlockSpec((1, feat, blk), out_map),
+        out_specs=pl.BlockSpec((1, feat, blk), lambda v, k, s, c, l: (v, 0, 0)),
         scratch_shapes=[pltpu.VMEM((feat, blk), jnp.float32)],
     )
     flops = 2 * nb * tiles * feat * blk * blk
     return pl.pallas_call(
-        functools.partial(_agg_kernel, nb, tiles - 1),
+        functools.partial(_agg_kernel, nb, steps - 1),
         grid_spec=grid_spec,
         out_shape=jax.ShapeDtypeStruct(own.shape, jnp.bfloat16),
         compiler_params=pltpu.CompilerParams(dimension_semantics=("arbitrary", "arbitrary")),
         cost_estimate=pl.CostEstimate(
             flops=flops, transcendentals=0, bytes_accessed=nb * tiles * (2 * feat * blk * 2 + blk * blk * 2) + own.size * 2
         ),
-    )(tile_src, tile_count, slot_live, own, pulled, tile_values)
+    )(tile_src, tile_count, slot_live, own, own, pulled, pulled, tile_values)
 
 
 def _spread_kernel(own_count, src_ref, cnt_ref, back_ref, tile_ref, out_ref):

time: 374 us -> 370 us (0.989)
  Pallas kernels: 35.6 us -> 31.7 us
    pallas_call x2, Pallas kernels: 25.7 us -> 21.4 us  [aggregate(): pl.pallas_call(functools.partial(_agg_kernel, nb, steps - 1), grid_spec=g...]
  transfers between devices with their start and end apart: 10 -> 10, of which waited for: 7 -> 7; matrix products, arithmetic and copies ran while one was open for 9% -> 9% of each run, Pallas kernels for 10% -> 9%
where the time goes in v15:
time: 370 us; the launch traced here: 368 us
  waiting for transfers between devices  177 us (48%)
  blocking collectives  59.1 us (16%)
  local copies, waits for them, and re-layouts  33.1 us (9%)
  Pallas kernels  31.7 us (9%)
  starting transfers between devices  31.6 us (9%)
  between operations  14.3 us (4%)
  matrix products  14.1 us (4%)
  other arithmetic  6.87 us (2%)
    all_to_all x1, waiting for transfers between devices, on_device(): lax.all_to_all(sent_first, ('dom', 'fsdp'), split_axis=0, concat_axis=0,...  89 us
    all_gather x1, waiting for transfers between devices, on_device(): lax.all_gather(jnp.concatenate([w_first, w_second, bias_cols], axis=1), '...  65.8 us
    all_to_all x1, blocking collectives, on_device(): lax.all_to_all(packed_terms.astype(jnp.bfloat16), 'fsdp', split_axis=0, c...  46.7 us
    pallas_call x2, Pallas kernels, aggregate(): pl.pallas_call(functools.partial(_agg_kernel, nb, steps - 1), grid_spec=g...  21.4 us
    all_to_all x1, starting transfers between devices, on_device(): lax.all_to_all(sent_second, ('dom', 'fsdp'), split_axis=0, concat_axis=0,...  14 us
    gather x1, local copies, waits for them, and re-layouts, on_device(): jnp.take(history_first, chosen.reshape(-1), axis=0, mode='clip')  13.5 us
    gather x1, local copies, waits for them, and re-layouts, on_device(): jnp.take(history_second, chosen.reshape(-1), axis=0, mode='clip')  13.4 us
    all_gather x1, blocking collectives, on_device(): counts_all = lax.all_gather(pull_count, 'dom', axis=0, tiled=True)  12.4 us
  transfers between devices with their start and end apart: 10, of which 7 were waited for; matrix products, arithmetic and copies ran while one was open for 9% of the time, Pallas kernels for 9%

profile of v15, /device:TPU:1, one launch (start us, length us, event | category | flops | bytes accessed | tf_op | source)
XLA Modules:
  0.0 367.8 jit_solution(9423434502014243405)
XLA Ops:
  7.2 12.4 %all-gather = s32[8,1,128]{2,1,0:T(1,128)S(1)} all-gather(s32[1,1,128]{2,1,0:T(1,128)} %bitcast.93), channel_id=1, replica_groups=mesh['dom'=8,'fsdp'=16] {'dom'}, dimensions={0}, use_global_device_ids=true | all-gather | bytes 4608 | tf_op jit(solution)/shard_map/all_gather | solution.py:172
  20.5 13.5 %gather_fusion = bf16[512,64,128]{2,1,0:T(8,128)(2,1)} fusion(bf16[128,64,128]{2,1,0:T(8,128)(2,1)S(1)} %copy-done, s32[1024]{0:T(1024)S(1)} %pad_clamp_fusion), kind=kCustom, calls=%fused_computation | custom fusion | bytes 16779264 | tf_op jit(solution)/shard_map/jit(_take)/gather | solution.py:181
  33.9 8.3 %all-to-all-start = ((bf16[128,4,64,128]{3,2,1,0:T(8,128)(2,1)}), bf16[128,4,64,128]{3,2,1,0:T(8,128)(2,1)}, u32[]{:S(2)}, u32[]{:S(2)}) async-start(bf16[128,4,64,128]{3,2,1,0:T(8,128)(2,1)} %bitcast.88), calls=%async_computation | async-start | bytes 16777216 | tf_op jit(solution)/shard_map/all_to_all | solution.py:183
  43.2 13.4 %gather_fusion.1 = bf16[512,64,128]{2,1,0:T(8,128)(2,1)} fusion(bf16[128,64,128]{2,1,0:T(8,128)(2,1)S(1)} %copy-done.2, s32[1024]{0:T(1024)S(1)} %pad_clamp_fusion), kind=kCustom, calls=%fused_computation.1 | custom fusion | bytes 16779264 | tf_op jit(solution)/shard_map/jit(_take)/gather | solution.py:182
  56.6 89.0 %all-to-all-done = bf16[128,4,64,128]{3,2,1,0:T(8,128)(2,1)} async-done(((bf16[128,4,64,128]{3,2,1,0:T(8,128)(2,1)}), bf16[128,4,64,128]{3,2,1,0:T(8,128)(2,1)}, u32[]{:S(2)}, u32[]{:S(2)}) %all-to-all-start) | async-done | bytes 8388640 | tf_op jit(solution)/shard_map/all_to_all | solution.py:183
  145.6 14.0 %all-to-all-start.1 = ((bf16[128,4,64,128]{3,2,1,0:T(8,128)(2,1)}), bf16[128,4,64,128]{3,2,1,0:T(8,128)(2,1)}, u32[]{:S(2)}, u32[]{:S(2)}) async-start(bf16[128,4,64,128]{3,2,1,0:T(8,128)(2,1)} %bitcast.87), calls=%async_computation.1 | async-start | bytes 16777216 | tf_op jit(solution)/shard_map/all_to_all | solution.py:184
  159.6 1.2 collective-permute-start.3
  161.7 10.7 %shard_map.147 = bf16[4,1024,128]{2,1,0:T(8,128)(2,1)} custom-call(s32[4,6]{1,0:T(4,128)} %src_ref.5, s32[4]{0:T(128)} %cnt_ref.5, s32[32]{0:T(128)} %reshape.94.live_ref, bf16[4,1024,128]{2,1,0:T(8,128)(2,1)} %own_b.1, bf16[4,1024,128]{2,1,0:T(8,128)(2,1)} %own_b.1, bf16[8,16,4,64,128]{4,3,2,1,0:T(8,128)(2,1)} %bitcast.4.pulled_a.pulled_b, ...), custom_call_target="tpu_custom_call" | custom-call | flops 805306368 | bytes 14417920 | tf_op jit(solution)/shard_map/pallas_call | solution.py:82
  172.3 1.3 constant_dynamic-slice_fusion.2
  174.8 65.8 %all-gather.3.cloned.1.call-done = bf16[1024,2176]{1,0:T(8,128)(2,1)} async-done(((bf16[64,2176]{1,0:T(8,128)(2,1)}), bf16[1024,2176]{1,0:T(8,128)(2,1)}) %all-gather.3.cloned.1.call-update) | async-done | bytes 4456464 | tf_op jit(solution)/shard_map/all_gather | solution.py:165
  240.6 3.8 %fusion.17.back_ref = bf16[4,1024,128]{2,1,0:T(8,128)(2,1)} fusion(bf16[4,1024,128]{2,1,0:T(8,128)(2,1)S(1)} %copy-done.5, bf16[1024,2176]{1,0:T(8,128)(2,1)} %all-gather.3.cloned.1.call-done), kind=kOutput, calls=%fused_computation.29 | convolution fusion | flops 1074266112 | bytes 4194304 | tf_op jit(solution)/shard_map/ab,vbn->van/dot_general | solution.py:192
  244.4 10.3 %shard_map.148 = f32[4,1024,128]{2,1,0:T(8,128)} custom-call(s32[4,6]{1,0:T(4,128)} %src_ref.5, s32[4]{0:T(128)} %cnt_ref.5, bf16[4,1024,128]{2,1,0:T(8,128)(2,1)} %fusion.17.back_ref, bf16[4,6,128,128]{3,2,1,0:T(8,128)(2,1)} %tile_ref.5), custom_call_target="tpu_custom_call" | custom-call | flops 805306368 | bytes 3932160 | tf_op jit(solution)/shard_map/pallas_call | solution.py:127
  255.8 4.5 %fusion.15 = (bf16[4,1024,128]{2,1,0:T(8,128)(2,1)}, f32[4,128,1024]{1,2,0:T(8,128)S(1)}) fusion(f32[1024]{0:T(1024)S(1)} %convert_reduce_fusion.1, bf16[4,1024,128]{2,1,0:T(8,128)(2,1)S(1)} %copy-done.4, bf16[1024,2176]{1,0:T(8,128)(2,1)} %all-gather.3.cloned.1.call-done), kind=kOutput, calls=%fused_computation.27 | convolution fusion | flops 1078984704 | bytes 6295552 | tf_op jit(solution)/shard_map/fh,vfn->vhn/dot_general | solution.py:205
  260.4 2.4 fusion.30
  263.7 8.7 %all-to-all-done.1 = bf16[128,4,64,128]{3,2,1,0:T(8,128)(2,1)} async-done(((bf16[128,4,64,128]{3,2,1,0:T(8,128)(2,1)}), bf16[128,4,64,128]{3,2,1,0:T(8,128)(2,1)}, u32[]{:S(2)}, u32[]{:S(2)}) %all-to-all-start.1) | async-done | bytes 8388640 | tf_op jit(solution)/shard_map/all_to_all | solution.py:184
  272.3 10.7 %shard_map.149 = bf16[4,1024,128]{2,1,0:T(8,128)(2,1)} custom-call(s32[4,6]{1,0:T(4,128)} %src_ref.5, s32[4]{0:T(128)} %cnt_ref.5, s32[32]{0:T(128)} %reshape.94.live_ref, bf16[4,1024,128]{2,1,0:T(8,128)(2,1)} %get-tuple-element.32.own_a.own_b, bf16[4,1024,128]{2,1,0:T(8,128)(2,1)} %get-tuple-element.32.own_a.own_b, ...), custom_call_target="tpu_custom_call" | custom-call | flops 805306368 | bytes 14417920 | tf_op jit(solution)/shard_map/pallas_call | solution.py:82
  283.1 1.3 constant_dynamic-slice_fusion
  287.5 2.1 fusion.11
  289.7 2.1 fusion.12
  292.1 46.7 %all_to_all.15 = bf16[16,64,1152]{2,1,0:T(8,128)(2,1)S(1)} all-to-all(bf16[16,64,1152]{2,1,0:T(8,128)(2,1)S(1)} %fusion.1), channel_id=1, replica_groups=mesh['dom'=8,'fsdp'=16] {'fsdp'}, dimensions={0} | all-to-all | bytes 4718592 | tf_op jit(solution)/shard_map/all_to_all | solution.py:230
  339.2 6.9 %collective-permute-done.4 = f32[64,1152]{1,0:T(8,128)S(1)} collective-permute-done((f32[64,1152]{1,0:T(8,128)S(1)}, f32[64,1152]{1,0:T(8,128)S(1)}, u32[]{:S(2)}, u32[]{:S(2)}) %collective-permute-start.4) | collective-permute-done | bytes 294944 | tf_op jit(solution)/shard_map/ppermute | solution.py:233
  346.2 3.4 collective-permute-start.5
  349.6 4.9 %collective-permute-done.5 = f32[64,1152]{1,0:T(8,128)S(1)} collective-permute-done((f32[64,1152]{1,0:T(8,128)S(1)}, f32[64,1152]{1,0:T(8,128)S(1)}, u32[]{:S(2)}, u32[]{:S(2)}) %collective-permute-start.5) | collective-permute-done | bytes 294944 | tf_op jit(solution)/shard_map/ppermute | solution.py:233
  354.5 3.2 collective-permute-start.6
  (52 shorter events, 12.9 us)
Async XLA Ops:
  7.2 13.3 %copy-start = (bf16[128,64,128]{2,1,0:T(8,128)(2,1)S(1)}, bf16[128,64,128]{2,1,0:T(8,128)(2,1)}, u32[]{:S(2)}) copy-start(bf16[128,64,128]{2,1,0:T(8,128)(2,1)} %param.15) | copy-start | bytes 6291460
  33.9 8.4 %copy-start.8 = (bf16[64]{0:T(256)(128)(2,1)S(1)}, bf16[64]{0:T(256)(128)(2,1)}, u32[]{:S(2)}) copy-start(bf16[64]{0:T(256)(128)(2,1)} %param.24) | copy-start | bytes 388
  33.9 8.4 %copy-start.6 = (bf16[64,1024]{1,0:T(8,128)(2,1)S(1)}, bf16[64,1024]{1,0:T(8,128)(2,1)}, u32[]{:S(2)}) copy-start(bf16[64,1024]{1,0:T(8,128)(2,1)} %param.23) | copy-start | bytes 393220
  33.9 8.4 %copy-start.7 = (bf16[64,1024]{1,0:T(8,128)(2,1)S(1)}, bf16[64,1024]{1,0:T(8,128)(2,1)}, u32[]{:S(2)}) copy-start(bf16[64,1024]{1,0:T(8,128)(2,1)} %param.22) | copy-start | bytes 393220
  33.9 9.2 %copy-start.2 = (bf16[128,64,128]{2,1,0:T(8,128)(2,1)S(1)}, bf16[128,64,128]{2,1,0:T(8,128)(2,1)}, u32[]{:S(2)}) copy-start(bf16[128,64,128]{2,1,0:T(8,128)(2,1)} %param.16) | copy-start | bytes 6291460
  33.9 111.7 %all-to-all-start = ((bf16[128,4,64,128]{3,2,1,0:T(8,128)(2,1)}), bf16[128,4,64,128]{3,2,1,0:T(8,128)(2,1)}, u32[]{:S(2)}, u32[]{:S(2)}) async-start(bf16[128,4,64,128]{3,2,1,0:T(8,128)(2,1)} %bitcast.88), calls=%async_computation | async-start | bytes 16777216 | tf_op jit(solution)/shard_map/all_to_all | solution.py:183
  42.2 198.4 %all-gather.3.cloned.1.call-start = ((), (), s32[]{:S(2)}) async-start(), calls=%async_computation.3 | async-start | bytes 4734976 | tf_op jit(solution)/shard_map/all_gather | solution.py:165
  145.6 14.0 %copy-start.5 = (bf16[4,1024,128]{2,1,0:T(8,128)(2,1)S(1)}, bf16[4,1024,128]{2,1,0:T(8,128)(2,1)}, u32[]{:S(2)}) copy-start(bf16[4,1024,128]{2,1,0:T(8,128)(2,1)} %param.25) | copy-start | bytes 3145732
  145.6 126.7 %all-to-all-start.1 = ((bf16[128,4,64,128]{3,2,1,0:T(8,128)(2,1)}), bf16[128,4,64,128]{3,2,1,0:T(8,128)(2,1)}, u32[]{:S(2)}, u32[]{:S(2)}) async-start(bf16[128,4,64,128]{3,2,1,0:T(8,128)(2,1)} %bitcast.87), calls=%async_computation.1 | async-start | bytes 16777216 | tf_op jit(solution)/shard_map/all_to_all | solution.py:184
  159.6 127.2 %collective-permute-start.3 = (bf16[4,1024,128]{2,1,0:T(8,128)(2,1)S(1)}, bf16[4,1024,128]{2,1,0:T(8,128)(2,1)}, u32[]{:S(2)}, u32[]{:S(2)}) collective-permute-start(bf16[4,1024,128]{2,1,0:T(8,128)(2,1)S(1)} %copy-done.5), channel_id=1, source_target_pairs={{0,16},{16,0},{32,48},{48,32},{64,80},{80,64},{96,112},{112,96},{1... | collective-permute-start | bytes 3145736 | tf_op jit(solution)/shard_map/ppermute | solution.py:190
  174.5 115.2 %collective-permute-start = (bf16[4,16,32,128]{3,2,0,1:T(8,128)(2,1)}, bf16[4,16,32,128]{3,2,0,1:T(8,128)(2,1)}, u32[]{:S(2)}, u32[]{:S(2)}) collective-permute-start(bf16[4,16,32,128]{3,2,0,1:T(8,128)(2,1)} %bitcast.86), channel_id=1, source_target_pairs={{0,16},{16,0},{32,48},{48,32},{64,80},{80,64},{96,112},{112,96},{1... | collective-permute-start | bytes 1572872 | tf_op jit(solution)/shard_map/ppermute | solution.py:213
  244.4 11.4 %copy-start.4 = (bf16[4,1024,128]{2,1,0:T(8,128)(2,1)S(1)}, bf16[4,1024,128]{2,1,0:T(8,128)(2,1)}, u32[]{:S(2)}) copy-start(bf16[4,1024,128]{2,1,0:T(8,128)(2,1)} %shard_map.147) | copy-start | bytes 3145732
  255.8 4.5 %copy-start.3 = (f32[4,1024,128]{2,1,0:T(8,128)S(1)}, f32[4,1024,128]{2,1,0:T(8,128)}, u32[]{:S(2)}) copy-start(f32[4,1024,128]{2,1,0:T(8,128)} %shard_map.148) | copy-start | bytes 6291460
  262.8 26.9 %collective-permute-start.1 = (bf16[4,1024,128]{2,1,0:T(8,128)(2,1)S(1)}, bf16[4,1024,128]{2,1,0:T(8,128)(2,1)}, u32[]{:S(2)}, u32[]{:S(2)}) collective-permute-start(bf16[4,1024,128]{2,1,0:T(8,128)(2,1)S(1)} %get-tuple-element.21), channel_id=1, source_target_pairs={{0,16},{16,0},{32,48},{48,32},{64,80},{80,64},{96,112},{112,96},{1... | collective-permute-start | bytes 3145736 | tf_op jit(solution)/shard_map/ppermute | solution.py:213
  285.3 2.3 collective-permute-start.2
  339.1 7.0 %collective-permute-start.4 = (f32[64,1152]{1,0:T(8,128)S(1)}, f32[64,1152]{1,0:T(8,128)S(1)}, u32[]{:S(2)}, u32[]{:S(2)}) collective-permute-start(f32[64,1152]{1,0:T(8,128)S(1)} %convert_reduce_fusion), channel_id=1, source_target_pairs={{0,32},{16,48},{32,0},{48,16},{64,96},{80,112},{96,64},{112,80},{1... | collective-permute-start | bytes 884744 | tf_op jit(solution)/shard_map/ppermute | solution.py:233
  346.1 14.8 %copy-start.1 = (bf16[128,64,128]{2,1,0:T(8,128)(2,1)S(1)}, bf16[128,64,128]{2,1,0:T(8,128)(2,1)}, u32[]{:S(2)}) copy-start(bf16[128,64,128]{2,1,0:T(8,128)(2,1)} %param.15) | copy-start | bytes 6291460
  346.2 8.3 %collective-permute-start.5 = (f32[64,1152]{1,0:T(8,128)S(1)}, f32[64,1152]{1,0:T(8,128)S(1)}, u32[]{:S(2)}, u32[]{:S(2)}) collective-permute-start(f32[64,1152]{1,0:T(8,128)S(1)} %add.72), channel_id=1, source_target_pairs={{0,64},{16,80},{32,96},{48,112},{64,0},{80,16},{96,32},{112,48},{1... | collective-permute-start | bytes 884744 | tf_op jit(solution)/shard_map/ppermute | solution.py:233
  354.5 4.4 %collective-permute-start.6 = (f32[64,1152]{1,0:T(8,128)S(1)}, f32[64,1152]{1,0:T(8,128)S(1)}, u32[]{:S(2)}, u32[]{:S(2)}) collective-permute-start(f32[64,1152]{1,0:T(8,128)S(1)} %add.73), channel_id=1, source_target_pairs={{0,16},{16,0},{32,48},{48,32},{64,80},{80,64},{96,112},{112,96},{1... | collective-permute-start | bytes 884744 | tf_op jit(solution)/shard_map/ppermute | solution.py:234
Sparse Core Ops, SparseCore 0:
  45.2 195.3 all-gather.2

commit v16 on v15

--- a/solution.py
+++ b/solution.py
@@ -12,7 +12,9 @@
     return jax.nn.gelu(inputs, approximate=True)
 
 
-def _agg_kernel(own_count, last_step, src_ref, cnt_ref, live_ref, own_a, own_b, pulled_a, pulled_b, tile_ref, out_ref, acc_ref):
+def _agg_kernel(own_count, last_step, per, src_ref, cnt_ref, live_ref, *refs):
+    own_refs, pulled_refs = refs[:per], refs[per : 2 * per]
+    tile_ref, out_ref, acc_ref = refs[2 * per :]
     v = pl.program_id(0)
     k = pl.program_id(1)
 
@@ -20,8 +22,8 @@
     def _():
         acc_ref[...] = jnp.zeros_like(acc_ref)
 
-    for j, own_ref, pulled_ref in ((0, own_a, pulled_a), (1, own_b, pulled_b)):
-        t = 2 * k + j
+    for j, own_ref, pulled_ref in zip(range(per), own_refs, pulled_refs):
+        t = per * k + j
         src = src_ref[v, t]
         tile_live = t < cnt_ref[v]
         own_ok = tile_live & (src < own_count)
@@ -46,21 +48,22 @@
     nb, feat, blk = own.shape
     dom, fsdp, cap = pulled.shape[0], pulled.shape[1], pulled.shape[2]
     tiles = tile_src.shape[1]
-    steps = tiles // 2
+    per = tiles
+    steps = tiles // per
 
     def eff(v, t, cnt_ref):
         return jnp.minimum(t, cnt_ref[v] - 1)
 
     def own_map(j):
         def index(v, k, src_ref, cnt_ref, live_ref):
-            s = src_ref[v, eff(v, 2 * k + j, cnt_ref)]
+            s = src_ref[v, eff(v, per * k + j, cnt_ref)]
             return (jnp.clip(s, 0, nb - 1), 0, 0)
 
         return index
 
     def pulled_map(j):
         def index(v, k, src_ref, cnt_ref, live_ref):
-            s = jnp.clip(src_ref[v, eff(v, 2 * k + j, cnt_ref)] - nb, 0, cap * dom - 1)
+            s = jnp.clip(src_ref[v, eff(v, per * k + j, cnt_ref)] - nb, 0, cap * dom - 1)
             return (s % dom, 0, s // dom, 0, 0)
 
         return index
@@ -68,26 +71,22 @@
     grid_spec = pltpu.PrefetchScalarGridSpec(
         num_scalar_prefetch=3,
         grid=(nb, steps),
-        in_specs=[
-            pl.BlockSpec((1, feat, blk), own_map(0)),
-            pl.BlockSpec((1, feat, blk), own_map(1)),
-            pl.BlockSpec((1, fsdp, 1) + pulled.shape[3:], pulled_map(0)),
-            pl.BlockSpec((1, fsdp, 1) + pulled.shape[3:], pulled_map(1)),
-            pl.BlockSpec((1, 2, blk, blk), lambda v, k, s, c, l: (v, k, 0, 0)),
-        ],
+        in_specs=[pl.BlockSpec((1, feat, blk), own_map(j)) for j in range(per)]
+        + [pl.BlockSpec((1, fsdp, 1) + pulled.shape[3:], pulled_map(j)) for j in range(per)]
+        + [pl.BlockSpec((1, per, blk, blk), lambda v, k, s, c, l: (v, k, 0, 0))],
         out_specs=pl.BlockSpec((1, feat, blk), lambda v, k, s, c, l: (v, 0, 0)),
         scratch_shapes=[pltpu.VMEM((feat, blk), jnp.float32)],
     )
     flops = 2 * nb * tiles * feat * blk * blk
     return pl.pallas_call(
-        functools.partial(_agg_kernel, nb, steps - 1),
+        functools.partial(_agg_kernel, nb, steps - 1, per),
         grid_spec=grid_spec,
         out_shape=jax.ShapeDtypeStruct(own.shape, jnp.bfloat16),
         compiler_params=pltpu.CompilerParams(dimension_semantics=("arbitrary", "arbitrary")),
         cost_estimate=pl.CostEstimate(
             flops=flops, transcendentals=0, bytes_accessed=nb * tiles * (2 * feat * blk * 2 + blk * blk * 2) + own.size * 2
         ),
-    )(tile_src, tile_count, slot_live, own, own, pulled, pulled, tile_values)
+    )(tile_src, tile_count, slot_live, *([own] * per), *([pulled] * per), tile_values)
 
 
 def _spread_kernel(own_count, src_ref, cnt_ref, back_ref, tile_ref, out_ref):

time: 370 us -> 369 us (level)
  Pallas kernels: 31.7 us -> 27.2 us
    pallas_call x2, Pallas kernels: 21.4 us -> 17.7 us  [aggregate(): pl.pallas_call(functools.partial(_agg_kernel, nb, steps - 1, per), grid_s...]
  transfers between devices with their start and end apart: 10 -> 10, of which waited for: 7 -> 7; matrix products, arithmetic and copies ran while one was open for 9% -> 9% of each run, Pallas kernels for 9% -> 7%
where the time goes in v16:
time: 369 us; the launch traced here: 368 us
  waiting for transfers between devices  180 us (49%)
  blocking collectives  59.9 us (16%)
  local copies, waits for them, and re-layouts  33.2 us (9%)
  starting transfers between devices  32.6 us (9%)
  Pallas kernels  27.2 us (7%)
  between operations  14.3 us (4%)
  matrix products  14.1 us (4%)
  other arithmetic  6.87 us (2%)
    all_to_all x1, waiting for transfers between devices, on_device(): lax.all_to_all(sent_first, ('dom', 'fsdp'), split_axis=0, concat_axis=0,...  89 us
    all_gather x1, waiting for transfers between devices, on_device(): lax.all_gather(jnp.concatenate([w_first, w_second, bias_cols], axis=1), '...  67.7 us
    all_to_all x1, blocking collectives, on_device(): lax.all_to_all(packed_terms.astype(jnp.bfloat16), 'fsdp', split_axis=0, c...  47.6 us
    pallas_call x2, Pallas kernels, aggregate(): pl.pallas_call(functools.partial(_agg_kernel, nb, steps - 1, per), grid_s...  17.7 us
    all_to_all x1, starting transfers between devices, on_device(): lax.all_to_all(sent_second, ('dom', 'fsdp'), split_axis=0, concat_axis=0,...  14 us
    gather x1, local copies, waits for them, and re-layouts, on_device(): jnp.take(history_first, chosen.reshape(-1), axis=0, mode='clip')  13.5 us
    gather x1, local copies, waits for them, and re-layouts, on_device(): jnp.take(history_second, chosen.reshape(-1), axis=0, mode='clip')  13.4 us
    all_gather x1, blocking collectives, on_device(): counts_all = lax.all_gather(pull_count, 'dom', axis=0, tiled=True)  12.4 us
  transfers between devices with their start and end apart: 10, of which 7 were waited for; matrix products, arithmetic and copies ran while one was open for 9% of the time, Pallas kernels for 7%

profile of v16, /device:TPU:1, one launch (start us, length us, event | category | flops | bytes accessed | tf_op | source)
XLA Modules:
  0.0 367.7 jit_solution(14564966523839235707)
XLA Ops:
  7.2 12.4 %all-gather = s32[8,1,128]{2,1,0:T(1,128)S(1)} all-gather(s32[1,1,128]{2,1,0:T(1,128)} %bitcast.93), channel_id=1, replica_groups=mesh['dom'=8,'fsdp'=16] {'dom'}, dimensions={0}, use_global_device_ids=true | all-gather | bytes 4608 | tf_op jit(solution)/shard_map/all_gather | solution.py:171
  20.5 13.5 %gather_fusion = bf16[512,64,128]{2,1,0:T(8,128)(2,1)} fusion(bf16[128,64,128]{2,1,0:T(8,128)(2,1)S(1)} %copy-done, s32[1024]{0:T(1024)S(1)} %pad_clamp_fusion), kind=kCustom, calls=%fused_computation | custom fusion | bytes 16779264 | tf_op jit(solution)/shard_map/jit(_take)/gather | solution.py:180
  33.9 8.3 %all-to-all-start = ((bf16[128,4,64,128]{3,2,1,0:T(8,128)(2,1)}), bf16[128,4,64,128]{3,2,1,0:T(8,128)(2,1)}, u32[]{:S(2)}, u32[]{:S(2)}) async-start(bf16[128,4,64,128]{3,2,1,0:T(8,128)(2,1)} %bitcast.88), calls=%async_computation | async-start | bytes 16777216 | tf_op jit(solution)/shard_map/all_to_all | solution.py:182
  43.2 13.4 %gather_fusion.1 = bf16[512,64,128]{2,1,0:T(8,128)(2,1)} fusion(bf16[128,64,128]{2,1,0:T(8,128)(2,1)S(1)} %copy-done.2, s32[1024]{0:T(1024)S(1)} %pad_clamp_fusion), kind=kCustom, calls=%fused_computation.1 | custom fusion | bytes 16779264 | tf_op jit(solution)/shard_map/jit(_take)/gather | solution.py:181
  56.6 89.0 %all-to-all-done = bf16[128,4,64,128]{3,2,1,0:T(8,128)(2,1)} async-done(((bf16[128,4,64,128]{3,2,1,0:T(8,128)(2,1)}), bf16[128,4,64,128]{3,2,1,0:T(8,128)(2,1)}, u32[]{:S(2)}, u32[]{:S(2)}) %all-to-all-start) | async-done | bytes 8388640 | tf_op jit(solution)/shard_map/all_to_all | solution.py:182
  145.6 14.0 %all-to-all-start.1 = ((bf16[128,4,64,128]{3,2,1,0:T(8,128)(2,1)}), bf16[128,4,64,128]{3,2,1,0:T(8,128)(2,1)}, u32[]{:S(2)}, u32[]{:S(2)}) async-start(bf16[128,4,64,128]{3,2,1,0:T(8,128)(2,1)} %bitcast.87), calls=%async_computation.1 | async-start | bytes 16777216 | tf_op jit(solution)/shard_map/all_to_all | solution.py:183
  159.6 1.4 collective-permute-start.3
  161.8 8.7 %shard_map.147 = bf16[4,1024,128]{2,1,0:T(8,128)(2,1)} custom-call(s32[4,6]{1,0:T(4,128)} %src_ref.5, s32[4]{0:T(128)} %cnt_ref.5, s32[32]{0:T(128)} %reshape.94.live_ref, bf16[4,1024,128]{2,1,0:T(8,128)(2,1)} %refs_5_.1, bf16[4,1024,128]{2,1,0:T(8,128)(2,1)} %refs_5_.1, bf16[4,1024,128]{2,1,0:T(8,128)(2,1)} %refs_5_.1, bf16[4,1024,128]{2,1,0:T(8,128)(2,1)} %refs_5_.1, ...), custom_call_target="tpu_custom_call" | custom-call | flops 805306368 | bytes 14417920 | tf_op jit(solution)/shard_map/pallas_call | solution.py:81
  170.5 1.3 constant_dynamic-slice_fusion.2
  173.0 67.7 %all-gather.3.cloned.1.call-done = bf16[1024,2176]{1,0:T(8,128)(2,1)} async-done(((bf16[64,2176]{1,0:T(8,128)(2,1)}), bf16[1024,2176]{1,0:T(8,128)(2,1)}) %all-gather.3.cloned.1.call-update) | async-done | bytes 4456464 | tf_op jit(solution)/shard_map/all_gather | solution.py:164
  240.6 3.8 %fusion.17.back_ref = bf16[4,1024,128]{2,1,0:T(8,128)(2,1)} fusion(bf16[4,1024,128]{2,1,0:T(8,128)(2,1)S(1)} %copy-done.5, bf16[1024,2176]{1,0:T(8,128)(2,1)} %all-gather.3.cloned.1.call-done), kind=kOutput, calls=%fused_computation.29 | convolution fusion | flops 1074266112 | bytes 4194304 | tf_op jit(solution)/shard_map/ab,vbn->van/dot_general | solution.py:191
  244.4 9.5 %shard_map.148 = f32[4,1024,128]{2,1,0:T(8,128)} custom-call(s32[4,6]{1,0:T(4,128)} %src_ref.5, s32[4]{0:T(128)} %cnt_ref.5, bf16[4,1024,128]{2,1,0:T(8,128)(2,1)} %fusion.17.back_ref, bf16[4,6,128,128]{3,2,1,0:T(8,128)(2,1)} %refs_12_.3), custom_call_target="tpu_custom_call" | custom-call | flops 805306368 | bytes 3932160 | tf_op jit(solution)/shard_map/pallas_call | solution.py:126
  255.0 4.5 %fusion.15 = (bf16[4,1024,128]{2,1,0:T(8,128)(2,1)}, f32[4,128,1024]{1,2,0:T(8,128)S(1)}) fusion(f32[1024]{0:T(1024)S(1)} %convert_reduce_fusion.1, bf16[4,1024,128]{2,1,0:T(8,128)(2,1)S(1)} %copy-done.4, bf16[1024,2176]{1,0:T(8,128)(2,1)} %all-gather.3.cloned.1.call-done), kind=kOutput, calls=%fused_computation.27 | convolution fusion | flops 1078984704 | bytes 6295552 | tf_op jit(solution)/shard_map/fh,vfn->vhn/dot_general | solution.py:204
  259.5 2.4 fusion.30
  262.7 9.6 %all-to-all-done.1 = bf16[128,4,64,128]{3,2,1,0:T(8,128)(2,1)} async-done(((bf16[128,4,64,128]{3,2,1,0:T(8,128)(2,1)}), bf16[128,4,64,128]{3,2,1,0:T(8,128)(2,1)}, u32[]{:S(2)}, u32[]{:S(2)}) %all-to-all-start.1) | async-done | bytes 8388640 | tf_op jit(solution)/shard_map/all_to_all | solution.py:183
  272.3 9.0 %shard_map.149 = bf16[4,1024,128]{2,1,0:T(8,128)(2,1)} custom-call(s32[4,6]{1,0:T(4,128)} %src_ref.5, s32[4]{0:T(128)} %cnt_ref.5, s32[32]{0:T(128)} %reshape.94.live_ref, bf16[4,1024,128]{2,1,0:T(8,128)(2,1)} %get-tuple-element.32.refs_0_.refs_1_.refs_2_.refs_3_.refs_4_.refs_5_, ...), custom_call_target="tpu_custom_call" | custom-call | flops 805306368 | bytes 14417920 | tf_op jit(solution)/shard_map/pallas_call | solution.py:81
  281.4 1.3 constant_dynamic-slice_fusion
  285.8 2.1 fusion.11
  288.0 2.1 fusion.12
  290.4 47.6 %all_to_all.15 = bf16[16,64,1152]{2,1,0:T(8,128)(2,1)S(1)} all-to-all(bf16[16,64,1152]{2,1,0:T(8,128)(2,1)S(1)} %fusion.1), channel_id=1, replica_groups=mesh['dom'=8,'fsdp'=16] {'fsdp'}, dimensions={0} | all-to-all | bytes 4718592 | tf_op jit(solution)/shard_map/all_to_all | solution.py:229
  338.4 7.0 %collective-permute-done.4 = f32[64,1152]{1,0:T(8,128)S(1)} collective-permute-done((f32[64,1152]{1,0:T(8,128)S(1)}, f32[64,1152]{1,0:T(8,128)S(1)}, u32[]{:S(2)}, u32[]{:S(2)}) %collective-permute-start.4) | collective-permute-done | bytes 294944 | tf_op jit(solution)/shard_map/ppermute | solution.py:232
  345.4 4.1 %collective-permute-start.5 = (f32[64,1152]{1,0:T(8,128)S(1)}, f32[64,1152]{1,0:T(8,128)S(1)}, u32[]{:S(2)}, u32[]{:S(2)}) collective-permute-start(f32[64,1152]{1,0:T(8,128)S(1)} %add.72), channel_id=1, source_target_pairs={{0,64},{16,80},{32,96},{48,112},{64,0},{80,16},{96,32},{112,48},{1... | collective-permute-start | bytes 884744 | tf_op jit(solution)/shard_map/ppermute | solution.py:232
  349.5 4.5 %collective-permute-done.5 = f32[64,1152]{1,0:T(8,128)S(1)} collective-permute-done((f32[64,1152]{1,0:T(8,128)S(1)}, f32[64,1152]{1,0:T(8,128)S(1)}, u32[]{:S(2)}, u32[]{:S(2)}) %collective-permute-start.5) | collective-permute-done | bytes 294944 | tf_op jit(solution)/shard_map/ppermute | solution.py:232
  354.0 3.6 collective-permute-start.6
  (52 shorter events, 12.7 us)
Async XLA Ops:
  7.2 13.3 %copy-start = (bf16[128,64,128]{2,1,0:T(8,128)(2,1)S(1)}, bf16[128,64,128]{2,1,0:T(8,128)(2,1)}, u32[]{:S(2)}) copy-start(bf16[128,64,128]{2,1,0:T(8,128)(2,1)} %param.15) | copy-start | bytes 6291460
  33.9 8.4 %copy-start.8 = (bf16[64]{0:T(256)(128)(2,1)S(1)}, bf16[64]{0:T(256)(128)(2,1)}, u32[]{:S(2)}) copy-start(bf16[64]{0:T(256)(128)(2,1)} %param.24) | copy-start | bytes 388
  33.9 8.4 %copy-start.6 = (bf16[64,1024]{1,0:T(8,128)(2,1)S(1)}, bf16[64,1024]{1,0:T(8,128)(2,1)}, u32[]{:S(2)}) copy-start(bf16[64,1024]{1,0:T(8,128)(2,1)} %param.23) | copy-start | bytes 393220
  33.9 8.4 %copy-start.7 = (bf16[64,1024]{1,0:T(8,128)(2,1)S(1)}, bf16[64,1024]{1,0:T(8,128)(2,1)}, u32[]{:S(2)}) copy-start(bf16[64,1024]{1,0:T(8,128)(2,1)} %param.22) | copy-start | bytes 393220
  33.9 9.2 %copy-start.2 = (bf16[128,64,128]{2,1,0:T(8,128)(2,1)S(1)}, bf16[128,64,128]{2,1,0:T(8,128)(2,1)}, u32[]{:S(2)}) copy-start(bf16[128,64,128]{2,1,0:T(8,128)(2,1)} %param.16) | copy-start | bytes 6291460
  33.9 111.7 %all-to-all-start = ((bf16[128,4,64,128]{3,2,1,0:T(8,128)(2,1)}), bf16[128,4,64,128]{3,2,1,0:T(8,128)(2,1)}, u32[]{:S(2)}, u32[]{:S(2)}) async-start(bf16[128,4,64,128]{3,2,1,0:T(8,128)(2,1)} %bitcast.88), calls=%async_computation | async-start | bytes 16777216 | tf_op jit(solution)/shard_map/all_to_all | solution.py:182
  42.3 198.4 %all-gather.3.cloned.1.call-start = ((), (), s32[]{:S(2)}) async-start(), calls=%async_computation.3 | async-start | bytes 4734976 | tf_op jit(solution)/shard_map/all_gather | solution.py:164
  145.6 14.0 %copy-start.5 = (bf16[4,1024,128]{2,1,0:T(8,128)(2,1)S(1)}, bf16[4,1024,128]{2,1,0:T(8,128)(2,1)}, u32[]{:S(2)}) copy-start(bf16[4,1024,128]{2,1,0:T(8,128)(2,1)} %param.25) | copy-start | bytes 3145732
  145.6 126.7 %all-to-all-start.1 = ((bf16[128,4,64,128]{3,2,1,0:T(8,128)(2,1)}), bf16[128,4,64,128]{3,2,1,0:T(8,128)(2,1)}, u32[]{:S(2)}, u32[]{:S(2)}) async-start(bf16[128,4,64,128]{3,2,1,0:T(8,128)(2,1)} %bitcast.87), calls=%async_computation.1 | async-start | bytes 16777216 | tf_op jit(solution)/shard_map/all_to_all | solution.py:183
  159.6 125.5 %collective-permute-start.3 = (bf16[4,1024,128]{2,1,0:T(8,128)(2,1)S(1)}, bf16[4,1024,128]{2,1,0:T(8,128)(2,1)}, u32[]{:S(2)}, u32[]{:S(2)}) collective-permute-start(bf16[4,1024,128]{2,1,0:T(8,128)(2,1)S(1)} %copy-done.5), channel_id=1, source_target_pairs={{0,16},{16,0},{32,48},{48,32},{64,80},{80,64},{96,112},{112,96},{1... | collective-permute-start | bytes 3145736 | tf_op jit(solution)/shard_map/ppermute | solution.py:189
  172.6 115.3 %collective-permute-start = (bf16[4,16,32,128]{3,2,0,1:T(8,128)(2,1)}, bf16[4,16,32,128]{3,2,0,1:T(8,128)(2,1)}, u32[]{:S(2)}, u32[]{:S(2)}) collective-permute-start(bf16[4,16,32,128]{3,2,0,1:T(8,128)(2,1)} %bitcast.86), channel_id=1, source_target_pairs={{0,16},{16,0},{32,48},{48,32},{64,80},{80,64},{96,112},{112,96},{1... | collective-permute-start | bytes 1572872 | tf_op jit(solution)/shard_map/ppermute | solution.py:212
  244.4 10.6 %copy-start.4 = (bf16[4,1024,128]{2,1,0:T(8,128)(2,1)S(1)}, bf16[4,1024,128]{2,1,0:T(8,128)(2,1)}, u32[]{:S(2)}) copy-start(bf16[4,1024,128]{2,1,0:T(8,128)(2,1)} %shard_map.147) | copy-start | bytes 3145732
  255.0 4.5 %copy-start.3 = (f32[4,1024,128]{2,1,0:T(8,128)S(1)}, f32[4,1024,128]{2,1,0:T(8,128)}, u32[]{:S(2)}) copy-start(f32[4,1024,128]{2,1,0:T(8,128)} %shard_map.148) | copy-start | bytes 6291460
  261.9 26.1 %collective-permute-start.1 = (bf16[4,1024,128]{2,1,0:T(8,128)(2,1)S(1)}, bf16[4,1024,128]{2,1,0:T(8,128)(2,1)}, u32[]{:S(2)}, u32[]{:S(2)}) collective-permute-start(bf16[4,1024,128]{2,1,0:T(8,128)(2,1)S(1)} %get-tuple-element.21), channel_id=1, source_target_pairs={{0,16},{16,0},{32,48},{48,32},{64,80},{80,64},{96,112},{112,96},{1... | collective-permute-start | bytes 3145736 | tf_op jit(solution)/shard_map/ppermute | solution.py:212
  283.6 2.3 collective-permute-start.2
  338.3 7.1 %collective-permute-start.4 = (f32[64,1152]{1,0:T(8,128)S(1)}, f32[64,1152]{1,0:T(8,128)S(1)}, u32[]{:S(2)}, u32[]{:S(2)}) collective-permute-start(f32[64,1152]{1,0:T(8,128)S(1)} %convert_reduce_fusion), channel_id=1, source_target_pairs={{0,32},{16,48},{32,0},{48,16},{64,96},{80,112},{96,64},{112,80},{1... | collective-permute-start | bytes 884744 | tf_op jit(solution)/shard_map/ppermute | solution.py:232
  345.4 15.5 %copy-start.1 = (bf16[128,64,128]{2,1,0:T(8,128)(2,1)S(1)}, bf16[128,64,128]{2,1,0:T(8,128)(2,1)}, u32[]{:S(2)}) copy-start(bf16[128,64,128]{2,1,0:T(8,128)(2,1)} %param.15) | copy-start | bytes 6291460
  345.4 8.5 %collective-permute-start.5 = (f32[64,1152]{1,0:T(8,128)S(1)}, f32[64,1152]{1,0:T(8,128)S(1)}, u32[]{:S(2)}, u32[]{:S(2)}) collective-permute-start(f32[64,1152]{1,0:T(8,128)S(1)} %add.72), channel_id=1, source_target_pairs={{0,64},{16,80},{32,96},{48,112},{64,0},{80,16},{96,32},{112,48},{1... | collective-permute-start | bytes 884744 | tf_op jit(solution)/shard_map/ppermute | solution.py:232
  354.0 4.8 %collective-permute-start.6 = (f32[64,1152]{1,0:T(8,128)S(1)}, f32[64,1152]{1,0:T(8,128)S(1)}, u32[]{:S(2)}, u32[]{:S(2)}) collective-permute-start(f32[64,1152]{1,0:T(8,128)S(1)} %add.73), channel_id=1, source_target_pairs={{0,16},{16,0},{32,48},{48,32},{64,80},{80,64},{96,112},{112,96},{1... | collective-permute-start | bytes 884744 | tf_op jit(solution)/shard_map/ppermute | solution.py:233
Sparse Core Ops, SparseCore 0:
  45.2 195.3 all-gather.2

commit v17 on v16

--- a/solution.py
+++ b/solution.py
@@ -12,9 +12,9 @@
     return jax.nn.gelu(inputs, approximate=True)
 
 
-def _agg_kernel(own_count, last_step, per, src_ref, cnt_ref, live_ref, *refs):
-    own_refs, pulled_refs = refs[:per], refs[per : 2 * per]
-    tile_ref, out_ref, acc_ref = refs[2 * per :]
+def _agg_kernel(own_count, last_step, per, src_ref, cnt_ref, live_ref, own_ref, *refs):
+    pulled_refs = refs[:per]
+    tile_ref, out_ref, acc_ref = refs[per:]
     v = pl.program_id(0)
     k = pl.program_id(1)
 
@@ -22,7 +22,7 @@
     def _():
         acc_ref[...] = jnp.zeros_like(acc_ref)
 
-    for j, own_ref, pulled_ref in zip(range(per), own_refs, pulled_refs):
+    for j, pulled_ref in zip(range(per), pulled_refs):
         t = per * k + j
         src = src_ref[v, t]
         tile_live = t < cnt_ref[v]
@@ -31,7 +31,9 @@
 
         @pl.when(own_ok)
         def _():
-            acc_ref[...] += jnp.dot(own_ref[0], tile_ref[0, j], preferred_element_type=jnp.float32)
+            acc_ref[...] += jnp.dot(
+                own_ref[jnp.clip(src, 0, own_count - 1)], tile_ref[0, j], preferred_element_type=jnp.float32
+            )
 
         @pl.when(pull_ok)
         def _():
@@ -54,13 +56,6 @@
     def eff(v, t, cnt_ref):
         return jnp.minimum(t, cnt_ref[v] - 1)
 
-    def own_map(j):
-        def index(v, k, src_ref, cnt_ref, live_ref):
-            s = src_ref[v, eff(v, per * k + j, cnt_ref)]
-            return (jnp.clip(s, 0, nb - 1), 0, 0)
-
-        return index
-
     def pulled_map(j):
         def index(v, k, src_ref, cnt_ref, live_ref):
             s = jnp.clip(src_ref[v, eff(v, per * k + j, cnt_ref)] - nb, 0, cap * dom - 1)
@@ -71,7 +66,7 @@
     grid_spec = pltpu.PrefetchScalarGridSpec(
         num_scalar_prefetch=3,
         grid=(nb, steps),
-        in_specs=[pl.BlockSpec((1, feat, blk), own_map(j)) for j in range(per)]
+        in_specs=[pl.BlockSpec((nb, feat, blk), lambda v, k, s, c, l: (0, 0, 0))]
         + [pl.BlockSpec((1, fsdp, 1) + pulled.shape[3:], pulled_map(j)) for j in range(per)]
         + [pl.BlockSpec((1, per, blk, blk), lambda v, k, s, c, l: (v, k, 0, 0))],
         out_specs=pl.BlockSpec((1, feat, blk), lambda v, k, s, c, l: (v, 0, 0)),
@@ -86,7 +81,7 @@
         cost_estimate=pl.CostEstimate(
             flops=flops, transcendentals=0, bytes_accessed=nb * tiles * (2 * feat * blk * 2 + blk * blk * 2) + own.size * 2
         ),
-    )(tile_src, tile_count, slot_live, *([own] * per), *([pulled] * per), tile_values)
+    )(tile_src, tile_count, slot_live, own, *([pulled] * per), tile_values)
 
 
 def _spread_kernel(own_count, src_ref, cnt_ref, back_ref, tile_ref, out_ref):

time: 369 us -> 366 us (level)
  transfers between devices with their start and end apart: 10 -> 10, of which waited for: 7 -> 7; matrix products, arithmetic and copies ran while one was open for 9% -> 10% of each run, Pallas kernels for 7% -> 8%
where the time goes in v17:
time: 366 us; the launch traced here: 365 us
  waiting for transfers between devices  178 us (49%)
  blocking collectives  59.5 us (16%)
  local copies, waits for them, and re-layouts  33.1 us (9%)
  starting transfers between devices  31.2 us (9%)
  Pallas kernels  27.4 us (7%)
  between operations  14.3 us (4%)
  matrix products  14.1 us (4%)
  other arithmetic  6.87 us (2%)
    all_to_all x1, waiting for transfers between devices, on_device(): lax.all_to_all(sent_first, ('dom', 'fsdp'), split_axis=0, concat_axis=0,...  89 us
    all_gather x1, waiting for transfers between devices, on_device(): lax.all_gather(jnp.concatenate([w_first, w_second, bias_cols], axis=1), '...  68.4 us
    all_to_all x1, blocking collectives, on_device(): lax.all_to_all(packed_terms.astype(jnp.bfloat16), 'fsdp', split_axis=0, c...  47.2 us
    pallas_call x2, Pallas kernels, aggregate(): pl.pallas_call(functools.partial(_agg_kernel, nb, steps - 1, per), grid_s...  15.4 us
    all_to_all x1, starting transfers between devices, on_device(): lax.all_to_all(sent_second, ('dom', 'fsdp'), split_axis=0, concat_axis=0,...  14 us
    gather x1, local copies, waits for them, and re-layouts, on_device(): jnp.take(history_first, chosen.reshape(-1), axis=0, mode='clip')  13.5 us
    gather x1, local copies, waits for them, and re-layouts, on_device(): jnp.take(history_second, chosen.reshape(-1), axis=0, mode='clip')  13.4 us
    all_gather x1, blocking collectives, on_device(): counts_all = lax.all_gather(pull_count, 'dom', axis=0, tiled=True)  12.4 us
  transfers between devices with their start and end apart: 10, of which 7 were waited for; matrix products, arithmetic and copies ran while one was open for 10% of the time, Pallas kernels for 8%

profile of v17, /device:TPU:1, one launch (start us, length us, event | category | flops | bytes accessed | tf_op | source)
XLA Modules:
  0.0 364.9 jit_solution(1423638243089915035)
XLA Ops:
  7.2 12.4 %all-gather = s32[8,1,128]{2,1,0:T(1,128)S(1)} all-gather(s32[1,1,128]{2,1,0:T(1,128)} %bitcast.93), channel_id=1, replica_groups=mesh['dom'=8,'fsdp'=16] {'dom'}, dimensions={0}, use_global_device_ids=true | all-gather | bytes 4608 | tf_op jit(solution)/shard_map/all_gather | solution.py:166
  20.5 13.5 %gather_fusion = bf16[512,64,128]{2,1,0:T(8,128)(2,1)} fusion(bf16[128,64,128]{2,1,0:T(8,128)(2,1)S(1)} %copy-done, s32[1024]{0:T(1024)S(1)} %pad_clamp_fusion), kind=kCustom, calls=%fused_computation | custom fusion | bytes 16779264 | tf_op jit(solution)/shard_map/jit(_take)/gather | solution.py:175
  33.9 8.3 %all-to-all-start = ((bf16[128,4,64,128]{3,2,1,0:T(8,128)(2,1)}), bf16[128,4,64,128]{3,2,1,0:T(8,128)(2,1)}, u32[]{:S(2)}, u32[]{:S(2)}) async-start(bf16[128,4,64,128]{3,2,1,0:T(8,128)(2,1)} %bitcast.88), calls=%async_computation | async-start | bytes 16777216 | tf_op jit(solution)/shard_map/all_to_all | solution.py:177
  43.2 13.4 %gather_fusion.1 = bf16[512,64,128]{2,1,0:T(8,128)(2,1)} fusion(bf16[128,64,128]{2,1,0:T(8,128)(2,1)S(1)} %copy-done.2, s32[1024]{0:T(1024)S(1)} %pad_clamp_fusion), kind=kCustom, calls=%fused_computation.1 | custom fusion | bytes 16779264 | tf_op jit(solution)/shard_map/jit(_take)/gather | solution.py:176
  56.6 89.0 %all-to-all-done = bf16[128,4,64,128]{3,2,1,0:T(8,128)(2,1)} async-done(((bf16[128,4,64,128]{3,2,1,0:T(8,128)(2,1)}), bf16[128,4,64,128]{3,2,1,0:T(8,128)(2,1)}, u32[]{:S(2)}, u32[]{:S(2)}) %all-to-all-start) | async-done | bytes 8388640 | tf_op jit(solution)/shard_map/all_to_all | solution.py:177
  145.6 14.0 %all-to-all-start.1 = ((bf16[128,4,64,128]{3,2,1,0:T(8,128)(2,1)}), bf16[128,4,64,128]{3,2,1,0:T(8,128)(2,1)}, u32[]{:S(2)}, u32[]{:S(2)}) async-start(bf16[128,4,64,128]{3,2,1,0:T(8,128)(2,1)} %bitcast.87), calls=%async_computation.1 | async-start | bytes 16777216 | tf_op jit(solution)/shard_map/all_to_all | solution.py:178
  159.6 1.4 collective-permute-start.3
  161.8 7.7 %shard_map.147 = bf16[4,1024,128]{2,1,0:T(8,128)(2,1)} custom-call(s32[4,6]{1,0:T(4,128)} %src_ref.5, s32[4]{0:T(128)} %cnt_ref.5, s32[32]{0:T(128)} %reshape.94.live_ref, bf16[4,1024,128]{2,1,0:T(8,128)(2,1)} %own_ref.1, bf16[8,16,4,64,128]{4,3,2,1,0:T(8,128)(2,1)} %bitcast.4.refs_0_.refs_1_.refs_2_.refs_3_.refs_4_.refs_5_, ...), custom_call_target="tpu_custom_call" | custom-call | flops 805306368 | bytes 14417920 | tf_op jit(solution)/shard_map/pallas_call | solution.py:76
  172.3 68.4 %all-gather.3.cloned.1.call-done = bf16[1024,2176]{1,0:T(8,128)(2,1)} async-done(((bf16[64,2176]{1,0:T(8,128)(2,1)}), bf16[1024,2176]{1,0:T(8,128)(2,1)}) %all-gather.3.cloned.1.call-update) | async-done | bytes 4456464 | tf_op jit(solution)/shard_map/all_gather | solution.py:159
  240.6 3.8 %fusion.17.back_ref = bf16[4,1024,128]{2,1,0:T(8,128)(2,1)} fusion(bf16[4,1024,128]{2,1,0:T(8,128)(2,1)S(1)} %copy-done.5, bf16[1024,2176]{1,0:T(8,128)(2,1)} %all-gather.3.cloned.1.call-done), kind=kOutput, calls=%fused_computation.29 | convolution fusion | flops 1074266112 | bytes 4194304 | tf_op jit(solution)/shard_map/ab,vbn->van/dot_general | solution.py:186
  244.4 12.0 %shard_map.148 = f32[4,1024,128]{2,1,0:T(8,128)} custom-call(s32[4,6]{1,0:T(4,128)} %src_ref.5, s32[4]{0:T(128)} %cnt_ref.5, bf16[4,1024,128]{2,1,0:T(8,128)(2,1)} %fusion.17.back_ref, bf16[4,6,128,128]{3,2,1,0:T(8,128)(2,1)} %refs_6_.3), custom_call_target="tpu_custom_call" | custom-call | flops 805306368 | bytes 3932160 | tf_op jit(solution)/shard_map/pallas_call | solution.py:121
  257.6 4.5 %fusion.15 = (bf16[4,1024,128]{2,1,0:T(8,128)(2,1)}, f32[4,128,1024]{1,2,0:T(8,128)S(1)}) fusion(f32[1024]{0:T(1024)S(1)} %convert_reduce_fusion.1, bf16[4,1024,128]{2,1,0:T(8,128)(2,1)S(1)} %copy-done.4, bf16[1024,2176]{1,0:T(8,128)(2,1)} %all-gather.3.cloned.1.call-done), kind=kOutput, calls=%fused_computation.27 | convolution fusion | flops 1078984704 | bytes 6295552 | tf_op jit(solution)/shard_map/fh,vfn->vhn/dot_general | solution.py:199
  262.1 2.4 fusion.30
  264.6 7.7 %all-to-all-done.1 = bf16[128,4,64,128]{3,2,1,0:T(8,128)(2,1)} async-done(((bf16[128,4,64,128]{3,2,1,0:T(8,128)(2,1)}), bf16[128,4,64,128]{3,2,1,0:T(8,128)(2,1)}, u32[]{:S(2)}, u32[]{:S(2)}) %all-to-all-start.1) | async-done | bytes 8388640 | tf_op jit(solution)/shard_map/all_to_all | solution.py:178
  272.3 7.7 %shard_map.149 = bf16[4,1024,128]{2,1,0:T(8,128)(2,1)} custom-call(s32[4,6]{1,0:T(4,128)} %src_ref.5, s32[4]{0:T(128)} %cnt_ref.5, s32[32]{0:T(128)} %reshape.94.live_ref, bf16[4,1024,128]{2,1,0:T(8,128)(2,1)} %get-tuple-element.32.own_ref, bf16[8,16,4,64,128]{4,3,2,1,0:T(8,128)(2,1)} %bitcast.19.refs_0_.refs_1_.refs_2_.refs_3_.refs_4_.refs_5_, ...), custom_call_target="tpu_custom_call" | custom-call | flops 805306368 | bytes 14417920 | tf_op jit(solution)/shard_map/pallas_call | solution.py:76
  280.0 1.3 constant_dynamic-slice_fusion
  284.5 2.1 fusion.11
  286.6 2.1 fusion.12
  289.0 47.2 %all_to_all.15 = bf16[16,64,1152]{2,1,0:T(8,128)(2,1)S(1)} all-to-all(bf16[16,64,1152]{2,1,0:T(8,128)(2,1)S(1)} %fusion.1), channel_id=1, replica_groups=mesh['dom'=8,'fsdp'=16] {'fsdp'}, dimensions={0} | all-to-all | bytes 4718592 | tf_op jit(solution)/shard_map/all_to_all | solution.py:224
  336.6 1.5 collective-permute-start.4
  338.0 5.5 %collective-permute-done.4 = f32[64,1152]{1,0:T(8,128)S(1)} collective-permute-done((f32[64,1152]{1,0:T(8,128)S(1)}, f32[64,1152]{1,0:T(8,128)S(1)}, u32[]{:S(2)}, u32[]{:S(2)}) %collective-permute-start.4) | collective-permute-done | bytes 294944 | tf_op jit(solution)/shard_map/ppermute | solution.py:227
  343.6 1.8 collective-permute-start.5
  345.4 5.8 %collective-permute-done.5 = f32[64,1152]{1,0:T(8,128)S(1)} collective-permute-done((f32[64,1152]{1,0:T(8,128)S(1)}, f32[64,1152]{1,0:T(8,128)S(1)}, u32[]{:S(2)}, u32[]{:S(2)}) %collective-permute-start.5) | collective-permute-done | bytes 294944 | tf_op jit(solution)/shard_map/ppermute | solution.py:227
  351.3 3.5 collective-permute-start.6
  (52 shorter events, 13.5 us)
Async XLA Ops:
  7.2 13.3 %copy-start = (bf16[128,64,128]{2,1,0:T(8,128)(2,1)S(1)}, bf16[128,64,128]{2,1,0:T(8,128)(2,1)}, u32[]{:S(2)}) copy-start(bf16[128,64,128]{2,1,0:T(8,128)(2,1)} %param.15) | copy-start | bytes 6291460
  33.9 8.4 %copy-start.8 = (bf16[64]{0:T(256)(128)(2,1)S(1)}, bf16[64]{0:T(256)(128)(2,1)}, u32[]{:S(2)}) copy-start(bf16[64]{0:T(256)(128)(2,1)} %param.24) | copy-start | bytes 388
  33.9 8.5 %copy-start.6 = (bf16[64,1024]{1,0:T(8,128)(2,1)S(1)}, bf16[64,1024]{1,0:T(8,128)(2,1)}, u32[]{:S(2)}) copy-start(bf16[64,1024]{1,0:T(8,128)(2,1)} %param.23) | copy-start | bytes 393220
  33.9 8.5 %copy-start.7 = (bf16[64,1024]{1,0:T(8,128)(2,1)S(1)}, bf16[64,1024]{1,0:T(8,128)(2,1)}, u32[]{:S(2)}) copy-start(bf16[64,1024]{1,0:T(8,128)(2,1)} %param.22) | copy-start | bytes 393220
  33.9 9.2 %copy-start.2 = (bf16[128,64,128]{2,1,0:T(8,128)(2,1)S(1)}, bf16[128,64,128]{2,1,0:T(8,128)(2,1)}, u32[]{:S(2)}) copy-start(bf16[128,64,128]{2,1,0:T(8,128)(2,1)} %param.16) | copy-start | bytes 6291460
  33.9 111.7 %all-to-all-start = ((bf16[128,4,64,128]{3,2,1,0:T(8,128)(2,1)}), bf16[128,4,64,128]{3,2,1,0:T(8,128)(2,1)}, u32[]{:S(2)}, u32[]{:S(2)}) async-start(bf16[128,4,64,128]{3,2,1,0:T(8,128)(2,1)} %bitcast.88), calls=%async_computation | async-start | bytes 16777216 | tf_op jit(solution)/shard_map/all_to_all | solution.py:177
  42.3 198.4 %all-gather.3.cloned.1.call-start = ((), (), s32[]{:S(2)}) async-start(), calls=%async_computation.3 | async-start | bytes 4734976 | tf_op jit(solution)/shard_map/all_gather | solution.py:159
  145.6 14.0 %copy-start.5 = (bf16[4,1024,128]{2,1,0:T(8,128)(2,1)S(1)}, bf16[4,1024,128]{2,1,0:T(8,128)(2,1)}, u32[]{:S(2)}) copy-start(bf16[4,1024,128]{2,1,0:T(8,128)(2,1)} %param.25) | copy-start | bytes 3145732
  145.6 126.7 %all-to-all-start.1 = ((bf16[128,4,64,128]{3,2,1,0:T(8,128)(2,1)}), bf16[128,4,64,128]{3,2,1,0:T(8,128)(2,1)}, u32[]{:S(2)}, u32[]{:S(2)}) async-start(bf16[128,4,64,128]{3,2,1,0:T(8,128)(2,1)} %bitcast.87), calls=%async_computation.1 | async-start | bytes 16777216 | tf_op jit(solution)/shard_map/all_to_all | solution.py:178
  159.6 124.1 %collective-permute-start.3 = (bf16[4,1024,128]{2,1,0:T(8,128)(2,1)S(1)}, bf16[4,1024,128]{2,1,0:T(8,128)(2,1)}, u32[]{:S(2)}, u32[]{:S(2)}) collective-permute-start(bf16[4,1024,128]{2,1,0:T(8,128)(2,1)S(1)} %copy-done.5), channel_id=1, source_target_pairs={{0,16},{16,0},{32,48},{48,32},{64,80},{80,64},{96,112},{112,96},{1... | collective-permute-start | bytes 3145736 | tf_op jit(solution)/shard_map/ppermute | solution.py:184
  171.7 114.9 %collective-permute-start = (bf16[4,16,32,128]{3,2,0,1:T(8,128)(2,1)}, bf16[4,16,32,128]{3,2,0,1:T(8,128)(2,1)}, u32[]{:S(2)}, u32[]{:S(2)}) collective-permute-start(bf16[4,16,32,128]{3,2,0,1:T(8,128)(2,1)} %bitcast.86), channel_id=1, source_target_pairs={{0,16},{16,0},{32,48},{48,32},{64,80},{80,64},{96,112},{112,96},{1... | collective-permute-start | bytes 1572872 | tf_op jit(solution)/shard_map/ppermute | solution.py:207
  244.4 13.1 %copy-start.4 = (bf16[4,1024,128]{2,1,0:T(8,128)(2,1)S(1)}, bf16[4,1024,128]{2,1,0:T(8,128)(2,1)}, u32[]{:S(2)}) copy-start(bf16[4,1024,128]{2,1,0:T(8,128)(2,1)} %shard_map.147) | copy-start | bytes 3145732
  257.6 4.5 %copy-start.3 = (f32[4,1024,128]{2,1,0:T(8,128)S(1)}, f32[4,1024,128]{2,1,0:T(8,128)}, u32[]{:S(2)}) copy-start(f32[4,1024,128]{2,1,0:T(8,128)} %shard_map.148) | copy-start | bytes 6291460
  264.5 22.1 %collective-permute-start.1 = (bf16[4,1024,128]{2,1,0:T(8,128)(2,1)S(1)}, bf16[4,1024,128]{2,1,0:T(8,128)(2,1)}, u32[]{:S(2)}, u32[]{:S(2)}) collective-permute-start(bf16[4,1024,128]{2,1,0:T(8,128)(2,1)S(1)} %get-tuple-element.21), channel_id=1, source_target_pairs={{0,16},{16,0},{32,48},{48,32},{64,80},{80,64},{96,112},{112,96},{1... | collective-permute-start | bytes 3145736 | tf_op jit(solution)/shard_map/ppermute | solution.py:207
  282.2 2.3 collective-permute-start.2
  336.6 7.0 %collective-permute-start.4 = (f32[64,1152]{1,0:T(8,128)S(1)}, f32[64,1152]{1,0:T(8,128)S(1)}, u32[]{:S(2)}, u32[]{:S(2)}) collective-permute-start(f32[64,1152]{1,0:T(8,128)S(1)} %convert_reduce_fusion), channel_id=1, source_target_pairs={{0,32},{16,48},{32,0},{48,16},{64,96},{80,112},{96,64},{112,80},{1... | collective-permute-start | bytes 884744 | tf_op jit(solution)/shard_map/ppermute | solution.py:227
  343.6 14.4 %copy-start.1 = (bf16[128,64,128]{2,1,0:T(8,128)(2,1)S(1)}, bf16[128,64,128]{2,1,0:T(8,128)(2,1)}, u32[]{:S(2)}) copy-start(bf16[128,64,128]{2,1,0:T(8,128)(2,1)} %param.15) | copy-start | bytes 6291460
  343.6 7.6 %collective-permute-start.5 = (f32[64,1152]{1,0:T(8,128)S(1)}, f32[64,1152]{1,0:T(8,128)S(1)}, u32[]{:S(2)}, u32[]{:S(2)}) collective-permute-start(f32[64,1152]{1,0:T(8,128)S(1)} %add.72), channel_id=1, source_target_pairs={{0,64},{16,80},{32,96},{48,112},{64,0},{80,16},{96,32},{112,48},{1... | collective-permute-start | bytes 884744 | tf_op jit(solution)/shard_map/ppermute | solution.py:227
  351.3 4.7 %collective-permute-start.6 = (f32[64,1152]{1,0:T(8,128)S(1)}, f32[64,1152]{1,0:T(8,128)S(1)}, u32[]{:S(2)}, u32[]{:S(2)}) collective-permute-start(f32[64,1152]{1,0:T(8,128)S(1)} %add.73), channel_id=1, source_target_pairs={{0,16},{16,0},{32,48},{48,32},{64,80},{80,64},{96,112},{112,96},{1... | collective-permute-start | bytes 884744 | tf_op jit(solution)/shard_map/ppermute | solution.py:228
Sparse Core Ops, SparseCore 0:
  45.2 195.3 all-gather.2

commit v18 on v17

--- a/solution.py
+++ b/solution.py
@@ -58,8 +58,14 @@
 
     def pulled_map(j):
         def index(v, k, src_ref, cnt_ref, live_ref):
-            s = jnp.clip(src_ref[v, eff(v, per * k + j, cnt_ref)] - nb, 0, cap * dom - 1)
-            return (s % dom, 0, s // dom, 0, 0)
+            t = per * k + j
+            pick = jnp.int32(0)
+            for earlier in range(nb):
+                s = src_ref[earlier, t]
+                use = (earlier <= v) & (t < cnt_ref[earlier]) & (s >= nb)
+                pick = jnp.where(use, s - nb, pick)
+            pick = jnp.clip(pick, 0, cap * dom - 1)
+            return (pick % dom, 0, pick // dom, 0, 0)
 
         return index
 

time: 366 us -> 367 us (level)
  Pallas kernels: 27.4 us -> 19.9 us
  blocking collectives: 59.5 us -> 65.8 us
  waiting for transfers between devices: 178 us -> 182 us
    all_to_all x1, blocking collectives: 47.2 us -> 53.4 us  [on_device(): lax.all_to_all(packed_terms.astype(jnp.bfloat16), 'fsdp', split_axis=0, c...]
    all_gather x1, waiting for transfers between devices: 68.4 us -> 73.5 us  [on_device(): lax.all_gather(jnp.concatenate([w_first, w_second, bias_cols], axis=1), '...]
    pallas_call x1, Pallas kernels: 12 us -> 6.98 us  [spread_back(): pl.pallas_call(functools.partial(_spread_kernel, nb), grid_spec=grid_spec...]
    all_to_all x1, waiting for transfers between devices: 7.73 us -> 3.82 us  [on_device(): lax.all_to_all(sent_second, ('dom', 'fsdp'), split_axis=0, concat_axis=0,...]
  transfers between devices with their start and end apart: 10 -> 10, of which waited for: 7 -> 7; matrix products, arithmetic and copies ran while one was open for 10% -> 9% of each run, Pallas kernels for 8% -> 5%
where the time goes in v18:
time: 367 us; the launch traced here: 368 us
  waiting for transfers between devices  182 us (50%)
  blocking collectives  65.8 us (18%)
  local copies, waits for them, and re-layouts  33.1 us (9%)
  starting transfers between devices  32.2 us (9%)
  Pallas kernels  19.9 us (5%)
  between operations  14.3 us (4%)
  matrix products  14.1 us (4%)
  other arithmetic  6.87 us (2%)
    all_to_all x1, waiting for transfers between devices, on_device(): lax.all_to_all(sent_first, ('dom', 'fsdp'), split_axis=0, concat_axis=0,...  89 us
    all_gather x1, waiting for transfers between devices, on_device(): lax.all_gather(jnp.concatenate([w_first, w_second, bias_cols], axis=1), '...  73.5 us
    all_to_all x1, blocking collectives, on_device(): lax.all_to_all(packed_terms.astype(jnp.bfloat16), 'fsdp', split_axis=0, c...  53.4 us
    all_to_all x1, starting transfers between devices, on_device(): lax.all_to_all(sent_second, ('dom', 'fsdp'), split_axis=0, concat_axis=0,...  14 us
    ppermute x2, waiting for transfers between devices, on_device(): lax.ppermute(shard, 'dom', [(d, d ^ flip) for d in range(dom_size)])  13.6 us
    gather x1, local copies, waits for them, and re-layouts, on_device(): jnp.take(history_first, chosen.reshape(-1), axis=0, mode='clip')  13.5 us
    gather x1, local copies, waits for them, and re-layouts, on_device(): jnp.take(history_second, chosen.reshape(-1), axis=0, mode='clip')  13.4 us
    pallas_call x2, Pallas kernels, aggregate(): pl.pallas_call(functools.partial(_agg_kernel, nb, steps - 1, per), grid_s...  12.9 us
  transfers between devices with their start and end apart: 10, of which 7 were waited for; matrix products, arithmetic and copies ran while one was open for 9% of the time, Pallas kernels for 5%

profile of v18, /device:TPU:1, one launch (start us, length us, event | category | flops | bytes accessed | tf_op | source)
XLA Modules:
  0.0 367.9 jit_solution(10486856661018367874)
XLA Ops:
  7.2 12.4 %all-gather = s32[8,1,128]{2,1,0:T(1,128)S(1)} all-gather(s32[1,1,128]{2,1,0:T(1,128)} %bitcast.93), channel_id=1, replica_groups=mesh['dom'=8,'fsdp'=16] {'dom'}, dimensions={0}, use_global_device_ids=true | all-gather | bytes 4608 | tf_op jit(solution)/shard_map/all_gather | solution.py:172
  20.5 13.5 %gather_fusion = bf16[512,64,128]{2,1,0:T(8,128)(2,1)} fusion(bf16[128,64,128]{2,1,0:T(8,128)(2,1)S(1)} %copy-done, s32[1024]{0:T(1024)S(1)} %pad_clamp_fusion), kind=kCustom, calls=%fused_computation | custom fusion | bytes 16779264 | tf_op jit(solution)/shard_map/jit(_take)/gather | solution.py:181
  34.0 8.3 %all-to-all-start = ((bf16[128,4,64,128]{3,2,1,0:T(8,128)(2,1)}), bf16[128,4,64,128]{3,2,1,0:T(8,128)(2,1)}, u32[]{:S(2)}, u32[]{:S(2)}) async-start(bf16[128,4,64,128]{3,2,1,0:T(8,128)(2,1)} %bitcast.88), calls=%async_computation | async-start | bytes 16777216 | tf_op jit(solution)/shard_map/all_to_all | solution.py:183
  43.2 13.4 %gather_fusion.1 = bf16[512,64,128]{2,1,0:T(8,128)(2,1)} fusion(bf16[128,64,128]{2,1,0:T(8,128)(2,1)S(1)} %copy-done.2, s32[1024]{0:T(1024)S(1)} %pad_clamp_fusion), kind=kCustom, calls=%fused_computation.1 | custom fusion | bytes 16779264 | tf_op jit(solution)/shard_map/jit(_take)/gather | solution.py:182
  56.6 89.0 %all-to-all-done = bf16[128,4,64,128]{3,2,1,0:T(8,128)(2,1)} async-done(((bf16[128,4,64,128]{3,2,1,0:T(8,128)(2,1)}), bf16[128,4,64,128]{3,2,1,0:T(8,128)(2,1)}, u32[]{:S(2)}, u32[]{:S(2)}) %all-to-all-start) | async-done | bytes 8388640 | tf_op jit(solution)/shard_map/all_to_all | solution.py:183
  145.6 14.0 %all-to-all-start.1 = ((bf16[128,4,64,128]{3,2,1,0:T(8,128)(2,1)}), bf16[128,4,64,128]{3,2,1,0:T(8,128)(2,1)}, u32[]{:S(2)}, u32[]{:S(2)}) async-start(bf16[128,4,64,128]{3,2,1,0:T(8,128)(2,1)} %bitcast.87), calls=%async_computation.1 | async-start | bytes 16777216 | tf_op jit(solution)/shard_map/all_to_all | solution.py:184
  159.6 1.4 collective-permute-start.3
  161.8 6.5 %shard_map.147 = bf16[4,1024,128]{2,1,0:T(8,128)(2,1)} custom-call(s32[4,6]{1,0:T(4,128)} %src_ref.5, s32[4]{0:T(128)} %cnt_ref.5, s32[32]{0:T(128)} %reshape.94.live_ref, bf16[4,1024,128]{2,1,0:T(8,128)(2,1)} %own_ref.1, bf16[8,16,4,64,128]{4,3,2,1,0:T(8,128)(2,1)} %bitcast.4.refs_0_.refs_1_.refs_2_.refs_3_.refs_4_.refs_5_, ...), custom_call_target="tpu_custom_call" | custom-call | flops 805306368 | bytes 14417920 | tf_op jit(solution)/shard_map/pallas_call | solution.py:82
  168.3 1.3 constant_dynamic-slice_fusion.2
  170.7 73.5 %all-gather.3.cloned.1.call-done = bf16[1024,2176]{1,0:T(8,128)(2,1)} async-done(((bf16[64,2176]{1,0:T(8,128)(2,1)}), bf16[1024,2176]{1,0:T(8,128)(2,1)}) %all-gather.3.cloned.1.call-update) | async-done | bytes 4456464 | tf_op jit(solution)/shard_map/all_gather | solution.py:165
  244.2 3.8 %fusion.17.back_ref = bf16[4,1024,128]{2,1,0:T(8,128)(2,1)} fusion(bf16[4,1024,128]{2,1,0:T(8,128)(2,1)S(1)} %copy-done.5, bf16[1024,2176]{1,0:T(8,128)(2,1)} %all-gather.3.cloned.1.call-done), kind=kOutput, calls=%fused_computation.29 | convolution fusion | flops 1074266112 | bytes 4194304 | tf_op jit(solution)/shard_map/ab,vbn->van/dot_general | solution.py:192
  248.0 7.0 %shard_map.148 = f32[4,1024,128]{2,1,0:T(8,128)} custom-call(s32[4,6]{1,0:T(4,128)} %src_ref.5, s32[4]{0:T(128)} %cnt_ref.5, bf16[4,1024,128]{2,1,0:T(8,128)(2,1)} %fusion.17.back_ref, bf16[4,6,128,128]{3,2,1,0:T(8,128)(2,1)} %refs_6_.3), custom_call_target="tpu_custom_call" | custom-call | flops 805306368 | bytes 3932160 | tf_op jit(solution)/shard_map/pallas_call | solution.py:127
  256.1 4.5 %fusion.15 = (bf16[4,1024,128]{2,1,0:T(8,128)(2,1)}, f32[4,128,1024]{1,2,0:T(8,128)S(1)}) fusion(f32[1024]{0:T(1024)S(1)} %convert_reduce_fusion.1, bf16[4,1024,128]{2,1,0:T(8,128)(2,1)S(1)} %copy-done.4, bf16[1024,2176]{1,0:T(8,128)(2,1)} %all-gather.3.cloned.1.call-done), kind=kOutput, calls=%fused_computation.27 | convolution fusion | flops 1078984704 | bytes 6295552 | tf_op jit(solution)/shard_map/fh,vfn->vhn/dot_general | solution.py:205
  260.6 2.4 fusion.30
  263.0 3.5 collective-permute-start.1
  266.5 3.8 %all-to-all-done.1 = bf16[128,4,64,128]{3,2,1,0:T(8,128)(2,1)} async-done(((bf16[128,4,64,128]{3,2,1,0:T(8,128)(2,1)}), bf16[128,4,64,128]{3,2,1,0:T(8,128)(2,1)}, u32[]{:S(2)}, u32[]{:S(2)}) %all-to-all-start.1) | async-done | bytes 8388640 | tf_op jit(solution)/shard_map/all_to_all | solution.py:184
  270.3 6.5 %shard_map.149 = bf16[4,1024,128]{2,1,0:T(8,128)(2,1)} custom-call(s32[4,6]{1,0:T(4,128)} %src_ref.5, s32[4]{0:T(128)} %cnt_ref.5, s32[32]{0:T(128)} %reshape.94.live_ref, bf16[4,1024,128]{2,1,0:T(8,128)(2,1)} %get-tuple-element.32.own_ref, bf16[8,16,4,64,128]{4,3,2,1,0:T(8,128)(2,1)} %bitcast.19.refs_0_.refs_1_.refs_2_.refs_3_.refs_4_.refs_5_, ...), custom_call_target="tpu_custom_call" | custom-call | flops 805306368 | bytes 14417920 | tf_op jit(solution)/shard_map/pallas_call | solution.py:82
  276.7 1.3 constant_dynamic-slice_fusion
  281.2 2.1 fusion.11
  283.3 2.1 fusion.12
  285.7 53.4 %all_to_all.15 = bf16[16,64,1152]{2,1,0:T(8,128)(2,1)S(1)} all-to-all(bf16[16,64,1152]{2,1,0:T(8,128)(2,1)S(1)} %fusion.1), channel_id=1, replica_groups=mesh['dom'=8,'fsdp'=16] {'fsdp'}, dimensions={0} | all-to-all | bytes 4718592 | tf_op jit(solution)/shard_map/all_to_all | solution.py:230
  339.6 6.9 %collective-permute-done.4 = f32[64,1152]{1,0:T(8,128)S(1)} collective-permute-done((f32[64,1152]{1,0:T(8,128)S(1)}, f32[64,1152]{1,0:T(8,128)S(1)}, u32[]{:S(2)}, u32[]{:S(2)}) %collective-permute-start.4) | collective-permute-done | bytes 294944 | tf_op jit(solution)/shard_map/ppermute | solution.py:233
  347.0 6.7 %collective-permute-done.5 = f32[64,1152]{1,0:T(8,128)S(1)} collective-permute-done((f32[64,1152]{1,0:T(8,128)S(1)}, f32[64,1152]{1,0:T(8,128)S(1)}, u32[]{:S(2)}, u32[]{:S(2)}) %collective-permute-start.5) | collective-permute-done | bytes 294944 | tf_op jit(solution)/shard_map/ppermute | solution.py:233
  353.8 4.1 %collective-permute-start.6 = (f32[64,1152]{1,0:T(8,128)S(1)}, f32[64,1152]{1,0:T(8,128)S(1)}, u32[]{:S(2)}, u32[]{:S(2)}) collective-permute-start(f32[64,1152]{1,0:T(8,128)S(1)} %add.73), channel_id=1, source_target_pairs={{0,16},{16,0},{32,48},{48,32},{64,80},{80,64},{96,112},{112,96},{1... | collective-permute-start | bytes 884744 | tf_op jit(solution)/shard_map/ppermute | solution.py:234
  (52 shorter events, 12.3 us)
Async XLA Ops:
  7.2 13.3 %copy-start = (bf16[128,64,128]{2,1,0:T(8,128)(2,1)S(1)}, bf16[128,64,128]{2,1,0:T(8,128)(2,1)}, u32[]{:S(2)}) copy-start(bf16[128,64,128]{2,1,0:T(8,128)(2,1)} %param.15) | copy-start | bytes 6291460
  33.9 8.4 %copy-start.8 = (bf16[64]{0:T(256)(128)(2,1)S(1)}, bf16[64]{0:T(256)(128)(2,1)}, u32[]{:S(2)}) copy-start(bf16[64]{0:T(256)(128)(2,1)} %param.24) | copy-start | bytes 388
  33.9 8.4 %copy-start.6 = (bf16[64,1024]{1,0:T(8,128)(2,1)S(1)}, bf16[64,1024]{1,0:T(8,128)(2,1)}, u32[]{:S(2)}) copy-start(bf16[64,1024]{1,0:T(8,128)(2,1)} %param.23) | copy-start | bytes 393220
  33.9 8.4 %copy-start.7 = (bf16[64,1024]{1,0:T(8,128)(2,1)S(1)}, bf16[64,1024]{1,0:T(8,128)(2,1)}, u32[]{:S(2)}) copy-start(bf16[64,1024]{1,0:T(8,128)(2,1)} %param.22) | copy-start | bytes 393220
  33.9 9.2 %copy-start.2 = (bf16[128,64,128]{2,1,0:T(8,128)(2,1)S(1)}, bf16[128,64,128]{2,1,0:T(8,128)(2,1)}, u32[]{:S(2)}) copy-start(bf16[128,64,128]{2,1,0:T(8,128)(2,1)} %param.16) | copy-start | bytes 6291460
  34.0 111.7 %all-to-all-start = ((bf16[128,4,64,128]{3,2,1,0:T(8,128)(2,1)}), bf16[128,4,64,128]{3,2,1,0:T(8,128)(2,1)}, u32[]{:S(2)}, u32[]{:S(2)}) async-start(bf16[128,4,64,128]{3,2,1,0:T(8,128)(2,1)} %bitcast.88), calls=%async_computation | async-start | bytes 16777216 | tf_op jit(solution)/shard_map/all_to_all | solution.py:183
  42.2 201.9 %all-gather.3.cloned.1.call-start = ((), (), s32[]{:S(2)}) async-start(), calls=%async_computation.3 | async-start | bytes 4734976 | tf_op jit(solution)/shard_map/all_gather | solution.py:165
  145.6 14.0 %copy-start.5 = (bf16[4,1024,128]{2,1,0:T(8,128)(2,1)S(1)}, bf16[4,1024,128]{2,1,0:T(8,128)(2,1)}, u32[]{:S(2)}) copy-start(bf16[4,1024,128]{2,1,0:T(8,128)(2,1)} %param.25) | copy-start | bytes 3145732
  145.6 124.7 %all-to-all-start.1 = ((bf16[128,4,64,128]{3,2,1,0:T(8,128)(2,1)}), bf16[128,4,64,128]{3,2,1,0:T(8,128)(2,1)}, u32[]{:S(2)}, u32[]{:S(2)}) async-start(bf16[128,4,64,128]{3,2,1,0:T(8,128)(2,1)} %bitcast.87), calls=%async_computation.1 | async-start | bytes 16777216 | tf_op jit(solution)/shard_map/all_to_all | solution.py:184
  159.6 121.0 %collective-permute-start.3 = (bf16[4,1024,128]{2,1,0:T(8,128)(2,1)S(1)}, bf16[4,1024,128]{2,1,0:T(8,128)(2,1)}, u32[]{:S(2)}, u32[]{:S(2)}) collective-permute-start(bf16[4,1024,128]{2,1,0:T(8,128)(2,1)S(1)} %copy-done.5), channel_id=1, source_target_pairs={{0,16},{16,0},{32,48},{48,32},{64,80},{80,64},{96,112},{112,96},{1... | collective-permute-start | bytes 3145736 | tf_op jit(solution)/shard_map/ppermute | solution.py:190
  170.4 112.9 %collective-permute-start = (bf16[4,16,32,128]{3,2,0,1:T(8,128)(2,1)}, bf16[4,16,32,128]{3,2,0,1:T(8,128)(2,1)}, u32[]{:S(2)}, u32[]{:S(2)}) collective-permute-start(bf16[4,16,32,128]{3,2,0,1:T(8,128)(2,1)} %bitcast.86), channel_id=1, source_target_pairs={{0,16},{16,0},{32,48},{48,32},{64,80},{80,64},{96,112},{112,96},{1... | collective-permute-start | bytes 1572872 | tf_op jit(solution)/shard_map/ppermute | solution.py:213
  248.0 8.1 %copy-start.4 = (bf16[4,1024,128]{2,1,0:T(8,128)(2,1)S(1)}, bf16[4,1024,128]{2,1,0:T(8,128)(2,1)}, u32[]{:S(2)}) copy-start(bf16[4,1024,128]{2,1,0:T(8,128)(2,1)} %shard_map.147) | copy-start | bytes 3145732
  256.1 4.5 %copy-start.3 = (f32[4,1024,128]{2,1,0:T(8,128)S(1)}, f32[4,1024,128]{2,1,0:T(8,128)}, u32[]{:S(2)}) copy-start(f32[4,1024,128]{2,1,0:T(8,128)} %shard_map.148) | copy-start | bytes 6291460
  263.0 20.3 %collective-permute-start.1 = (bf16[4,1024,128]{2,1,0:T(8,128)(2,1)S(1)}, bf16[4,1024,128]{2,1,0:T(8,128)(2,1)}, u32[]{:S(2)}, u32[]{:S(2)}) collective-permute-start(bf16[4,1024,128]{2,1,0:T(8,128)(2,1)S(1)} %get-tuple-element.21), channel_id=1, source_target_pairs={{0,16},{16,0},{32,48},{48,32},{64,80},{80,64},{96,112},{112,96},{1... | collective-permute-start | bytes 3145736 | tf_op jit(solution)/shard_map/ppermute | solution.py:213
  278.9 2.3 collective-permute-start.2
  339.5 7.0 %collective-permute-start.4 = (f32[64,1152]{1,0:T(8,128)S(1)}, f32[64,1152]{1,0:T(8,128)S(1)}, u32[]{:S(2)}, u32[]{:S(2)}) collective-permute-start(f32[64,1152]{1,0:T(8,128)S(1)} %convert_reduce_fusion), channel_id=1, source_target_pairs={{0,32},{16,48},{32,0},{48,16},{64,96},{80,112},{96,64},{112,80},{1... | collective-permute-start | bytes 884744 | tf_op jit(solution)/shard_map/ppermute | solution.py:233
  346.5 14.6 %copy-start.1 = (bf16[128,64,128]{2,1,0:T(8,128)(2,1)S(1)}, bf16[128,64,128]{2,1,0:T(8,128)(2,1)}, u32[]{:S(2)}) copy-start(bf16[128,64,128]{2,1,0:T(8,128)(2,1)} %param.15) | copy-start | bytes 6291460
  346.6 7.2 %collective-permute-start.5 = (f32[64,1152]{1,0:T(8,128)S(1)}, f32[64,1152]{1,0:T(8,128)S(1)}, u32[]{:S(2)}, u32[]{:S(2)}) collective-permute-start(f32[64,1152]{1,0:T(8,128)S(1)} %add.72), channel_id=1, source_target_pairs={{0,64},{16,80},{32,96},{48,112},{64,0},{80,16},{96,32},{112,48},{1... | collective-permute-start | bytes 884744 | tf_op jit(solution)/shard_map/ppermute | solution.py:233
  353.8 5.3 %collective-permute-start.6 = (f32[64,1152]{1,0:T(8,128)S(1)}, f32[64,1152]{1,0:T(8,128)S(1)}, u32[]{:S(2)}, u32[]{:S(2)}) collective-permute-start(f32[64,1152]{1,0:T(8,128)S(1)} %add.73), channel_id=1, source_target_pairs={{0,16},{16,0},{32,48},{48,32},{64,80},{80,64},{96,112},{112,96},{1... | collective-permute-start | bytes 884744 | tf_op jit(solution)/shard_map/ppermute | solution.py:234
Sparse Core Ops, SparseCore 0:
  45.2 198.9 all-gather.2

commit v19 on v17

--- a/solution.py
+++ b/solution.py
@@ -84,22 +84,23 @@
     )(tile_src, tile_count, slot_live, own, *([pulled] * per), tile_values)
 
 
-def _spread_kernel(own_count, src_ref, cnt_ref, back_ref, tile_ref, out_ref):
+def _spread_kernel(own_count, tiles, src_ref, cnt_ref, back_ref, tile_ref, out_ref):
     v = pl.program_id(0)
-    t = pl.program_id(1)
-
-    @pl.when((v == 0) & (t == 0))
+
+    @pl.when(v == 0)
     def _():
         out_ref[...] = jnp.zeros_like(out_ref)
 
-    src = src_ref[v, t]
-
-    @pl.when((t < cnt_ref[v]) & (src < own_count))
-    def _():
-        term = lax.dot_general(
-            back_ref[0], tile_ref[0, 0], (((1,), (1,)), ((), ())), preferred_element_type=jnp.float32
-        )
-        out_ref[src] = out_ref[src] + term
+    for t in range(tiles):
+        src = src_ref[v, t]
+
+        @pl.when((t < cnt_ref[v]) & (src < own_count))
+        def _():
+            term = lax.dot_general(
+                back_ref[0], tile_ref[0, t], (((1,), (1,)), ((), ())), preferred_element_type=jnp.float32
+            )
+            target = jnp.clip(src, 0, own_count - 1)
+            out_ref[target] = out_ref[target] + term
 
 
 def spread_back(back_second, tile_src, tile_count, tile_values):
@@ -111,18 +112,18 @@
 
     grid_spec = pltpu.PrefetchScalarGridSpec(
         num_scalar_prefetch=2,
-        grid=(nb, tiles),
+        grid=(nb,),
         in_specs=[
-            pl.BlockSpec((1, width, blk), lambda v, t, s, c: (v, 0, 0)),
-            pl.BlockSpec((1, 1, blk, blk), lambda v, t, s, c: (v, eff(v, t, c), 0, 0)),
+            pl.BlockSpec((1, width, blk), lambda v, s, c: (v, 0, 0)),
+            pl.BlockSpec((1, tiles, blk, blk), lambda v, s, c: (v, 0, 0, 0)),
         ],
-        out_specs=pl.BlockSpec((nb, width, blk), lambda v, t, s, c: (0, 0, 0)),
+        out_specs=pl.BlockSpec((nb, width, blk), lambda v, s, c: (0, 0, 0)),
     )
     return pl.pallas_call(
-        functools.partial(_spread_kernel, nb),
+        functools.partial(_spread_kernel, nb, tiles),
         grid_spec=grid_spec,
         out_shape=jax.ShapeDtypeStruct(back_second.shape, jnp.float32),
-        compiler_params=pltpu.CompilerParams(dimension_semantics=("arbitrary", "arbitrary")),
+        compiler_params=pltpu.CompilerParams(dimension_semantics=("arbitrary",)),
         cost_estimate=pl.CostEstimate(
             flops=2 * nb * tiles * width * blk * blk,
             transcendentals=0,

time: 366 us -> 361 us (0.986)
  waiting for transfers between devices: 178 us -> 187 us
  Pallas kernels: 27.4 us -> 21.1 us
  blocking collectives: 59.5 us -> 53.5 us
    pallas_call x1, Pallas kernels: 12 us -> 4.74 us  [spread_back(): pl.pallas_call(functools.partial(_spread_kernel, nb, tiles), grid_spec=gr...]
    all_to_all x1, waiting for transfers between devices: 7.73 us -> 14.8 us  [on_device(): lax.all_to_all(sent_second, ('dom', 'fsdp'), split_axis=0, concat_axis=0,...]
    all_to_all x1, blocking collectives: 47.2 us -> 41.2 us  [on_device(): lax.all_to_all(packed_terms.astype(jnp.bfloat16), 'fsdp', split_axis=0, c...]
  transfers between devices with their start and end apart: 10 -> 10, of which waited for: 7 -> 7; matrix products, arithmetic and copies ran while one was open for 10% -> 10% of each run, Pallas kernels for 8% -> 6%
where the time goes in v19:
time: 361 us
  waiting for transfers between devices  187 us (52%)
  blocking collectives  53.5 us (15%)
  local copies, waits for them, and re-layouts  33.1 us (9%)
  starting transfers between devices  31.3 us (9%)
  Pallas kernels  21.1 us (6%)
  between operations  14.2 us (4%)
  matrix products  14.1 us (4%)
  other arithmetic  6.87 us (2%)
    all_to_all x1, waiting for transfers between devices, on_device(): lax.all_to_all(sent_first, ('dom', 'fsdp'), split_axis=0, concat_axis=0,...  89 us
    all_gather x1, waiting for transfers between devices, on_device(): lax.all_gather(jnp.concatenate([w_first, w_second, bias_cols], axis=1), '...  68.2 us
    all_to_all x1, blocking collectives, on_device(): lax.all_to_all(packed_terms.astype(jnp.bfloat16), 'fsdp', split_axis=0, c...  41.2 us
    pallas_call x2, Pallas kernels, aggregate(): pl.pallas_call(functools.partial(_agg_kernel, nb, steps - 1, per), grid_s...  16.4 us
    all_to_all x1, waiting for transfers between devices, on_device(): lax.all_to_all(sent_second, ('dom', 'fsdp'), split_axis=0, concat_axis=0,...  14.8 us
    all_to_all x1, starting transfers between devices, on_device(): lax.all_to_all(sent_second, ('dom', 'fsdp'), split_axis=0, concat_axis=0,...  14.1 us
    gather x1, local copies, waits for them, and re-layouts, on_device(): jnp.take(history_first, chosen.reshape(-1), axis=0, mode='clip')  13.5 us
    gather x1, local copies, waits for them, and re-layouts, on_device(): jnp.take(history_second, chosen.reshape(-1), axis=0, mode='clip')  13.4 us
  transfers between devices with their start and end apart: 10, of which 7 were waited for; matrix products, arithmetic and copies ran while one was open for 10% of the time, Pallas kernels for 6%

profile of v19, /device:TPU:1, one launch (start us, length us, event | category | flops | bytes accessed | tf_op | source)
XLA Modules:
  0.0 361.0 jit_solution(9203818540471572498)
XLA Ops:
  7.2 12.4 %all-gather = s32[8,1,128]{2,1,0:T(1,128)S(1)} all-gather(s32[1,1,128]{2,1,0:T(1,128)} %bitcast.93), channel_id=1, replica_groups=mesh['dom'=8,'fsdp'=16] {'dom'}, dimensions={0}, use_global_device_ids=true | all-gather | bytes 4608 | tf_op jit(solution)/shard_map/all_gather | solution.py:167
  20.5 13.5 %gather_fusion = bf16[512,64,128]{2,1,0:T(8,128)(2,1)} fusion(bf16[128,64,128]{2,1,0:T(8,128)(2,1)S(1)} %copy-done, s32[1024]{0:T(1024)S(1)} %pad_clamp_fusion), kind=kCustom, calls=%fused_computation | custom fusion | bytes 16779264 | tf_op jit(solution)/shard_map/jit(_take)/gather | solution.py:176
  33.9 8.3 %all-to-all-start = ((bf16[128,4,64,128]{3,2,1,0:T(8,128)(2,1)}), bf16[128,4,64,128]{3,2,1,0:T(8,128)(2,1)}, u32[]{:S(2)}, u32[]{:S(2)}) async-start(bf16[128,4,64,128]{3,2,1,0:T(8,128)(2,1)} %bitcast.88), calls=%async_computation | async-start | bytes 16777216 | tf_op jit(solution)/shard_map/all_to_all | solution.py:178
  43.2 13.4 %gather_fusion.1 = bf16[512,64,128]{2,1,0:T(8,128)(2,1)} fusion(bf16[128,64,128]{2,1,0:T(8,128)(2,1)S(1)} %copy-done.2, s32[1024]{0:T(1024)S(1)} %pad_clamp_fusion), kind=kCustom, calls=%fused_computation.1 | custom fusion | bytes 16779264 | tf_op jit(solution)/shard_map/jit(_take)/gather | solution.py:177
  56.6 89.0 %all-to-all-done = bf16[128,4,64,128]{3,2,1,0:T(8,128)(2,1)} async-done(((bf16[128,4,64,128]{3,2,1,0:T(8,128)(2,1)}), bf16[128,4,64,128]{3,2,1,0:T(8,128)(2,1)}, u32[]{:S(2)}, u32[]{:S(2)}) %all-to-all-start) | async-done | bytes 8388640 | tf_op jit(solution)/shard_map/all_to_all | solution.py:178
  145.6 14.1 %all-to-all-start.1 = ((bf16[128,4,64,128]{3,2,1,0:T(8,128)(2,1)}), bf16[128,4,64,128]{3,2,1,0:T(8,128)(2,1)}, u32[]{:S(2)}, u32[]{:S(2)}) async-start(bf16[128,4,64,128]{3,2,1,0:T(8,128)(2,1)} %bitcast.87), calls=%async_computation.1 | async-start | bytes 16777216 | tf_op jit(solution)/shard_map/all_to_all | solution.py:179
  159.7 1.4 collective-permute-start.3
  161.9 8.2 %shard_map.147 = bf16[4,1024,128]{2,1,0:T(8,128)(2,1)} custom-call(s32[4,6]{1,0:T(4,128)} %src_ref.5, s32[4]{0:T(128)} %cnt_ref.5, s32[32]{0:T(128)} %reshape.94.live_ref, bf16[4,1024,128]{2,1,0:T(8,128)(2,1)} %own_ref.1, bf16[8,16,4,64,128]{4,3,2,1,0:T(8,128)(2,1)} %bitcast.4.refs_0_.refs_1_.refs_2_.refs_3_.refs_4_.refs_5_, ...), custom_call_target="tpu_custom_call" | custom-call | flops 805306368 | bytes 14417920 | tf_op jit(solution)/shard_map/pallas_call | solution.py:76
  170.1 1.3 constant_dynamic-slice_fusion.2
  172.2 68.2 %all-gather.3.cloned.1.call-done = bf16[1024,2176]{1,0:T(8,128)(2,1)} async-done(((bf16[64,2176]{1,0:T(8,128)(2,1)}), bf16[1024,2176]{1,0:T(8,128)(2,1)}) %all-gather.3.cloned.1.call-update) | async-done | bytes 4456464 | tf_op jit(solution)/shard_map/all_gather | solution.py:160
  240.4 3.8 %fusion.17.back_ref = bf16[4,1024,128]{2,1,0:T(8,128)(2,1)} fusion(bf16[4,1024,128]{2,1,0:T(8,128)(2,1)S(1)} %copy-done.5, bf16[1024,2176]{1,0:T(8,128)(2,1)} %all-gather.3.cloned.1.call-done), kind=kOutput, calls=%fused_computation.29 | convolution fusion | flops 1074266112 | bytes 4194304 | tf_op jit(solution)/shard_map/ab,vbn->van/dot_general | solution.py:187
  244.2 4.7 %shard_map.148 = f32[4,1024,128]{2,1,0:T(8,128)} custom-call(s32[4,6]{1,0:T(4,128)} %src_ref.5, s32[4]{0:T(128)} %cnt_ref.5, bf16[4,1024,128]{2,1,0:T(8,128)(2,1)} %fusion.17.back_ref, bf16[4,6,128,128]{3,2,1,0:T(8,128)(2,1)} %refs_6_.3), custom_call_target="tpu_custom_call" | custom-call | flops 805306368 | bytes 3932160 | tf_op jit(solution)/shard_map/pallas_call | solution.py:122
  250.1 4.5 %fusion.15 = (bf16[4,1024,128]{2,1,0:T(8,128)(2,1)}, f32[4,128,1024]{1,2,0:T(8,128)S(1)}) fusion(f32[1024]{0:T(1024)S(1)} %convert_reduce_fusion.1, bf16[4,1024,128]{2,1,0:T(8,128)(2,1)S(1)} %copy-done.4, bf16[1024,2176]{1,0:T(8,128)(2,1)} %all-gather.3.cloned.1.call-done), kind=kOutput, calls=%fused_computation.27 | convolution fusion | flops 1078984704 | bytes 6295552 | tf_op jit(solution)/shard_map/fh,vfn->vhn/dot_general | solution.py:200
  254.6 2.4 fusion.30
  258.0 14.8 %all-to-all-done.1 = bf16[128,4,64,128]{3,2,1,0:T(8,128)(2,1)} async-done(((bf16[128,4,64,128]{3,2,1,0:T(8,128)(2,1)}), bf16[128,4,64,128]{3,2,1,0:T(8,128)(2,1)}, u32[]{:S(2)}, u32[]{:S(2)}) %all-to-all-start.1) | async-done | bytes 8388640 | tf_op jit(solution)/shard_map/all_to_all | solution.py:179
  272.8 8.2 %shard_map.149 = bf16[4,1024,128]{2,1,0:T(8,128)(2,1)} custom-call(s32[4,6]{1,0:T(4,128)} %src_ref.5, s32[4]{0:T(128)} %cnt_ref.5, s32[32]{0:T(128)} %reshape.94.live_ref, bf16[4,1024,128]{2,1,0:T(8,128)(2,1)} %get-tuple-element.32.own_ref, bf16[8,16,4,64,128]{4,3,2,1,0:T(8,128)(2,1)} %bitcast.19.refs_0_.refs_1_.refs_2_.refs_3_.refs_4_.refs_5_, ...), custom_call_target="tpu_custom_call" | custom-call | flops 805306368 | bytes 14417920 | tf_op jit(solution)/shard_map/pallas_call | solution.py:76
  281.0 1.3 constant_dynamic-slice_fusion
  285.4 2.1 fusion.11
  287.6 2.1 fusion.12
  290.0 41.2 %all_to_all.15 = bf16[16,64,1152]{2,1,0:T(8,128)(2,1)S(1)} all-to-all(bf16[16,64,1152]{2,1,0:T(8,128)(2,1)S(1)} %fusion.1), channel_id=1, replica_groups=mesh['dom'=8,'fsdp'=16] {'fsdp'}, dimensions={0} | all-to-all | bytes 4718592 | tf_op jit(solution)/shard_map/all_to_all | solution.py:225
  331.5 2.4 collective-permute-start.4
  333.9 5.8 %collective-permute-done.4 = f32[64,1152]{1,0:T(8,128)S(1)} collective-permute-done((f32[64,1152]{1,0:T(8,128)S(1)}, f32[64,1152]{1,0:T(8,128)S(1)}, u32[]{:S(2)}, u32[]{:S(2)}) %collective-permute-start.4) | collective-permute-done | bytes 294944 | tf_op jit(solution)/shard_map/ppermute | solution.py:228
  340.6 7.0 %collective-permute-done.5 = f32[64,1152]{1,0:T(8,128)S(1)} collective-permute-done((f32[64,1152]{1,0:T(8,128)S(1)}, f32[64,1152]{1,0:T(8,128)S(1)}, u32[]{:S(2)}, u32[]{:S(2)}) %collective-permute-start.5) | collective-permute-done | bytes 294944 | tf_op jit(solution)/shard_map/ppermute | solution.py:228
  347.6 3.2 collective-permute-start.6
  (52 shorter events, 13.4 us)
Async XLA Ops:
  7.2 13.3 %copy-start = (bf16[128,64,128]{2,1,0:T(8,128)(2,1)S(1)}, bf16[128,64,128]{2,1,0:T(8,128)(2,1)}, u32[]{:S(2)}) copy-start(bf16[128,64,128]{2,1,0:T(8,128)(2,1)} %param.15) | copy-start | bytes 6291460
  33.9 8.4 %copy-start.8 = (bf16[64]{0:T(256)(128)(2,1)S(1)}, bf16[64]{0:T(256)(128)(2,1)}, u32[]{:S(2)}) copy-start(bf16[64]{0:T(256)(128)(2,1)} %param.24) | copy-start | bytes 388
  33.9 8.4 %copy-start.6 = (bf16[64,1024]{1,0:T(8,128)(2,1)S(1)}, bf16[64,1024]{1,0:T(8,128)(2,1)}, u32[]{:S(2)}) copy-start(bf16[64,1024]{1,0:T(8,128)(2,1)} %param.23) | copy-start | bytes 393220
  33.9 8.4 %copy-start.7 = (bf16[64,1024]{1,0:T(8,128)(2,1)S(1)}, bf16[64,1024]{1,0:T(8,128)(2,1)}, u32[]{:S(2)}) copy-start(bf16[64,1024]{1,0:T(8,128)(2,1)} %param.22) | copy-start | bytes 393220
  33.9 9.2 %copy-start.2 = (bf16[128,64,128]{2,1,0:T(8,128)(2,1)S(1)}, bf16[128,64,128]{2,1,0:T(8,128)(2,1)}, u32[]{:S(2)}) copy-start(bf16[128,64,128]{2,1,0:T(8,128)(2,1)} %param.16) | copy-start | bytes 6291460
  33.9 111.7 %all-to-all-start = ((bf16[128,4,64,128]{3,2,1,0:T(8,128)(2,1)}), bf16[128,4,64,128]{3,2,1,0:T(8,128)(2,1)}, u32[]{:S(2)}, u32[]{:S(2)}) async-start(bf16[128,4,64,128]{3,2,1,0:T(8,128)(2,1)} %bitcast.88), calls=%async_computation | async-start | bytes 16777216 | tf_op jit(solution)/shard_map/all_to_all | solution.py:178
  42.2 198.2 %all-gather.3.cloned.1.call-start = ((), (), s32[]{:S(2)}) async-start(), calls=%async_computation.3 | async-start | bytes 4734976 | tf_op jit(solution)/shard_map/all_gather | solution.py:160
  145.6 14.1 %copy-start.5 = (bf16[4,1024,128]{2,1,0:T(8,128)(2,1)S(1)}, bf16[4,1024,128]{2,1,0:T(8,128)(2,1)}, u32[]{:S(2)}) copy-start(bf16[4,1024,128]{2,1,0:T(8,128)(2,1)} %param.25) | copy-start | bytes 3145732
  145.6 127.2 %all-to-all-start.1 = ((bf16[128,4,64,128]{3,2,1,0:T(8,128)(2,1)}), bf16[128,4,64,128]{3,2,1,0:T(8,128)(2,1)}, u32[]{:S(2)}, u32[]{:S(2)}) async-start(bf16[128,4,64,128]{3,2,1,0:T(8,128)(2,1)} %bitcast.87), calls=%async_computation.1 | async-start | bytes 16777216 | tf_op jit(solution)/shard_map/all_to_all | solution.py:179
  159.7 125.1 %collective-permute-start.3 = (bf16[4,1024,128]{2,1,0:T(8,128)(2,1)S(1)}, bf16[4,1024,128]{2,1,0:T(8,128)(2,1)}, u32[]{:S(2)}, u32[]{:S(2)}) collective-permute-start(bf16[4,1024,128]{2,1,0:T(8,128)(2,1)S(1)} %copy-done.5), channel_id=1, source_target_pairs={{0,16},{16,0},{32,48},{48,32},{64,80},{80,64},{96,112},{112,96},{1... | collective-permute-start | bytes 3145736 | tf_op jit(solution)/shard_map/ppermute | solution.py:185
  172.2 115.4 %collective-permute-start = (bf16[4,16,32,128]{3,2,0,1:T(8,128)(2,1)}, bf16[4,16,32,128]{3,2,0,1:T(8,128)(2,1)}, u32[]{:S(2)}, u32[]{:S(2)}) collective-permute-start(bf16[4,16,32,128]{3,2,0,1:T(8,128)(2,1)} %bitcast.86), channel_id=1, source_target_pairs={{0,16},{16,0},{32,48},{48,32},{64,80},{80,64},{96,112},{112,96},{1... | collective-permute-start | bytes 1572872 | tf_op jit(solution)/shard_map/ppermute | solution.py:208
  244.2 5.8 %copy-start.4 = (bf16[4,1024,128]{2,1,0:T(8,128)(2,1)S(1)}, bf16[4,1024,128]{2,1,0:T(8,128)(2,1)}, u32[]{:S(2)}) copy-start(bf16[4,1024,128]{2,1,0:T(8,128)(2,1)} %shard_map.147) | copy-start | bytes 3145732
  250.1 4.5 %copy-start.3 = (f32[4,1024,128]{2,1,0:T(8,128)S(1)}, f32[4,1024,128]{2,1,0:T(8,128)}, u32[]{:S(2)}) copy-start(f32[4,1024,128]{2,1,0:T(8,128)} %shard_map.148) | copy-start | bytes 6291460
  257.0 30.6 %collective-permute-start.1 = (bf16[4,1024,128]{2,1,0:T(8,128)(2,1)S(1)}, bf16[4,1024,128]{2,1,0:T(8,128)(2,1)}, u32[]{:S(2)}, u32[]{:S(2)}) collective-permute-start(bf16[4,1024,128]{2,1,0:T(8,128)(2,1)S(1)} %get-tuple-element.21), channel_id=1, source_target_pairs={{0,16},{16,0},{32,48},{48,32},{64,80},{80,64},{96,112},{112,96},{1... | collective-permute-start | bytes 3145736 | tf_op jit(solution)/shard_map/ppermute | solution.py:208
  283.2 2.3 collective-permute-start.2
  331.5 8.2 %collective-permute-start.4 = (f32[64,1152]{1,0:T(8,128)S(1)}, f32[64,1152]{1,0:T(8,128)S(1)}, u32[]{:S(2)}, u32[]{:S(2)}) collective-permute-start(f32[64,1152]{1,0:T(8,128)S(1)} %convert_reduce_fusion), channel_id=1, source_target_pairs={{0,32},{16,48},{32,0},{48,16},{64,96},{80,112},{96,64},{112,80},{1... | collective-permute-start | bytes 884744 | tf_op jit(solution)/shard_map/ppermute | solution.py:228
  339.7 14.4 %copy-start.1 = (bf16[128,64,128]{2,1,0:T(8,128)(2,1)S(1)}, bf16[128,64,128]{2,1,0:T(8,128)(2,1)}, u32[]{:S(2)}) copy-start(bf16[128,64,128]{2,1,0:T(8,128)(2,1)} %param.15) | copy-start | bytes 6291460
  339.7 7.9 %collective-permute-start.5 = (f32[64,1152]{1,0:T(8,128)S(1)}, f32[64,1152]{1,0:T(8,128)S(1)}, u32[]{:S(2)}, u32[]{:S(2)}) collective-permute-start(f32[64,1152]{1,0:T(8,128)S(1)} %add.72), channel_id=1, source_target_pairs={{0,64},{16,80},{32,96},{48,112},{64,0},{80,16},{96,32},{112,48},{1... | collective-permute-start | bytes 884744 | tf_op jit(solution)/shard_map/ppermute | solution.py:228
  347.6 4.4 %collective-permute-start.6 = (f32[64,1152]{1,0:T(8,128)S(1)}, f32[64,1152]{1,0:T(8,128)S(1)}, u32[]{:S(2)}, u32[]{:S(2)}) collective-permute-start(f32[64,1152]{1,0:T(8,128)S(1)} %add.73), channel_id=1, source_target_pairs={{0,16},{16,0},{32,48},{48,32},{64,80},{80,64},{96,112},{112,96},{1... | collective-permute-start | bytes 884744 | tf_op jit(solution)/shard_map/ppermute | solution.py:229
Sparse Core Ops, SparseCore 0:
  45.2 195.1 all-gather.2
